TPU v7x, 32 devices: a whole 2x2x4 slice. The times are simulated.
32 devices in a mesh: lat: 8 (over y, x, core), lon: 4 (over z).
Axes of the slice: x: 2, y: 2, z: 4, core: 2. Of those that a mesh axis runs over, the one named last changes fastest.
Arguments:
- features: bfloat16 [192, 180, 256], P('lat', 'lon'), may hold values from -6 to 6
- obs_mask: int32 [192, 180, 8], P('lat', 'lon'), may hold values 0 or 1
- filter_taps: bfloat16 [192, 4, 3, 17], replicated, may hold values from 0.049804688 to 1
- band_width: int32 [192], replicated, may hold values from 1 to 8, as said below
- mixing: bfloat16 [8, 4, 32, 32], replicated, may hold values from -0.5 to 0.5
- cotangent: bfloat16 [192, 180, 256], P('lat', 'lon'), may hold values from -6 to 6
Outputs:
- infilled: bfloat16 [192, 180, 256], P('lat', 'lon')
- input_grad: bfloat16 [192, 180, 256], P('lat', 'lon')
- weight_grad: float32 [8, 4, 32, 32], replicated
Inputs may be any that keep to these rules, and one draw needn't show every extreme that they name: band_width is 8 at the first and last cycle and 1 at cycle 192 // 2.
All inputs are finite; a program needn't handle non-finite values. No bound on the sum of `obs_mask` on one device may be relied on, other than what follows from the above.
Results may differ from a plain program's by a relative error of at most 0.005.
Values may be sent and summed in bfloat16 or wider, within the bound.
No kernel may reach another device: no remote copies, remote signals or barrier semaphores. Data moves between devices by JAX's collectives and lax.ppermute only.
A program may use at most 128 MiB of HBM per device.

v0:
```python
import math

import jax
import jax.numpy as jnp
from jax import lax
from jax.sharding import PartitionSpec as P


def with_halo(block, sides, width, periodic):
    for axis, dim in sides:
        count = lax.axis_size(axis)
        forward = [(i, i + 1) for i in range(count - 1)]
        if periodic:
            forward.append((count - 1, 0))
        backward = [(target, source) for source, target in forward]
        low = lax.ppermute(
            lax.slice_in_dim(block, block.shape[dim] - width, None, axis=dim), axis, forward
        )
        high = lax.ppermute(lax.slice_in_dim(block, 0, width, axis=dim), axis, backward)
        block = jnp.concatenate([low, block, high], axis=dim)
    return block


def passed_along(block, axis, distance):
    devices = range(lax.axis_size(axis))
    route = [(i - distance, i) for i in devices if i - distance in devices]
    return lax.ppermute(block, axis, route)


def from_behind(x, axis, by):
    size = lax.axis_size(axis)
    return lax.ppermute(x, axis, [(i, (i + by) % size) for i in range(size)])


def local(features, obs_mask, filter_taps, band_width, mixing, cotangent):
    row_count, col_count, chan_count = features.shape
    group_count = obs_mask.shape[2]
    group_width = chan_count // group_count
    basis_count = mixing.shape[1]
    tap_count = filter_taps.shape[3]
    tap_reach = (tap_count - 1) // 2
    padded_cols = col_count + 2 * tap_reach
    mask_values = obs_mask.astype(jnp.bfloat16)
    masked = (
        features.reshape(row_count, col_count, group_count, group_width) * mask_values[..., None]
    ).reshape(row_count, col_count, chan_count)
    wide_input, wide_mask = (
        with_halo(masked, (("lon", 1),), tap_reach, True),
        with_halo(mask_values, (("lon", 1),), tap_reach, True),
    )
    full_input, full_mask = (
        with_halo(wide_input, (("lat", 0),), 1, False),
        with_halo(wide_mask, (("lat", 0),), 1, False),
    )
    offsets = jnp.arange(tap_count) - tap_reach
    allowed = jnp.abs(offsets)[None, :] <= band_width[:, None]
    global_taps = filter_taps * allowed[:, None, None, :].astype(jnp.bfloat16)
    first_row = lax.axis_index("lat") * row_count
    local_taps = lax.dynamic_slice_in_dim(global_taps, first_row, row_count, 0)
    padded_index = jnp.arange(padded_cols)
    output_index = jnp.arange(col_count)
    tap_index = jnp.arange(tap_count)
    forward_table = (
        padded_index[None, :, None] - output_index[None, None, :] == tap_index[:, None, None]
    ).astype(jnp.bfloat16)
    band_blocks = jnp.einsum(
        "ibed,dpj->ibepj", local_taps, forward_table, preferred_element_type=jnp.float32
    ).astype(jnp.bfloat16)
    numerator = jnp.zeros((row_count, basis_count, col_count, chan_count), jnp.float32)
    denominator = jnp.zeros((row_count, basis_count, col_count, group_count), jnp.float32)
    for lat_step in range(3):
        band_block = band_blocks[:, :, lat_step]
        numerator = numerator + jnp.einsum(
            "ibpj,ipc->ibjc",
            band_block,
            full_input[lat_step : lat_step + row_count],
            preferred_element_type=jnp.float32,
        )
        denominator = denominator + jnp.einsum(
            "ibpj,ipg->ibjg",
            band_block,
            full_mask[lat_step : lat_step + row_count],
            preferred_element_type=jnp.float32,
        )
    safe_denom = jnp.maximum(denominator, 1.0)
    scaled = (
        numerator.reshape(row_count, basis_count, col_count, group_count, group_width)
        / safe_denom[..., None]
    ).astype(jnp.bfloat16)
    infilled = (
        jnp.einsum("ibjgc,gbco->ijgo", scaled, mixing, preferred_element_type=jnp.float32)
        .reshape(row_count, col_count, chan_count)
        .astype(jnp.bfloat16)
    )
    upstream = cotangent.reshape(row_count, col_count, group_count, group_width)
    local_grad = jnp.einsum(
        "ibjgc,ijgo->gbco", scaled, upstream, preferred_element_type=jnp.float32
    )
    cell_count = row_count * lax.axis_size("lat") * col_count * lax.axis_size("lon")
    weight_grad = lax.psum(local_grad, ("lat", "lon")) * (1.0 / math.sqrt(cell_count))
    back_prop = jnp.einsum("ijgo,gbco->ibjgc", upstream, mixing, preferred_element_type=jnp.float32)
    pulled = (
        (back_prop / safe_denom[..., None])
        .astype(jnp.bfloat16)
        .reshape(row_count, basis_count, col_count, chan_count)
    )
    collected = jnp.zeros((row_count + 2, padded_cols, chan_count), jnp.float32)
    for lat_step in range(3):
        term_rows = jnp.einsum(
            "ibpj,ibjc->ipc",
            band_blocks[:, :, lat_step],
            pulled,
            preferred_element_type=jnp.float32,
        )
        collected = collected.at[lat_step : lat_step + row_count].add(term_rows)
    from_below = passed_along(collected[0:1], "lat", -1)
    from_above = passed_along(collected[row_count + 1 : row_count + 2], "lat", 1)
    inner_rows = collected[1 : row_count + 1]
    inner_rows = inner_rows.at[row_count - 1 : row_count].add(from_below)
    inner_rows = inner_rows.at[0:1].add(from_above)
    left_rim = inner_rows[:, :tap_reach]
    right_rim = inner_rows[:, col_count + tap_reach :]
    from_right = from_behind(left_rim.astype(jnp.bfloat16), "lon", -1).astype(left_rim.dtype)
    from_left = from_behind(right_rim, "lon", 1)
    gathered = inner_rows[:, tap_reach : tap_reach + col_count]
    gathered = gathered.at[:, col_count - tap_reach :].add(from_right)
    gathered = gathered.at[:, :tap_reach].add(from_left)
    input_grad = (
        (gathered.reshape(row_count, col_count, group_count, group_width) * mask_values[..., None])
        .reshape(row_count, col_count, chan_count)
        .astype(jnp.bfloat16)
    )
    return (infilled, input_grad, weight_grad)


def solution(mesh):
    placed = (P("lat", "lon", None), P("lat", "lon", None), P(), P(), P(), P("lat", "lon", None))
    return jax.shard_map(
        local,
        mesh=mesh,
        in_specs=placed,
        out_specs=(P("lat", "lon", None), P("lat", "lon", None), P()),
        check_vma=False,
    )
```

profile of v0, /device:TPU:0, one launch (start us, length us, event | category | flops | bytes accessed | tf_op | source)
XLA Modules:
  0.0 297.3 jit_solution(17708958694991090387)
XLA Ops:
  7.2 0.9 convert_element_type.43
  8.2 0.1 fusion.56
  8.2 3.1 %collective-permute-start.4 = (bf16[24,8,8]{1,2,0:T(8,128)(2,1)S(1)}, bf16[24,8,8]{1,2,0:T(8,128)(2,1)S(1)}, u32[]{:S(2)}, u32[]{:S(2)}) collective-permute-start(bf16[24,8,8]{1,2,0:T(8,128)(2,1)S(1)} %get-tuple-element.109), channel_id=1, source_target_pairs={{0,1},{1,2},{2,3},{3,0},{4,5},{5,6},{6,7},{7,4},{8,9},{9,10},{10,1... | collective-permute-start | bytes 9224 | tf_op jit(solution)/shard_map/ppermute | solution.py:16
  11.3 2.1 collective-permute-start.5
  13.5 0.3 copy.59
  13.7 0.8 compare_convert_fusion
  14.5 0.1 copy.57
  14.6 1.0 constant_dynamic-slice_fusion
  15.6 0.2 copy.113
  15.8 1.4 mul.42
  17.2 2.3 mul.43
  19.5 1.0 convolution_convert_fusion
  20.5 1.6 slice_bitcast_fusion
  22.1 0.2 copy_multiply_fusion.1
  22.3 3.9 %reshape.274 = bf16[24,45,8,32]{3,2,0,1:T(8,128)(2,1)} reshape(bf16[24,45,256]{2,0,1:T(8,128)(2,1)} %param.25) | data formatting | bytes 1105920 | tf_op jit(solution)/shard_map/reshape | solution.py:95
  26.2 4.9 %copy.97 = bf16[24,45,8,32,1]{1,3,0,4,2:T(8,128)(2,1)} copy(bf16[24,45,8,32,1]{3,2,0,1,4:T(8,128)(2,1)} %bitcast.110) | data formatting | bytes 1105920 | tf_op jit(solution)/shard_map/reshape | solution.py:95
  31.2 0.1 pad_maximum_fusion.21
  31.3 1.6 collective-permute-start.6
  32.9 1.5 collective-permute-start.7
  34.4 1.2 fusion.14
  35.6 2.1 collective-permute-done.7
  37.7 1.2 fusion.7
  38.9 1.2 fusion.4
  40.1 0.2 copy.69
  40.4 3.7 %fusion = bf16[24,4,45,8,32]{2,4,0,1,3:T(8,128)(2,1)} fusion(f32[24,4,45,8]{2,0,1,3:T(8,128)S(1)} %copy.69, bf16[24,45,8,32,1]{1,3,0,4,2:T(8,128)(2,1)S(1)} %copy-done.15, bf16[8,4,32,32]{3,2,1,0:T(8,128)(2,1)S(1)} %copy-done), kind=kOutput, calls=%fused_computation.1 | convolution fusion | flops 72990720 | bytes 2968576 | tf_op jit(solution)/shard_map/ijgo,gbco->ibjgc/dot_general | solution.py:101
  44.1 12.5 %copy.111 = bf16[24,4,45,8,32]{4,3,2,1,0:T(8,128)(2,1)} copy(bf16[24,4,45,8,32]{2,4,0,1,3:T(8,128)(2,1)} %fusion) | data formatting | bytes 4423680 | tf_op jit(solution)/shard_map/reshape | solution.py:105
  56.6 10.6 %reshape.294 = bf16[24,4,45,256]{3,2,1,0:T(8,128)(2,1)S(1)} reshape(bf16[24,4,45,8,32]{4,3,2,1,0:T(8,128)(2,1)} %copy.111) | data formatting | bytes 4423680 | tf_op jit(solution)/shard_map/reshape | solution.py:105
  67.2 1.9 convolution_bitcast_fusion
  69.1 0.2 scatter-add.24
  69.2 1.1 copy-done.6
  70.3 0.8 fusion.1
  71.1 0.4 copy-done.9
  71.5 2.1 constant_dynamic-update-slice_fusion
  73.6 1.2 copy-done.1
  74.9 1.3 collective-permute-start.8
  76.3 3.8 %collective-permute-start.1 = (bf16[24,8,256]{2,1,0:T(8,128)(2,1)S(1)}, bf16[24,8,256]{2,1,0:T(8,128)(2,1)S(1)}, u32[]{:S(2)}, u32[]{:S(2)}) collective-permute-start(bf16[24,8,256]{2,1,0:T(8,128)(2,1)S(1)} %get-tuple-element.106), channel_id=1, source_target_pairs={{1,0},{2,1},{3,2},{0,3},{5,4},{6,5},{7,6},{4,7},{9,8},{10,9},{11,1... | collective-permute-start | bytes 294920 | tf_op jit(solution)/shard_map/ppermute | solution.py:19
  80.1 0.3 copy.82
  80.3 3.2 %mul.45 = f32[24,45,8,32]{3,2,0,1:T(8,128)} broadcast(f32[24,45,8]{2,0,1:T(8,128)S(1)} %copy.82), dimensions={0,1,2} | broadcast | bytes 1140480 | tf_op jit(solution)/shard_map/mul | solution.py:129
  83.5 4.5 %mul.46 = f32[24,45,256]{2,0,1:T(8,128)} reshape(f32[24,45,8,32]{3,2,0,1:T(8,128)} %mul.45) | data formatting | bytes 2211840 | tf_op jit(solution)/shard_map/mul | solution.py:129
  88.0 0.1 slice.279
  88.2 1.0 fusion.52
  89.1 4.3 %collective-permute-start.9 = (f32[1,61,256]{2,1,0:T(8,128)S(1)}, f32[1,61,256]{2,1,0:T(8,128)S(1)}, u32[]{:S(2)}, u32[]{:S(2)}) collective-permute-start(f32[1,61,256]{2,1,0:T(8,128)S(1)} %get-tuple-element.101), channel_id=1, source_target_pairs={{0,4},{4,8},{8,12},{12,16},{16,20},{20,24},{24,28},{1,5},{5,9},{9,... | collective-permute-start | bytes 187400 | tf_op jit(solution)/shard_map/ppermute | solution.py:27
  93.5 0.1 pad_maximum_fusion.10
  93.6 1.3 collective-permute-start.3
  94.9 4.8 %collective-permute-start.2 = (bf16[1,61,256]{2,1,0:T(8,128)(2,1)S(1)}, bf16[1,61,256]{2,1,0:T(8,128)(2,1)S(1)}, u32[]{:S(2)}, u32[]{:S(2)}) collective-permute-start(bf16[1,61,256]{2,1,0:T(8,128)(2,1)S(1)} %get-tuple-element.104), channel_id=1, source_target_pairs={{0,4},{4,8},{8,12},{12,16},{16,20},{20,24},{24,28},{1,5},{5,9},{9,... | collective-permute-start | bytes 93704 | tf_op jit(solution)/shard_map/ppermute | solution.py:16
  99.8 0.8 fusion.16
  100.6 1.1 slice.284
  101.7 0.7 copy-done.4
  102.5 0.8 fusion.20
  103.2 3.0 add_add_fusion
  106.2 11.7 %reshape.293 = f32[24,4,45,8,32]{4,3,2,1,0:T(8,128)} reshape(f32[24,4,45,256]{3,2,1,0:T(8,128)} %add_add_fusion) | data formatting | bytes 8847360 | tf_op jit(solution)/shard_map/reshape | solution.py:87
  117.9 17.1 %copy.70 = f32[24,4,45,8,32]{2,4,0,1,3:T(8,128)} copy(f32[24,4,45,8,32]{4,3,2,1,0:T(8,128)} %reshape.293) | data formatting | bytes 8847360 | tf_op jit(solution)/shard_map/reshape | solution.py:87
  135.0 9.5 %divide_convert_fusion = bf16[24,4,45,8,32]{2,4,0,1,3:T(8,128)(2,1)} fusion(f32[24,4,45,8,32]{2,4,0,1,3:T(8,128)} %copy.70, f32[24,4,45,8]{2,0,1,3:T(8,128)S(1)} %copy-done.18), kind=kLoop, calls=%fused_computation.2 | loop fusion | flops 2211840 | bytes 6773760 | tf_op jit(solution)/shard_map/convert_element_type | solution.py:89
  144.5 5.4 %convolution_bitcast_fusion.1 = f32[8,4,32,32]{3,2,1,0:T(8,128)} fusion(bf16[24,4,45,8,32]{2,4,0,1,3:T(8,128)(2,1)} %divide_convert_fusion, bf16[24,45,8,32,1]{1,3,0,4,2:T(8,128)(2,1)S(1)} %copy-done.16), kind=kOutput, calls=%fused_computation.11 | convolution fusion | flops 70778880 | bytes 2895872 | tf_op jit(solution)/shard_map/ibjgc,ijgo->gbco/dot_general | solution.py:96
  149.8 4.9 %fusion.2 = bf16[24,45,8,32]{1,3,0,2:T(8,128)(2,1)} fusion(bf16[24,4,45,8,32]{2,4,0,1,3:T(8,128)(2,1)} %divide_convert_fusion, bf16[8,4,32,32]{3,2,1,0:T(8,128)(2,1)S(1)} %copy-done), kind=kOutput, calls=%fused_computation.9 | convolution fusion | flops 71055360 | bytes 2830336 | tf_op jit(solution)/shard_map/ibjgc,gbco->ijgo/dot_general | solution.py:91
  154.8 5.2 %copy.73 = bf16[24,45,8,32]{3,2,0,1:T(8,128)(2,1)S(1)} copy(bf16[24,45,8,32]{1,3,0,2:T(8,128)(2,1)} %fusion.2) | data formatting | bytes 1105920 | tf_op jit(solution)/shard_map/convert_element_type | solution.py:93
  160.0 2.3 convert_element_type.47
  162.4 1.3 fusion.51
  163.7 1.4 collective-permute-start.11
  165.1 121.7 %all-reduce.3.cloned.1.call-done = f32[8,4,32,32]{3,2,1,0:T(8,128)} async-done(((f32[8,4,32,32]{3,2,1,0:T(8,128)}), f32[8,4,32,32]{3,2,1,0:T(8,128)}) %all-reduce.3.cloned.1.call-update) | async-done | bytes 131088 | tf_op jit(solution)/shard_map/psum | solution.py:100
  286.7 1.9 broadcast_multiply_fusion
  288.6 0.3 scatter-add.31
  289.0 0.5 fusion.5
  289.4 1.0 copy.85
  (61 shorter events, 0.4 us)
Async XLA Ops:
  7.2 33.2 %copy-start = (bf16[8,4,32,32]{3,2,1,0:T(8,128)(2,1)S(1)}, bf16[8,4,32,32]{3,2,1,0:T(8,128)(2,1)}, u32[]{:S(2)}) copy-start(bf16[8,4,32,32]{3,2,1,0:T(8,128)(2,1)} %param.24) | copy-start | bytes 196612
  7.2 279.5 %all-reduce.3.cloned.1.call-start = ((), (), s32[]{:S(2)}) async-start(), calls=%async_computation | async-start | bytes 1048576 | tf_op jit(solution)/shard_map/psum | solution.py:100
  8.2 22.9 %collective-permute-start.4 = (bf16[24,8,8]{1,2,0:T(8,128)(2,1)S(1)}, bf16[24,8,8]{1,2,0:T(8,128)(2,1)S(1)}, u32[]{:S(2)}, u32[]{:S(2)}) collective-permute-start(bf16[24,8,8]{1,2,0:T(8,128)(2,1)S(1)} %get-tuple-element.109), channel_id=1, source_target_pairs={{0,1},{1,2},{2,3},{3,0},{4,5},{5,6},{6,7},{7,4},{8,9},{9,10},{10,1... | collective-permute-start | bytes 9224 | tf_op jit(solution)/shard_map/ppermute | solution.py:16
  11.3 19.8 %collective-permute-start.5 = (bf16[24,8,8]{1,2,0:T(8,128)(2,1)S(1)}, bf16[24,8,8]{1,2,0:T(8,128)(2,1)S(1)}, u32[]{:S(2)}, u32[]{:S(2)}) collective-permute-start(bf16[24,8,8]{1,2,0:T(8,128)(2,1)S(1)} %get-tuple-element.110), channel_id=1, source_target_pairs={{1,0},{2,1},{3,2},{0,3},{5,4},{6,5},{7,6},{4,7},{9,8},{10,9},{11,1... | collective-permute-start | bytes 9224 | tf_op jit(solution)/shard_map/ppermute | solution.py:19
  20.5 1.6 copy-start.14
  20.5 1.6 copy-start.19
  22.1 12.2 %copy-start.5 = (bf16[24,4,61,45]{2,0,3,1:T(8,128)(2,1)}, bf16[24,4,61,45]{2,0,3,1:T(8,128)(2,1)S(1)}, u32[]{:S(2)}) copy-start(bf16[24,4,61,45]{2,0,3,1:T(8,128)(2,1)S(1)} %get-tuple-element.97) | copy-start | bytes 1581124
  22.1 16.8 %copy-start.3 = (bf16[24,4,61,45]{2,0,3,1:T(8,128)(2,1)}, bf16[24,4,61,45]{2,0,3,1:T(8,128)(2,1)S(1)}, u32[]{:S(2)}) copy-start(bf16[24,4,61,45]{2,0,3,1:T(8,128)(2,1)S(1)} %get-tuple-element.98) | copy-start | bytes 1581124
  31.2 6.5 %copy-start.8 = (bf16[24,4,61,45]{2,0,3,1:T(8,128)(2,1)S(1)}, bf16[24,4,61,45]{2,0,3,1:T(8,128)(2,1)}, u32[]{:S(2)}) copy-start(bf16[24,4,61,45]{2,0,3,1:T(8,128)(2,1)} %get-tuple-element.96) | copy-start | bytes 1581124
  31.3 7.6 %collective-permute-start.6 = (bf16[1,61,8]{1,2,0:T(8,128)(2,1)S(1)}, bf16[1,61,8]{1,2,0:T(8,128)(2,1)S(1)}, u32[]{:S(2)}, u32[]{:S(2)}) collective-permute-start(bf16[1,61,8]{1,2,0:T(8,128)(2,1)S(1)} %get-tuple-element.107), channel_id=1, source_target_pairs={{0,4},{4,8},{8,12},{12,16},{16,20},{20,24},{24,28},{1,5},{5,9},{9,... | collective-permute-start | bytes 2936 | tf_op jit(solution)/shard_map/ppermute | solution.py:16
  32.9 4.8 %collective-permute-start.7 = (bf16[1,61,8]{1,2,0:T(8,128)(2,1)S(1)}, bf16[1,61,8]{1,2,0:T(8,128)(2,1)S(1)}, u32[]{:S(2)}, u32[]{:S(2)}) collective-permute-start(bf16[1,61,8]{1,2,0:T(8,128)(2,1)S(1)} %get-tuple-element.108), channel_id=1, source_target_pairs={{4,0},{8,4},{12,8},{16,12},{20,16},{24,20},{28,24},{5,1},{9,5},{13... | collective-permute-start | bytes 2936 | tf_op jit(solution)/shard_map/ppermute | solution.py:19
  38.9 1.5 copy-start.15
  40.4 3.7 %copy-start.17 = (f32[24,4,45,8]{2,0,1,3:T(8,128)}, f32[24,4,45,8]{2,0,1,3:T(8,128)S(1)}, u32[]{:S(2)}) copy-start(f32[24,4,45,8]{2,0,1,3:T(8,128)S(1)} %copy.69) | copy-start | bytes 414724
  69.1 1.2 copy-start.6
  70.3 1.2 copy-start.9
  73.6 1.2 copy-start.1
  74.9 13.3 %collective-permute-start.8 = (f32[1,61,256]{2,1,0:T(8,128)S(1)}, f32[1,61,256]{2,1,0:T(8,128)S(1)}, u32[]{:S(2)}, u32[]{:S(2)}) collective-permute-start(f32[1,61,256]{2,1,0:T(8,128)S(1)} %slice.281), channel_id=1, source_target_pairs={{4,0},{8,4},{12,8},{16,12},{20,16},{24,20},{28,24},{5,1},{9,5},{13... | collective-permute-start | bytes 187400 | tf_op jit(solution)/shard_map/ppermute | solution.py:27
  76.2 17.3 %collective-permute-start = (bf16[24,8,256]{2,1,0:T(8,128)(2,1)S(1)}, bf16[24,8,256]{2,1,0:T(8,128)(2,1)S(1)}, u32[]{:S(2)}, u32[]{:S(2)}) collective-permute-start(bf16[24,8,256]{2,1,0:T(8,128)(2,1)S(1)} %get-tuple-element.105), channel_id=1, source_target_pairs={{0,1},{1,2},{2,3},{3,0},{4,5},{5,6},{6,7},{7,4},{8,9},{9,10},{10,1... | collective-permute-start | bytes 294920 | tf_op jit(solution)/shard_map/ppermute | solution.py:16
  76.3 17.2 %collective-permute-start.1 = (bf16[24,8,256]{2,1,0:T(8,128)(2,1)S(1)}, bf16[24,8,256]{2,1,0:T(8,128)(2,1)S(1)}, u32[]{:S(2)}, u32[]{:S(2)}) collective-permute-start(bf16[24,8,256]{2,1,0:T(8,128)(2,1)S(1)} %get-tuple-element.106), channel_id=1, source_target_pairs={{1,0},{2,1},{3,2},{0,3},{5,4},{6,5},{7,6},{4,7},{9,8},{10,9},{11,1... | collective-permute-start | bytes 294920 | tf_op jit(solution)/shard_map/ppermute | solution.py:19
  83.5 4.5 %copy-start.2 = (f32[26,61,256]{2,1,0:T(8,128)S(1)}, f32[26,61,256]{2,1,0:T(8,128)}, u32[]{:S(2)}) copy-start(f32[26,61,256]{2,1,0:T(8,128)} %copy-done.1) | copy-start | bytes 4872196
  88.1 11.6 %copy-start.7 = (bf16[24,4,61,45]{2,0,3,1:T(8,128)(2,1)S(1)}, bf16[24,4,61,45]{2,0,3,1:T(8,128)(2,1)}, u32[]{:S(2)}) copy-start(bf16[24,4,61,45]{2,0,3,1:T(8,128)(2,1)} %copy-done.5) | copy-start | bytes 1581124
  89.1 11.4 %collective-permute-start.9 = (f32[1,61,256]{2,1,0:T(8,128)S(1)}, f32[1,61,256]{2,1,0:T(8,128)S(1)}, u32[]{:S(2)}, u32[]{:S(2)}) collective-permute-start(f32[1,61,256]{2,1,0:T(8,128)S(1)} %get-tuple-element.101), channel_id=1, source_target_pairs={{0,4},{4,8},{8,12},{12,16},{16,20},{20,24},{24,28},{1,5},{5,9},{9,... | collective-permute-start | bytes 187400 | tf_op jit(solution)/shard_map/ppermute | solution.py:27
  93.6 9.6 %collective-permute-start.3 = (bf16[1,61,256]{2,1,0:T(8,128)(2,1)S(1)}, bf16[1,61,256]{2,1,0:T(8,128)(2,1)S(1)}, u32[]{:S(2)}, u32[]{:S(2)}) collective-permute-start(bf16[1,61,256]{2,1,0:T(8,128)(2,1)S(1)} %get-tuple-element.103), channel_id=1, source_target_pairs={{4,0},{8,4},{12,8},{16,12},{20,16},{24,20},{28,24},{5,1},{9,5},{13... | collective-permute-start | bytes 93704 | tf_op jit(solution)/shard_map/ppermute | solution.py:19
  94.9 6.8 %collective-permute-start.2 = (bf16[1,61,256]{2,1,0:T(8,128)(2,1)S(1)}, bf16[1,61,256]{2,1,0:T(8,128)(2,1)S(1)}, u32[]{:S(2)}, u32[]{:S(2)}) collective-permute-start(bf16[1,61,256]{2,1,0:T(8,128)(2,1)S(1)} %get-tuple-element.104), channel_id=1, source_target_pairs={{0,4},{4,8},{8,12},{12,16},{16,20},{20,24},{24,28},{1,5},{5,9},{9,... | collective-permute-start | bytes 93704 | tf_op jit(solution)/shard_map/ppermute | solution.py:16
  100.5 1.9 copy-start.4
  100.6 2.7 copy-start.11
  101.7 1.5 copy-start.10
  101.7 60.6 %collective-permute-start.10 = (bf16[24,8,256]{2,1,0:T(8,128)(2,1)S(1)}, bf16[24,8,256]{2,1,0:T(8,128)(2,1)S(1)}, u32[]{:S(2)}, u32[]{:S(2)}) collective-permute-start(bf16[24,8,256]{2,1,0:T(8,128)(2,1)S(1)} %slice.305), channel_id=1, source_target_pairs={{0,3},{1,0},{2,1},{3,2},{4,7},{5,4},{6,5},{7,6},{8,11},{9,8},{10,9... | collective-permute-start | bytes 294920 | tf_op jit(solution)/shard_map/ppermute | solution.py:32
  117.9 17.1 %copy-start.18 = (f32[24,4,45,8]{2,0,1,3:T(8,128)S(1)}, f32[24,4,45,8]{2,0,1,3:T(8,128)}, u32[]{:S(2)}) copy-start(f32[24,4,45,8]{2,0,1,3:T(8,128)} %copy-done.17) | copy-start | bytes 414724
  135.0 9.5 %copy-start.16 = (bf16[24,45,8,32,1]{1,3,0,4,2:T(8,128)(2,1)S(1)}, bf16[24,45,8,32,1]{1,3,0,4,2:T(8,128)(2,1)}, u32[]{:S(2)}) copy-start(bf16[24,45,8,32,1]{1,3,0,4,2:T(8,128)(2,1)} %copy.97) | copy-start | bytes 1658884
  162.4 126.3 %copy-start.12 = (f32[24,45,256]{2,1,0:T(8,128)S(1)}, f32[24,45,256]{2,1,0:T(8,128)}, u32[]{:S(2)}) copy-start(f32[24,45,256]{2,1,0:T(8,128)} %slice.284) | copy-start | bytes 3317764
  162.4 126.6 %copy-start.13 = (f32[24,45,256]{2,0,1:T(8,128)S(1)}, f32[24,45,256]{2,0,1:T(8,128)}, u32[]{:S(2)}) copy-start(f32[24,45,256]{2,0,1:T(8,128)} %mul.46) | copy-start | bytes 3317764
  163.7 125.2 %collective-permute-start.11 = (f32[24,8,256]{2,1,0:T(8,128)S(1)}, f32[24,8,256]{2,1,0:T(8,128)S(1)}, u32[]{:S(2)}, u32[]{:S(2)}) collective-permute-start(f32[24,8,256]{2,1,0:T(8,128)S(1)} %get-tuple-element.99), channel_id=1, source_target_pairs={{0,1},{1,2},{2,3},{3,0},{4,5},{5,6},{6,7},{7,4},{8,9},{9,10},{10,1... | collective-permute-start | bytes 589832 | tf_op jit(solution)/shard_map/ppermute | solution.py:32
Sparse Core Ops, SparseCore 0:
  154.9 131.7 all-reduce.2
where the time goes:
time: 299 us; the launch traced here: 297 us
  waiting for transfers between devices  124 us (41%)
  local copies, waits for them, and re-layouts  89.6 us (30%)
  matrix products  27.9 us (9%)
  starting transfers between devices  25.3 us (8%)
  other arithmetic  16.3 us (5%)
  between operations  14.5 us (5%)
    psum x1, waiting for transfers between devices, local(): lax.psum(local_grad, ('lat', 'lon')) * (1.0 / math.sqrt(cell_count))  122 us
    reshape x2, local copies, waits for them, and re-layouts, local(): numerator.reshape(row_count, basis_count, col_count, group_count, group_w...  28.8 us
    reshape x2, local copies, waits for them, and re-layouts, local(): pulled = (back_prop / safe_denom[..., None]).astype(jnp.bfloat16).reshape...  23.1 us
    ppermute x4, starting transfers between devices, with_halo(): lax.ppermute(lax.slice_in_dim(block, block.shape[dim] - width, None, axis...  9.58 us
    convert_element_type x1, other arithmetic, local(): scaled = (numerator.reshape(row_count, basis_count, col_count, group_coun...  9.49 us
    reshape x2, local copies, waits for them, and re-layouts, local(): upstream = cotangent.reshape(row_count, col_count, group_count, group_width)  8.84 us
    ppermute x4, starting transfers between devices, with_halo(): lax.ppermute(lax.slice_in_dim(block, 0, width, axis=dim), axis, backward)  8.67 us
    mul x2, local copies, waits for them, and re-layouts, local(): gathered.reshape(row_count, col_count, group_count, group_width)  7.63 us
  transfers between devices with their start and end apart: 13, of which 2 were waited for; matrix products, arithmetic and copies ran while one was open for 32% of the time, Pallas kernels for 0%

commit v1 on v0

--- a/solution.py
+++ b/solution.py
@@ -30,6 +30,20 @@
 def from_behind(x, axis, by):
     size = lax.axis_size(axis)
     return lax.ppermute(x, axis, [(i, (i + by) % size) for i in range(size)])
+
+
+def butterfly_sum(value, axes):
+    for axis in axes:
+        count = lax.axis_size(axis)
+        if count & (count - 1):
+            value = lax.psum(value, axis)
+            continue
+        step = 1
+        while step < count:
+            partner = lax.ppermute(value, axis, [(i, i ^ step) for i in range(count)])
+            value = value + partner
+            step *= 2
+    return value
 
 
 def local(features, obs_mask, filter_taps, band_width, mixing, cotangent):
@@ -97,7 +111,7 @@
         "ibjgc,ijgo->gbco", scaled, upstream, preferred_element_type=jnp.float32
     )
     cell_count = row_count * lax.axis_size("lat") * col_count * lax.axis_size("lon")
-    weight_grad = lax.psum(local_grad, ("lat", "lon")) * (1.0 / math.sqrt(cell_count))
+    weight_grad = butterfly_sum(local_grad, ("lon", "lat")) * (1.0 / math.sqrt(cell_count))
     back_prop = jnp.einsum("ijgo,gbco->ibjgc", upstream, mixing, preferred_element_type=jnp.float32)
     pulled = (
         (back_prop / safe_denom[..., None])

time: 299 us -> 225 us (0.75)
  waiting for transfers between devices: 124 us -> 59.2 us
  between operations: 14.5 us -> 1.12 us
  starting transfers between devices: 25.3 us -> 31.2 us
    psum x1 -> x0, waiting for transfers between devices: 122 us -> none  [local(): lax.psum(local_grad, ('lat', 'lon')) * (1.0 / math.sqrt(cell_count))]
    ppermute x0 -> x5, waiting for transfers between devices: none -> 56.3 us  [butterfly_sum(): partner = lax.ppermute(value, axis, [(i, i ^ step) for i in range(count)])]
    ppermute x0 -> x5, starting transfers between devices: none -> 5.44 us  [butterfly_sum(): partner = lax.ppermute(value, axis, [(i, i ^ step) for i in range(count)])]
  transfers between devices with their start and end apart: 13 -> 17, of which waited for: 2 -> 6; matrix products, arithmetic and copies ran while one was open for 32% -> 43% of each run, Pallas kernels for 0% -> 0%
where the time goes in v1:
time: 225 us; the launch traced here: 223 us
  local copies, waits for them, and re-layouts  88.9 us (40%)
  waiting for transfers between devices  59.2 us (26%)
  starting transfers between devices  31.2 us (14%)
  matrix products  26.4 us (12%)
  other arithmetic  16.4 us (7%)
    ppermute x5, waiting for transfers between devices, butterfly_sum(): partner = lax.ppermute(value, axis, [(i, i ^ step) for i in range(count)])  56.3 us
    reshape x2, local copies, waits for them, and re-layouts, local(): numerator.reshape(row_count, basis_count, col_count, group_count, group_w...  28.7 us
    reshape x2, local copies, waits for them, and re-layouts, local(): pulled = (back_prop / safe_denom[..., None]).astype(jnp.bfloat16).reshape...  23.1 us
    ppermute x4, starting transfers between devices, with_halo(): lax.ppermute(lax.slice_in_dim(block, block.shape[dim] - width, None, axis...  9.81 us
    convert_element_type x1, other arithmetic, local(): scaled = (numerator.reshape(row_count, basis_count, col_count, group_coun...  9.36 us
    reshape x2, local copies, waits for them, and re-layouts, local(): upstream = cotangent.reshape(row_count, col_count, group_count, group_width)  8.82 us
    ppermute x4, starting transfers between devices, with_halo(): lax.ppermute(lax.slice_in_dim(block, 0, width, axis=dim), axis, backward)  8.67 us
    convert_element_type x2, local copies, waits for them, and re-layouts, local(): infilled = jnp.einsum('ibjgc,gbco->ijgo', scaled, mixing, preferred_eleme...  7.53 us
  transfers between devices with their start and end apart: 17, of which 6 were waited for; matrix products, arithmetic and copies ran while one was open for 43% of the time, Pallas kernels for 0%

profile of v1, /device:TPU:0, one launch (start us, length us, event | category | flops | bytes accessed | tf_op | source)
XLA Modules:
  0.0 223.2 jit_solution(2409607782765063517)
XLA Ops:
  0.6 0.9 convert_element_type.43
  1.7 3.1 %collective-permute-start.4 = (bf16[24,8,8]{1,2,0:T(8,128)(2,1)S(1)}, bf16[24,8,8]{1,2,0:T(8,128)(2,1)S(1)}, u32[]{:S(2)}, u32[]{:S(2)}) collective-permute-start(bf16[24,8,8]{1,2,0:T(8,128)(2,1)S(1)} %get-tuple-element.109), channel_id=1, source_target_pairs={{0,1},{1,2},{2,3},{3,0},{4,5},{5,6},{6,7},{7,4},{8,9},{9,10},{10,1... | collective-permute-start | bytes 9224 | tf_op jit(solution)/shard_map/ppermute | solution.py:16
  4.8 2.1 collective-permute-start.5
  6.9 0.3 copy.59
  7.2 0.8 compare_convert_fusion
  8.1 1.0 constant_dynamic-slice_fusion
  9.2 1.4 mul.42
  10.6 2.3 %mul.43 = bf16[24,45,256]{2,0,1:T(8,128)(2,1)} reshape(bf16[24,45,8,32]{3,2,0,1:T(8,128)(2,1)S(1)} %mul.42) | data formatting | bytes 1105920 | tf_op jit(solution)/shard_map/mul | solution.py:59
  12.9 1.0 convolution_convert_fusion
  14.0 1.6 slice_bitcast_fusion
  15.6 0.2 copy_multiply_fusion.1
  15.7 3.9 %reshape.274 = bf16[24,45,8,32]{3,2,0,1:T(8,128)(2,1)} reshape(bf16[24,45,256]{2,0,1:T(8,128)(2,1)} %param.25) | data formatting | bytes 1105920 | tf_op jit(solution)/shard_map/reshape | solution.py:109
  19.7 4.9 %copy.97 = bf16[24,45,8,32,1]{1,3,0,4,2:T(8,128)(2,1)} copy(bf16[24,45,8,32,1]{3,2,0,1,4:T(8,128)(2,1)} %bitcast.110) | data formatting | bytes 1105920 | tf_op jit(solution)/shard_map/reshape | solution.py:109
  24.7 1.6 collective-permute-start.6
  26.3 1.5 collective-permute-start.7
  27.8 1.2 fusion.14
  29.0 2.1 collective-permute-done.7
  31.1 1.2 fusion.7
  32.3 1.2 fusion.4
  33.6 0.2 copy.69
  33.8 3.7 %fusion = bf16[24,4,45,8,32]{2,4,0,1,3:T(8,128)(2,1)} fusion(f32[24,4,45,8]{2,0,1,3:T(8,128)S(1)} %copy.69, bf16[24,45,8,32,1]{1,3,0,4,2:T(8,128)(2,1)S(1)} %copy-done.10, bf16[8,4,32,32]{3,2,1,0:T(8,128)(2,1)S(1)} %copy-done), kind=kOutput, calls=%fused_computation.1 | convolution fusion | flops 72990720 | bytes 2968576 | tf_op jit(solution)/shard_map/ijgo,gbco->ibjgc/dot_general | solution.py:115
  37.5 12.6 %copy.111 = bf16[24,4,45,8,32]{4,3,2,1,0:T(8,128)(2,1)} copy(bf16[24,4,45,8,32]{2,4,0,1,3:T(8,128)(2,1)} %fusion) | data formatting | bytes 4423680 | tf_op jit(solution)/shard_map/reshape | solution.py:119
  50.1 10.6 %reshape.294 = bf16[24,4,45,256]{3,2,1,0:T(8,128)(2,1)S(1)} reshape(bf16[24,4,45,8,32]{4,3,2,1,0:T(8,128)(2,1)} %copy.111) | data formatting | bytes 4423680 | tf_op jit(solution)/shard_map/reshape | solution.py:119
  60.6 1.9 convolution_bitcast_fusion
  62.5 0.2 scatter-add.24
  62.7 1.1 copy-done.4
  63.8 0.8 fusion.1
  64.6 0.4 copy-done.6
  65.0 0.9 constant_dynamic-update-slice_fusion
  65.9 1.3 collective-permute-start.8
  67.3 3.8 %collective-permute-start.1 = (bf16[24,8,256]{2,1,0:T(8,128)(2,1)S(1)}, bf16[24,8,256]{2,1,0:T(8,128)(2,1)S(1)}, u32[]{:S(2)}, u32[]{:S(2)}) collective-permute-start(bf16[24,8,256]{2,1,0:T(8,128)(2,1)S(1)} %get-tuple-element.106), channel_id=1, source_target_pairs={{1,0},{2,1},{3,2},{0,3},{5,4},{6,5},{7,6},{4,7},{9,8},{10,9},{11,1... | collective-permute-start | bytes 294920 | tf_op jit(solution)/shard_map/ppermute | solution.py:19
  71.4 4.4 %collective-permute-start.9 = (f32[1,61,256]{2,1,0:T(8,128)S(1)}, f32[1,61,256]{2,1,0:T(8,128)S(1)}, u32[]{:S(2)}, u32[]{:S(2)}) collective-permute-start(f32[1,61,256]{2,1,0:T(8,128)S(1)} %get-tuple-element.101), channel_id=1, source_target_pairs={{0,4},{4,8},{8,12},{12,16},{16,20},{20,24},{24,28},{1,5},{5,9},{9,... | collective-permute-start | bytes 187400 | tf_op jit(solution)/shard_map/ppermute | solution.py:27
  75.9 1.3 collective-permute-start.3
  77.3 5.1 %collective-permute-start.2 = (bf16[1,61,256]{2,1,0:T(8,128)(2,1)S(1)}, bf16[1,61,256]{2,1,0:T(8,128)(2,1)S(1)}, u32[]{:S(2)}, u32[]{:S(2)}) collective-permute-start(bf16[1,61,256]{2,1,0:T(8,128)(2,1)S(1)} %get-tuple-element.104), channel_id=1, source_target_pairs={{0,4},{4,8},{8,12},{12,16},{16,20},{20,24},{24,28},{1,5},{5,9},{9,... | collective-permute-start | bytes 93704 | tf_op jit(solution)/shard_map/ppermute | solution.py:16
  82.3 0.8 fusion.16
  83.1 0.8 fusion.20
  83.9 3.0 %add_add_fusion = f32[24,4,45,256]{3,2,1,0:T(8,128)} fusion(f32[24,4,45,256]{3,2,1,0:T(8,128)S(1)} %fusion.20, f32[24,4,45,256]{3,2,1,0:T(8,128)S(1)} %fusion.16, bf16[24,4,61,45]{2,0,3,1:T(8,128)(2,1)S(1)} %copy-done.6, bf16[1,61,256]{2,1,0:T(8,128)(2,1)S(1)} %collective-permute-done.3, bf16[24,8,256]{2,1,0:T(8,128)(2,1)S(1)} %collective-permute-done.1, ...), kind=kOutput, calls=%fused_computation.3 | convolution fusion | flops 140132352 | bytes 14578880 | tf_op jit(solution)/shard_map/ibpj,ipc->ibjc/dot_general | solution.py:87
  86.8 11.7 %reshape.293 = f32[24,4,45,8,32]{4,3,2,1,0:T(8,128)} reshape(f32[24,4,45,256]{3,2,1,0:T(8,128)} %add_add_fusion) | data formatting | bytes 8847360 | tf_op jit(solution)/shard_map/reshape | solution.py:101
  98.6 17.0 %copy.70 = f32[24,4,45,8,32]{2,4,0,1,3:T(8,128)} copy(f32[24,4,45,8,32]{4,3,2,1,0:T(8,128)} %reshape.293) | data formatting | bytes 8847360 | tf_op jit(solution)/shard_map/reshape | solution.py:101
  115.6 9.4 %divide_convert_fusion = bf16[24,4,45,8,32]{2,4,0,1,3:T(8,128)(2,1)} fusion(f32[24,4,45,8,32]{2,4,0,1,3:T(8,128)} %copy.70, f32[24,4,45,8]{2,0,1,3:T(8,128)S(1)} %copy-done.12), kind=kLoop, calls=%fused_computation.2 | loop fusion | flops 2211840 | bytes 6773760 | tf_op jit(solution)/shard_map/convert_element_type | solution.py:103
  124.9 5.0 %convolution_bitcast_fusion.1 = f32[8,4,32,32]{3,2,1,0:T(8,128)S(1)} fusion(bf16[24,4,45,8,32]{2,4,0,1,3:T(8,128)(2,1)} %divide_convert_fusion, bf16[24,45,8,32,1]{1,3,0,4,2:T(8,128)(2,1)} %copy.97), kind=kOutput, calls=%fused_computation.11 | convolution fusion | flops 70778880 | bytes 2895872 | tf_op jit(solution)/shard_map/ibjgc,ijgo->gbco/dot_general | solution.py:110
  130.0 1.2 collective-permute-start.10
  131.2 0.3 copy.82
  131.5 3.1 %mul.45 = f32[24,45,8,32]{3,2,0,1:T(8,128)} broadcast(f32[24,45,8]{2,0,1:T(8,128)S(1)} %copy.82), dimensions={0,1,2} | broadcast | bytes 1140480 | tf_op jit(solution)/shard_map/mul | solution.py:143
  134.6 4.3 %mul.46 = f32[24,45,256]{2,0,1:T(8,128)} reshape(f32[24,45,8,32]{3,2,0,1:T(8,128)} %mul.45) | data formatting | bytes 2211840 | tf_op jit(solution)/shard_map/mul | solution.py:143
  138.9 1.2 slice.284
  140.1 4.0 %collective-permute-done.12 = f32[8,4,32,32]{3,2,1,0:T(8,128)} collective-permute-done((f32[8,4,32,32]{3,2,1,0:T(8,128)S(1)}, f32[8,4,32,32]{3,2,1,0:T(8,128)}, u32[]{:S(2)}, u32[]{:S(2)}) %collective-permute-start.12) | collective-permute-done | bytes 131104 | tf_op jit(solution)/shard_map/ppermute | solution.py:43
  144.1 1.1 add.95
  145.3 0.8 collective-permute-done.10
  146.2 0.3 collective-permute-start.11
  146.5 28.8 %collective-permute-done.13 = f32[8,4,32,32]{3,2,1,0:T(8,128)S(1)} collective-permute-done((f32[8,4,32,32]{3,2,1,0:T(8,128)S(1)}, f32[8,4,32,32]{3,2,1,0:T(8,128)S(1)}, u32[]{:S(2)}, u32[]{:S(2)}) %collective-permute-start.13) | collective-permute-done | bytes 131104 | tf_op jit(solution)/shard_map/ppermute | solution.py:43
  175.3 0.2 collective-permute-start.14
  175.5 5.0 %fusion.2 = bf16[24,45,8,32]{1,3,0,2:T(8,128)(2,1)} fusion(bf16[24,4,45,8,32]{2,4,0,1,3:T(8,128)(2,1)} %divide_convert_fusion, bf16[8,4,32,32]{3,2,1,0:T(8,128)(2,1)S(1)} %copy-done), kind=kOutput, calls=%fused_computation.9 | convolution fusion | flops 71055360 | bytes 2830336 | tf_op jit(solution)/shard_map/ibjgc,gbco->ijgo/dot_general | solution.py:105
  180.5 5.2 %copy.73 = bf16[24,45,8,32]{3,2,0,1:T(8,128)(2,1)S(1)} copy(bf16[24,45,8,32]{1,3,0,2:T(8,128)(2,1)} %fusion.2) | data formatting | bytes 1105920 | tf_op jit(solution)/shard_map/convert_element_type | solution.py:107
  185.7 2.3 %convert_element_type.47 = bf16[24,45,256]{2,0,1:T(8,128)(2,1)} reshape(bf16[24,45,8,32]{3,2,0,1:T(8,128)(2,1)S(1)} %copy.73) | data formatting | bytes 1105920 | tf_op jit(solution)/shard_map/convert_element_type | solution.py:107
  188.0 1.8 scatter-add.31
  189.8 1.3 add.97
  191.1 5.0 %collective-permute-start.15 = (f32[8,4,32,32]{3,2,1,0:T(8,128)S(1)}, f32[8,4,32,32]{3,2,1,0:T(8,128)S(1)}, u32[]{:S(2)}, u32[]{:S(2)}) collective-permute-start(f32[8,4,32,32]{3,2,1,0:T(8,128)S(1)} %add.97), channel_id=1, source_target_pairs={{0,8},{4,12},{8,0},{12,4},{16,24},{20,28},{24,16},{28,20},{1,9},{5... | collective-permute-start | bytes 393224 | tf_op jit(solution)/shard_map/ppermute | solution.py:43
  196.2 1.0 fusion.34
  197.1 11.5 %collective-permute-done.15 = f32[8,4,32,32]{3,2,1,0:T(8,128)S(1)} collective-permute-done((f32[8,4,32,32]{3,2,1,0:T(8,128)S(1)}, f32[8,4,32,32]{3,2,1,0:T(8,128)S(1)}, u32[]{:S(2)}, u32[]{:S(2)}) %collective-permute-start.15) | collective-permute-done | bytes 131104 | tf_op jit(solution)/shard_map/ppermute | solution.py:43
  208.8 0.5 fusion.5
  209.3 1.0 copy.85
  210.2 12.1 %collective-permute-done.16 = f32[8,4,32,32]{3,2,1,0:T(8,128)S(1)} collective-permute-done((f32[8,4,32,32]{3,2,1,0:T(8,128)S(1)}, f32[8,4,32,32]{3,2,1,0:T(8,128)S(1)}, u32[]{:S(2)}, u32[]{:S(2)}) %collective-permute-start.16) | collective-permute-done | bytes 131104 | tf_op jit(solution)/shard_map/ppermute | solution.py:43
  222.4 0.9 add_multiply_fusion
  (60 shorter events, 1.4 us)
Async XLA Ops:
  0.6 33.2 %copy-start = (bf16[8,4,32,32]{3,2,1,0:T(8,128)(2,1)S(1)}, bf16[8,4,32,32]{3,2,1,0:T(8,128)(2,1)}, u32[]{:S(2)}) copy-start(bf16[8,4,32,32]{3,2,1,0:T(8,128)(2,1)} %param.24) | copy-start | bytes 196612
  1.7 22.9 %collective-permute-start.4 = (bf16[24,8,8]{1,2,0:T(8,128)(2,1)S(1)}, bf16[24,8,8]{1,2,0:T(8,128)(2,1)S(1)}, u32[]{:S(2)}, u32[]{:S(2)}) collective-permute-start(bf16[24,8,8]{1,2,0:T(8,128)(2,1)S(1)} %get-tuple-element.109), channel_id=1, source_target_pairs={{0,1},{1,2},{2,3},{3,0},{4,5},{5,6},{6,7},{7,4},{8,9},{9,10},{10,1... | collective-permute-start | bytes 9224 | tf_op jit(solution)/shard_map/ppermute | solution.py:16
  4.8 19.8 %collective-permute-start.5 = (bf16[24,8,8]{1,2,0:T(8,128)(2,1)S(1)}, bf16[24,8,8]{1,2,0:T(8,128)(2,1)S(1)}, u32[]{:S(2)}, u32[]{:S(2)}) collective-permute-start(bf16[24,8,8]{1,2,0:T(8,128)(2,1)S(1)} %get-tuple-element.110), channel_id=1, source_target_pairs={{1,0},{2,1},{3,2},{0,3},{5,4},{6,5},{7,6},{4,7},{9,8},{10,9},{11,1... | collective-permute-start | bytes 9224 | tf_op jit(solution)/shard_map/ppermute | solution.py:19
  13.9 1.6 copy-start.9
  14.0 1.6 copy-start.13
  15.6 12.2 %copy-start.3 = (bf16[24,4,61,45]{2,0,3,1:T(8,128)(2,1)}, bf16[24,4,61,45]{2,0,3,1:T(8,128)(2,1)S(1)}, u32[]{:S(2)}) copy-start(bf16[24,4,61,45]{2,0,3,1:T(8,128)(2,1)S(1)} %get-tuple-element.97) | copy-start | bytes 1581124
  15.6 16.7 %copy-start.1 = (bf16[24,4,61,45]{2,0,3,1:T(8,128)(2,1)}, bf16[24,4,61,45]{2,0,3,1:T(8,128)(2,1)S(1)}, u32[]{:S(2)}) copy-start(bf16[24,4,61,45]{2,0,3,1:T(8,128)(2,1)S(1)} %get-tuple-element.98) | copy-start | bytes 1581124
  24.6 6.5 %copy-start.5 = (bf16[24,4,61,45]{2,0,3,1:T(8,128)(2,1)S(1)}, bf16[24,4,61,45]{2,0,3,1:T(8,128)(2,1)}, u32[]{:S(2)}) copy-start(bf16[24,4,61,45]{2,0,3,1:T(8,128)(2,1)} %get-tuple-element.96) | copy-start | bytes 1581124
  24.7 7.6 %collective-permute-start.6 = (bf16[1,61,8]{1,2,0:T(8,128)(2,1)S(1)}, bf16[1,61,8]{1,2,0:T(8,128)(2,1)S(1)}, u32[]{:S(2)}, u32[]{:S(2)}) collective-permute-start(bf16[1,61,8]{1,2,0:T(8,128)(2,1)S(1)} %get-tuple-element.107), channel_id=1, source_target_pairs={{0,4},{4,8},{8,12},{12,16},{16,20},{20,24},{24,28},{1,5},{5,9},{9,... | collective-permute-start | bytes 2936 | tf_op jit(solution)/shard_map/ppermute | solution.py:16
  26.3 4.8 %collective-permute-start.7 = (bf16[1,61,8]{1,2,0:T(8,128)(2,1)S(1)}, bf16[1,61,8]{1,2,0:T(8,128)(2,1)S(1)}, u32[]{:S(2)}, u32[]{:S(2)}) collective-permute-start(bf16[1,61,8]{1,2,0:T(8,128)(2,1)S(1)} %get-tuple-element.108), channel_id=1, source_target_pairs={{4,0},{8,4},{12,8},{16,12},{20,16},{24,20},{28,24},{5,1},{9,5},{13... | collective-permute-start | bytes 2936 | tf_op jit(solution)/shard_map/ppermute | solution.py:19
  32.3 1.5 copy-start.10
  33.8 3.7 %copy-start.11 = (f32[24,4,45,8]{2,0,1,3:T(8,128)}, f32[24,4,45,8]{2,0,1,3:T(8,128)S(1)}, u32[]{:S(2)}) copy-start(f32[24,4,45,8]{2,0,1,3:T(8,128)S(1)} %copy.69) | copy-start | bytes 414724
  62.5 1.2 copy-start.4
  63.8 1.2 copy-start.6
  65.9 5.4 %collective-permute-start.8 = (f32[1,61,256]{2,1,0:T(8,128)S(1)}, f32[1,61,256]{2,1,0:T(8,128)S(1)}, u32[]{:S(2)}, u32[]{:S(2)}) collective-permute-start(f32[1,61,256]{2,1,0:T(8,128)S(1)} %slice.281), channel_id=1, source_target_pairs={{4,0},{8,4},{12,8},{16,12},{20,16},{24,20},{28,24},{5,1},{9,5},{13... | collective-permute-start | bytes 187400 | tf_op jit(solution)/shard_map/ppermute | solution.py:27
  67.3 8.5 %collective-permute-start = (bf16[24,8,256]{2,1,0:T(8,128)(2,1)S(1)}, bf16[24,8,256]{2,1,0:T(8,128)(2,1)S(1)}, u32[]{:S(2)}, u32[]{:S(2)}) collective-permute-start(bf16[24,8,256]{2,1,0:T(8,128)(2,1)S(1)} %get-tuple-element.105), channel_id=1, source_target_pairs={{0,1},{1,2},{2,3},{3,0},{4,5},{5,6},{6,7},{7,4},{8,9},{9,10},{10,1... | collective-permute-start | bytes 294920 | tf_op jit(solution)/shard_map/ppermute | solution.py:16
  67.3 8.5 %collective-permute-start.1 = (bf16[24,8,256]{2,1,0:T(8,128)(2,1)S(1)}, bf16[24,8,256]{2,1,0:T(8,128)(2,1)S(1)}, u32[]{:S(2)}, u32[]{:S(2)}) collective-permute-start(bf16[24,8,256]{2,1,0:T(8,128)(2,1)S(1)} %get-tuple-element.106), channel_id=1, source_target_pairs={{1,0},{2,1},{3,2},{0,3},{5,4},{6,5},{7,6},{4,7},{9,8},{10,9},{11,1... | collective-permute-start | bytes 294920 | tf_op jit(solution)/shard_map/ppermute | solution.py:19
  71.4 58.6 %collective-permute-start.9 = (f32[1,61,256]{2,1,0:T(8,128)S(1)}, f32[1,61,256]{2,1,0:T(8,128)S(1)}, u32[]{:S(2)}, u32[]{:S(2)}) collective-permute-start(f32[1,61,256]{2,1,0:T(8,128)S(1)} %get-tuple-element.101), channel_id=1, source_target_pairs={{0,4},{4,8},{8,12},{12,16},{16,20},{20,24},{24,28},{1,5},{5,9},{9,... | collective-permute-start | bytes 187400 | tf_op jit(solution)/shard_map/ppermute | solution.py:27
  75.9 7.9 %collective-permute-start.3 = (bf16[1,61,256]{2,1,0:T(8,128)(2,1)S(1)}, bf16[1,61,256]{2,1,0:T(8,128)(2,1)S(1)}, u32[]{:S(2)}, u32[]{:S(2)}) collective-permute-start(bf16[1,61,256]{2,1,0:T(8,128)(2,1)S(1)} %get-tuple-element.103), channel_id=1, source_target_pairs={{4,0},{8,4},{12,8},{16,12},{20,16},{24,20},{28,24},{5,1},{9,5},{13... | collective-permute-start | bytes 93704 | tf_op jit(solution)/shard_map/ppermute | solution.py:19
  77.2 5.9 %copy-start.2 = (bf16[24,4,61,45]{2,0,3,1:T(8,128)(2,1)S(1)}, bf16[24,4,61,45]{2,0,3,1:T(8,128)(2,1)}, u32[]{:S(2)}) copy-start(bf16[24,4,61,45]{2,0,3,1:T(8,128)(2,1)} %copy-done.1) | copy-start | bytes 1581124
  77.3 5.8 %collective-permute-start.2 = (bf16[1,61,256]{2,1,0:T(8,128)(2,1)S(1)}, bf16[1,61,256]{2,1,0:T(8,128)(2,1)S(1)}, u32[]{:S(2)}, u32[]{:S(2)}) collective-permute-start(bf16[1,61,256]{2,1,0:T(8,128)(2,1)S(1)} %get-tuple-element.104), channel_id=1, source_target_pairs={{0,4},{4,8},{8,12},{12,16},{16,20},{20,24},{24,28},{1,5},{5,9},{9,... | collective-permute-start | bytes 93704 | tf_op jit(solution)/shard_map/ppermute | solution.py:16
  98.6 17.0 %copy-start.12 = (f32[24,4,45,8]{2,0,1,3:T(8,128)S(1)}, f32[24,4,45,8]{2,0,1,3:T(8,128)}, u32[]{:S(2)}) copy-start(f32[24,4,45,8]{2,0,1,3:T(8,128)} %copy-done.11) | copy-start | bytes 414724
  129.9 14.2 %collective-permute-start.12 = (f32[8,4,32,32]{3,2,1,0:T(8,128)S(1)}, f32[8,4,32,32]{3,2,1,0:T(8,128)}, u32[]{:S(2)}, u32[]{:S(2)}) collective-permute-start(f32[8,4,32,32]{3,2,1,0:T(8,128)S(1)} %convolution_bitcast_fusion.1), channel_id=1, source_target_pairs={{0,1},{1,0},{2,3},{3,2},{4,5},{5,4},{6,7},{7,6},{8,9},{9,8},{10,11... | collective-permute-start | bytes 393224 | tf_op jit(solution)/shard_map/ppermute | solution.py:43
  130.0 16.1 %collective-permute-start.10 = (bf16[24,8,256]{2,1,0:T(8,128)(2,1)S(1)}, bf16[24,8,256]{2,1,0:T(8,128)(2,1)S(1)}, u32[]{:S(2)}, u32[]{:S(2)}) collective-permute-start(bf16[24,8,256]{2,1,0:T(8,128)(2,1)S(1)} %slice.305), channel_id=1, source_target_pairs={{0,3},{1,0},{2,1},{3,2},{4,7},{5,4},{6,5},{7,6},{8,11},{9,8},{10,9... | collective-permute-start | bytes 294920 | tf_op jit(solution)/shard_map/ppermute | solution.py:32
  145.2 30.0 %collective-permute-start.13 = (f32[8,4,32,32]{3,2,1,0:T(8,128)S(1)}, f32[8,4,32,32]{3,2,1,0:T(8,128)S(1)}, u32[]{:S(2)}, u32[]{:S(2)}) collective-permute-start(f32[8,4,32,32]{3,2,1,0:T(8,128)S(1)} %add.95), channel_id=1, source_target_pairs={{0,2},{1,3},{2,0},{3,1},{4,6},{5,7},{6,4},{7,5},{8,10},{9,11},{10,... | collective-permute-start | bytes 393224 | tf_op jit(solution)/shard_map/ppermute | solution.py:43
  146.2 50.0 %collective-permute-start.11 = (f32[24,8,256]{2,1,0:T(8,128)S(1)}, f32[24,8,256]{2,1,0:T(8,128)}, u32[]{:S(2)}, u32[]{:S(2)}) collective-permute-start(f32[24,8,256]{2,1,0:T(8,128)S(1)} %get-tuple-element.99), channel_id=1, source_target_pairs={{0,1},{1,2},{2,3},{3,0},{4,5},{5,6},{6,7},{7,4},{8,9},{9,10},{10,1... | collective-permute-start | bytes 589832 | tf_op jit(solution)/shard_map/ppermute | solution.py:32
  175.3 14.5 %collective-permute-start.14 = (f32[8,4,32,32]{3,2,1,0:T(8,128)S(1)}, f32[8,4,32,32]{3,2,1,0:T(8,128)}, u32[]{:S(2)}, u32[]{:S(2)}) collective-permute-start(f32[8,4,32,32]{3,2,1,0:T(8,128)S(1)} %add.96), channel_id=1, source_target_pairs={{0,4},{4,0},{8,12},{12,8},{16,20},{20,16},{24,28},{28,24},{1,5},{5... | collective-permute-start | bytes 393224 | tf_op jit(solution)/shard_map/ppermute | solution.py:43
  189.8 6.3 %copy-start.7 = (f32[24,45,256]{2,1,0:T(8,128)S(1)}, f32[24,45,256]{2,1,0:T(8,128)}, u32[]{:S(2)}) copy-start(f32[24,45,256]{2,1,0:T(8,128)} %scatter-add.31) | copy-start | bytes 3317764
  189.8 18.9 %copy-start.8 = (f32[24,45,256]{2,0,1:T(8,128)S(1)}, f32[24,45,256]{2,0,1:T(8,128)}, u32[]{:S(2)}) copy-start(f32[24,45,256]{2,0,1:T(8,128)} %mul.46) | copy-start | bytes 3317764
  191.1 17.5 %collective-permute-start.15 = (f32[8,4,32,32]{3,2,1,0:T(8,128)S(1)}, f32[8,4,32,32]{3,2,1,0:T(8,128)S(1)}, u32[]{:S(2)}, u32[]{:S(2)}) collective-permute-start(f32[8,4,32,32]{3,2,1,0:T(8,128)S(1)} %add.97), channel_id=1, source_target_pairs={{0,8},{4,12},{8,0},{12,4},{16,24},{20,28},{24,16},{28,20},{1,9},{5... | collective-permute-start | bytes 393224 | tf_op jit(solution)/shard_map/ppermute | solution.py:43
  208.7 13.7 %collective-permute-start.16 = (f32[8,4,32,32]{3,2,1,0:T(8,128)S(1)}, f32[8,4,32,32]{3,2,1,0:T(8,128)S(1)}, u32[]{:S(2)}, u32[]{:S(2)}) collective-permute-start(f32[8,4,32,32]{3,2,1,0:T(8,128)S(1)} %add.98), channel_id=1, source_target_pairs={{0,16},{4,20},{8,24},{12,28},{16,0},{20,4},{24,8},{28,12},{1,17},{... | collective-permute-start | bytes 393224 | tf_op jit(solution)/shard_map/ppermute | solution.py:43

commit v2 on v1

v2 whole, which is shorter than its diff:
```python
import math

import jax
import jax.numpy as jnp
from jax import lax
from jax.experimental import pallas as pl
from jax.experimental.pallas import tpu as pltpu
from jax.sharding import PartitionSpec as P


def with_halo(block, sides, width, periodic):
    for axis, dim in sides:
        count = lax.axis_size(axis)
        forward = [(i, i + 1) for i in range(count - 1)]
        if periodic:
            forward.append((count - 1, 0))
        backward = [(target, source) for source, target in forward]
        low = lax.ppermute(
            lax.slice_in_dim(block, block.shape[dim] - width, None, axis=dim), axis, forward
        )
        high = lax.ppermute(lax.slice_in_dim(block, 0, width, axis=dim), axis, backward)
        block = jnp.concatenate([low, block, high], axis=dim)
    return block


def passed_along(block, axis, distance):
    devices = range(lax.axis_size(axis))
    route = [(i - distance, i) for i in devices if i - distance in devices]
    return lax.ppermute(block, axis, route)


def from_behind(x, axis, by):
    size = lax.axis_size(axis)
    return lax.ppermute(x, axis, [(i, (i + by) % size) for i in range(size)])


def butterfly_sum(value, axes):
    for axis in axes:
        count = lax.axis_size(axis)
        if count & (count - 1):
            value = lax.psum(value, axis)
            continue
        step = 1
        while step < count:
            partner = lax.ppermute(value, axis, [(i, i ^ step) for i in range(count)])
            value = value + partner
            step *= 2
    return value


def conv_kernel(x_ref, m_ref, t_ref, cot_ref, w_ref, wt_ref, inf_ref, wg_ref, col_ref, pulled_ref):
    rows = t_ref.shape[0]
    basis_count = w_ref.shape[0]
    col_pad = cot_ref.shape[1]
    col_count = inf_ref.shape[1]
    lane_rows = x_ref.shape[0] // (rows + 2)
    window = 3 * lane_rows
    col_ref[...] = jnp.zeros_like(col_ref)
    wg_ref[...] = jnp.zeros_like(wg_ref)

    def body(i, carry):
        start = pl.multiple_of(i * lane_rows, lane_rows)
        band = t_ref[i]
        numerator = jnp.dot(band, x_ref[pl.ds(start, window), :], preferred_element_type=jnp.float32)
        denominator = jnp.dot(band, m_ref[pl.ds(start, window), :], preferred_element_type=jnp.float32)
        safe = jnp.maximum(denominator, 1.0)
        scaled = (numerator / safe).astype(jnp.bfloat16)
        upstream = cot_ref[i]
        out = jnp.zeros((col_pad, upstream.shape[1]), jnp.float32)
        for b in range(basis_count):
            part = scaled[b * col_pad : (b + 1) * col_pad]
            out = out + jnp.dot(part, w_ref[b], preferred_element_type=jnp.float32)
            wg_ref[b] += lax.dot_general(
                part, upstream, (((0,), (0,)), ((), ())), preferred_element_type=jnp.float32
            )
            back = jnp.dot(upstream, wt_ref[b], preferred_element_type=jnp.float32)
            pulled_ref[b * col_pad : (b + 1) * col_pad, :] = (
                back / safe[b * col_pad : (b + 1) * col_pad]
            ).astype(jnp.bfloat16)
        inf_ref[i] = out[:col_count].astype(inf_ref.dtype)
        term = lax.dot_general(
            band, pulled_ref[...], (((0,), (0,)), ((), ())), preferred_element_type=jnp.float32
        )
        col_ref[pl.ds(start, window), :] += term
        return carry

    lax.fori_loop(0, rows, body, 0)


def local(features, obs_mask, filter_taps, band_width, mixing, cotangent):
    row_count, col_count, chan_count = features.shape
    group_count = obs_mask.shape[2]
    group_width = chan_count // group_count
    basis_count = mixing.shape[1]
    tap_count = filter_taps.shape[3]
    tap_reach = (tap_count - 1) // 2
    padded_cols = col_count + 2 * tap_reach
    lane_rows = -(-padded_cols // 16) * 16
    col_pad = -(-col_count // 16) * 16
    mask_values = obs_mask.astype(jnp.bfloat16)
    masked = (
        features.reshape(row_count, col_count, group_count, group_width) * mask_values[..., None]
    ).reshape(row_count, col_count, chan_count)
    packed = jnp.concatenate([masked, mask_values], axis=-1)
    packed = with_halo(packed, (("lat", 0),), 1, False)
    packed = with_halo(packed, (("lon", 1),), tap_reach, True)
    packed = jnp.pad(packed, ((0, 0), (0, lane_rows - padded_cols), (0, 0)))
    full_input = packed[..., :chan_count].reshape((row_count + 2) * lane_rows, chan_count)
    full_mask = jnp.repeat(packed[..., chan_count:], group_width, axis=-1).reshape(
        (row_count + 2) * lane_rows, chan_count
    )

    offsets = jnp.arange(tap_count) - tap_reach
    allowed = jnp.abs(offsets)[None, :] <= band_width[:, None]
    global_taps = filter_taps * allowed[:, None, None, :].astype(jnp.bfloat16)
    first_row = lax.axis_index("lat") * row_count
    local_taps = lax.dynamic_slice_in_dim(global_taps, first_row, row_count, 0)
    padded_index = jnp.arange(lane_rows)
    output_index = jnp.arange(col_pad)
    tap_index = jnp.arange(tap_count)
    forward_table = (
        (padded_index[None, None, :] - output_index[None, :, None] == tap_index[:, None, None])
        & (output_index[None, :, None] < col_count)
    ).astype(jnp.bfloat16)
    band = (
        jnp.einsum("ibae,ejp->ibjap", local_taps, forward_table, preferred_element_type=jnp.float32)
        .astype(jnp.bfloat16)
        .reshape(row_count, basis_count * col_pad, 3 * lane_rows)
    )

    eye = jnp.eye(group_count, dtype=mixing.dtype)
    mix_blocks = jnp.einsum("gbco,gh->bgcho", mixing, eye).reshape(basis_count, chan_count, chan_count)
    mix_blocks_t = jnp.einsum("gbco,gh->bhogc", mixing, eye).reshape(
        basis_count, chan_count, chan_count
    )
    upstream = jnp.pad(cotangent, ((0, 0), (0, col_pad - col_count), (0, 0)))

    infilled, grad_blocks, collected = pl.pallas_call(
        conv_kernel,
        out_shape=(
            jax.ShapeDtypeStruct((row_count, col_count, chan_count), jnp.bfloat16),
            jax.ShapeDtypeStruct((basis_count, chan_count, chan_count), jnp.float32),
            jax.ShapeDtypeStruct(((row_count + 2) * lane_rows, chan_count), jnp.float32),
        ),
        in_specs=[pl.BlockSpec(memory_space=pltpu.VMEM)] * 6,
        out_specs=[pl.BlockSpec(memory_space=pltpu.VMEM)] * 3,
        scratch_shapes=[pltpu.VMEM((basis_count * col_pad, chan_count), jnp.bfloat16)],
        compiler_params=pltpu.CompilerParams(vmem_limit_bytes=48 * 1024 * 1024),
    )(full_input, full_mask, band, upstream, mix_blocks, mix_blocks_t)

    diagonal = jnp.eye(group_count, dtype=jnp.float32)[None, :, None, :, None]
    local_grad = jnp.sum(
        grad_blocks.reshape(basis_count, group_count, group_width, group_count, group_width)
        * diagonal,
        axis=3,
    ).transpose(1, 0, 2, 3)
    cell_count = row_count * lax.axis_size("lat") * col_count * lax.axis_size("lon")
    weight_grad = butterfly_sum(local_grad, ("lon", "lat")) * (1.0 / math.sqrt(cell_count))

    collected = collected.reshape(row_count + 2, lane_rows, chan_count)[:, :padded_cols]
    from_below = passed_along(collected[0:1], "lat", -1)
    from_above = passed_along(collected[row_count + 1 : row_count + 2], "lat", 1)
    inner_rows = collected[1 : row_count + 1]
    inner_rows = inner_rows.at[row_count - 1 : row_count].add(from_below)
    inner_rows = inner_rows.at[0:1].add(from_above)
    left_rim = inner_rows[:, :tap_reach]
    right_rim = inner_rows[:, col_count + tap_reach :]
    from_right = from_behind(left_rim.astype(jnp.bfloat16), "lon", -1).astype(left_rim.dtype)
    from_left = from_behind(right_rim, "lon", 1)
    gathered = inner_rows[:, tap_reach : tap_reach + col_count]
    gathered = gathered.at[:, col_count - tap_reach :].add(from_right)
    gathered = gathered.at[:, :tap_reach].add(from_left)
    input_grad = (
        (gathered.reshape(row_count, col_count, group_count, group_width) * mask_values[..., None])
        .reshape(row_count, col_count, chan_count)
        .astype(jnp.bfloat16)
    )
    return (infilled, input_grad, weight_grad)


def solution(mesh):
    placed = (P("lat", "lon", None), P("lat", "lon", None), P(), P(), P(), P("lat", "lon", None))
    return jax.shard_map(
        local,
        mesh=mesh,
        in_specs=placed,
        out_specs=(P("lat", "lon", None), P("lat", "lon", None), P()),
        check_vma=False,
    )
```

time: 225 us -> 182 us (0.81)
  local copies, waits for them, and re-layouts: 88.9 us -> 58.1 us
  matrix products: 26.4 us -> 1.13 us
  Pallas kernels: 0 us -> 19.9 us
  starting transfers between devices: 31.2 us -> 19.1 us
  waiting for transfers between devices: 59.2 us -> 66.1 us
    reshape x6 -> x5, local copies, waits for them, and re-layouts: 60.7 us -> 19.7 us  [the longest x1 9.47 us: local(): band = jnp.einsum('ibae,ejp->ibjap', local_taps, forward_table, preferred...]
    dot_general x13 -> x1, matrix products: 26.4 us -> 1.13 us  [local(): jnp.einsum('ibae,ejp->ibjap', local_taps, forward_table, preferred_elemen...]
    pallas_call x0 -> x1, Pallas kernels: none -> 19.9 us  [local(): pl.pallas_call(conv_kernel, out_shape=(jax.ShapeDtypeStruct((row_count, c...]
    convert_element_type x1, other arithmetic: 9.36 us -> 0.01 us  [local(): diagonal = jnp.eye(group_count, dtype=jnp.float32)[None, :, None, :, None]]
    another operation x0 -> x3, local copies, waits for them, and re-layouts: none -> 5.6 us  [the longest x2 5.51 us: local(): jnp.repeat(packed[..., chan_count:], group_width, axis=-1)]
    ppermute x4 -> x2, starting transfers between devices: 8.67 us -> 3.56 us  [with_halo(): lax.ppermute(lax.slice_in_dim(block, 0, width, axis=dim), axis, backward)]
    ppermute x4 -> x2, starting transfers between devices: 9.81 us -> 4.84 us  [with_halo(): lax.ppermute(lax.slice_in_dim(block, block.shape[dim] - width, None, axis...]
    slice x5, local copies, waits for them, and re-layouts: 0.13 us -> 4.46 us  [the longest x2 2.83 us: local(): packed[..., :chan_count].reshape((row_count + 2) * lane_rows, chan_count)]
  transfers between devices with their start and end apart: 17 -> 13, of which waited for: 6 -> 7; matrix products, arithmetic and copies ran while one was open for 43% -> 26% of each run, Pallas kernels for 0% -> 0%
where the time goes in v2:
time: 182 us; the launch traced here: 181 us
  waiting for transfers between devices  66.1 us (36%)
  local copies, waits for them, and re-layouts  58.1 us (32%)
  Pallas kernels  19.9 us (11%)
  starting transfers between devices  19.1 us (10%)
  other arithmetic  15.5 us (9%)
    ppermute x5, waiting for transfers between devices, butterfly_sum(): partner = lax.ppermute(value, axis, [(i, i ^ step) for i in range(count)])  56.4 us
    pallas_call x1, Pallas kernels, local(): pl.pallas_call(conv_kernel, out_shape=(jax.ShapeDtypeStruct((row_count, c...  19.9 us
    reshape x1, local copies, waits for them, and re-layouts, local(): band = jnp.einsum('ibae,ejp->ibjap', local_taps, forward_table, preferred...  9.47 us
    mul x2, local copies, waits for them, and re-layouts, local(): gathered.reshape(row_count, col_count, group_count, group_width)  6.66 us
    unnamed x29, local copies, waits for them, and re-layouts  6.59 us
    ppermute x2, waiting for transfers between devices, with_halo(): lax.ppermute(lax.slice_in_dim(block, 0, width, axis=dim), axis, backward)  5.63 us
    another operation x2, local copies, waits for them, and re-layouts, local(): jnp.repeat(packed[..., chan_count:], group_width, axis=-1)  5.51 us
    ppermute x2, starting transfers between devices, with_halo(): lax.ppermute(lax.slice_in_dim(block, block.shape[dim] - width, None, axis...  4.84 us
  transfers between devices with their start and end apart: 13, of which 7 were waited for; matrix products, arithmetic and copies ran while one was open for 26% of the time, Pallas kernels for 0%

profile of v2, /device:TPU:0, one launch (start us, length us, event | category | flops | bytes accessed | tf_op | source)
XLA Modules:
  0.0 180.9 jit_solution(4328485906002541977)
XLA Ops:
  0.6 1.2 copy.56
  1.9 1.4 mul.47
  3.3 1.5 mul.48
  4.9 1.3 mul.49
  6.1 0.8 pad_maximum_fusion.5
  6.9 2.4 %collective-permute-start = (bf16[1,45,264]{2,0,1:T(2,128)(2,1)}, bf16[1,45,264]{2,0,1:T(2,128)(2,1)S(1)}, u32[]{:S(2)}, u32[]{:S(2)}) collective-permute-start(bf16[1,45,264]{2,0,1:T(2,128)(2,1)} %get-tuple-element.76), channel_id=1, source_target_pairs={{0,4},{4,8},{8,12},{12,16},{16,20},{20,24},{24,28},{1,5},{5,9},{9,... | collective-permute-start | bytes 71288 | tf_op jit(solution)/shard_map/ppermute | solution.py:18
  9.3 1.3 collective-permute-start.1
  10.7 0.1 constant_dynamic-slice_fusion
  10.8 0.2 copy.79
  11.0 0.1 copy.59
  11.2 0.2 copy.64
  11.5 1.7 multiply_bitcast_fusion
  13.2 1.1 convert_bitcast_fusion
  14.4 4.8 %copy.61 = bf16[24,4,48,3,64]{4,3,2,1,0:T(4,128)(2,1)} copy(bf16[24,4,48,3,64]{4,0,3,1,2:T(8,128)(2,1)S(1)} %convert_bitcast_fusion) | data formatting | bytes 3538944 | tf_op jit(solution)/shard_map/convert_element_type | solution.py:127
  19.2 9.5 %reshape.209.t_ref = bf16[24,192,192]{2,1,0:T(8,128)(2,1)} reshape(bf16[24,4,48,3,64]{4,3,2,1,0:T(4,128)(2,1)} %copy.61) | data formatting | bytes 3538944 | tf_op jit(solution)/shard_map/reshape | solution.py:128
  28.7 2.1 %reshape.216 = bf16[4,256,256]{1,2,0:T(8,128)(2,1)} reshape(bf16[4,8,32,8,32]{2,1,4,3,0:T(8,128)(2,1)S(1)} %get-tuple-element.79) | data formatting | bytes 1048576 | tf_op jit(solution)/shard_map/reshape | solution.py:132
  30.8 1.3 copy.74.w_ref
  32.1 3.1 %reshape.211.wt_ref = bf16[4,256,256]{2,1,0:T(8,128)(2,1)S(1)} reshape(bf16[4,8,32,8,32]{4,3,2,1,0:T(8,128)(2,1)} %get-tuple-element.78) | data formatting | bytes 1048576 | tf_op jit(solution)/shard_map/reshape | solution.py:133
  35.2 0.1 copy.62
  35.4 0.2 pad_maximum_fusion.3
  35.6 2.4 %collective-permute-start.2 = (bf16[26,8,264]{2,0,1:T(8,128)(2,1)S(1)}, bf16[26,8,264]{2,0,1:T(8,128)(2,1)S(1)}, u32[]{:S(2)}, u32[]{:S(2)}) collective-permute-start(bf16[26,8,264]{2,0,1:T(8,128)(2,1)S(1)} %get-tuple-element.74), channel_id=1, source_target_pairs={{0,1},{1,2},{2,3},{3,0},{4,5},{5,6},{6,7},{7,4},{8,9},{9,10},{10,1... | collective-permute-start | bytes 329480 | tf_op jit(solution)/shard_map/ppermute | solution.py:18
  38.1 2.3 %collective-permute-start.3 = (bf16[26,8,264]{2,0,1:T(8,128)(2,1)S(1)}, bf16[26,8,264]{2,0,1:T(8,128)(2,1)S(1)}, u32[]{:S(2)}, u32[]{:S(2)}) collective-permute-start(bf16[26,8,264]{2,0,1:T(8,128)(2,1)S(1)} %get-tuple-element.75), channel_id=1, source_target_pairs={{1,0},{2,1},{3,2},{0,3},{5,4},{6,5},{7,6},{4,7},{9,8},{10,9},{11,1... | collective-permute-start | bytes 329480 | tf_op jit(solution)/shard_map/ppermute | solution.py:21
  40.4 3.9 %collective-permute-done.2 = bf16[26,8,264]{2,0,1:T(8,128)(2,1)S(1)} collective-permute-done((bf16[26,8,264]{2,0,1:T(8,128)(2,1)S(1)}, bf16[26,8,264]{2,0,1:T(8,128)(2,1)S(1)}, u32[]{:S(2)}, u32[]{:S(2)}) %collective-permute-start.2) | collective-permute-done | bytes 109856 | tf_op jit(solution)/shard_map/ppermute | solution.py:18
  44.3 5.6 %collective-permute-done.3 = bf16[26,8,264]{2,0,1:T(8,128)(2,1)S(1)} collective-permute-done((bf16[26,8,264]{2,0,1:T(8,128)(2,1)S(1)}, bf16[26,8,264]{2,0,1:T(8,128)(2,1)S(1)}, u32[]{:S(2)}, u32[]{:S(2)}) %collective-permute-start.3) | collective-permute-done | bytes 109856 | tf_op jit(solution)/shard_map/ppermute | solution.py:21
  49.9 3.4 %fusion.7 = bf16[26,64,264]{2,0,1:T(8,128)(2,1)S(1)} fusion(bf16[26,8,264]{2,0,1:T(8,128)(2,1)S(1)} %collective-permute-done.3, bf16[26,8,264]{2,0,1:T(8,128)(2,1)S(1)} %collective-permute-done.2, bf16[1,45,264]{2,0,1:T(2,128)(2,1)S(1)} %collective-permute-done.1, bf16[1,45,264]{2,0,1:T(2,128)(2,1)S(1)} %collective-permute-done, ...), kind=kLoop, calls=%fused_computation.12 | loop fusion | flops 8346624 | bytes 1716000 | tf_op jit(solution)/shard_map/concatenate | solution.py:22
  53.4 0.1 slice.156
  53.5 1.1 slice.155
  54.6 0.6 copy.58
  55.2 1.6 broadcast_in_dim.2
  56.9 4.0 %reshape_reshape.3 = bf16[1664,256]{0,1:T(8,128)(2,1)} reshape(bf16[26,64,8,32]{1,0,3,2:T(8,128)(2,1)} %broadcast_in_dim.2) | data formatting | bytes 1703936 | tf_op jit(solution)/shard_map/reshape;reshape | solution.py:109
  60.9 1.5 copy.66.m_ref
  62.4 1.7 copy.57
  64.1 19.9 %shard_map.85 = (bf16[24,45,256]{2,1,0:T(8,128)(2,1)S(1)}, f32[4,256,256]{2,1,0:T(8,128)S(1)}, f32[1664,256]{1,0:T(8,128)}) custom-call(bf16[1664,256]{1,0:T(8,128)(2,1)S(1)} %bitcast.34, bf16[1664,256]{1,0:T(8,128)(2,1)S(1)} %copy.66.m_ref, bf16[24,192,192]{2,1,0:T(8,128)(2,1)} %reshape.209.t_ref, bf16[24,48,256]{2,1,0:T(8,128)(2,1)S(1)} %pad.17.cot_ref, ...), custom_call_target="tpu_custom_call" | custom-call | tf_op jit(solution)/shard_map/pallas_call | solution.py:138
  84.0 1.0 copy-done.1
  85.0 3.7 %reshape.213 = f32[4,8,32,8,32]{4,3,2,1,0:T(8,128)} reshape(f32[4,256,256]{2,1,0:T(8,128)} %copy-done.1) | data formatting | bytes 2097152 | tf_op jit(solution)/shard_map/reshape | solution.py:153
  88.7 0.9 fusion.23
  89.7 1.4 collective-permute-start.4
  91.2 3.5 %multiply_reduce_fusion = f32[4,8,32,32]{3,2,1,0:T(8,128)S(1)} fusion(f32[4,8,32,8,32]{4,3,2,1,0:T(8,128)} %reshape.213, f32[8,8]{1,0:T(8,128)S(1)} %fusion.21), kind=kLoop, calls=%fused_computation | loop fusion | flops 491520 | bytes 1179904 | tf_op jit(solution)/shard_map/reduce_sum | solution.py:152
  94.7 0.1 slice.157
  94.9 0.7 collective-permute-start.8
  95.6 0.9 copy.75
  96.6 2.8 %collective-permute-start.5 = (f32[1,61,256]{2,0,1:T(1,128)S(1)}, f32[1,61,256]{2,0,1:T(1,128)S(1)}, u32[]{:S(2)}, u32[]{:S(2)}) collective-permute-start(f32[1,61,256]{2,0,1:T(1,128)S(1)} %copy.78), channel_id=1, source_target_pairs={{0,4},{4,8},{8,12},{12,16},{16,20},{20,24},{24,28},{1,5},{5,9},{9,... | collective-permute-start | bytes 187400 | tf_op jit(solution)/shard_map/ppermute | solution.py:29
  99.3 0.1 copy_add_fusion
  99.4 2.6 %scatter-add.14 = f32[24,61,256]{2,0,1:T(8,128)S(1)} dynamic-update-slice(f32[24,61,256]{2,0,1:T(8,128)S(1)} %copy.75, f32[1,61,256]{2,0,1:T(1,128)S(1)} %copy_add_fusion, s32[]{:T(128)} %constant.126.clone.1, s32[]{:T(128)} %constant.124.clone.1, s32[]{:T(128)} %constant.124.clone.1) | dynamic-update-slice | bytes 124932 | tf_op jit(solution)/shard_map/scatter-add | solution.py:164
  102.1 2.6 %scatter-add.15 = f32[24,61,256]{2,0,1:T(8,128)S(1)} dynamic-update-slice(f32[24,61,256]{2,0,1:T(8,128)S(1)} %scatter-add.14, f32[1,61,256]{2,0,1:T(1,128)S(1)} %slice_add_fusion.2, s32[]{:T(128)} %constant.124.clone.1, s32[]{:T(128)} %constant.124.clone.1, s32[]{:T(128)} %constant.124.clone.1) | dynamic-update-slice | bytes 124932 | tf_op jit(solution)/shard_map/scatter-add | solution.py:165
  104.8 1.3 collective-permute-start.6
  106.1 3.6 %collective-permute-done.8 = f32[8,4,32,32]{3,2,0,1:T(8,128)} collective-permute-done((f32[8,4,32,32]{3,2,0,1:T(8,128)S(1)}, f32[8,4,32,32]{3,2,0,1:T(8,128)}, u32[]{:S(2)}, u32[]{:S(2)}) %collective-permute-start.8) | collective-permute-done | bytes 131104 | tf_op jit(solution)/shard_map/ppermute | solution.py:45
  109.7 1.1 bitcast_add_fusion
  110.9 0.2 collective-permute-done.6
  111.1 1.0 copy-done.2
  112.1 0.5 collective-permute-start.7
  112.6 28.7 %collective-permute-done.9 = f32[8,4,32,32]{3,2,0,1:T(8,128)S(1)} collective-permute-done((f32[8,4,32,32]{3,2,0,1:T(8,128)S(1)}, f32[8,4,32,32]{3,2,0,1:T(8,128)S(1)}, u32[]{:S(2)}, u32[]{:S(2)}) %collective-permute-start.9) | collective-permute-done | bytes 131104 | tf_op jit(solution)/shard_map/ppermute | solution.py:45
  141.4 0.9 add.61
  142.3 3.2 %mul.53 = f32[24,45,8,32]{3,2,0,1:T(8,128)} broadcast(bf16[24,45,8]{2,0,1:T(8,128)(2,1)S(1)} %convert_element_type.41), dimensions={0,1,2} | broadcast | bytes 1123200 | tf_op jit(solution)/shard_map/mul | solution.py:174
  145.4 3.5 %mul.54 = f32[24,45,256]{2,0,1:T(8,128)S(1)} reshape(f32[24,45,8,32]{3,2,0,1:T(8,128)} %mul.53) | data formatting | bytes 2211840 | tf_op jit(solution)/shard_map/mul | solution.py:174
  148.9 1.0 copy.71
  149.9 1.1 add.62
  151.0 2.5 %collective-permute-start.11 = (f32[8,4,32,32]{3,2,0,1:T(8,128)S(1)}, f32[8,4,32,32]{3,2,0,1:T(8,128)S(1)}, u32[]{:S(2)}, u32[]{:S(2)}) collective-permute-start(f32[8,4,32,32]{3,2,0,1:T(8,128)S(1)} %add.62), channel_id=1, source_target_pairs={{0,8},{4,12},{8,0},{12,4},{16,24},{20,28},{24,16},{28,20},{1,9},{5... | collective-permute-start | bytes 393224 | tf_op jit(solution)/shard_map/ppermute | solution.py:45
  153.6 12.5 %collective-permute-done.11 = f32[8,4,32,32]{3,2,0,1:T(8,128)S(1)} collective-permute-done((f32[8,4,32,32]{3,2,0,1:T(8,128)S(1)}, f32[8,4,32,32]{3,2,0,1:T(8,128)S(1)}, u32[]{:S(2)}, u32[]{:S(2)}) %collective-permute-start.11) | collective-permute-done | bytes 131104 | tf_op jit(solution)/shard_map/ppermute | solution.py:45
  166.2 1.4 collective-permute-start.12
  167.5 0.9 multiply_convert_fusion
  168.5 11.5 %collective-permute-done.12 = f32[8,4,32,32]{3,2,0,1:T(8,128)S(1)} collective-permute-done((f32[8,4,32,32]{3,2,0,1:T(8,128)S(1)}, f32[8,4,32,32]{3,2,0,1:T(8,128)S(1)}, u32[]{:S(2)}, u32[]{:S(2)}) %collective-permute-start.12) | collective-permute-done | bytes 131104 | tf_op jit(solution)/shard_map/ppermute | solution.py:45
  180.0 0.1 add_multiply_fusion
  180.1 0.8 copy.72
  (44 shorter events, 0.9 us)
Async XLA Ops:
  0.6 10.0 %copy-start = (bf16[192,4,3,17]{0,1,3,2:T(4,128)(2,1)S(1)}, bf16[192,4,3,17]{0,1,3,2:T(4,128)(2,1)}, u32[]{:S(2)}) copy-start(bf16[192,4,3,17]{0,1,3,2:T(4,128)(2,1)} %param.16) | copy-start | bytes 235012
  4.8 6.1 %copy-start.9 = (s32[192]{0:T(256)S(1)}, s32[192]{0:T(256)}, u32[]{:S(2)}) copy-start(s32[192]{0:T(256)} %param.17) | copy-start | bytes 2308
  4.8 6.3 %copy-start.8 = (bf16[8,4,32,32]{3,2,1,0:T(8,128)(2,1)S(1)}, bf16[8,4,32,32]{3,2,1,0:T(8,128)(2,1)}, u32[]{:S(2)}) copy-start(bf16[8,4,32,32]{3,2,1,0:T(8,128)(2,1)} %param.18) | copy-start | bytes 196612
  6.9 28.5 %collective-permute-start = (bf16[1,45,264]{2,0,1:T(2,128)(2,1)}, bf16[1,45,264]{2,0,1:T(2,128)(2,1)S(1)}, u32[]{:S(2)}, u32[]{:S(2)}) collective-permute-start(bf16[1,45,264]{2,0,1:T(2,128)(2,1)} %get-tuple-element.76), channel_id=1, source_target_pairs={{0,4},{4,8},{8,12},{12,16},{16,20},{20,24},{24,28},{1,5},{5,9},{9,... | collective-permute-start | bytes 71288 | tf_op jit(solution)/shard_map/ppermute | solution.py:18
  9.3 26.1 %collective-permute-start.1 = (bf16[1,45,264]{2,0,1:T(2,128)(2,1)}, bf16[1,45,264]{2,0,1:T(2,128)(2,1)S(1)}, u32[]{:S(2)}, u32[]{:S(2)}) collective-permute-start(bf16[1,45,264]{2,0,1:T(2,128)(2,1)} %get-tuple-element.77), channel_id=1, source_target_pairs={{4,0},{8,4},{12,8},{16,12},{20,16},{24,20},{28,24},{5,1},{9,5},{13... | collective-permute-start | bytes 71288 | tf_op jit(solution)/shard_map/ppermute | solution.py:21
  30.8 4.4 %copy-start.7 = (bf16[24,45,256]{2,0,1:T(8,128)(2,1)S(1)}, bf16[24,45,256]{2,0,1:T(8,128)(2,1)}, u32[]{:S(2)}) copy-start(bf16[24,45,256]{2,0,1:T(8,128)(2,1)} %param.19) | copy-start | bytes 1658884
  35.6 8.7 %collective-permute-start.2 = (bf16[26,8,264]{2,0,1:T(8,128)(2,1)S(1)}, bf16[26,8,264]{2,0,1:T(8,128)(2,1)S(1)}, u32[]{:S(2)}, u32[]{:S(2)}) collective-permute-start(bf16[26,8,264]{2,0,1:T(8,128)(2,1)S(1)} %get-tuple-element.74), channel_id=1, source_target_pairs={{0,1},{1,2},{2,3},{3,0},{4,5},{5,6},{6,7},{7,4},{8,9},{9,10},{10,1... | collective-permute-start | bytes 329480 | tf_op jit(solution)/shard_map/ppermute | solution.py:18
  38.1 11.8 %collective-permute-start.3 = (bf16[26,8,264]{2,0,1:T(8,128)(2,1)S(1)}, bf16[26,8,264]{2,0,1:T(8,128)(2,1)S(1)}, u32[]{:S(2)}, u32[]{:S(2)}) collective-permute-start(bf16[26,8,264]{2,0,1:T(8,128)(2,1)S(1)} %get-tuple-element.75), channel_id=1, source_target_pairs={{1,0},{2,1},{3,2},{0,3},{5,4},{6,5},{7,6},{4,7},{9,8},{10,9},{11,1... | collective-permute-start | bytes 329480 | tf_op jit(solution)/shard_map/ppermute | solution.py:21
  84.0 1.0 copy-start.1
  89.7 5.0 %copy-start.6 = (f32[1664,256]{1,0:T(8,128)S(1)}, f32[1664,256]{1,0:T(8,128)}, u32[]{:S(2)}) copy-start(f32[1664,256]{1,0:T(8,128)} %get-tuple-element.55) | copy-start | bytes 5111812
  89.7 9.6 %collective-permute-start.4 = (f32[1,61,256]{2,0,1:T(1,128)S(1)}, f32[1,61,256]{2,0,1:T(1,128)S(1)}, u32[]{:S(2)}, u32[]{:S(2)}) collective-permute-start(f32[1,61,256]{2,0,1:T(1,128)S(1)} %copy.77), channel_id=1, source_target_pairs={{4,0},{8,4},{12,8},{16,12},{20,16},{24,20},{28,24},{5,1},{9,5},{13... | collective-permute-start | bytes 187400 | tf_op jit(solution)/shard_map/ppermute | solution.py:29
  94.7 1.8 copy-start.4
  94.9 14.8 %collective-permute-start.8 = (f32[8,4,32,32]{3,2,0,1:T(8,128)S(1)}, f32[8,4,32,32]{3,2,0,1:T(8,128)}, u32[]{:S(2)}, u32[]{:S(2)}) collective-permute-start(f32[8,4,32,32]{3,2,0,1:T(8,128)S(1)} %bitcast.35), channel_id=1, source_target_pairs={{0,1},{1,0},{2,3},{3,2},{4,5},{5,4},{6,7},{7,6},{8,9},{9,8},{10,11... | collective-permute-start | bytes 393224 | tf_op jit(solution)/shard_map/ppermute | solution.py:45
  96.6 5.4 %collective-permute-start.5 = (f32[1,61,256]{2,0,1:T(1,128)S(1)}, f32[1,61,256]{2,0,1:T(1,128)S(1)}, u32[]{:S(2)}, u32[]{:S(2)}) collective-permute-start(f32[1,61,256]{2,0,1:T(1,128)S(1)} %copy.78), channel_id=1, source_target_pairs={{0,4},{4,8},{8,12},{12,16},{16,20},{20,24},{24,28},{1,5},{5,9},{9,... | collective-permute-start | bytes 187400 | tf_op jit(solution)/shard_map/ppermute | solution.py:29
  104.6 5.1 %copy-start.5 = (f32[4,8,32,32]{3,2,1,0:T(8,128)S(1)}, f32[4,8,32,32]{3,2,1,0:T(8,128)}, u32[]{:S(2)}) copy-start(f32[4,8,32,32]{3,2,1,0:T(8,128)} %copy-done.4) | copy-start | bytes 393220
  104.8 6.3 %collective-permute-start.6 = (bf16[24,8,256]{2,0,1:T(8,128)(2,1)S(1)}, bf16[24,8,256]{2,0,1:T(8,128)(2,1)S(1)}, u32[]{:S(2)}, u32[]{:S(2)}) collective-permute-start(bf16[24,8,256]{2,0,1:T(8,128)(2,1)S(1)} %slice.175), channel_id=1, source_target_pairs={{0,3},{1,0},{2,1},{3,2},{4,7},{5,4},{6,5},{7,6},{8,11},{9,8},{10,9... | collective-permute-start | bytes 294920 | tf_op jit(solution)/shard_map/ppermute | solution.py:34
  110.8 30.6 %collective-permute-start.9 = (f32[8,4,32,32]{3,2,0,1:T(8,128)S(1)}, f32[8,4,32,32]{3,2,0,1:T(8,128)S(1)}, u32[]{:S(2)}, u32[]{:S(2)}) collective-permute-start(f32[8,4,32,32]{3,2,0,1:T(8,128)S(1)} %bitcast_add_fusion), channel_id=1, source_target_pairs={{0,2},{1,3},{2,0},{3,1},{4,6},{5,7},{6,4},{7,5},{8,10},{9,11},{10,... | collective-permute-start | bytes 393224 | tf_op jit(solution)/shard_map/ppermute | solution.py:45
  111.1 1.0 copy-start.2
  112.1 41.4 %collective-permute-start.7 = (f32[24,8,256]{2,0,1:T(8,128)S(1)}, f32[24,8,256]{2,0,1:T(8,128)S(1)}, u32[]{:S(2)}, u32[]{:S(2)}) collective-permute-start(f32[24,8,256]{2,0,1:T(8,128)S(1)} %get-tuple-element.72), channel_id=1, source_target_pairs={{0,1},{1,2},{2,3},{3,0},{4,5},{5,6},{6,7},{7,4},{8,9},{9,10},{10,1... | collective-permute-start | bytes 589832 | tf_op jit(solution)/shard_map/ppermute | solution.py:34
  142.3 7.7 %collective-permute-start.10 = (f32[8,4,32,32]{3,2,0,1:T(8,128)}, f32[8,4,32,32]{3,2,0,1:T(8,128)S(1)}, u32[]{:S(2)}, u32[]{:S(2)}) collective-permute-start(f32[8,4,32,32]{3,2,0,1:T(8,128)} %add.61), channel_id=1, source_target_pairs={{0,4},{4,0},{8,12},{12,8},{16,20},{20,16},{24,28},{28,24},{1,5},{5... | collective-permute-start | bytes 393224 | tf_op jit(solution)/shard_map/ppermute | solution.py:45
  148.9 4.6 %copy-start.3 = (f32[24,45,256]{2,0,1:T(8,128)S(1)}, f32[24,45,256]{2,0,1:T(8,128)}, u32[]{:S(2)}) copy-start(f32[24,45,256]{2,0,1:T(8,128)} %copy-done.2) | copy-start | bytes 3317764
  151.0 15.1 %collective-permute-start.11 = (f32[8,4,32,32]{3,2,0,1:T(8,128)S(1)}, f32[8,4,32,32]{3,2,0,1:T(8,128)S(1)}, u32[]{:S(2)}, u32[]{:S(2)}) collective-permute-start(f32[8,4,32,32]{3,2,0,1:T(8,128)S(1)} %add.62), channel_id=1, source_target_pairs={{0,8},{4,12},{8,0},{12,4},{16,24},{20,28},{24,16},{28,20},{1,9},{5... | collective-permute-start | bytes 393224 | tf_op jit(solution)/shard_map/ppermute | solution.py:45
  166.2 13.8 %collective-permute-start.12 = (f32[8,4,32,32]{3,2,0,1:T(8,128)S(1)}, f32[8,4,32,32]{3,2,0,1:T(8,128)S(1)}, u32[]{:S(2)}, u32[]{:S(2)}) collective-permute-start(f32[8,4,32,32]{3,2,0,1:T(8,128)S(1)} %add.63), channel_id=1, source_target_pairs={{0,16},{4,20},{8,24},{12,28},{16,0},{20,4},{24,8},{28,12},{1,17},{... | collective-permute-start | bytes 393224 | tf_op jit(solution)/shard_map/ppermute | solution.py:45

commit v3 on v2

--- a/solution.py
+++ b/solution.py
@@ -49,20 +49,21 @@
 
 
 def conv_kernel(x_ref, m_ref, t_ref, cot_ref, w_ref, wt_ref, inf_ref, wg_ref, col_ref, pulled_ref):
-    rows = t_ref.shape[0]
-    basis_count = w_ref.shape[0]
-    col_pad = cot_ref.shape[1]
+    rows, basis_count, lat_taps, col_pad, lane_rows = t_ref.shape
     col_count = inf_ref.shape[1]
-    lane_rows = x_ref.shape[0] // (rows + 2)
-    window = 3 * lane_rows
     col_ref[...] = jnp.zeros_like(col_ref)
     wg_ref[...] = jnp.zeros_like(wg_ref)
 
     def body(i, carry):
-        start = pl.multiple_of(i * lane_rows, lane_rows)
-        band = t_ref[i]
-        numerator = jnp.dot(band, x_ref[pl.ds(start, window), :], preferred_element_type=jnp.float32)
-        denominator = jnp.dot(band, m_ref[pl.ds(start, window), :], preferred_element_type=jnp.float32)
+        bands = [t_ref[i, :, a].reshape(basis_count * col_pad, lane_rows) for a in range(lat_taps)]
+        numerator = None
+        denominator = None
+        for a in range(lat_taps):
+            start = pl.multiple_of((i + a) * lane_rows, lane_rows)
+            num = jnp.dot(bands[a], x_ref[pl.ds(start, lane_rows), :], preferred_element_type=jnp.float32)
+            den = jnp.dot(bands[a], m_ref[pl.ds(start, lane_rows), :], preferred_element_type=jnp.float32)
+            numerator = num if numerator is None else numerator + num
+            denominator = den if denominator is None else denominator + den
         safe = jnp.maximum(denominator, 1.0)
         scaled = (numerator / safe).astype(jnp.bfloat16)
         upstream = cot_ref[i]
@@ -78,10 +79,13 @@
                 back / safe[b * col_pad : (b + 1) * col_pad]
             ).astype(jnp.bfloat16)
         inf_ref[i] = out[:col_count].astype(inf_ref.dtype)
-        term = lax.dot_general(
-            band, pulled_ref[...], (((0,), (0,)), ((), ())), preferred_element_type=jnp.float32
-        )
-        col_ref[pl.ds(start, window), :] += term
+        pulled = pulled_ref[...]
+        for a in range(lat_taps):
+            start = pl.multiple_of((i + a) * lane_rows, lane_rows)
+            term = lax.dot_general(
+                bands[a], pulled, (((0,), (0,)), ((), ())), preferred_element_type=jnp.float32
+            )
+            col_ref[pl.ds(start, lane_rows), :] += term
         return carry
 
     lax.fori_loop(0, rows, body, 0)
@@ -123,9 +127,8 @@
         & (output_index[None, :, None] < col_count)
     ).astype(jnp.bfloat16)
     band = (
-        jnp.einsum("ibae,ejp->ibjap", local_taps, forward_table, preferred_element_type=jnp.float32)
+        jnp.einsum("ibae,ejp->ibajp", local_taps, forward_table, preferred_element_type=jnp.float32)
         .astype(jnp.bfloat16)
-        .reshape(row_count, basis_count * col_pad, 3 * lane_rows)
     )
 
     eye = jnp.eye(group_count, dtype=mixing.dtype)
@@ -155,7 +158,8 @@
         axis=3,
     ).transpose(1, 0, 2, 3)
     cell_count = row_count * lax.axis_size("lat") * col_count * lax.axis_size("lon")
-    weight_grad = butterfly_sum(local_grad, ("lon", "lat")) * (1.0 / math.sqrt(cell_count))
+    dense = butterfly_sum(local_grad.reshape(-1, 128), ("lon", "lat"))
+    weight_grad = dense.reshape(local_grad.shape) * (1.0 / math.sqrt(cell_count))
 
     collected = collected.reshape(row_count + 2, lane_rows, chan_count)[:, :padded_cols]
     from_below = passed_along(collected[0:1], "lat", -1)

time: 182 us -> 136 us (0.75)
  waiting for transfers between devices: 66.1 us -> 28.2 us
  local copies, waits for them, and re-layouts: 58.1 us -> 48.4 us
  other arithmetic: 15.5 us -> 12.3 us
  starting transfers between devices: 19.1 us -> 21.9 us
  Pallas kernels: 19.9 us -> 22.4 us
    ppermute x5, waiting for transfers between devices: 56.4 us -> 17 us  [butterfly_sum(): partner = lax.ppermute(value, axis, [(i, i ^ step) for i in range(count)])]
    reshape x1, local copies, waits for them, and re-layouts: 9.47 us -> 0.16 us  [local(): dense = butterfly_sum(local_grad.reshape(-1, 128), ('lon', 'lat'))]
    convert_element_type x1 -> x0, local copies, waits for them, and re-layouts: 4.83 us -> none  [local(): band = jnp.einsum('ibae,ejp->ibjap', local_taps, forward_table, preferred...]
    add x4, other arithmetic: 3.16 us -> 0.07 us  [butterfly_sum(): value = value + partner]
    dot_general x0 -> x1, local copies, waits for them, and re-layouts: none -> 2.58 us  [local(): jnp.einsum('ibae,ejp->ibajp', local_taps, forward_table, preferred_elemen...]
    pallas_call x1, Pallas kernels: 19.9 us -> 22.4 us  [local(): pl.pallas_call(conv_kernel, out_shape=(jax.ShapeDtypeStruct((row_count, c...]
    ppermute x5, starting transfers between devices: 4.65 us -> 6.79 us  [butterfly_sum(): partner = lax.ppermute(value, axis, [(i, i ^ step) for i in range(count)])]
    unnamed x29 -> x24, local copies, waits for them, and re-layouts: 6.59 us -> 7.16 us
  transfers between devices with their start and end apart: 13 -> 13, of which waited for: 7 -> 6; matrix products, arithmetic and copies ran while one was open for 26% -> 25% of each run, Pallas kernels for 0% -> 0%
where the time goes in v3:
time: 136 us
  local copies, waits for them, and re-layouts  48.4 us (36%)
  waiting for transfers between devices  28.2 us (21%)
  Pallas kernels  22.4 us (16%)
  starting transfers between devices  21.9 us (16%)
  other arithmetic  12.3 us (9%)
    pallas_call x1, Pallas kernels, local(): pl.pallas_call(conv_kernel, out_shape=(jax.ShapeDtypeStruct((row_count, c...  22.4 us
    ppermute x5, waiting for transfers between devices, butterfly_sum(): partner = lax.ppermute(value, axis, [(i, i ^ step) for i in range(count)])  17 us
    unnamed x24, local copies, waits for them, and re-layouts  7.16 us
    ppermute x5, starting transfers between devices, butterfly_sum(): partner = lax.ppermute(value, axis, [(i, i ^ step) for i in range(count)])  6.79 us
    mul x2, local copies, waits for them, and re-layouts, local(): gathered.reshape(row_count, col_count, group_count, group_width)  6.64 us
    ppermute x2, waiting for transfers between devices, with_halo(): lax.ppermute(lax.slice_in_dim(block, 0, width, axis=dim), axis, backward)  5.62 us
    another operation x2, local copies, waits for them, and re-layouts, local(): jnp.repeat(packed[..., chan_count:], group_width, axis=-1)  5.51 us
    ppermute x2, starting transfers between devices, with_halo(): lax.ppermute(lax.slice_in_dim(block, block.shape[dim] - width, None, axis...  4.84 us
  transfers between devices with their start and end apart: 13, of which 6 were waited for; matrix products, arithmetic and copies ran while one was open for 25% of the time, Pallas kernels for 0%

profile of v3, /device:TPU:0, one launch (start us, length us, event | category | flops | bytes accessed | tf_op | source)
XLA Modules:
  0.0 135.5 jit_solution(16762702127607348719)
XLA Ops:
  0.6 1.2 copy.71
  1.9 1.4 %mul.50 = bf16[24,45,8,32]{3,2,0,1:T(8,128)(2,1)S(1)} broadcast(bf16[24,45,8]{2,0,1:T(8,128)(2,1)S(1)} %convert_element_type.38), dimensions={0,1,2} | broadcast | bytes 570240 | tf_op jit(solution)/shard_map/mul | solution.py:106
  3.3 1.5 %mul.51 = bf16[24,45,256]{2,0,1:T(8,128)(2,1)S(1)} reshape(bf16[24,45,8,32]{3,2,0,1:T(8,128)(2,1)S(1)} %mul.50) | data formatting | bytes 1105920 | tf_op jit(solution)/shard_map/mul | solution.py:106
  4.9 1.3 mul.52
  6.1 0.8 pad_maximum_fusion.5
  6.9 2.4 %collective-permute-start = (bf16[1,45,264]{2,0,1:T(2,128)(2,1)}, bf16[1,45,264]{2,0,1:T(2,128)(2,1)S(1)}, u32[]{:S(2)}, u32[]{:S(2)}) collective-permute-start(bf16[1,45,264]{2,0,1:T(2,128)(2,1)} %get-tuple-element.79), channel_id=1, source_target_pairs={{0,4},{4,8},{8,12},{12,16},{16,20},{20,24},{24,28},{1,5},{5,9},{9,... | collective-permute-start | bytes 71288 | tf_op jit(solution)/shard_map/ppermute | solution.py:18
  9.3 1.3 collective-permute-start.1
  10.7 0.1 constant_dynamic-slice_fusion
  10.8 0.2 copy.95
  11.0 0.1 compare_convert_fusion
  11.0 0.1 copy.74
  11.2 0.2 copy.79
  11.4 0.1 copy.78
  11.5 1.7 %multiply_bitcast_fusion = (bf16[4,8,32,8,32]{4,3,2,1,0:T(8,128)(2,1)}, bf16[4,8,32,8,32]{2,1,4,3,0:T(8,128)(2,1)S(1)}) fusion(bf16[8,4,32,32]{2,0,3,1:T(8,128)(2,1)S(1)} %copy.79, bf16[8,8]{0,1:T(8,128)(2,1)S(1)} %copy.78), kind=kLoop, calls=%fused_computation.9 | loop fusion | flops 262144 | bytes 1114240 | tf_op jit(solution)/shard_map/gbco,gh->bhogc/transpose | solution.py:136
  13.2 1.1 fusion.13
  14.3 2.6 %copy.98.t_ref = bf16[24,4,3,48,64]{4,3,2,1,0:T(8,128)(2,1)} copy(bf16[24,4,3,48,64]{4,0,3,2,1:T(8,128)(2,1)S(1)} %fusion.13) | data formatting | bytes 3538944 | tf_op jit(solution)/shard_map/ibae,ejp->ibajp/dot_general | solution.py:130
  16.9 2.1 %reshape.219 = bf16[4,256,256]{1,2,0:T(8,128)(2,1)} reshape(bf16[4,8,32,8,32]{2,1,4,3,0:T(8,128)(2,1)S(1)} %get-tuple-element.82) | data formatting | bytes 1048576 | tf_op jit(solution)/shard_map/reshape | solution.py:135
  19.0 1.2 copy.90.w_ref
  20.3 3.2 %reshape.213.wt_ref = bf16[4,256,256]{2,1,0:T(8,128)(2,1)S(1)} reshape(bf16[4,8,32,8,32]{4,3,2,1,0:T(8,128)(2,1)} %get-tuple-element.81) | data formatting | bytes 1048576 | tf_op jit(solution)/shard_map/reshape | solution.py:136
  23.5 0.1 copy.77
  23.7 0.2 pad_maximum_fusion.3
  23.9 2.4 %collective-permute-start.2 = (bf16[26,8,264]{2,0,1:T(8,128)(2,1)S(1)}, bf16[26,8,264]{2,0,1:T(8,128)(2,1)S(1)}, u32[]{:S(2)}, u32[]{:S(2)}) collective-permute-start(bf16[26,8,264]{2,0,1:T(8,128)(2,1)S(1)} %get-tuple-element.77), channel_id=1, source_target_pairs={{0,1},{1,2},{2,3},{3,0},{4,5},{5,6},{6,7},{7,4},{8,9},{9,10},{10,1... | collective-permute-start | bytes 329480 | tf_op jit(solution)/shard_map/ppermute | solution.py:18
  26.3 2.3 %collective-permute-start.3 = (bf16[26,8,264]{2,0,1:T(8,128)(2,1)S(1)}, bf16[26,8,264]{2,0,1:T(8,128)(2,1)S(1)}, u32[]{:S(2)}, u32[]{:S(2)}) collective-permute-start(bf16[26,8,264]{2,0,1:T(8,128)(2,1)S(1)} %get-tuple-element.78), channel_id=1, source_target_pairs={{1,0},{2,1},{3,2},{0,3},{5,4},{6,5},{7,6},{4,7},{9,8},{10,9},{11,1... | collective-permute-start | bytes 329480 | tf_op jit(solution)/shard_map/ppermute | solution.py:21
  28.6 3.9 %collective-permute-done.2 = bf16[26,8,264]{2,0,1:T(8,128)(2,1)S(1)} collective-permute-done((bf16[26,8,264]{2,0,1:T(8,128)(2,1)S(1)}, bf16[26,8,264]{2,0,1:T(8,128)(2,1)S(1)}, u32[]{:S(2)}, u32[]{:S(2)}) %collective-permute-start.2) | collective-permute-done | bytes 109856 | tf_op jit(solution)/shard_map/ppermute | solution.py:18
  32.6 5.6 %collective-permute-done.3 = bf16[26,8,264]{2,0,1:T(8,128)(2,1)S(1)} collective-permute-done((bf16[26,8,264]{2,0,1:T(8,128)(2,1)S(1)}, bf16[26,8,264]{2,0,1:T(8,128)(2,1)S(1)}, u32[]{:S(2)}, u32[]{:S(2)}) %collective-permute-start.3) | collective-permute-done | bytes 109856 | tf_op jit(solution)/shard_map/ppermute | solution.py:21
  38.2 3.4 %fusion.7 = bf16[26,64,264]{2,0,1:T(8,128)(2,1)S(1)} fusion(bf16[26,8,264]{2,0,1:T(8,128)(2,1)S(1)} %collective-permute-done.3, bf16[26,8,264]{2,0,1:T(8,128)(2,1)S(1)} %collective-permute-done.2, bf16[1,45,264]{2,0,1:T(2,128)(2,1)S(1)} %collective-permute-done.1, bf16[1,45,264]{2,0,1:T(2,128)(2,1)S(1)} %collective-permute-done, ...), kind=kLoop, calls=%fused_computation.12 | loop fusion | flops 8346624 | bytes 1716000 | tf_op jit(solution)/shard_map/concatenate | solution.py:22
  41.6 0.1 slice.156
  41.7 1.1 slice.155
  42.8 0.6 copy.73
  43.5 1.7 %broadcast_in_dim.2 = bf16[26,64,8,32]{1,0,3,2:T(8,128)(2,1)} broadcast(bf16[26,64,8]{1,0,2:T(8,128)(2,1)S(1)} %copy.73), dimensions={0,1,2} | broadcast | bytes 878592 | tf_op jit(solution)/shard_map/broadcast_in_dim | solution.py:113
  45.1 4.0 %reshape_reshape.3 = bf16[1664,256]{0,1:T(8,128)(2,1)} reshape(bf16[26,64,8,32]{1,0,3,2:T(8,128)(2,1)} %broadcast_in_dim.2) | data formatting | bytes 1703936 | tf_op jit(solution)/shard_map/reshape;reshape | solution.py:113
  49.1 1.5 %copy.81.m_ref = bf16[1664,256]{1,0:T(8,128)(2,1)S(1)} copy(bf16[1664,256]{0,1:T(8,128)(2,1)} %reshape_reshape.3) | data formatting | bytes 1703936 | tf_op jit(solution)/shard_map/reshape;reshape | solution.py:113
  50.6 1.7 %copy.72 = bf16[26,64,256]{2,1,0:T(8,128)(2,1)S(1)} copy(bf16[26,64,256]{2,0,1:T(8,128)(2,1)} %slice.155) | data formatting | bytes 1703936 | tf_op jit(solution)/shard_map/slice | solution.py:112
  52.3 22.4 %shard_map.85 = (bf16[24,45,256]{2,1,0:T(8,128)(2,1)S(1)}, f32[4,256,256]{2,1,0:T(8,128)S(1)}, f32[1664,256]{1,0:T(8,128)}) custom-call(bf16[1664,256]{1,0:T(8,128)(2,1)S(1)} %bitcast.35, bf16[1664,256]{1,0:T(8,128)(2,1)S(1)} %copy.81.m_ref, bf16[24,4,3,48,64]{4,3,2,1,0:T(8,128)(2,1)} %copy.98.t_ref, bf16[24,48,256]{2,1,0:T(8,128)(2,1)S(1)} %pad.17.cot_ref, ...), custom_call_target="tpu_custom_call" | custom-call | tf_op jit(solution)/shard_map/pallas_call | solution.py:141
  74.7 1.0 copy-done.1
  75.7 3.9 %reshape.215 = f32[4,8,32,8,32]{4,3,2,1,0:T(8,128)} reshape(f32[4,256,256]{2,1,0:T(8,128)} %copy-done.1) | data formatting | bytes 2097152 | tf_op jit(solution)/shard_map/reshape | solution.py:156
  79.7 1.3 collective-permute-start.4
  81.0 3.6 %multiply_reduce_fusion = f32[4,8,32,32]{3,2,1,0:T(8,128)S(1)} fusion(f32[4,8,32,8,32]{4,3,2,1,0:T(8,128)} %reshape.215, f32[8,8]{1,0:T(8,128)S(1)} %fusion.22), kind=kLoop, calls=%fused_computation.1 | loop fusion | flops 491520 | bytes 1179904 | tf_op jit(solution)/shard_map/reduce_sum | solution.py:155
  84.6 1.3 slice.157
  85.9 0.2 reshape.216
  86.1 0.7 collective-permute-start.8
  86.8 2.3 %copy.91 = f32[24,61,256]{2,0,1:T(8,128)S(1)} copy(f32[24,61,256]{2,1,0:T(8,128)} %slice.157) | data formatting | bytes 2998272
  89.1 0.1 copy.94
  89.2 2.8 %collective-permute-start.5 = (f32[1,61,256]{2,0,1:T(1,128)S(1)}, f32[1,61,256]{2,0,1:T(1,128)S(1)}, u32[]{:S(2)}, u32[]{:S(2)}) collective-permute-start(f32[1,61,256]{2,0,1:T(1,128)S(1)} %copy.94), channel_id=1, source_target_pairs={{0,4},{4,8},{8,12},{12,16},{16,20},{20,24},{24,28},{1,5},{5,9},{9,... | collective-permute-start | bytes 187400 | tf_op jit(solution)/shard_map/ppermute | solution.py:29
  91.9 0.1 copy_add_fusion
  92.0 2.6 %scatter-add.14 = f32[24,61,256]{2,0,1:T(8,128)S(1)} dynamic-update-slice(f32[24,61,256]{2,0,1:T(8,128)S(1)} %copy.91, f32[1,61,256]{2,0,1:T(1,128)S(1)} %copy_add_fusion, s32[]{:T(128)} %constant.126.clone.1, s32[]{:T(128)} %constant.123.clone.1, s32[]{:T(128)} %constant.123.clone.1) | dynamic-update-slice | bytes 124932 | tf_op jit(solution)/shard_map/scatter-add | solution.py:168
  94.7 2.6 %scatter-add.15 = f32[24,61,256]{2,0,1:T(8,128)S(1)} dynamic-update-slice(f32[24,61,256]{2,0,1:T(8,128)S(1)} %scatter-add.14, f32[1,61,256]{2,0,1:T(1,128)S(1)} %slice_add_fusion.2, s32[]{:T(128)} %constant.123.clone.1, s32[]{:T(128)} %constant.123.clone.1, s32[]{:T(128)} %constant.123.clone.1) | dynamic-update-slice | bytes 124932 | tf_op jit(solution)/shard_map/scatter-add | solution.py:169
  97.3 1.3 collective-permute-start.6
  98.6 0.1 slice.162
  98.7 1.6 %collective-permute-start.9 = (f32[256,128]{1,0:T(8,128)S(1)}, f32[256,128]{1,0:T(8,128)S(1)}, u32[]{:S(2)}, u32[]{:S(2)}) collective-permute-start(f32[256,128]{1,0:T(8,128)S(1)} %add.60), channel_id=1, source_target_pairs={{0,2},{1,3},{2,0},{3,1},{4,6},{5,7},{6,4},{7,5},{8,10},{9,11},{10,... | collective-permute-start | bytes 393224 | tf_op jit(solution)/shard_map/ppermute | solution.py:45
  100.3 1.6 %collective-permute-done.6 = bf16[24,8,256]{2,0,1:T(8,128)(2,1)S(1)} collective-permute-done((bf16[24,8,256]{2,0,1:T(8,128)(2,1)S(1)}, bf16[24,8,256]{2,0,1:T(8,128)(2,1)S(1)}, u32[]{:S(2)}, u32[]{:S(2)}) %collective-permute-start.6) | collective-permute-done | bytes 98336 | tf_op jit(solution)/shard_map/ppermute | solution.py:34
  102.0 1.0 copy-done.2
  103.0 1.4 %collective-permute-start.7 = (f32[24,8,256]{2,0,1:T(8,128)S(1)}, f32[24,8,256]{2,0,1:T(8,128)S(1)}, u32[]{:S(2)}, u32[]{:S(2)}) collective-permute-start(f32[24,8,256]{2,0,1:T(8,128)S(1)} %get-tuple-element.75), channel_id=1, source_target_pairs={{0,1},{1,2},{2,3},{3,0},{4,5},{5,6},{6,7},{7,4},{8,9},{9,10},{10,1... | collective-permute-start | bytes 589832 | tf_op jit(solution)/shard_map/ppermute | solution.py:34
  104.4 8.5 %collective-permute-done.9 = f32[256,128]{1,0:T(8,128)S(1)} collective-permute-done((f32[256,128]{1,0:T(8,128)S(1)}, f32[256,128]{1,0:T(8,128)S(1)}, u32[]{:S(2)}, u32[]{:S(2)}) %collective-permute-start.9) | collective-permute-done | bytes 131104 | tf_op jit(solution)/shard_map/ppermute | solution.py:45
  112.9 1.1 collective-permute-start.10
  114.0 3.2 %mul.56 = f32[24,45,8,32]{3,2,0,1:T(8,128)} broadcast(bf16[24,45,8]{2,0,1:T(8,128)(2,1)S(1)} %convert_element_type.38), dimensions={0,1,2} | broadcast | bytes 1123200 | tf_op jit(solution)/shard_map/mul | solution.py:178
  117.2 3.5 %mul.57 = f32[24,45,256]{2,0,1:T(8,128)S(1)} reshape(f32[24,45,8,32]{3,2,0,1:T(8,128)} %mul.56) | data formatting | bytes 2211840 | tf_op jit(solution)/shard_map/mul | solution.py:178
  120.7 1.0 copy.87
  121.7 3.3 %collective-permute-start.11 = (f32[256,128]{1,0:T(8,128)S(1)}, f32[256,128]{1,0:T(8,128)S(1)}, u32[]{:S(2)}, u32[]{:S(2)}) collective-permute-start(f32[256,128]{1,0:T(8,128)S(1)} %add.62), channel_id=1, source_target_pairs={{0,8},{4,12},{8,0},{12,4},{16,24},{20,28},{24,16},{28,20},{1,9},{5... | collective-permute-start | bytes 393224 | tf_op jit(solution)/shard_map/ppermute | solution.py:45
  125.0 4.1 %collective-permute-done.11 = f32[256,128]{1,0:T(8,128)S(1)} collective-permute-done((f32[256,128]{1,0:T(8,128)S(1)}, f32[256,128]{1,0:T(8,128)S(1)}, u32[]{:S(2)}, u32[]{:S(2)}) %collective-permute-start.11) | collective-permute-done | bytes 131104 | tf_op jit(solution)/shard_map/ppermute | solution.py:45
  129.1 0.1 collective-permute-start.12
  129.2 0.9 multiply_convert_fusion
  130.1 4.4 %collective-permute-done.12 = f32[256,128]{1,0:T(8,128)S(1)} collective-permute-done((f32[256,128]{1,0:T(8,128)S(1)}, f32[256,128]{1,0:T(8,128)S(1)}, u32[]{:S(2)}, u32[]{:S(2)}) %collective-permute-start.12) | collective-permute-done | bytes 131104 | tf_op jit(solution)/shard_map/ppermute | solution.py:45
  134.5 1.0 mul.63
  (41 shorter events, 0.5 us)
Async XLA Ops:
  0.6 10.0 %copy-start = (bf16[192,4,3,17]{0,1,3,2:T(4,128)(2,1)S(1)}, bf16[192,4,3,17]{0,1,3,2:T(4,128)(2,1)}, u32[]{:S(2)}) copy-start(bf16[192,4,3,17]{0,1,3,2:T(4,128)(2,1)} %param.16) | copy-start | bytes 235012
  4.8 6.1 %copy-start.7 = (s32[192]{0:T(256)S(1)}, s32[192]{0:T(256)}, u32[]{:S(2)}) copy-start(s32[192]{0:T(256)} %param.17) | copy-start | bytes 2308
  4.8 6.3 %copy-start.6 = (bf16[8,4,32,32]{3,2,1,0:T(8,128)(2,1)S(1)}, bf16[8,4,32,32]{3,2,1,0:T(8,128)(2,1)}, u32[]{:S(2)}) copy-start(bf16[8,4,32,32]{3,2,1,0:T(8,128)(2,1)} %param.18) | copy-start | bytes 196612
  6.9 16.8 %collective-permute-start = (bf16[1,45,264]{2,0,1:T(2,128)(2,1)}, bf16[1,45,264]{2,0,1:T(2,128)(2,1)S(1)}, u32[]{:S(2)}, u32[]{:S(2)}) collective-permute-start(bf16[1,45,264]{2,0,1:T(2,128)(2,1)} %get-tuple-element.79), channel_id=1, source_target_pairs={{0,4},{4,8},{8,12},{12,16},{16,20},{20,24},{24,28},{1,5},{5,9},{9,... | collective-permute-start | bytes 71288 | tf_op jit(solution)/shard_map/ppermute | solution.py:18
  9.3 14.4 %collective-permute-start.1 = (bf16[1,45,264]{2,0,1:T(2,128)(2,1)}, bf16[1,45,264]{2,0,1:T(2,128)(2,1)S(1)}, u32[]{:S(2)}, u32[]{:S(2)}) collective-permute-start(bf16[1,45,264]{2,0,1:T(2,128)(2,1)} %get-tuple-element.80), channel_id=1, source_target_pairs={{4,0},{8,4},{12,8},{16,12},{20,16},{24,20},{28,24},{5,1},{9,5},{13... | collective-permute-start | bytes 71288 | tf_op jit(solution)/shard_map/ppermute | solution.py:21
  20.3 3.2 %copy-start.5 = (bf16[24,45,256]{2,0,1:T(8,128)(2,1)S(1)}, bf16[24,45,256]{2,0,1:T(8,128)(2,1)}, u32[]{:S(2)}) copy-start(bf16[24,45,256]{2,0,1:T(8,128)(2,1)} %param.19) | copy-start | bytes 1658884
  23.9 8.7 %collective-permute-start.2 = (bf16[26,8,264]{2,0,1:T(8,128)(2,1)S(1)}, bf16[26,8,264]{2,0,1:T(8,128)(2,1)S(1)}, u32[]{:S(2)}, u32[]{:S(2)}) collective-permute-start(bf16[26,8,264]{2,0,1:T(8,128)(2,1)S(1)} %get-tuple-element.77), channel_id=1, source_target_pairs={{0,1},{1,2},{2,3},{3,0},{4,5},{5,6},{6,7},{7,4},{8,9},{9,10},{10,1... | collective-permute-start | bytes 329480 | tf_op jit(solution)/shard_map/ppermute | solution.py:18
  26.3 11.8 %collective-permute-start.3 = (bf16[26,8,264]{2,0,1:T(8,128)(2,1)S(1)}, bf16[26,8,264]{2,0,1:T(8,128)(2,1)S(1)}, u32[]{:S(2)}, u32[]{:S(2)}) collective-permute-start(bf16[26,8,264]{2,0,1:T(8,128)(2,1)S(1)} %get-tuple-element.78), channel_id=1, source_target_pairs={{1,0},{2,1},{3,2},{0,3},{5,4},{6,5},{7,6},{4,7},{9,8},{10,9},{11,1... | collective-permute-start | bytes 329480 | tf_op jit(solution)/shard_map/ppermute | solution.py:21
  74.7 1.0 copy-start.1
  75.7 3.9 %copy-start.4 = (f32[1664,256]{1,0:T(8,128)S(1)}, f32[1664,256]{1,0:T(8,128)}, u32[]{:S(2)}) copy-start(f32[1664,256]{1,0:T(8,128)} %get-tuple-element.55) | copy-start | bytes 5111812
  79.7 12.2 %collective-permute-start.4 = (f32[1,61,256]{2,0,1:T(1,128)S(1)}, f32[1,61,256]{2,0,1:T(1,128)S(1)}, u32[]{:S(2)}, u32[]{:S(2)}) collective-permute-start(f32[1,61,256]{2,0,1:T(1,128)S(1)} %copy.93), channel_id=1, source_target_pairs={{4,0},{8,4},{12,8},{16,12},{20,16},{24,20},{28,24},{5,1},{9,5},{13... | collective-permute-start | bytes 187400 | tf_op jit(solution)/shard_map/ppermute | solution.py:29
  86.1 12.6 %collective-permute-start.8 = (f32[256,128]{1,0:T(8,128)S(1)}, f32[256,128]{1,0:T(8,128)S(1)}, u32[]{:S(2)}, u32[]{:S(2)}) collective-permute-start(f32[256,128]{1,0:T(8,128)S(1)} %reshape.216), channel_id=1, source_target_pairs={{0,1},{1,0},{2,3},{3,2},{4,5},{5,4},{6,7},{7,6},{8,9},{9,8},{10,11... | collective-permute-start | bytes 393224 | tf_op jit(solution)/shard_map/ppermute | solution.py:45
  89.2 5.4 %collective-permute-start.5 = (f32[1,61,256]{2,0,1:T(1,128)S(1)}, f32[1,61,256]{2,0,1:T(1,128)S(1)}, u32[]{:S(2)}, u32[]{:S(2)}) collective-permute-start(f32[1,61,256]{2,0,1:T(1,128)S(1)} %copy.94), channel_id=1, source_target_pairs={{0,4},{4,8},{8,12},{12,16},{16,20},{20,24},{24,28},{1,5},{5,9},{9,... | collective-permute-start | bytes 187400 | tf_op jit(solution)/shard_map/ppermute | solution.py:29
  97.3 4.7 %collective-permute-start.6 = (bf16[24,8,256]{2,0,1:T(8,128)(2,1)S(1)}, bf16[24,8,256]{2,0,1:T(8,128)(2,1)S(1)}, u32[]{:S(2)}, u32[]{:S(2)}) collective-permute-start(bf16[24,8,256]{2,0,1:T(8,128)(2,1)S(1)} %slice.175), channel_id=1, source_target_pairs={{0,3},{1,0},{2,1},{3,2},{4,7},{5,4},{6,5},{7,6},{8,11},{9,8},{10,9... | collective-permute-start | bytes 294920 | tf_op jit(solution)/shard_map/ppermute | solution.py:34
  98.7 14.2 %collective-permute-start.9 = (f32[256,128]{1,0:T(8,128)S(1)}, f32[256,128]{1,0:T(8,128)S(1)}, u32[]{:S(2)}, u32[]{:S(2)}) collective-permute-start(f32[256,128]{1,0:T(8,128)S(1)} %add.60), channel_id=1, source_target_pairs={{0,2},{1,3},{2,0},{3,1},{4,6},{5,7},{6,4},{7,5},{8,10},{9,11},{10,... | collective-permute-start | bytes 393224 | tf_op jit(solution)/shard_map/ppermute | solution.py:45
  102.0 1.0 copy-start.2
  103.0 22.0 %collective-permute-start.7 = (f32[24,8,256]{2,0,1:T(8,128)S(1)}, f32[24,8,256]{2,0,1:T(8,128)S(1)}, u32[]{:S(2)}, u32[]{:S(2)}) collective-permute-start(f32[24,8,256]{2,0,1:T(8,128)S(1)} %get-tuple-element.75), channel_id=1, source_target_pairs={{0,1},{1,2},{2,3},{3,0},{4,5},{5,6},{6,7},{7,4},{8,9},{9,10},{10,1... | collective-permute-start | bytes 589832 | tf_op jit(solution)/shard_map/ppermute | solution.py:34
  112.9 8.7 %collective-permute-start.10 = (f32[256,128]{1,0:T(8,128)S(1)}, f32[256,128]{1,0:T(8,128)S(1)}, u32[]{:S(2)}, u32[]{:S(2)}) collective-permute-start(f32[256,128]{1,0:T(8,128)S(1)} %add.61), channel_id=1, source_target_pairs={{0,4},{4,0},{8,12},{12,8},{16,20},{20,16},{24,28},{28,24},{1,5},{5... | collective-permute-start | bytes 393224 | tf_op jit(solution)/shard_map/ppermute | solution.py:45
  120.7 4.3 %copy-start.3 = (f32[24,45,256]{2,0,1:T(8,128)S(1)}, f32[24,45,256]{2,0,1:T(8,128)}, u32[]{:S(2)}) copy-start(f32[24,45,256]{2,0,1:T(8,128)} %copy-done.2) | copy-start | bytes 3317764
  121.7 7.4 %collective-permute-start.11 = (f32[256,128]{1,0:T(8,128)S(1)}, f32[256,128]{1,0:T(8,128)S(1)}, u32[]{:S(2)}, u32[]{:S(2)}) collective-permute-start(f32[256,128]{1,0:T(8,128)S(1)} %add.62), channel_id=1, source_target_pairs={{0,8},{4,12},{8,0},{12,4},{16,24},{20,28},{24,16},{28,20},{1,9},{5... | collective-permute-start | bytes 393224 | tf_op jit(solution)/shard_map/ppermute | solution.py:45
  129.1 5.4 %collective-permute-start.12 = (f32[256,128]{1,0:T(8,128)S(1)}, f32[256,128]{1,0:T(8,128)S(1)}, u32[]{:S(2)}, u32[]{:S(2)}) collective-permute-start(f32[256,128]{1,0:T(8,128)S(1)} %add.63), channel_id=1, source_target_pairs={{0,16},{4,20},{8,24},{12,28},{16,0},{20,4},{24,8},{28,12},{1,17},{... | collective-permute-start | bytes 393224 | tf_op jit(solution)/shard_map/ppermute | solution.py:45

commit v4 on v3

--- a/solution.py
+++ b/solution.py
@@ -158,7 +158,7 @@
         axis=3,
     ).transpose(1, 0, 2, 3)
     cell_count = row_count * lax.axis_size("lat") * col_count * lax.axis_size("lon")
-    dense = butterfly_sum(local_grad.reshape(-1, 128), ("lon", "lat"))
+    dense = lax.psum(local_grad.reshape(-1, 128), ("lat", "lon"))
     weight_grad = dense.reshape(local_grad.shape) * (1.0 / math.sqrt(cell_count))
 
     collected = collected.reshape(row_count + 2, lane_rows, chan_count)[:, :padded_cols]

time: 136 us -> 244 us (1.79)
  waiting for transfers between devices: 28.2 us -> 125 us
  between operations: 1.07 us -> 14.4 us
  starting transfers between devices: 21.9 us -> 16.2 us
  other arithmetic: 12.3 us -> 15.8 us
    psum x0 -> x1, waiting for transfers between devices: none -> 123 us  [local(): dense = lax.psum(local_grad.reshape(-1, 128), ('lat', 'lon'))]
    ppermute x5 -> x0, waiting for transfers between devices: 17 us -> none  [butterfly_sum(): partner = lax.ppermute(value, axis, [(i, i ^ step) for i in range(count)])]
    ppermute x5 -> x0, starting transfers between devices: 6.79 us -> none  [butterfly_sum(): partner = lax.ppermute(value, axis, [(i, i ^ step) for i in range(count)])]
    ppermute x2, waiting for transfers between devices: 5.62 us -> 1.6 us  [with_halo(): lax.ppermute(lax.slice_in_dim(block, 0, width, axis=dim), axis, backward)]
    ppermute x2, waiting for transfers between devices: 3.95 us -> 0.01 us  [with_halo(): lax.ppermute(lax.slice_in_dim(block, block.shape[dim] - width, None, axis...]
    unnamed x24 -> x18, local copies, waits for them, and re-layouts: 7.16 us -> 3.68 us
    ppermute x2, starting transfers between devices: 4.05 us -> 6.52 us  [passed_along(): return lax.ppermute(block, axis, route)]
  transfers between devices with their start and end apart: 13 -> 9, of which waited for: 6 -> 2; matrix products, arithmetic and copies ran while one was open for 25% -> 15% of each run, Pallas kernels for 0% -> 0%
where the time goes in v4:
time: 244 us; the launch traced here: 243 us
  waiting for transfers between devices  125 us (51%)
  local copies, waits for them, and re-layouts  47.7 us (20%)
  Pallas kernels  22.6 us (9%)
  starting transfers between devices  16.2 us (7%)
  other arithmetic  15.8 us (6%)
  between operations  14.4 us (6%)
    psum x1, waiting for transfers between devices, local(): dense = lax.psum(local_grad.reshape(-1, 128), ('lat', 'lon'))  123 us
    pallas_call x1, Pallas kernels, local(): pl.pallas_call(conv_kernel, out_shape=(jax.ShapeDtypeStruct((row_count, c...  22.6 us
    mul x2, local copies, waits for them, and re-layouts, local(): gathered.reshape(row_count, col_count, group_count, group_width)  7.5 us
    ppermute x2, starting transfers between devices, passed_along(): return lax.ppermute(block, axis, route)  6.52 us
    another operation x2, local copies, waits for them, and re-layouts, local(): jnp.repeat(packed[..., chan_count:], group_width, axis=-1)  5.52 us
  transfers between devices with their start and end apart: 9, of which 2 were waited for; matrix products, arithmetic and copies ran while one was open for 15% of the time, Pallas kernels for 0%

profile of v4, /device:TPU:0, one launch (start us, length us, event | category | flops | bytes accessed | tf_op | source)
XLA Modules:
  0.0 242.8 jit_solution(4229020158672194245)
XLA Ops:
  7.2 0.0 copy-start
  7.2 0.0 all-reduce.4.cloned.1.call-start
  7.2 1.2 copy.71
  8.5 1.4 mul.50
  9.8 1.5 mul.51
  11.4 0.0 copy-start.4
  11.4 0.0 copy-start.3
  11.4 1.3 mul.52
  12.7 0.8 pad_maximum_fusion.5
  13.5 2.4 collective-permute-start
  15.9 1.3 collective-permute-start.1
  17.2 0.1 compare_convert_fusion
  17.3 0.1 copy.74
  17.4 0.1 constant_dynamic-slice_fusion
  17.6 0.2 copy.79
  17.8 0.1 copy.78
  17.9 1.7 multiply_bitcast_fusion
  19.6 0.2 copy.95
  19.7 1.6 collective-permute-done.1
  21.3 0.9 pad_maximum_fusion.3
  22.3 1.6 collective-permute-start.2
  23.8 2.2 collective-permute-start.3
  26.1 1.1 fusion.13
  27.2 2.6 %copy.98.t_ref = bf16[24,4,3,48,64]{4,3,2,1,0:T(8,128)(2,1)} copy(bf16[24,4,3,48,64]{4,0,3,2,1:T(8,128)(2,1)S(1)} %fusion.13) | data formatting | bytes 3538944 | tf_op jit(solution)/shard_map/ibae,ejp->ibajp/dot_general | solution.py:130
  29.8 2.1 reshape.219
  32.0 1.2 copy.90.w_ref
  33.2 0.0 copy-start.2
  33.2 3.2 %reshape.213.wt_ref = bf16[4,256,256]{2,1,0:T(8,128)(2,1)S(1)} reshape(bf16[4,8,32,8,32]{4,3,2,1,0:T(8,128)(2,1)} %get-tuple-element.81) | data formatting | bytes 1048576 | tf_op jit(solution)/shard_map/reshape | solution.py:136
  36.4 0.1 copy.77
  36.5 3.1 %mul.56 = f32[24,45,8,32]{3,2,0,1:T(8,128)} broadcast(bf16[24,45,8]{2,0,1:T(8,128)(2,1)S(1)} %convert_element_type.38), dimensions={0,1,2} | broadcast | bytes 1123200 | tf_op jit(solution)/shard_map/mul | solution.py:178
  39.7 4.4 %mul.57 = f32[24,45,256]{2,0,1:T(8,128)} reshape(f32[24,45,8,32]{3,2,0,1:T(8,128)} %mul.56) | data formatting | bytes 2211840 | tf_op jit(solution)/shard_map/mul | solution.py:178
  44.1 0.0 collective-permute-done.2
  44.1 4.1 %fusion.7 = bf16[26,64,264]{2,0,1:T(8,128)(2,1)S(1)} fusion(bf16[26,8,264]{2,0,1:T(8,128)(2,1)} %collective-permute-done.3, bf16[26,8,264]{2,0,1:T(8,128)(2,1)} %collective-permute-done.2, bf16[1,45,264]{2,0,1:T(2,128)(2,1)S(1)} %collective-permute-done.1, bf16[1,45,264]{2,0,1:T(2,128)(2,1)S(1)} %collective-permute-done, ...), kind=kLoop, calls=%fused_computation.12 | loop fusion | flops 8346624 | bytes 1716000 | tf_op jit(solution)/shard_map/concatenate | solution.py:22
  48.3 0.1 slice.156
  48.4 1.1 slice.155
  49.5 0.6 copy.73
  50.1 1.6 broadcast_in_dim.2
  51.7 4.0 %reshape_reshape.3 = bf16[1664,256]{0,1:T(8,128)(2,1)} reshape(bf16[26,64,8,32]{1,0,3,2:T(8,128)(2,1)} %broadcast_in_dim.2) | data formatting | bytes 1703936 | tf_op jit(solution)/shard_map/reshape;reshape | solution.py:113
  55.7 1.5 copy.81.m_ref
  57.3 1.7 copy.72
  59.0 22.6 %shard_map.85 = (bf16[24,45,256]{2,1,0:T(8,128)(2,1)S(1)}, f32[4,256,256]{2,1,0:T(8,128)S(1)}, f32[1664,256]{1,0:T(8,128)}) custom-call(bf16[1664,256]{1,0:T(8,128)(2,1)S(1)} %bitcast.35, bf16[1664,256]{1,0:T(8,128)(2,1)S(1)} %copy.81.m_ref, bf16[24,4,3,48,64]{4,3,2,1,0:T(8,128)(2,1)} %copy.98.t_ref, bf16[24,48,256]{2,1,0:T(8,128)(2,1)S(1)} %pad.17.cot_ref, ...), custom_call_target="tpu_custom_call" | custom-call | tf_op jit(solution)/shard_map/pallas_call | solution.py:141
  81.6 1.1 fusion.24
  82.7 0.1 copy.93
  82.7 1.3 collective-permute-start.4
  84.0 1.6 slice.157
  85.6 0.9 copy.91
  86.5 0.1 copy.94
  86.6 5.2 %collective-permute-start.5 = (f32[1,61,256]{2,0,1:T(1,128)S(1)}, f32[1,61,256]{2,0,1:T(1,128)S(1)}, u32[]{:S(2)}, u32[]{:S(2)}) collective-permute-start(f32[1,61,256]{2,0,1:T(1,128)S(1)} %copy.94), channel_id=1, source_target_pairs={{0,4},{4,8},{8,12},{12,16},{16,20},{20,24},{24,28},{1,5},{5,9},{9,... | collective-permute-start | bytes 187400 | tf_op jit(solution)/shard_map/ppermute | solution.py:29
  91.8 3.7 %reshape.215 = f32[4,8,32,8,32]{4,3,2,1,0:T(8,128)} reshape(f32[4,256,256]{2,1,0:T(8,128)} %copy-done.1) | data formatting | bytes 2097152 | tf_op jit(solution)/shard_map/reshape | solution.py:156
  95.5 0.1 copy_add_fusion
  95.6 2.6 %scatter-add.14 = f32[24,61,256]{2,0,1:T(8,128)S(1)} dynamic-update-slice(f32[24,61,256]{2,0,1:T(8,128)S(1)} %copy.91, f32[1,61,256]{2,0,1:T(1,128)S(1)} %copy_add_fusion, s32[]{:T(128)} %constant.126.clone.1, s32[]{:T(128)} %constant.123.clone.1, s32[]{:T(128)} %constant.123.clone.1) | dynamic-update-slice | bytes 124932 | tf_op jit(solution)/shard_map/scatter-add | solution.py:168
  98.2 0.1 slice_add_fusion.2
  98.3 2.6 %scatter-add.15 = f32[24,61,256]{2,0,1:T(8,128)S(1)} dynamic-update-slice(f32[24,61,256]{2,0,1:T(8,128)S(1)} %scatter-add.14, f32[1,61,256]{2,0,1:T(1,128)S(1)} %slice_add_fusion.2, s32[]{:T(128)} %constant.123.clone.1, s32[]{:T(128)} %constant.123.clone.1, s32[]{:T(128)} %constant.123.clone.1) | dynamic-update-slice | bytes 124932 | tf_op jit(solution)/shard_map/scatter-add | solution.py:169
  100.9 1.8 collective-permute-start.6
  102.7 3.6 %multiply_reduce_fusion = f32[4,8,32,32]{3,2,1,0:T(8,128)S(1)} fusion(f32[4,8,32,8,32]{4,3,2,1,0:T(8,128)} %reshape.215, f32[8,8]{1,0:T(8,128)S(1)} %fusion.22), kind=kLoop, calls=%fused_computation.1 | loop fusion | flops 491520 | bytes 1179904 | tf_op jit(solution)/shard_map/reduce_sum | solution.py:155
  106.3 0.8 reshape.216
  107.1 0.0 all-reduce.4.cloned.1.call-update
  107.1 1.0 copy.87
  108.1 0.1 slice.162
  108.2 0.3 collective-permute-start.7
  108.6 123.3 %all-reduce.4.cloned.1.call-done = f32[256,128]{1,0:T(8,128)} async-done(((f32[256,128]{1,0:T(8,128)}), f32[256,128]{1,0:T(8,128)}) %all-reduce.4.cloned.1.call-update) | async-done | bytes 131088 | tf_op jit(solution)/shard_map/psum | solution.py:161
  231.9 0.9 broadcast_multiply_fusion
  232.8 1.0 mul.63
  233.8 2.2 multiply_convert_fusion
  (24 shorter events, 0.3 us)
Async XLA Ops:
  7.2 10.3 %copy-start = (bf16[192,4,3,17]{0,1,3,2:T(4,128)(2,1)S(1)}, bf16[192,4,3,17]{0,1,3,2:T(4,128)(2,1)}, u32[]{:S(2)}) copy-start(bf16[192,4,3,17]{0,1,3,2:T(4,128)(2,1)} %param.16) | copy-start | bytes 235012
  7.2 224.7 %all-reduce.4.cloned.1.call-start = ((), (), s32[]{:S(2)}) async-start(), calls=%async_computation | async-start | bytes 262144 | tf_op jit(solution)/shard_map/psum | solution.py:161
  11.4 5.8 %copy-start.4 = (s32[192]{0:T(256)S(1)}, s32[192]{0:T(256)}, u32[]{:S(2)}) copy-start(s32[192]{0:T(256)} %param.17) | copy-start | bytes 2308
  11.4 6.2 %copy-start.3 = (bf16[8,4,32,32]{3,2,1,0:T(8,128)(2,1)S(1)}, bf16[8,4,32,32]{3,2,1,0:T(8,128)(2,1)}, u32[]{:S(2)}) copy-start(bf16[8,4,32,32]{3,2,1,0:T(8,128)(2,1)} %param.18) | copy-start | bytes 196612
  13.5 6.3 %collective-permute-start = (bf16[1,45,264]{2,0,1:T(2,128)(2,1)}, bf16[1,45,264]{2,0,1:T(2,128)(2,1)S(1)}, u32[]{:S(2)}, u32[]{:S(2)}) collective-permute-start(bf16[1,45,264]{2,0,1:T(2,128)(2,1)} %get-tuple-element.79), channel_id=1, source_target_pairs={{0,4},{4,8},{8,12},{12,16},{16,20},{20,24},{24,28},{1,5},{5,9},{9,... | collective-permute-start | bytes 71288 | tf_op jit(solution)/shard_map/ppermute | solution.py:18
  15.9 5.5 %collective-permute-start.1 = (bf16[1,45,264]{2,0,1:T(2,128)(2,1)}, bf16[1,45,264]{2,0,1:T(2,128)(2,1)S(1)}, u32[]{:S(2)}, u32[]{:S(2)}) collective-permute-start(bf16[1,45,264]{2,0,1:T(2,128)(2,1)} %get-tuple-element.80), channel_id=1, source_target_pairs={{4,0},{8,4},{12,8},{16,12},{20,16},{24,20},{28,24},{5,1},{9,5},{13... | collective-permute-start | bytes 71288 | tf_op jit(solution)/shard_map/ppermute | solution.py:21
  22.3 21.8 %collective-permute-start.2 = (bf16[26,8,264]{2,0,1:T(8,128)(2,1)}, bf16[26,8,264]{2,0,1:T(8,128)(2,1)}, u32[]{:S(2)}, u32[]{:S(2)}) collective-permute-start(bf16[26,8,264]{2,0,1:T(8,128)(2,1)} %get-tuple-element.77), channel_id=1, source_target_pairs={{0,1},{1,2},{2,3},{3,0},{4,5},{5,6},{6,7},{7,4},{8,9},{9,10},{10,1... | collective-permute-start | bytes 329480 | tf_op jit(solution)/shard_map/ppermute | solution.py:18
  23.8 20.3 %collective-permute-start.3 = (bf16[26,8,264]{2,0,1:T(8,128)(2,1)}, bf16[26,8,264]{2,0,1:T(8,128)(2,1)}, u32[]{:S(2)}, u32[]{:S(2)}) collective-permute-start(bf16[26,8,264]{2,0,1:T(8,128)(2,1)} %get-tuple-element.78), channel_id=1, source_target_pairs={{1,0},{2,1},{3,2},{0,3},{5,4},{6,5},{7,6},{4,7},{9,8},{10,9},{11,1... | collective-permute-start | bytes 329480 | tf_op jit(solution)/shard_map/ppermute | solution.py:21
  33.2 3.2 %copy-start.2 = (bf16[24,45,256]{2,0,1:T(8,128)(2,1)S(1)}, bf16[24,45,256]{2,0,1:T(8,128)(2,1)}, u32[]{:S(2)}) copy-start(bf16[24,45,256]{2,0,1:T(8,128)(2,1)} %param.19) | copy-start | bytes 1658884
  81.6 4.1 %copy-start.1 = (f32[4,256,256]{2,1,0:T(8,128)}, f32[4,256,256]{2,1,0:T(8,128)S(1)}, u32[]{:S(2)}) copy-start(f32[4,256,256]{2,1,0:T(8,128)S(1)} %get-tuple-element.56) | copy-start | bytes 3145732
  82.7 12.8 %collective-permute-start.4 = (f32[1,61,256]{2,0,1:T(1,128)S(1)}, f32[1,61,256]{2,0,1:T(1,128)S(1)}, u32[]{:S(2)}, u32[]{:S(2)}) collective-permute-start(f32[1,61,256]{2,0,1:T(1,128)S(1)} %copy.93), channel_id=1, source_target_pairs={{4,0},{8,4},{12,8},{16,12},{20,16},{24,20},{28,24},{5,1},{9,5},{13... | collective-permute-start | bytes 187400 | tf_op jit(solution)/shard_map/ppermute | solution.py:29
  86.6 11.6 %collective-permute-start.5 = (f32[1,61,256]{2,0,1:T(1,128)S(1)}, f32[1,61,256]{2,0,1:T(1,128)S(1)}, u32[]{:S(2)}, u32[]{:S(2)}) collective-permute-start(f32[1,61,256]{2,0,1:T(1,128)S(1)} %copy.94), channel_id=1, source_target_pairs={{0,4},{4,8},{8,12},{12,16},{16,20},{20,24},{24,28},{1,5},{5,9},{9,... | collective-permute-start | bytes 187400 | tf_op jit(solution)/shard_map/ppermute | solution.py:29
  100.9 7.3 %collective-permute-start.6 = (bf16[24,8,256]{2,0,1:T(8,128)(2,1)S(1)}, bf16[24,8,256]{2,0,1:T(8,128)(2,1)S(1)}, u32[]{:S(2)}, u32[]{:S(2)}) collective-permute-start(bf16[24,8,256]{2,0,1:T(8,128)(2,1)S(1)} %slice.175), channel_id=1, source_target_pairs={{0,3},{1,0},{2,1},{3,2},{4,7},{5,4},{6,5},{7,6},{8,11},{9,8},{10,9... | collective-permute-start | bytes 294920 | tf_op jit(solution)/shard_map/ppermute | solution.py:34
  108.2 125.6 %collective-permute-start.7 = (f32[24,8,256]{2,0,1:T(8,128)S(1)}, f32[24,8,256]{2,0,1:T(8,128)S(1)}, u32[]{:S(2)}, u32[]{:S(2)}) collective-permute-start(f32[24,8,256]{2,0,1:T(8,128)S(1)} %get-tuple-element.75), channel_id=1, source_target_pairs={{0,1},{1,2},{2,3},{3,0},{4,5},{5,6},{6,7},{7,4},{8,9},{9,10},{10,1... | collective-permute-start | bytes 589832 | tf_op jit(solution)/shard_map/ppermute | solution.py:34
Sparse Core Ops, SparseCore 0:
  107.2 124.6 all-reduce.3

commit v5 on v4

--- a/solution.py
+++ b/solution.py
@@ -34,7 +34,7 @@
     return lax.ppermute(x, axis, [(i, (i + by) % size) for i in range(size)])
 
 
-def butterfly_sum(value, axes):
+def butterfly_sum(value, axes, skip=0):
     for axis in axes:
         count = lax.axis_size(axis)
         if count & (count - 1):
@@ -42,48 +42,71 @@
             continue
         step = 1
         while step < count:
+            if skip:
+                skip -= 1
+                step *= 2
+                continue
             partner = lax.ppermute(value, axis, [(i, i ^ step) for i in range(count)])
             value = value + partner
             step *= 2
     return value
 
 
-def conv_kernel(x_ref, m_ref, t_ref, cot_ref, w_ref, wt_ref, inf_ref, wg_ref, col_ref, pulled_ref):
+def forward_kernel(x_ref, m_ref, t_ref, cot_ref, w_ref, wt_ref, inf_ref, wg_ref, pulled_ref, acc_ref):
     rows, basis_count, lat_taps, col_pad, lane_rows = t_ref.shape
     col_count = inf_ref.shape[1]
-    col_ref[...] = jnp.zeros_like(col_ref)
-    wg_ref[...] = jnp.zeros_like(wg_ref)
+    chan_count = w_ref.shape[1]
+    group_width = wg_ref.shape[1]
+    acc_ref[...] = jnp.zeros_like(acc_ref)
 
     def body(i, carry):
-        bands = [t_ref[i, :, a].reshape(basis_count * col_pad, lane_rows) for a in range(lat_taps)]
         numerator = None
         denominator = None
         for a in range(lat_taps):
+            band = t_ref[i, :, a].reshape(basis_count * col_pad, lane_rows)
             start = pl.multiple_of((i + a) * lane_rows, lane_rows)
-            num = jnp.dot(bands[a], x_ref[pl.ds(start, lane_rows), :], preferred_element_type=jnp.float32)
-            den = jnp.dot(bands[a], m_ref[pl.ds(start, lane_rows), :], preferred_element_type=jnp.float32)
+            num = jnp.dot(band, x_ref[pl.ds(start, lane_rows), :], preferred_element_type=jnp.float32)
+            den = jnp.dot(band, m_ref[pl.ds(start, lane_rows), :], preferred_element_type=jnp.float32)
             numerator = num if numerator is None else numerator + num
             denominator = den if denominator is None else denominator + den
         safe = jnp.maximum(denominator, 1.0)
         scaled = (numerator / safe).astype(jnp.bfloat16)
         upstream = cot_ref[i]
-        out = jnp.zeros((col_pad, upstream.shape[1]), jnp.float32)
+        out = jnp.zeros((col_pad, chan_count), jnp.float32)
         for b in range(basis_count):
             part = scaled[b * col_pad : (b + 1) * col_pad]
             out = out + jnp.dot(part, w_ref[b], preferred_element_type=jnp.float32)
-            wg_ref[b] += lax.dot_general(
+            acc_ref[b] += lax.dot_general(
                 part, upstream, (((0,), (0,)), ((), ())), preferred_element_type=jnp.float32
             )
             back = jnp.dot(upstream, wt_ref[b], preferred_element_type=jnp.float32)
-            pulled_ref[b * col_pad : (b + 1) * col_pad, :] = (
+            pulled_ref[i, b * col_pad : (b + 1) * col_pad, :] = (
                 back / safe[b * col_pad : (b + 1) * col_pad]
             ).astype(jnp.bfloat16)
         inf_ref[i] = out[:col_count].astype(inf_ref.dtype)
-        pulled = pulled_ref[...]
+        return carry
+
+    lax.fori_loop(0, rows, body, 0)
+    lane = lax.broadcasted_iota(jnp.int32, (group_width, chan_count), 1) // group_width
+    for b in range(basis_count):
+        total = jnp.zeros((group_width, chan_count), jnp.float32)
+        for g in range(chan_count // group_width):
+            block = acc_ref[b, g * group_width : (g + 1) * group_width, :]
+            total = total + jnp.where(lane == g, block, 0.0)
+        wg_ref[b] = total
+
+
+def adjoint_kernel(t_ref, pulled_ref, order_ref, col_ref):
+    rows, basis_count, lat_taps, col_pad, lane_rows = t_ref.shape
+    col_ref[...] = jnp.zeros_like(col_ref)
+
+    def body(i, carry):
+        pulled = pulled_ref[i]
         for a in range(lat_taps):
+            band = t_ref[i, :, a].reshape(basis_count * col_pad, lane_rows)
             start = pl.multiple_of((i + a) * lane_rows, lane_rows)
             term = lax.dot_general(
-                bands[a], pulled, (((0,), (0,)), ((), ())), preferred_element_type=jnp.float32
+                band, pulled, (((0,), (0,)), ((), ())), preferred_element_type=jnp.float32
             )
             col_ref[pl.ds(start, lane_rows), :] += term
         return carry
@@ -138,28 +161,49 @@
     )
     upstream = jnp.pad(cotangent, ((0, 0), (0, col_pad - col_count), (0, 0)))
 
-    infilled, grad_blocks, collected = pl.pallas_call(
-        conv_kernel,
+    vmem = pl.BlockSpec(memory_space=pltpu.VMEM)
+    params = pltpu.CompilerParams(vmem_limit_bytes=48 * 1024 * 1024)
+    infilled, grad_blocks, pulled = pl.pallas_call(
+        forward_kernel,
         out_shape=(
             jax.ShapeDtypeStruct((row_count, col_count, chan_count), jnp.bfloat16),
-            jax.ShapeDtypeStruct((basis_count, chan_count, chan_count), jnp.float32),
-            jax.ShapeDtypeStruct(((row_count + 2) * lane_rows, chan_count), jnp.float32),
+            jax.ShapeDtypeStruct((basis_count, group_width, chan_count), jnp.float32),
+            jax.ShapeDtypeStruct((row_count, basis_count * col_pad, chan_count), jnp.bfloat16),
         ),
-        in_specs=[pl.BlockSpec(memory_space=pltpu.VMEM)] * 6,
-        out_specs=[pl.BlockSpec(memory_space=pltpu.VMEM)] * 3,
-        scratch_shapes=[pltpu.VMEM((basis_count * col_pad, chan_count), jnp.bfloat16)],
-        compiler_params=pltpu.CompilerParams(vmem_limit_bytes=48 * 1024 * 1024),
+        in_specs=[vmem] * 6,
+        out_specs=[vmem] * 3,
+        scratch_shapes=[pltpu.VMEM((basis_count, chan_count, chan_count), jnp.float32)],
+        compiler_params=params,
+        cost_estimate=pl.CostEstimate(
+            flops=2 * row_count * basis_count * col_pad * chan_count * (6 * lane_rows + 3 * chan_count),
+            transcendentals=0,
+            bytes_accessed=8 * (row_count + 2) * lane_rows * chan_count,
+        ),
     )(full_input, full_mask, band, upstream, mix_blocks, mix_blocks_t)
 
-    diagonal = jnp.eye(group_count, dtype=jnp.float32)[None, :, None, :, None]
-    local_grad = jnp.sum(
-        grad_blocks.reshape(basis_count, group_count, group_width, group_count, group_width)
-        * diagonal,
-        axis=3,
-    ).transpose(1, 0, 2, 3)
     cell_count = row_count * lax.axis_size("lat") * col_count * lax.axis_size("lon")
-    dense = lax.psum(local_grad.reshape(-1, 128), ("lat", "lon"))
-    weight_grad = dense.reshape(local_grad.shape) * (1.0 / math.sqrt(cell_count))
+    lat_count = lax.axis_size("lat")
+    if lat_count % 2 == 0:
+        first = lax.ppermute(grad_blocks, "lat", [(i, i ^ 1) for i in range(lat_count)])
+        dense = butterfly_sum(grad_blocks + first, ("lat", "lon"), skip=1)
+    else:
+        first = grad_blocks
+        dense = butterfly_sum(grad_blocks, ("lat", "lon"))
+    dense = dense * (1.0 / math.sqrt(cell_count))
+    weight_grad = dense.reshape(basis_count, group_width, group_count, group_width).transpose(2, 0, 1, 3)
+
+    collected = pl.pallas_call(
+        adjoint_kernel,
+        out_shape=jax.ShapeDtypeStruct(((row_count + 2) * lane_rows, chan_count), jnp.float32),
+        in_specs=[vmem, vmem, pl.BlockSpec(memory_space=pl.ANY)],
+        out_specs=vmem,
+        compiler_params=params,
+        cost_estimate=pl.CostEstimate(
+            flops=6 * row_count * basis_count * col_pad * lane_rows * chan_count,
+            transcendentals=0,
+            bytes_accessed=6 * (row_count + 2) * lane_rows * chan_count,
+        ),
+    )(band, pulled, first)
 
     collected = collected.reshape(row_count + 2, lane_rows, chan_count)[:, :padded_cols]
     from_below = passed_along(collected[0:1], "lat", -1)

time: 244 us -> 124 us (0.51)
  waiting for transfers between devices: 125 us -> 12.6 us
  between operations: 14.4 us -> 1.07 us
  starting transfers between devices: 16.2 us -> 27.4 us
  Pallas kernels: 22.6 us -> 28.5 us
  other arithmetic: 15.8 us -> 10.2 us
  local copies, waits for them, and re-layouts: 47.7 us -> 42.6 us
    psum x1 -> x0, waiting for transfers between devices: 123 us -> none  [local(): dense = lax.psum(local_grad.reshape(-1, 128), ('lat', 'lon'))]
    ppermute x0 -> x5, starting transfers between devices: none -> 13.5 us  [the longest x4 11 us: butterfly_sum(): partner = lax.ppermute(value, axis, [(i, i ^ step) for i in range(count)])]
    ppermute x0 -> x5, waiting for transfers between devices: none -> 10.9 us  [the longest x4 9.89 us: butterfly_sum(): partner = lax.ppermute(value, axis, [(i, i ^ step) for i in range(count)])]
    pallas_call x1 -> x2, Pallas kernels: 22.6 us -> 28.5 us  [the longest x1 21.1 us: local(): pl.pallas_call(forward_kernel, out_shape=(jax.ShapeDtypeStruct((row_count...]
    reduce_sum x1 -> x0, other arithmetic: 3.57 us -> none  [local(): jnp.sum(grad_blocks.reshape(basis_count, group_count, group_width, group_...]
    reshape x2, local copies, waits for them, and re-layouts: 4.55 us -> 1.06 us  [local(): dense.reshape(basis_count, group_width, group_count, group_width)]
    unnamed x18 -> x26, local copies, waits for them, and re-layouts: 3.68 us -> 6.49 us
  transfers between devices with their start and end apart: 9 -> 13, of which waited for: 2 -> 5; matrix products, arithmetic and copies ran while one was open for 15% -> 21% of each run, Pallas kernels for 0% -> 0%
where the time goes in v5:
time: 124 us
  local copies, waits for them, and re-layouts  42.6 us (34%)
  Pallas kernels  28.5 us (23%)
  starting transfers between devices  27.4 us (22%)
  waiting for transfers between devices  12.6 us (10%)
  other arithmetic  10.2 us (8%)
    pallas_call x1, Pallas kernels, local(): pl.pallas_call(forward_kernel, out_shape=(jax.ShapeDtypeStruct((row_count...  21.1 us
    ppermute x4, starting transfers between devices, butterfly_sum(): partner = lax.ppermute(value, axis, [(i, i ^ step) for i in range(count)])  11 us
    ppermute x4, waiting for transfers between devices, butterfly_sum(): partner = lax.ppermute(value, axis, [(i, i ^ step) for i in range(count)])  9.89 us
    pallas_call x1, Pallas kernels, local(): pl.pallas_call(adjoint_kernel, out_shape=jax.ShapeDtypeStruct(((row_count...  7.41 us
    mul x2, local copies, waits for them, and re-layouts, local(): gathered.reshape(row_count, col_count, group_count, group_width)  6.65 us
    unnamed x26, local copies, waits for them, and re-layouts  6.49 us
    another operation x2, local copies, waits for them, and re-layouts, local(): jnp.repeat(packed[..., chan_count:], group_width, axis=-1)  5.52 us
    ppermute x2, starting transfers between devices, passed_along(): return lax.ppermute(block, axis, route)  4.33 us
  transfers between devices with their start and end apart: 13, of which 5 were waited for; matrix products, arithmetic and copies ran while one was open for 21% of the time, Pallas kernels for 0%

profile of v5, /device:TPU:0, one launch (start us, length us, event | category | flops | bytes accessed | tf_op | source)
XLA Modules:
  0.0 123.5 jit_solution(13727715123075952303)
XLA Ops:
  0.6 1.2 copy.40
  1.9 1.4 %mul.39 = bf16[24,45,8,32]{3,2,0,1:T(8,128)(2,1)S(1)} broadcast(bf16[24,45,8]{2,0,1:T(8,128)(2,1)S(1)} %convert_element_type.31), dimensions={0,1,2} | broadcast | bytes 570240 | tf_op jit(solution)/shard_map/mul | solution.py:129
  3.3 1.5 %mul.40 = bf16[24,45,256]{2,0,1:T(8,128)(2,1)S(1)} reshape(bf16[24,45,8,32]{3,2,0,1:T(8,128)(2,1)S(1)} %mul.39) | data formatting | bytes 1105920 | tf_op jit(solution)/shard_map/mul | solution.py:129
  4.9 1.3 %mul.41 = bf16[24,45,256]{2,0,1:T(8,128)(2,1)S(1)} multiply(bf16[24,45,256]{2,0,1:T(8,128)(2,1)} %param.14, bf16[24,45,256]{2,0,1:T(8,128)(2,1)S(1)} %mul.40) | non-fusion elementwise | flops 276480 | bytes 1658880 | tf_op jit(solution)/shard_map/mul | solution.py:129
  6.2 0.8 pad_maximum_fusion.5
  6.9 2.4 %collective-permute-start = (bf16[1,45,264]{2,0,1:T(2,128)(2,1)}, bf16[1,45,264]{2,0,1:T(2,128)(2,1)S(1)}, u32[]{:S(2)}, u32[]{:S(2)}) collective-permute-start(bf16[1,45,264]{2,0,1:T(2,128)(2,1)} %get-tuple-element.73), channel_id=1, source_target_pairs={{0,4},{4,8},{8,12},{12,16},{16,20},{20,24},{24,28},{1,5},{5,9},{9,... | collective-permute-start | bytes 71288 | tf_op jit(solution)/shard_map/ppermute | solution.py:18
  9.3 1.3 %collective-permute-start.1 = (bf16[1,45,264]{2,0,1:T(2,128)(2,1)}, bf16[1,45,264]{2,0,1:T(2,128)(2,1)S(1)}, u32[]{:S(2)}, u32[]{:S(2)}) collective-permute-start(bf16[1,45,264]{2,0,1:T(2,128)(2,1)} %get-tuple-element.74), channel_id=1, source_target_pairs={{4,0},{8,4},{12,8},{16,12},{20,16},{24,20},{28,24},{5,1},{9,5},{13... | collective-permute-start | bytes 71288 | tf_op jit(solution)/shard_map/ppermute | solution.py:21
  10.7 0.1 compare_convert_fusion
  10.8 0.1 copy.43
  10.9 0.1 constant_dynamic-slice_fusion
  11.1 0.2 copy.47
  11.3 1.7 %multiply_bitcast_fusion = (bf16[4,8,32,8,32]{4,3,2,1,0:T(8,128)(2,1)}, bf16[4,8,32,8,32]{2,1,4,3,0:T(8,128)(2,1)S(1)}) fusion(bf16[8,4,32,32]{2,0,3,1:T(8,128)(2,1)S(1)} %copy.47, bf16[8,8]{0,1:T(8,128)(2,1)S(1)} %fusion.22), kind=kLoop, calls=%fused_computation.8 | loop fusion | flops 262144 | bytes 1114240 | tf_op jit(solution)/shard_map/gbco,gh->bhogc/transpose | solution.py:159
  13.0 0.2 copy.63
  13.1 1.7 %collective-permute-done.1 = bf16[1,45,264]{2,0,1:T(2,128)(2,1)S(1)} collective-permute-done((bf16[1,45,264]{2,0,1:T(2,128)(2,1)}, bf16[1,45,264]{2,0,1:T(2,128)(2,1)S(1)}, u32[]{:S(2)}, u32[]{:S(2)}) %collective-permute-start.1) | collective-permute-done | bytes 23792 | tf_op jit(solution)/shard_map/ppermute | solution.py:21
  14.8 0.9 pad_maximum_fusion.3
  15.7 1.6 %collective-permute-start.2 = (bf16[26,8,264]{2,0,1:T(8,128)(2,1)}, bf16[26,8,264]{2,0,1:T(8,128)(2,1)}, u32[]{:S(2)}, u32[]{:S(2)}) collective-permute-start(bf16[26,8,264]{2,0,1:T(8,128)(2,1)} %get-tuple-element.71), channel_id=1, source_target_pairs={{0,1},{1,2},{2,3},{3,0},{4,5},{5,6},{6,7},{7,4},{8,9},{9,10},{10,1... | collective-permute-start | bytes 329480 | tf_op jit(solution)/shard_map/ppermute | solution.py:18
  17.3 2.2 %collective-permute-start.3 = (bf16[26,8,264]{2,0,1:T(8,128)(2,1)}, bf16[26,8,264]{2,0,1:T(8,128)(2,1)}, u32[]{:S(2)}, u32[]{:S(2)}) collective-permute-start(bf16[26,8,264]{2,0,1:T(8,128)(2,1)} %get-tuple-element.72), channel_id=1, source_target_pairs={{1,0},{2,1},{3,2},{0,3},{5,4},{6,5},{7,6},{4,7},{9,8},{10,9},{11,1... | collective-permute-start | bytes 329480 | tf_op jit(solution)/shard_map/ppermute | solution.py:21
  19.6 1.1 fusion.13
  20.7 2.6 %copy.67.t_ref = bf16[24,4,3,48,64]{4,3,2,1,0:T(8,128)(2,1)} copy(bf16[24,4,3,48,64]{4,0,3,2,1:T(8,128)(2,1)S(1)} %fusion.13) | data formatting | bytes 3538944 | tf_op jit(solution)/shard_map/ibae,ejp->ibajp/dot_general | solution.py:153
  23.3 2.1 %reshape.204 = bf16[4,256,256]{1,2,0:T(8,128)(2,1)} reshape(bf16[4,8,32,8,32]{2,1,4,3,0:T(8,128)(2,1)S(1)} %get-tuple-element.76) | data formatting | bytes 1048576 | tf_op jit(solution)/shard_map/reshape | solution.py:158
  25.4 1.2 %copy.58.w_ref = bf16[4,256,256]{2,1,0:T(8,128)(2,1)S(1)} copy(bf16[4,256,256]{1,2,0:T(8,128)(2,1)} %reshape.204) | data formatting | bytes 1048576 | tf_op jit(solution)/shard_map/reshape | solution.py:158
  26.7 3.2 %reshape.199.wt_ref = bf16[4,256,256]{2,1,0:T(8,128)(2,1)S(1)} reshape(bf16[4,8,32,8,32]{4,3,2,1,0:T(8,128)(2,1)} %get-tuple-element.75) | data formatting | bytes 1048576 | tf_op jit(solution)/shard_map/reshape | solution.py:159
  29.9 0.1 copy.46
  30.1 4.1 %fusion.7 = bf16[26,64,264]{2,0,1:T(8,128)(2,1)S(1)} fusion(bf16[26,8,264]{2,0,1:T(8,128)(2,1)} %collective-permute-done.3, bf16[26,8,264]{2,0,1:T(8,128)(2,1)} %collective-permute-done.2, bf16[1,45,264]{2,0,1:T(2,128)(2,1)S(1)} %collective-permute-done.1, bf16[1,45,264]{2,0,1:T(2,128)(2,1)S(1)} %collective-permute-done, ...), kind=kLoop, calls=%fused_computation.11 | loop fusion | flops 8346624 | bytes 1716000 | tf_op jit(solution)/shard_map/concatenate | solution.py:22
  34.2 0.1 slice.156
  34.3 1.1 slice.155
  35.5 0.6 copy.42
  36.1 1.7 %broadcast_in_dim.2 = bf16[26,64,8,32]{1,0,3,2:T(8,128)(2,1)} broadcast(bf16[26,64,8]{1,0,2:T(8,128)(2,1)S(1)} %copy.42), dimensions={0,1,2} | broadcast | bytes 878592 | tf_op jit(solution)/shard_map/broadcast_in_dim | solution.py:136
  37.8 4.0 %reshape_reshape.3 = bf16[1664,256]{0,1:T(8,128)(2,1)} reshape(bf16[26,64,8,32]{1,0,3,2:T(8,128)(2,1)} %broadcast_in_dim.2) | data formatting | bytes 1703936 | tf_op jit(solution)/shard_map/reshape;reshape | solution.py:136
  41.8 1.5 %copy.49.m_ref = bf16[1664,256]{1,0:T(8,128)(2,1)S(1)} copy(bf16[1664,256]{0,1:T(8,128)(2,1)} %reshape_reshape.3) | data formatting | bytes 1703936 | tf_op jit(solution)/shard_map/reshape;reshape | solution.py:136
  43.3 1.7 %copy.41 = bf16[26,64,256]{2,1,0:T(8,128)(2,1)S(1)} copy(bf16[26,64,256]{2,0,1:T(8,128)(2,1)} %slice.155) | data formatting | bytes 1703936 | tf_op jit(solution)/shard_map/slice | solution.py:135
  45.0 21.1 %shard_map.85 = (bf16[24,45,256]{2,1,0:T(8,128)(2,1)S(1)}, f32[4,32,256]{2,1,0:T(8,128)S(1)}, bf16[24,192,256]{2,1,0:T(8,128)(2,1)}) custom-call(bf16[1664,256]{1,0:T(8,128)(2,1)S(1)} %bitcast.37, bf16[1664,256]{1,0:T(8,128)(2,1)S(1)} %copy.49.m_ref, bf16[24,4,3,48,64]{4,3,2,1,0:T(8,128)(2,1)} %copy.67.t_ref, bf16[24,48,256]{2,1,0:T(8,128)(2,1)S(1)} %pad.17.cot_ref, ...), custom_call_target="tpu_custom_call" | custom-call | flops 2717908992 | bytes 3407872 | tf_op jit(solution)/shard_map/pallas_call | solution.py:166
  66.1 2.5 %collective-permute-start.4 = (f32[4,32,256]{2,1,0:T(8,128)S(1)}, f32[4,32,256]{2,1,0:T(8,128)S(1)}, u32[]{:S(2)}, u32[]{:S(2)}) collective-permute-start(f32[4,32,256]{2,1,0:T(8,128)S(1)} %get-tuple-element.56), channel_id=1, source_target_pairs={{0,4},{4,0},{8,12},{12,8},{16,20},{20,16},{24,28},{28,24},{1,5},{5... | collective-permute-start | bytes 393224 | tf_op jit(solution)/shard_map/ppermute | solution.py:187
  68.6 1.0 collective-permute-done.4.order_ref
  69.6 1.7 %copy-done.1 = bf16[24,192,256]{2,1,0:T(8,128)(2,1)S(1)} copy-done((bf16[24,192,256]{2,1,0:T(8,128)(2,1)S(1)}, bf16[24,192,256]{2,1,0:T(8,128)(2,1)}, u32[]{:S(2)}) %copy-start.1) | copy-done | bytes 2359320
  71.2 7.4 %shard_map.86 = f32[1664,256]{1,0:T(8,128)S(1)} custom-call(bf16[24,4,3,48,64]{4,3,2,1,0:T(8,128)(2,1)} %copy.67.t_ref, bf16[24,192,256]{2,1,0:T(8,128)(2,1)S(1)} %copy-done.1, f32[4,32,256]{2,1,0:T(8,128)S(1)} %collective-permute-done.4.order_ref), custom_call_target="tpu_custom_call" | custom-call | flops 452984832 | bytes 2555904 | tf_op jit(solution)/shard_map/pallas_call | solution.py:195
  78.7 0.1 copy.61
  78.7 1.3 %collective-permute-start.5 = (f32[1,61,256]{2,0,1:T(1,128)S(1)}, f32[1,61,256]{2,0,1:T(1,128)S(1)}, u32[]{:S(2)}, u32[]{:S(2)}) collective-permute-start(f32[1,61,256]{2,0,1:T(1,128)S(1)} %copy.61), channel_id=1, source_target_pairs={{4,0},{8,4},{12,8},{16,12},{20,16},{24,20},{28,24},{5,1},{9,5},{13... | collective-permute-start | bytes 187400 | tf_op jit(solution)/shard_map/ppermute | solution.py:29
  80.0 0.1 slice.157
  80.2 0.9 copy.59
  81.1 0.1 copy.62
  81.1 3.0 %collective-permute-start.6 = (f32[1,61,256]{2,0,1:T(1,128)S(1)}, f32[1,61,256]{2,0,1:T(1,128)S(1)}, u32[]{:S(2)}, u32[]{:S(2)}) collective-permute-start(f32[1,61,256]{2,0,1:T(1,128)S(1)} %copy.62), channel_id=1, source_target_pairs={{0,4},{4,8},{8,12},{12,16},{16,20},{20,24},{24,28},{1,5},{5,9},{9,... | collective-permute-start | bytes 187400 | tf_op jit(solution)/shard_map/ppermute | solution.py:29
  84.2 0.1 copy_add_fusion
  84.3 2.6 %scatter-add.14 = f32[24,61,256]{2,0,1:T(8,128)S(1)} dynamic-update-slice(f32[24,61,256]{2,0,1:T(8,128)S(1)} %copy.59, f32[1,61,256]{2,0,1:T(1,128)S(1)} %copy_add_fusion, s32[]{:T(128)} %constant.125.clone.1, s32[]{:T(128)} %constant.122.clone.1, s32[]{:T(128)} %constant.122.clone.1) | dynamic-update-slice | bytes 124932 | tf_op jit(solution)/shard_map/scatter-add | solution.py:212
  86.9 0.1 slice_add_fusion.2
  86.9 2.6 %scatter-add.15 = f32[24,61,256]{2,0,1:T(8,128)S(1)} dynamic-update-slice(f32[24,61,256]{2,0,1:T(8,128)S(1)} %scatter-add.14, f32[1,61,256]{2,0,1:T(1,128)S(1)} %slice_add_fusion.2, s32[]{:T(128)} %constant.122.clone.1, s32[]{:T(128)} %constant.122.clone.1, s32[]{:T(128)} %constant.122.clone.1) | dynamic-update-slice | bytes 124932 | tf_op jit(solution)/shard_map/scatter-add | solution.py:213
  89.5 1.8 %collective-permute-start.7 = (bf16[24,8,256]{2,0,1:T(8,128)(2,1)S(1)}, bf16[24,8,256]{2,0,1:T(8,128)(2,1)S(1)}, u32[]{:S(2)}, u32[]{:S(2)}) collective-permute-start(bf16[24,8,256]{2,0,1:T(8,128)(2,1)S(1)} %slice.175), channel_id=1, source_target_pairs={{0,3},{1,0},{2,1},{3,2},{4,7},{5,4},{6,5},{7,6},{8,11},{9,8},{10,9... | collective-permute-start | bytes 294920 | tf_op jit(solution)/shard_map/ppermute | solution.py:34
  91.3 2.9 %collective-permute-start.9 = (f32[4,32,256]{2,1,0:T(8,128)S(1)}, f32[4,32,256]{2,1,0:T(8,128)S(1)}, u32[]{:S(2)}, u32[]{:S(2)}) collective-permute-start(f32[4,32,256]{2,1,0:T(8,128)S(1)} %add.60), channel_id=1, source_target_pairs={{0,8},{4,12},{8,0},{12,4},{16,24},{20,28},{24,16},{28,20},{1,9},{5... | collective-permute-start | bytes 393224 | tf_op jit(solution)/shard_map/ppermute | solution.py:49
  94.3 0.1 slice.162
  94.4 1.0 copy-done.4
  95.4 0.3 collective-permute-start.8
  95.7 1.9 %collective-permute-done.9 = f32[4,32,256]{2,1,0:T(8,128)S(1)} collective-permute-done((f32[4,32,256]{2,1,0:T(8,128)S(1)}, f32[4,32,256]{2,1,0:T(8,128)S(1)}, u32[]{:S(2)}, u32[]{:S(2)}) %collective-permute-start.9) | collective-permute-done | bytes 131104 | tf_op jit(solution)/shard_map/ppermute | solution.py:49
  97.6 4.1 %collective-permute-start.10 = (f32[4,32,256]{2,1,0:T(8,128)S(1)}, f32[4,32,256]{2,1,0:T(8,128)S(1)}, u32[]{:S(2)}, u32[]{:S(2)}) collective-permute-start(f32[4,32,256]{2,1,0:T(8,128)S(1)} %add.61), channel_id=1, source_target_pairs={{0,16},{4,20},{8,24},{12,28},{16,0},{20,4},{24,8},{28,12},{1,17},{... | collective-permute-start | bytes 393224 | tf_op jit(solution)/shard_map/ppermute | solution.py:49
  101.6 3.2 %mul.45 = f32[24,45,8,32]{3,2,0,1:T(8,128)} broadcast(bf16[24,45,8]{2,0,1:T(8,128)(2,1)S(1)} %copy-done.3), dimensions={0,1,2} | broadcast | bytes 1123200 | tf_op jit(solution)/shard_map/mul | solution.py:222
  104.8 3.5 %mul.46 = f32[24,45,256]{2,0,1:T(8,128)S(1)} reshape(f32[24,45,8,32]{3,2,0,1:T(8,128)} %mul.45) | data formatting | bytes 2211840 | tf_op jit(solution)/shard_map/mul | solution.py:222
  108.3 1.0 copy.55
  109.3 0.3 collective-permute-start.11
  109.6 0.1 copy-done.5
  109.8 4.6 %collective-permute-done.11 = f32[4,32,256]{2,1,0:T(8,128)S(1)} collective-permute-done((f32[4,32,256]{2,1,0:T(8,128)S(1)}, f32[4,32,256]{2,1,0:T(8,128)S(1)}, u32[]{:S(2)}, u32[]{:S(2)}) %collective-permute-start.11) | collective-permute-done | bytes 131104 | tf_op jit(solution)/shard_map/ppermute | solution.py:49
  114.4 3.7 %collective-permute-start.12 = (f32[4,32,256]{2,1,0:T(8,128)S(1)}, f32[4,32,256]{2,1,0:T(8,128)S(1)}, u32[]{:S(2)}, u32[]{:S(2)}) collective-permute-start(f32[4,32,256]{2,1,0:T(8,128)S(1)} %add.63), channel_id=1, source_target_pairs={{0,2},{1,3},{2,0},{3,1},{4,6},{5,7},{6,4},{7,5},{8,10},{9,11},{10,... | collective-permute-start | bytes 393224 | tf_op jit(solution)/shard_map/ppermute | solution.py:49
  118.1 0.9 multiply_convert_fusion
  119.0 3.4 %collective-permute-done.12 = f32[4,32,256]{2,1,0:T(8,128)S(1)} collective-permute-done((f32[4,32,256]{2,1,0:T(8,128)S(1)}, f32[4,32,256]{2,1,0:T(8,128)S(1)}, u32[]{:S(2)}, u32[]{:S(2)}) %collective-permute-start.12) | collective-permute-done | bytes 131104 | tf_op jit(solution)/shard_map/ppermute | solution.py:49
  122.5 0.2 reshape.201
  122.7 0.9 copy.68
  (39 shorter events, 0.4 us)
Async XLA Ops:
  0.6 10.3 %copy-start = (bf16[192,4,3,17]{0,1,3,2:T(4,128)(2,1)S(1)}, bf16[192,4,3,17]{0,1,3,2:T(4,128)(2,1)}, u32[]{:S(2)}) copy-start(bf16[192,4,3,17]{0,1,3,2:T(4,128)(2,1)} %param.16) | copy-start | bytes 235012
  1.9 28.2 %copy-start.2 = (bf16[24,45,8]{2,0,1:T(8,128)(2,1)}, bf16[24,45,8]{2,0,1:T(8,128)(2,1)S(1)}, u32[]{:S(2)}) copy-start(bf16[24,45,8]{2,0,1:T(8,128)(2,1)S(1)} %convert_element_type.31) | copy-start | bytes 51844
  4.9 5.8 %copy-start.8 = (s32[192]{0:T(256)S(1)}, s32[192]{0:T(256)}, u32[]{:S(2)}) copy-start(s32[192]{0:T(256)} %param.17) | copy-start | bytes 2308
  4.9 6.2 %copy-start.7 = (bf16[8,4,32,32]{3,2,1,0:T(8,128)(2,1)S(1)}, bf16[8,4,32,32]{3,2,1,0:T(8,128)(2,1)}, u32[]{:S(2)}) copy-start(bf16[8,4,32,32]{3,2,1,0:T(8,128)(2,1)} %param.18) | copy-start | bytes 196612
  6.9 6.2 %collective-permute-start = (bf16[1,45,264]{2,0,1:T(2,128)(2,1)}, bf16[1,45,264]{2,0,1:T(2,128)(2,1)S(1)}, u32[]{:S(2)}, u32[]{:S(2)}) collective-permute-start(bf16[1,45,264]{2,0,1:T(2,128)(2,1)} %get-tuple-element.73), channel_id=1, source_target_pairs={{0,4},{4,8},{8,12},{12,16},{16,20},{20,24},{24,28},{1,5},{5,9},{9,... | collective-permute-start | bytes 71288 | tf_op jit(solution)/shard_map/ppermute | solution.py:18
  9.3 5.5 %collective-permute-start.1 = (bf16[1,45,264]{2,0,1:T(2,128)(2,1)}, bf16[1,45,264]{2,0,1:T(2,128)(2,1)S(1)}, u32[]{:S(2)}, u32[]{:S(2)}) collective-permute-start(bf16[1,45,264]{2,0,1:T(2,128)(2,1)} %get-tuple-element.74), channel_id=1, source_target_pairs={{4,0},{8,4},{12,8},{16,12},{20,16},{24,20},{28,24},{5,1},{9,5},{13... | collective-permute-start | bytes 71288 | tf_op jit(solution)/shard_map/ppermute | solution.py:21
  15.7 14.3 %collective-permute-start.2 = (bf16[26,8,264]{2,0,1:T(8,128)(2,1)}, bf16[26,8,264]{2,0,1:T(8,128)(2,1)}, u32[]{:S(2)}, u32[]{:S(2)}) collective-permute-start(bf16[26,8,264]{2,0,1:T(8,128)(2,1)} %get-tuple-element.71), channel_id=1, source_target_pairs={{0,1},{1,2},{2,3},{3,0},{4,5},{5,6},{6,7},{7,4},{8,9},{9,10},{10,1... | collective-permute-start | bytes 329480 | tf_op jit(solution)/shard_map/ppermute | solution.py:18
  17.3 12.7 %collective-permute-start.3 = (bf16[26,8,264]{2,0,1:T(8,128)(2,1)}, bf16[26,8,264]{2,0,1:T(8,128)(2,1)}, u32[]{:S(2)}, u32[]{:S(2)}) collective-permute-start(bf16[26,8,264]{2,0,1:T(8,128)(2,1)} %get-tuple-element.72), channel_id=1, source_target_pairs={{1,0},{2,1},{3,2},{0,3},{5,4},{6,5},{7,6},{4,7},{9,8},{10,9},{11,1... | collective-permute-start | bytes 329480 | tf_op jit(solution)/shard_map/ppermute | solution.py:21
  26.7 3.2 %copy-start.6 = (bf16[24,45,256]{2,0,1:T(8,128)(2,1)S(1)}, bf16[24,45,256]{2,0,1:T(8,128)(2,1)}, u32[]{:S(2)}) copy-start(bf16[24,45,256]{2,0,1:T(8,128)(2,1)} %param.19) | copy-start | bytes 1658884
  66.1 3.5 %collective-permute-start.4 = (f32[4,32,256]{2,1,0:T(8,128)S(1)}, f32[4,32,256]{2,1,0:T(8,128)S(1)}, u32[]{:S(2)}, u32[]{:S(2)}) collective-permute-start(f32[4,32,256]{2,1,0:T(8,128)S(1)} %get-tuple-element.56), channel_id=1, source_target_pairs={{0,4},{4,0},{8,12},{12,8},{16,20},{20,16},{24,28},{28,24},{1,5},{5... | collective-permute-start | bytes 393224 | tf_op jit(solution)/shard_map/ppermute | solution.py:187
  69.6 1.7 %copy-start.1 = (bf16[24,192,256]{2,1,0:T(8,128)(2,1)S(1)}, bf16[24,192,256]{2,1,0:T(8,128)(2,1)}, u32[]{:S(2)}) copy-start(bf16[24,192,256]{2,1,0:T(8,128)(2,1)} %get-tuple-element.55.pulled_ref) | copy-start | bytes 7077892
  78.7 5.4 %collective-permute-start.5 = (f32[1,61,256]{2,0,1:T(1,128)S(1)}, f32[1,61,256]{2,0,1:T(1,128)S(1)}, u32[]{:S(2)}, u32[]{:S(2)}) collective-permute-start(f32[1,61,256]{2,0,1:T(1,128)S(1)} %copy.61), channel_id=1, source_target_pairs={{4,0},{8,4},{12,8},{16,12},{20,16},{24,20},{28,24},{5,1},{9,5},{13... | collective-permute-start | bytes 187400 | tf_op jit(solution)/shard_map/ppermute | solution.py:29
  81.1 5.7 %collective-permute-start.6 = (f32[1,61,256]{2,0,1:T(1,128)S(1)}, f32[1,61,256]{2,0,1:T(1,128)S(1)}, u32[]{:S(2)}, u32[]{:S(2)}) collective-permute-start(f32[1,61,256]{2,0,1:T(1,128)S(1)} %copy.62), channel_id=1, source_target_pairs={{0,4},{4,8},{8,12},{12,16},{16,20},{20,24},{24,28},{1,5},{5,9},{9,... | collective-permute-start | bytes 187400 | tf_op jit(solution)/shard_map/ppermute | solution.py:29
  89.5 4.8 %collective-permute-start.7 = (bf16[24,8,256]{2,0,1:T(8,128)(2,1)S(1)}, bf16[24,8,256]{2,0,1:T(8,128)(2,1)S(1)}, u32[]{:S(2)}, u32[]{:S(2)}) collective-permute-start(bf16[24,8,256]{2,0,1:T(8,128)(2,1)S(1)} %slice.175), channel_id=1, source_target_pairs={{0,3},{1,0},{2,1},{3,2},{4,7},{5,4},{6,5},{7,6},{8,11},{9,8},{10,9... | collective-permute-start | bytes 294920 | tf_op jit(solution)/shard_map/ppermute | solution.py:34
  91.3 10.3 %copy-start.3 = (bf16[24,45,8]{2,0,1:T(8,128)(2,1)S(1)}, bf16[24,45,8]{2,0,1:T(8,128)(2,1)}, u32[]{:S(2)}) copy-start(bf16[24,45,8]{2,0,1:T(8,128)(2,1)} %copy-done.2) | copy-start | bytes 51844
  91.3 6.2 %collective-permute-start.9 = (f32[4,32,256]{2,1,0:T(8,128)S(1)}, f32[4,32,256]{2,1,0:T(8,128)S(1)}, u32[]{:S(2)}, u32[]{:S(2)}) collective-permute-start(f32[4,32,256]{2,1,0:T(8,128)S(1)} %add.60), channel_id=1, source_target_pairs={{0,8},{4,12},{8,0},{12,4},{16,24},{20,28},{24,16},{28,20},{1,9},{5... | collective-permute-start | bytes 393224 | tf_op jit(solution)/shard_map/ppermute | solution.py:49
  94.4 1.0 copy-start.4
  95.4 14.2 %collective-permute-start.8 = (f32[24,8,256]{2,0,1:T(8,128)S(1)}, f32[24,8,256]{2,0,1:T(8,128)S(1)}, u32[]{:S(2)}, u32[]{:S(2)}) collective-permute-start(f32[24,8,256]{2,0,1:T(8,128)S(1)} %get-tuple-element.69), channel_id=1, source_target_pairs={{0,1},{1,2},{2,3},{3,0},{4,5},{5,6},{6,7},{7,4},{8,9},{9,10},{10,1... | collective-permute-start | bytes 589832 | tf_op jit(solution)/shard_map/ppermute | solution.py:34
  97.6 11.7 %collective-permute-start.10 = (f32[4,32,256]{2,1,0:T(8,128)S(1)}, f32[4,32,256]{2,1,0:T(8,128)S(1)}, u32[]{:S(2)}, u32[]{:S(2)}) collective-permute-start(f32[4,32,256]{2,1,0:T(8,128)S(1)} %add.61), channel_id=1, source_target_pairs={{0,16},{4,20},{8,24},{12,28},{16,0},{20,4},{24,8},{28,12},{1,17},{... | collective-permute-start | bytes 393224 | tf_op jit(solution)/shard_map/ppermute | solution.py:49
  108.3 1.4 %copy-start.5 = (f32[24,45,256]{2,0,1:T(8,128)S(1)}, f32[24,45,256]{2,0,1:T(8,128)}, u32[]{:S(2)}) copy-start(f32[24,45,256]{2,0,1:T(8,128)} %copy-done.4) | copy-start | bytes 3317764
  109.3 5.1 %collective-permute-start.11 = (f32[4,32,256]{2,1,0:T(8,128)S(1)}, f32[4,32,256]{2,1,0:T(8,128)S(1)}, u32[]{:S(2)}, u32[]{:S(2)}) collective-permute-start(f32[4,32,256]{2,1,0:T(8,128)S(1)} %add.62), channel_id=1, source_target_pairs={{0,1},{1,0},{2,3},{3,2},{4,5},{5,4},{6,7},{7,6},{8,9},{9,8},{10,11... | collective-permute-start | bytes 393224 | tf_op jit(solution)/shard_map/ppermute | solution.py:49
  114.4 8.0 %collective-permute-start.12 = (f32[4,32,256]{2,1,0:T(8,128)S(1)}, f32[4,32,256]{2,1,0:T(8,128)S(1)}, u32[]{:S(2)}, u32[]{:S(2)}) collective-permute-start(f32[4,32,256]{2,1,0:T(8,128)S(1)} %add.63), channel_id=1, source_target_pairs={{0,2},{1,3},{2,0},{3,1},{4,6},{5,7},{6,4},{7,5},{8,10},{9,11},{10,... | collective-permute-start | bytes 393224 | tf_op jit(solution)/shard_map/ppermute | solution.py:49

commit v6 on v5

--- a/solution.py
+++ b/solution.py
@@ -125,17 +125,23 @@
     lane_rows = -(-padded_cols // 16) * 16
     col_pad = -(-col_count // 16) * 16
     mask_values = obs_mask.astype(jnp.bfloat16)
-    masked = (
-        features.reshape(row_count, col_count, group_count, group_width) * mask_values[..., None]
-    ).reshape(row_count, col_count, chan_count)
+    spread = (
+        jnp.arange(chan_count)[None, :] // group_width == jnp.arange(group_count)[:, None]
+    ).astype(jnp.bfloat16)
+    own_mask = jnp.dot(
+        mask_values.reshape(row_count * col_count, group_count), spread,
+        preferred_element_type=jnp.float32,
+    ).astype(jnp.bfloat16).reshape(row_count, col_count, chan_count)
+    masked = features * own_mask
     packed = jnp.concatenate([masked, mask_values], axis=-1)
     packed = with_halo(packed, (("lat", 0),), 1, False)
     packed = with_halo(packed, (("lon", 1),), tap_reach, True)
     packed = jnp.pad(packed, ((0, 0), (0, lane_rows - padded_cols), (0, 0)))
     full_input = packed[..., :chan_count].reshape((row_count + 2) * lane_rows, chan_count)
-    full_mask = jnp.repeat(packed[..., chan_count:], group_width, axis=-1).reshape(
-        (row_count + 2) * lane_rows, chan_count
-    )
+    full_mask = jnp.dot(
+        packed[..., chan_count:].reshape((row_count + 2) * lane_rows, group_count), spread,
+        preferred_element_type=jnp.float32,
+    ).astype(jnp.bfloat16)
 
     offsets = jnp.arange(tap_count) - tap_reach
     allowed = jnp.abs(offsets)[None, :] <= band_width[:, None]
@@ -208,21 +214,21 @@
     collected = collected.reshape(row_count + 2, lane_rows, chan_count)[:, :padded_cols]
     from_below = passed_along(collected[0:1], "lat", -1)
     from_above = passed_along(collected[row_count + 1 : row_count + 2], "lat", 1)
-    inner_rows = collected[1 : row_count + 1]
-    inner_rows = inner_rows.at[row_count - 1 : row_count].add(from_below)
-    inner_rows = inner_rows.at[0:1].add(from_above)
+    inner_rows = (
+        collected[1 : row_count + 1]
+        + jnp.pad(from_above, ((0, row_count - 1), (0, 0), (0, 0)))
+        + jnp.pad(from_below, ((row_count - 1, 0), (0, 0), (0, 0)))
+    )
     left_rim = inner_rows[:, :tap_reach]
     right_rim = inner_rows[:, col_count + tap_reach :]
     from_right = from_behind(left_rim.astype(jnp.bfloat16), "lon", -1).astype(left_rim.dtype)
     from_left = from_behind(right_rim, "lon", 1)
-    gathered = inner_rows[:, tap_reach : tap_reach + col_count]
-    gathered = gathered.at[:, col_count - tap_reach :].add(from_right)
-    gathered = gathered.at[:, :tap_reach].add(from_left)
-    input_grad = (
-        (gathered.reshape(row_count, col_count, group_count, group_width) * mask_values[..., None])
-        .reshape(row_count, col_count, chan_count)
-        .astype(jnp.bfloat16)
-    )
+    gathered = (
+        inner_rows[:, tap_reach : tap_reach + col_count]
+        + jnp.pad(from_right, ((0, 0), (col_count - tap_reach, 0), (0, 0)))
+        + jnp.pad(from_left, ((0, 0), (0, col_count - tap_reach), (0, 0)))
+    )
+    input_grad = (gathered * own_mask).astype(jnp.bfloat16)
     return (infilled, input_grad, weight_grad)
 
 

time: 124 us -> 97.4 us (0.79)
  local copies, waits for them, and re-layouts: 42.6 us -> 17.3 us
  starting transfers between devices: 27.4 us -> 24.9 us
  matrix products: 1.14 us -> 2.59 us
    mul x4 -> x0, local copies, waits for them, and re-layouts: 9.57 us -> none  [the longest x2 6.65 us: local(): gathered.reshape(row_count, col_count, group_count, group_width)]
    another operation x2 -> x0, local copies, waits for them, and re-layouts: 5.52 us -> none  [local(): jnp.repeat(packed[..., chan_count:], group_width, axis=-1)]
    scatter-add x2 -> x0, local copies, waits for them, and re-layouts: 5.11 us -> none  [the longest x1 2.56 us: local(): inner_rows = inner_rows.at[0:1].add(from_above)]
    concatenate x1, other arithmetic: 4.14 us -> 1.29 us  [with_halo(): block = jnp.concatenate([low, block, high], axis=dim)]
    slice x2 -> x1, local copies, waits for them, and re-layouts: 2.83 us -> 0.06 us  [local(): packed[..., :chan_count].reshape((row_count + 2) * lane_rows, chan_count)]
    ppermute x4, waiting for transfers between devices: 9.89 us -> 12.3 us  [butterfly_sum(): partner = lax.ppermute(value, axis, [(i, i ^ step) for i in range(count)])]
    ppermute x4, starting transfers between devices: 11 us -> 9.23 us  [butterfly_sum(): partner = lax.ppermute(value, axis, [(i, i ^ step) for i in range(count)])]
    broadcast_in_dim x1 -> x0, local copies, waits for them, and re-layouts: 1.68 us -> none  [local(): jnp.repeat(packed[..., chan_count:], group_width, axis=-1)]
  transfers between devices with their start and end apart: 13 -> 13, of which waited for: 5 -> 4; matrix products, arithmetic and copies ran while one was open for 21% -> 19% of each run, Pallas kernels for 0% -> 8%
where the time goes in v6:
time: 97.4 us; the launch traced here: 96.7 us
  Pallas kernels  28.6 us (29%)
  starting transfers between devices  24.9 us (26%)
  local copies, waits for them, and re-layouts  17.3 us (18%)
  waiting for transfers between devices  13.3 us (14%)
  other arithmetic  9.08 us (9%)
  matrix products  2.59 us (3%)
  between operations  1.02 us (1%)
    pallas_call x1, Pallas kernels, local(): pl.pallas_call(forward_kernel, out_shape=(jax.ShapeDtypeStruct((row_count...  21.1 us
    ppermute x4, waiting for transfers between devices, butterfly_sum(): partner = lax.ppermute(value, axis, [(i, i ^ step) for i in range(count)])  12.3 us
    ppermute x4, starting transfers between devices, butterfly_sum(): partner = lax.ppermute(value, axis, [(i, i ^ step) for i in range(count)])  9.23 us
    pallas_call x1, Pallas kernels, local(): pl.pallas_call(adjoint_kernel, out_shape=jax.ShapeDtypeStruct(((row_count...  7.41 us
    unnamed x25, local copies, waits for them, and re-layouts  6.06 us
    ppermute x2, starting transfers between devices, with_halo(): lax.ppermute(lax.slice_in_dim(block, block.shape[dim] - width, None, axis...  4.78 us
    reshape x2, local copies, waits for them, and re-layouts, local(): jnp.einsum('gbco,gh->bgcho', mixing, eye)  3.38 us
    ppermute x2, starting transfers between devices, with_halo(): lax.ppermute(lax.slice_in_dim(block, 0, width, axis=dim), axis, backward)  3.32 us
  transfers between devices with their start and end apart: 13, of which 4 were waited for; matrix products, arithmetic and copies ran while one was open for 19% of the time, Pallas kernels for 8%

profile of v6, /device:TPU:0, one launch (start us, length us, event | category | flops | bytes accessed | tf_op | source)
XLA Modules:
  0.0 96.7 jit_solution(2274313268128913844)
XLA Ops:
  0.6 0.0 copy-start
  0.7 1.0 convert_element_type.46
  1.7 0.2 copy.37
  1.9 0.1 reshape.117
  2.0 0.4 fusion.6
  2.4 0.2 reshape.118
  2.6 0.0 copy-start.9
  2.6 0.0 copy-start.6
  2.6 0.1 copy_multiply_fusion
  2.8 0.6 pad_maximum_fusion.5
  3.4 2.4 %collective-permute-start = (bf16[1,45,264]{2,1,0:T(8,128)(2,1)}, bf16[1,45,264]{2,1,0:T(8,128)(2,1)S(1)}, u32[]{:S(2)}, u32[]{:S(2)}) collective-permute-start(bf16[1,45,264]{2,1,0:T(8,128)(2,1)} %get-tuple-element.22), channel_id=1, source_target_pairs={{0,4},{4,8},{8,12},{12,16},{16,20},{20,24},{24,28},{1,5},{5,9},{9,... | collective-permute-start | bytes 71288 | tf_op jit(solution)/shard_map/ppermute | solution.py:18
  5.8 1.3 %collective-permute-start.1 = (bf16[1,45,264]{2,1,0:T(8,128)(2,1)}, bf16[1,45,264]{2,1,0:T(8,128)(2,1)}, u32[]{:S(2)}, u32[]{:S(2)}) collective-permute-start(bf16[1,45,264]{2,1,0:T(8,128)(2,1)} %get-tuple-element.23), channel_id=1, source_target_pairs={{4,0},{8,4},{12,8},{16,12},{20,16},{24,20},{28,24},{5,1},{9,5},{13... | collective-permute-start | bytes 71288 | tf_op jit(solution)/shard_map/ppermute | solution.py:21
  7.1 0.6 iota_subtract_fusion
  7.7 0.1 compare_convert_fusion
  7.8 0.1 copy.39
  7.9 0.1 constant_dynamic-slice_fusion
  8.1 0.9 copy.43
  9.0 2.6 %multiply_bitcast_fusion = (bf16[4,8,32,8,32]{4,3,2,1,0:T(8,128)(2,1)}, bf16[4,8,32,8,32]{2,1,4,3,0:T(8,128)(2,1)S(1)}) fusion(bf16[8,4,32,32]{2,0,3,1:T(8,128)(2,1)} %copy.43, bf16[8,8]{0,1:T(8,128)(2,1)S(1)} %fusion.27), kind=kLoop, calls=%fused_computation.1 | loop fusion | flops 262144 | bytes 1114240 | tf_op jit(solution)/shard_map/gbco,gh->bhogc/transpose | solution.py:165
  11.6 0.5 iota_compare_fusion.6
  12.1 0.2 copy.52
  12.3 0.0 collective-permute-done
  12.3 0.0 collective-permute-done.1
  12.3 1.7 %pad_maximum_fusion.3 = (bf16[26,8,264]{2,1,0:T(8,128)(2,1)}, bf16[26,8,264]{2,1,0:T(8,128)(2,1)}) fusion(bf16[1,45,264]{2,1,0:T(8,128)(2,1)} %collective-permute-done.1, bf16[1,45,264]{2,1,0:T(8,128)(2,1)S(1)} %collective-permute-done, bf16[24,45,8]{2,1,0:T(8,128)(2,1)} %copy-done.2, bf16[24,45,256]{2,1,0:T(8,128)(2,1)S(1)} %copy_multiply_fusion), kind=kLoop, calls=%fused_computation.36 | loop fusion | flops 878592 | bytes 837408 | tf_op jit(solution)/shard_map/slice | solution.py:19
  14.1 2.4 %collective-permute-start.2 = (bf16[26,8,264]{2,1,0:T(8,128)(2,1)}, bf16[26,8,264]{2,1,0:T(8,128)(2,1)}, u32[]{:S(2)}, u32[]{:S(2)}) collective-permute-start(bf16[26,8,264]{2,1,0:T(8,128)(2,1)} %get-tuple-element.20), channel_id=1, source_target_pairs={{0,1},{1,2},{2,3},{3,0},{4,5},{5,6},{6,7},{7,4},{8,9},{9,10},{10,1... | collective-permute-start | bytes 329480 | tf_op jit(solution)/shard_map/ppermute | solution.py:18
  16.5 2.0 %collective-permute-start.3 = (bf16[26,8,264]{2,1,0:T(8,128)(2,1)}, bf16[26,8,264]{2,1,0:T(8,128)(2,1)}, u32[]{:S(2)}, u32[]{:S(2)}) collective-permute-start(bf16[26,8,264]{2,1,0:T(8,128)(2,1)} %get-tuple-element.21), channel_id=1, source_target_pairs={{1,0},{2,1},{3,2},{0,3},{5,4},{6,5},{7,6},{4,7},{9,8},{10,9},{11,1... | collective-permute-start | bytes 329480 | tf_op jit(solution)/shard_map/ppermute | solution.py:21
  18.5 1.9 %fusion.18 = bf16[24,4,3,48,64]{4,0,3,2,1:T(8,128)(2,1)S(1)} fusion(s32[48,64]{1,0:T(8,128)} %iota_subtract_fusion, pred[48]{0:T(512)(128)(4,1)} %iota_compare_fusion.6, bf16[24,4,3,17]{3,0,2,1:T(8,128)(2,1)S(1)} %copy.52, bf16[24,17]{1,0:T(8,128)(2,1)S(1)} %constant_dynamic-slice_fusion.1), kind=kOutput, calls=%fused_computation.28 | convolution fusion | flops 30205056 | bytes 1792416 | tf_op jit(solution)/shard_map/ibae,ejp->ibajp/dot_general | solution.py:159
  20.4 2.6 %copy.56.t_ref = bf16[24,4,3,48,64]{4,3,2,1,0:T(8,128)(2,1)} copy(bf16[24,4,3,48,64]{4,0,3,2,1:T(8,128)(2,1)S(1)} %fusion.18) | data formatting | bytes 3538944 | tf_op jit(solution)/shard_map/ibae,ejp->ibajp/dot_general | solution.py:159
  22.9 2.1 %reshape.127 = bf16[4,256,256]{1,2,0:T(8,128)(2,1)} reshape(bf16[4,8,32,8,32]{2,1,4,3,0:T(8,128)(2,1)S(1)} %get-tuple-element.25) | data formatting | bytes 1048576 | tf_op jit(solution)/shard_map/reshape | solution.py:164
  25.1 1.2 %copy.51.w_ref = bf16[4,256,256]{2,1,0:T(8,128)(2,1)S(1)} copy(bf16[4,256,256]{1,2,0:T(8,128)(2,1)} %reshape.127) | data formatting | bytes 1048576 | tf_op jit(solution)/shard_map/reshape | solution.py:164
  26.3 0.0 copy-start.5
  26.3 3.2 %reshape.122.wt_ref = bf16[4,256,256]{2,1,0:T(8,128)(2,1)S(1)} reshape(bf16[4,8,32,8,32]{4,3,2,1,0:T(8,128)(2,1)} %get-tuple-element.24) | data formatting | bytes 1048576 | tf_op jit(solution)/shard_map/reshape | solution.py:165
  29.5 0.0 copy-start.3
  29.5 0.1 copy.42
  29.7 0.0 collective-permute-done.3
  29.7 0.8 copy-done.3
  30.5 1.3 %fusion.9 = bf16[26,64,264]{2,1,0:T(8,128)(2,1)S(1)} fusion(bf16[26,8,264]{2,1,0:T(8,128)(2,1)} %collective-permute-done.3, bf16[26,8,264]{2,1,0:T(8,128)(2,1)} %collective-permute-done.2, bf16[1,45,264]{2,1,0:T(8,128)(2,1)} %collective-permute-done.1, bf16[1,45,264]{2,1,0:T(8,128)(2,1)S(1)} %collective-permute-done, bf16[24,45,8]{2,1,0:T(8,128)(2,1)S(1)} %copy-done.3, ...), kind=kLoop, calls=%fused_computation.16 | loop fusion | flops 8346624 | bytes 1716000 | tf_op jit(solution)/shard_map/concatenate | solution.py:22
  31.8 0.1 slice.54
  31.9 0.1 slice.53
  32.0 0.5 copy-done.8
  32.4 0.4 convolution_convert_fusion.m_ref
  32.8 21.1 %shard_map.85 = (bf16[24,45,256]{2,1,0:T(8,128)(2,1)S(1)}, f32[4,32,256]{2,1,0:T(8,128)S(1)}, bf16[24,192,256]{2,1,0:T(8,128)(2,1)}) custom-call(bf16[1664,256]{1,0:T(8,128)(2,1)S(1)} %bitcast.34, bf16[1664,256]{1,0:T(8,128)(2,1)S(1)} %convolution_convert_fusion.m_ref, bf16[24,4,3,48,64]{4,3,2,1,0:T(8,128)(2,1)} %copy.56.t_ref, ...), custom_call_target="tpu_custom_call" | custom-call | flops 2717908992 | bytes 3407872 | tf_op jit(solution)/shard_map/pallas_call | solution.py:172
  53.9 2.1 %collective-permute-start.4 = (f32[4,32,256]{2,1,0:T(8,128)S(1)}, f32[4,32,256]{2,1,0:T(8,128)S(1)}, u32[]{:S(2)}, u32[]{:S(2)}) collective-permute-start(f32[4,32,256]{2,1,0:T(8,128)S(1)} %get-tuple-element.8), channel_id=1, source_target_pairs={{0,4},{4,0},{8,12},{12,8},{16,20},{20,16},{24,28},{28,24},{1,5},{5... | collective-permute-start | bytes 393224 | tf_op jit(solution)/shard_map/ppermute | solution.py:193
  56.1 1.0 %collective-permute-done.4.order_ref = f32[4,32,256]{2,1,0:T(8,128)S(1)} collective-permute-done((f32[4,32,256]{2,1,0:T(8,128)S(1)}, f32[4,32,256]{2,1,0:T(8,128)S(1)}, u32[]{:S(2)}, u32[]{:S(2)}) %collective-permute-start.4) | collective-permute-done | bytes 131104 | tf_op jit(solution)/shard_map/ppermute | solution.py:193
  57.1 2.6 %collective-permute-start.9 = (f32[4,32,256]{2,1,0:T(8,128)S(1)}, f32[4,32,256]{2,1,0:T(8,128)S(1)}, u32[]{:S(2)}, u32[]{:S(2)}) collective-permute-start(f32[4,32,256]{2,1,0:T(8,128)S(1)} %add.58), channel_id=1, source_target_pairs={{0,8},{4,12},{8,0},{12,4},{16,24},{20,28},{24,16},{28,20},{1,9},{5... | collective-permute-start | bytes 393224 | tf_op jit(solution)/shard_map/ppermute | solution.py:49
  59.6 1.7 %copy-done.1 = bf16[24,192,256]{2,1,0:T(8,128)(2,1)S(1)} copy-done((bf16[24,192,256]{2,1,0:T(8,128)(2,1)S(1)}, bf16[24,192,256]{2,1,0:T(8,128)(2,1)}, u32[]{:S(2)}) %copy-start.1) | copy-done | bytes 2359320
  61.3 7.4 %shard_map.86 = f32[1664,256]{1,0:T(8,128)S(1)} custom-call(bf16[24,4,3,48,64]{4,3,2,1,0:T(8,128)(2,1)} %copy.56.t_ref, bf16[24,192,256]{2,1,0:T(8,128)(2,1)S(1)} %copy-done.1, f32[4,32,256]{2,1,0:T(8,128)S(1)} %collective-permute-done.4.order_ref), custom_call_target="tpu_custom_call" | custom-call | flops 452984832 | bytes 2555904 | tf_op jit(solution)/shard_map/pallas_call | solution.py:201
  68.7 1.8 %collective-permute-start.5 = (f32[1,61,256]{2,1,0:T(8,128)S(1)}, f32[1,61,256]{2,1,0:T(8,128)S(1)}, u32[]{:S(2)}, u32[]{:S(2)}) collective-permute-start(f32[1,61,256]{2,1,0:T(8,128)S(1)} %get-tuple-element.18), channel_id=1, source_target_pairs={{0,4},{4,8},{8,12},{12,16},{16,20},{20,24},{24,28},{1,5},{5,9},{9,... | collective-permute-start | bytes 187400 | tf_op jit(solution)/shard_map/ppermute | solution.py:29
  70.5 1.3 %collective-permute-start.6 = (f32[1,61,256]{2,1,0:T(8,128)S(1)}, f32[1,61,256]{2,1,0:T(8,128)S(1)}, u32[]{:S(2)}, u32[]{:S(2)}) collective-permute-start(f32[1,61,256]{2,1,0:T(8,128)S(1)} %get-tuple-element.19), channel_id=1, source_target_pairs={{4,0},{8,4},{12,8},{16,12},{20,16},{24,20},{28,24},{5,1},{9,5},{13... | collective-permute-start | bytes 187400 | tf_op jit(solution)/shard_map/ppermute | solution.py:29
  71.8 0.0 collective-permute-done.9
  71.8 5.0 %collective-permute-start.10 = (f32[4,32,256]{2,1,0:T(8,128)S(1)}, f32[4,32,256]{2,1,0:T(8,128)S(1)}, u32[]{:S(2)}, u32[]{:S(2)}) collective-permute-start(f32[4,32,256]{2,1,0:T(8,128)S(1)} %add.59), channel_id=1, source_target_pairs={{0,16},{4,20},{8,24},{12,28},{16,0},{20,4},{24,8},{28,12},{1,17},{... | collective-permute-start | bytes 393224 | tf_op jit(solution)/shard_map/ppermute | solution.py:49
  76.8 0.1 fusion.7
  77.0 0.1 collective-permute-start.8
  77.0 2.7 %collective-permute-done.10 = f32[4,32,256]{2,1,0:T(8,128)S(1)} collective-permute-done((f32[4,32,256]{2,1,0:T(8,128)S(1)}, f32[4,32,256]{2,1,0:T(8,128)S(1)}, u32[]{:S(2)}, u32[]{:S(2)}) %collective-permute-start.10) | collective-permute-done | bytes 131104 | tf_op jit(solution)/shard_map/ppermute | solution.py:49
  79.8 0.1 collective-permute-start.11
  79.9 2.3 %collective-permute-start.7 = (bf16[24,8,256]{2,1,0:T(8,128)(2,1)S(1)}, bf16[24,8,256]{2,1,0:T(8,128)(2,1)S(1)}, u32[]{:S(2)}, u32[]{:S(2)}) collective-permute-start(bf16[24,8,256]{2,1,0:T(8,128)(2,1)S(1)} %slice.72), channel_id=1, source_target_pairs={{0,3},{1,0},{2,1},{3,2},{4,7},{5,4},{6,5},{7,6},{8,11},{9,8},{10,9... | collective-permute-start | bytes 294920 | tf_op jit(solution)/shard_map/ppermute | solution.py:34
  82.2 1.0 %copy.46 = bf16[24,45,256]{2,0,1:T(8,128)(2,1)} copy(bf16[24,45,256]{2,1,0:T(8,128)(2,1)S(1)} %get-tuple-element.15) | data formatting | bytes 1105920
  83.1 4.9 %collective-permute-done.11 = f32[4,32,256]{2,1,0:T(8,128)S(1)} collective-permute-done((f32[4,32,256]{2,1,0:T(8,128)S(1)}, f32[4,32,256]{2,1,0:T(8,128)S(1)}, u32[]{:S(2)}, u32[]{:S(2)}) %collective-permute-start.11) | collective-permute-done | bytes 131104 | tf_op jit(solution)/shard_map/ppermute | solution.py:49
  88.1 1.6 %collective-permute-start.12 = (f32[4,32,256]{2,1,0:T(8,128)S(1)}, f32[4,32,256]{2,1,0:T(8,128)S(1)}, u32[]{:S(2)}, u32[]{:S(2)}) collective-permute-start(f32[4,32,256]{2,1,0:T(8,128)S(1)} %add.61), channel_id=1, source_target_pairs={{0,2},{1,3},{2,0},{3,1},{4,6},{5,7},{6,4},{7,5},{8,10},{9,11},{10,... | collective-permute-start | bytes 393224 | tf_op jit(solution)/shard_map/ppermute | solution.py:49
  89.7 0.0 collective-permute-done.8
  89.7 0.3 fusion.15
  90.0 1.0 %copy.47 = bf16[24,45,256]{2,0,1:T(8,128)(2,1)} copy(bf16[24,45,256]{2,1,0:T(8,128)(2,1)S(1)} %fusion.15) | data formatting | bytes 1105920
  91.0 4.7 %collective-permute-done.12 = f32[4,32,256]{2,1,0:T(8,128)S(1)} collective-permute-done((f32[4,32,256]{2,1,0:T(8,128)S(1)}, f32[4,32,256]{2,1,0:T(8,128)S(1)}, u32[]{:S(2)}, u32[]{:S(2)}) %collective-permute-start.12) | collective-permute-done | bytes 131104 | tf_op jit(solution)/shard_map/ppermute | solution.py:49
  95.7 0.2 reshape.124
  95.8 0.9 copy.57
  (30 shorter events, 0.3 us)
Async XLA Ops:
  0.6 7.3 %copy-start = (bf16[192,4,3,17]{0,1,3,2:T(4,128)(2,1)S(1)}, bf16[192,4,3,17]{0,1,3,2:T(4,128)(2,1)}, u32[]{:S(2)}) copy-start(bf16[192,4,3,17]{0,1,3,2:T(4,128)(2,1)} %param.8) | copy-start | bytes 235012
  0.6 1.9 %copy-start.4 = (bf16[24,45,256]{2,0,1:T(8,128)(2,1)S(1)}, bf16[24,45,256]{2,0,1:T(8,128)(2,1)}, u32[]{:S(2)}) copy-start(bf16[24,45,256]{2,0,1:T(8,128)(2,1)} %param.6) | copy-start | bytes 1658884
  0.7 1.7 %copy-start.7 = (s32[256]{0:T(256)}, s32[256]{0:T(256)S(1)}, u32[]{:S(2)}) copy-start(s32[256]{0:T(256)S(1)} %and_select_fusion) | copy-start | bytes 3076
  1.9 0.9 copy-start.2
  2.6 5.1 %copy-start.9 = (s32[192]{0:T(256)S(1)}, s32[192]{0:T(256)}, u32[]{:S(2)}) copy-start(s32[192]{0:T(256)} %param.9) | copy-start | bytes 2308
  2.6 5.5 %copy-start.6 = (bf16[8,4,32,32]{3,2,1,0:T(8,128)(2,1)S(1)}, bf16[8,4,32,32]{3,2,1,0:T(8,128)(2,1)}, u32[]{:S(2)}) copy-start(bf16[8,4,32,32]{3,2,1,0:T(8,128)(2,1)} %param.10) | copy-start | bytes 196612
  3.4 8.9 %collective-permute-start = (bf16[1,45,264]{2,1,0:T(8,128)(2,1)}, bf16[1,45,264]{2,1,0:T(8,128)(2,1)S(1)}, u32[]{:S(2)}, u32[]{:S(2)}) collective-permute-start(bf16[1,45,264]{2,1,0:T(8,128)(2,1)} %get-tuple-element.22), channel_id=1, source_target_pairs={{0,4},{4,8},{8,12},{12,16},{16,20},{20,24},{24,28},{1,5},{5,9},{9,... | collective-permute-start | bytes 71288 | tf_op jit(solution)/shard_map/ppermute | solution.py:18
  5.8 6.5 %collective-permute-start.1 = (bf16[1,45,264]{2,1,0:T(8,128)(2,1)}, bf16[1,45,264]{2,1,0:T(8,128)(2,1)}, u32[]{:S(2)}, u32[]{:S(2)}) collective-permute-start(bf16[1,45,264]{2,1,0:T(8,128)(2,1)} %get-tuple-element.23), channel_id=1, source_target_pairs={{4,0},{8,4},{12,8},{16,12},{20,16},{24,20},{28,24},{5,1},{9,5},{13... | collective-permute-start | bytes 71288 | tf_op jit(solution)/shard_map/ppermute | solution.py:21
  14.1 15.7 %collective-permute-start.2 = (bf16[26,8,264]{2,1,0:T(8,128)(2,1)}, bf16[26,8,264]{2,1,0:T(8,128)(2,1)}, u32[]{:S(2)}, u32[]{:S(2)}) collective-permute-start(bf16[26,8,264]{2,1,0:T(8,128)(2,1)} %get-tuple-element.20), channel_id=1, source_target_pairs={{0,1},{1,2},{2,3},{3,0},{4,5},{5,6},{6,7},{7,4},{8,9},{9,10},{10,1... | collective-permute-start | bytes 329480 | tf_op jit(solution)/shard_map/ppermute | solution.py:18
  16.5 13.3 %collective-permute-start.3 = (bf16[26,8,264]{2,1,0:T(8,128)(2,1)}, bf16[26,8,264]{2,1,0:T(8,128)(2,1)}, u32[]{:S(2)}, u32[]{:S(2)}) collective-permute-start(bf16[26,8,264]{2,1,0:T(8,128)(2,1)} %get-tuple-element.21), channel_id=1, source_target_pairs={{1,0},{2,1},{3,2},{0,3},{5,4},{6,5},{7,6},{4,7},{9,8},{10,9},{11,1... | collective-permute-start | bytes 329480 | tf_op jit(solution)/shard_map/ppermute | solution.py:21
  26.3 3.2 %copy-start.5 = (bf16[24,45,256]{2,0,1:T(8,128)(2,1)S(1)}, bf16[24,45,256]{2,0,1:T(8,128)(2,1)}, u32[]{:S(2)}) copy-start(bf16[24,45,256]{2,0,1:T(8,128)(2,1)} %param.11) | copy-start | bytes 1658884
  29.5 1.0 copy-start.3
  31.8 0.6 copy-start.8
  53.9 3.1 %collective-permute-start.4 = (f32[4,32,256]{2,1,0:T(8,128)S(1)}, f32[4,32,256]{2,1,0:T(8,128)S(1)}, u32[]{:S(2)}, u32[]{:S(2)}) collective-permute-start(f32[4,32,256]{2,1,0:T(8,128)S(1)} %get-tuple-element.8), channel_id=1, source_target_pairs={{0,4},{4,0},{8,12},{12,8},{16,20},{20,16},{24,28},{28,24},{1,5},{5... | collective-permute-start | bytes 393224 | tf_op jit(solution)/shard_map/ppermute | solution.py:193
  57.1 14.7 %collective-permute-start.9 = (f32[4,32,256]{2,1,0:T(8,128)S(1)}, f32[4,32,256]{2,1,0:T(8,128)S(1)}, u32[]{:S(2)}, u32[]{:S(2)}) collective-permute-start(f32[4,32,256]{2,1,0:T(8,128)S(1)} %add.58), channel_id=1, source_target_pairs={{0,8},{4,12},{8,0},{12,4},{16,24},{20,28},{24,16},{28,20},{1,9},{5... | collective-permute-start | bytes 393224 | tf_op jit(solution)/shard_map/ppermute | solution.py:49
  59.6 1.7 %copy-start.1 = (bf16[24,192,256]{2,1,0:T(8,128)(2,1)S(1)}, bf16[24,192,256]{2,1,0:T(8,128)(2,1)}, u32[]{:S(2)}) copy-start(bf16[24,192,256]{2,1,0:T(8,128)(2,1)} %get-tuple-element.7.pulled_ref) | copy-start | bytes 7077892
  68.7 8.1 %collective-permute-start.5 = (f32[1,61,256]{2,1,0:T(8,128)S(1)}, f32[1,61,256]{2,1,0:T(8,128)S(1)}, u32[]{:S(2)}, u32[]{:S(2)}) collective-permute-start(f32[1,61,256]{2,1,0:T(8,128)S(1)} %get-tuple-element.18), channel_id=1, source_target_pairs={{0,4},{4,8},{8,12},{12,16},{16,20},{20,24},{24,28},{1,5},{5,9},{9,... | collective-permute-start | bytes 187400 | tf_op jit(solution)/shard_map/ppermute | solution.py:29
  70.5 6.3 %collective-permute-start.6 = (f32[1,61,256]{2,1,0:T(8,128)S(1)}, f32[1,61,256]{2,1,0:T(8,128)S(1)}, u32[]{:S(2)}, u32[]{:S(2)}) collective-permute-start(f32[1,61,256]{2,1,0:T(8,128)S(1)} %get-tuple-element.19), channel_id=1, source_target_pairs={{4,0},{8,4},{12,8},{16,12},{20,16},{24,20},{28,24},{5,1},{9,5},{13... | collective-permute-start | bytes 187400 | tf_op jit(solution)/shard_map/ppermute | solution.py:29
  71.8 7.9 %collective-permute-start.10 = (f32[4,32,256]{2,1,0:T(8,128)S(1)}, f32[4,32,256]{2,1,0:T(8,128)S(1)}, u32[]{:S(2)}, u32[]{:S(2)}) collective-permute-start(f32[4,32,256]{2,1,0:T(8,128)S(1)} %add.59), channel_id=1, source_target_pairs={{0,16},{4,20},{8,24},{12,28},{16,0},{20,4},{24,8},{28,12},{1,17},{... | collective-permute-start | bytes 393224 | tf_op jit(solution)/shard_map/ppermute | solution.py:49
  77.0 12.7 %collective-permute-start.8 = (f32[24,8,256]{2,1,0:T(8,128)S(1)}, f32[24,8,256]{2,1,0:T(8,128)S(1)}, u32[]{:S(2)}, u32[]{:S(2)}) collective-permute-start(f32[24,8,256]{2,1,0:T(8,128)S(1)} %slice.60), channel_id=1, source_target_pairs={{0,1},{1,2},{2,3},{3,0},{4,5},{5,6},{6,7},{7,4},{8,9},{9,10},{10,1... | collective-permute-start | bytes 589832 | tf_op jit(solution)/shard_map/ppermute | solution.py:34
  79.8 8.3 %collective-permute-start.11 = (f32[4,32,256]{2,1,0:T(8,128)S(1)}, f32[4,32,256]{2,1,0:T(8,128)S(1)}, u32[]{:S(2)}, u32[]{:S(2)}) collective-permute-start(f32[4,32,256]{2,1,0:T(8,128)S(1)} %add.60), channel_id=1, source_target_pairs={{0,1},{1,0},{2,3},{3,2},{4,5},{5,4},{6,7},{7,6},{8,9},{9,8},{10,11... | collective-permute-start | bytes 393224 | tf_op jit(solution)/shard_map/ppermute | solution.py:49
  79.9 9.8 %collective-permute-start.7 = (bf16[24,8,256]{2,1,0:T(8,128)(2,1)S(1)}, bf16[24,8,256]{2,1,0:T(8,128)(2,1)S(1)}, u32[]{:S(2)}, u32[]{:S(2)}) collective-permute-start(bf16[24,8,256]{2,1,0:T(8,128)(2,1)S(1)} %slice.72), channel_id=1, source_target_pairs={{0,3},{1,0},{2,1},{3,2},{4,7},{5,4},{6,5},{7,6},{8,11},{9,8},{10,9... | collective-permute-start | bytes 294920 | tf_op jit(solution)/shard_map/ppermute | solution.py:34
  88.1 7.6 %collective-permute-start.12 = (f32[4,32,256]{2,1,0:T(8,128)S(1)}, f32[4,32,256]{2,1,0:T(8,128)S(1)}, u32[]{:S(2)}, u32[]{:S(2)}) collective-permute-start(f32[4,32,256]{2,1,0:T(8,128)S(1)} %add.61), channel_id=1, source_target_pairs={{0,2},{1,3},{2,0},{3,1},{4,6},{5,7},{6,4},{7,5},{8,10},{9,11},{10,... | collective-permute-start | bytes 393224 | tf_op jit(solution)/shard_map/ppermute | solution.py:49

commit v7 on v6

--- a/solution.py
+++ b/solution.py
@@ -52,7 +52,7 @@
     return value
 
 
-def forward_kernel(x_ref, m_ref, t_ref, cot_ref, w_ref, wt_ref, inf_ref, wg_ref, pulled_ref, acc_ref):
+def forward_kernel(x_ref, m_ref, t_ref, cot_ref, w_ref, inf_ref, wg_ref, pulled_ref, acc_ref):
     rows, basis_count, lat_taps, col_pad, lane_rows = t_ref.shape
     col_count = inf_ref.shape[1]
     chan_count = w_ref.shape[1]
@@ -79,7 +79,9 @@
             acc_ref[b] += lax.dot_general(
                 part, upstream, (((0,), (0,)), ((), ())), preferred_element_type=jnp.float32
             )
-            back = jnp.dot(upstream, wt_ref[b], preferred_element_type=jnp.float32)
+            back = lax.dot_general(
+                upstream, w_ref[b], (((1,), (1,)), ((), ())), preferred_element_type=jnp.float32
+            )
             pulled_ref[i, b * col_pad : (b + 1) * col_pad, :] = (
                 back / safe[b * col_pad : (b + 1) * col_pad]
             ).astype(jnp.bfloat16)
@@ -162,9 +164,6 @@
 
     eye = jnp.eye(group_count, dtype=mixing.dtype)
     mix_blocks = jnp.einsum("gbco,gh->bgcho", mixing, eye).reshape(basis_count, chan_count, chan_count)
-    mix_blocks_t = jnp.einsum("gbco,gh->bhogc", mixing, eye).reshape(
-        basis_count, chan_count, chan_count
-    )
     upstream = jnp.pad(cotangent, ((0, 0), (0, col_pad - col_count), (0, 0)))
 
     vmem = pl.BlockSpec(memory_space=pltpu.VMEM)
@@ -176,7 +175,7 @@
             jax.ShapeDtypeStruct((basis_count, group_width, chan_count), jnp.float32),
             jax.ShapeDtypeStruct((row_count, basis_count * col_pad, chan_count), jnp.bfloat16),
         ),
-        in_specs=[vmem] * 6,
+        in_specs=[vmem] * 5,
         out_specs=[vmem] * 3,
         scratch_shapes=[pltpu.VMEM((basis_count, chan_count, chan_count), jnp.float32)],
         compiler_params=params,
@@ -185,7 +184,7 @@
             transcendentals=0,
             bytes_accessed=8 * (row_count + 2) * lane_rows * chan_count,
         ),
-    )(full_input, full_mask, band, upstream, mix_blocks, mix_blocks_t)
+    )(full_input, full_mask, band, upstream, mix_blocks)
 
     cell_count = row_count * lax.axis_size("lat") * col_count * lax.axis_size("lon")
     lat_count = lax.axis_size("lat")

time: 97.4 us -> 83.4 us (0.86)
  local copies, waits for them, and re-layouts: 17.3 us -> 9.48 us
  other arithmetic: 9.08 us -> 4.34 us
  waiting for transfers between devices: 13.3 us -> 17.9 us
  Pallas kernels: 28.6 us -> 25.8 us
  starting transfers between devices: 24.9 us -> 22.6 us
    ppermute x2, waiting for transfers between devices: 0.01 us -> 4.3 us  [with_halo(): lax.ppermute(lax.slice_in_dim(block, 0, width, axis=dim), axis, backward)]
    reshape x1 -> x0, local copies, waits for them, and re-layouts: 3.18 us -> none  [local(): jnp.einsum('gbco,gh->bhogc', mixing, eye)]
    pallas_call x1, Pallas kernels: 21.1 us -> 18.4 us  [local(): pl.pallas_call(forward_kernel, out_shape=(jax.ShapeDtypeStruct((row_count...]
    unnamed x25 -> x20, local copies, waits for them, and re-layouts: 6.06 us -> 3.37 us
    transpose x1, other arithmetic: 2.65 us -> 0.67 us  [local(): jnp.einsum('gbco,gh->bgcho', mixing, eye)]
    reshape x2 -> x1, local copies, waits for them, and re-layouts: 3.38 us -> 1.44 us  [local(): jnp.einsum('gbco,gh->bgcho', mixing, eye)]
    ppermute x1, starting transfers between devices: 2.12 us -> 0.22 us  [local(): lax.ppermute(grad_blocks, 'lat', [(i, i ^ 1) for i in range(lat_count)])]
    slice x2, other arithmetic: 2.38 us -> 0.81 us  [with_halo(): lax.slice_in_dim(block, block.shape[dim] - width, None, axis=dim)]
  transfers between devices with their start and end apart: 13 -> 13, of which waited for: 4 -> 7; matrix products, arithmetic and copies ran while one was open for 19% -> 12% of each run, Pallas kernels for 8% -> 9%
where the time goes in v7:
time: 83.4 us; the launch traced here: 83 us
  Pallas kernels  25.8 us (31%)
  starting transfers between devices  22.6 us (27%)
  waiting for transfers between devices  17.9 us (21%)
  local copies, waits for them, and re-layouts  9.48 us (11%)
  other arithmetic  4.34 us (5%)
  matrix products  1.86 us (2%)
  between operations  1.01 us (1%)
    pallas_call x1, Pallas kernels, local(): pl.pallas_call(forward_kernel, out_shape=(jax.ShapeDtypeStruct((row_count...  18.4 us
    ppermute x4, waiting for transfers between devices, butterfly_sum(): partner = lax.ppermute(value, axis, [(i, i ^ step) for i in range(count)])  11.9 us
    ppermute x4, starting transfers between devices, butterfly_sum(): partner = lax.ppermute(value, axis, [(i, i ^ step) for i in range(count)])  9.05 us
    pallas_call x1, Pallas kernels, local(): pl.pallas_call(adjoint_kernel, out_shape=jax.ShapeDtypeStruct(((row_count...  7.41 us
    ppermute x2, waiting for transfers between devices, with_halo(): lax.ppermute(lax.slice_in_dim(block, 0, width, axis=dim), axis, backward)  4.3 us
    ppermute x2, starting transfers between devices, with_halo(): lax.ppermute(lax.slice_in_dim(block, block.shape[dim] - width, None, axis...  3.98 us
    ppermute x2, starting transfers between devices, with_halo(): lax.ppermute(lax.slice_in_dim(block, 0, width, axis=dim), axis, backward)  3.54 us
    unnamed x20, local copies, waits for them, and re-layouts  3.37 us
  transfers between devices with their start and end apart: 13, of which 7 were waited for; matrix products, arithmetic and copies ran while one was open for 12% of the time, Pallas kernels for 9%

profile of v7, /device:TPU:0, one launch (start us, length us, event | category | flops | bytes accessed | tf_op | source)
XLA Modules:
  0.0 83.0 jit_solution(5522527911601352292)
XLA Ops:
  0.6 0.0 copy-start
  0.6 0.0 copy-start.5
  0.7 1.0 %convert_element_type.46 = bf16[24,45,8]{1,2,0:T(8,128)(2,1)S(1)} convert(s32[24,45,8]{1,2,0:T(8,128)} %param.7) | non-fusion elementwise | flops 8640 | bytes 51840 | tf_op jit(solution)/shard_map/convert_element_type | solution.py:129
  1.6 0.2 copy.35
  1.9 0.1 reshape.114
  2.0 0.4 fusion.6
  2.4 0.2 reshape.115
  2.6 0.0 copy-done.5
  2.6 0.0 copy-start.1
  2.6 0.0 copy-start.7
  2.6 0.1 copy_multiply_fusion
  2.8 2.4 %collective-permute-start = (bf16[1,45,264]{2,1,0:T(8,128)(2,1)S(1)}, bf16[1,45,264]{2,1,0:T(8,128)(2,1)S(1)}, u32[]{:S(2)}, u32[]{:S(2)}) collective-permute-start(bf16[1,45,264]{2,1,0:T(8,128)(2,1)S(1)} %get-tuple-element.22), channel_id=1, source_target_pairs={{0,4},{4,8},{8,12},{12,16},{16,20},{20,24},{24,28},{1,5},{5,9},{9,... | collective-permute-start | bytes 71288 | tf_op jit(solution)/shard_map/ppermute | solution.py:18
  5.2 1.3 %collective-permute-start.1 = (bf16[1,45,264]{2,1,0:T(8,128)(2,1)S(1)}, bf16[1,45,264]{2,1,0:T(8,128)(2,1)S(1)}, u32[]{:S(2)}, u32[]{:S(2)}) collective-permute-start(bf16[1,45,264]{2,1,0:T(8,128)(2,1)S(1)} %get-tuple-element.23), channel_id=1, source_target_pairs={{4,0},{8,4},{12,8},{16,12},{20,16},{24,20},{28,24},{5,1},{9,5},{13... | collective-permute-start | bytes 71288 | tf_op jit(solution)/shard_map/ppermute | solution.py:21
  6.5 0.0 copy-done
  6.5 0.1 constant_dynamic-slice_fusion
  6.6 0.2 copy.48
  6.8 0.0 copy-done.7
  6.8 0.1 compare_convert_fusion
  6.9 0.1 copy.37
  7.0 0.0 copy-start.6
  7.0 1.1 %fusion.18 = bf16[24,4,3,48,64]{4,0,3,2,1:T(8,128)(2,1)S(1)} fusion(s32[48,64]{1,0:T(8,128)S(1)} %iota_subtract_fusion, pred[48]{0:T(512)(128)(4,1)S(1)} %iota_compare_fusion.6, bf16[24,4,3,17]{3,0,2,1:T(8,128)(2,1)S(1)} %copy.48, bf16[24,17]{1,0:T(8,128)(2,1)S(1)} %constant_dynamic-slice_fusion.1), kind=kOutput, calls=%fused_computation.27 | convolution fusion | flops 30205056 | bytes 1792416 | tf_op jit(solution)/shard_map/ibae,ejp->ibajp/dot_general | solution.py:161
  8.2 0.0 collective-permute-done
  8.2 2.2 %collective-permute-done.1 = bf16[1,45,264]{2,1,0:T(8,128)(2,1)S(1)} collective-permute-done((bf16[1,45,264]{2,1,0:T(8,128)(2,1)S(1)}, bf16[1,45,264]{2,1,0:T(8,128)(2,1)S(1)}, u32[]{:S(2)}, u32[]{:S(2)}) %collective-permute-start.1) | collective-permute-done | bytes 23792 | tf_op jit(solution)/shard_map/ppermute | solution.py:21
  10.4 0.8 pad_maximum_fusion.3
  11.2 1.6 %collective-permute-start.2 = (bf16[26,8,264]{2,1,0:T(8,128)(2,1)}, bf16[26,8,264]{2,1,0:T(8,128)(2,1)S(1)}, u32[]{:S(2)}, u32[]{:S(2)}) collective-permute-start(bf16[26,8,264]{2,1,0:T(8,128)(2,1)} %get-tuple-element.20), channel_id=1, source_target_pairs={{0,1},{1,2},{2,3},{3,0},{4,5},{5,6},{6,7},{7,4},{8,9},{9,10},{10,1... | collective-permute-start | bytes 329480 | tf_op jit(solution)/shard_map/ppermute | solution.py:18
  12.7 2.2 %collective-permute-start.3 = (bf16[26,8,264]{2,1,0:T(8,128)(2,1)}, bf16[26,8,264]{2,1,0:T(8,128)(2,1)}, u32[]{:S(2)}, u32[]{:S(2)}) collective-permute-start(bf16[26,8,264]{2,1,0:T(8,128)(2,1)} %get-tuple-element.21), channel_id=1, source_target_pairs={{1,0},{2,1},{3,2},{0,3},{5,4},{6,5},{7,6},{4,7},{9,8},{10,9},{11,1... | collective-permute-start | bytes 329480 | tf_op jit(solution)/shard_map/ppermute | solution.py:21
  15.0 0.0 copy-done.6
  15.0 0.7 multiply_bitcast_fusion
  15.7 2.6 %copy.52.t_ref = bf16[24,4,3,48,64]{4,3,2,1,0:T(8,128)(2,1)} copy(bf16[24,4,3,48,64]{4,0,3,2,1:T(8,128)(2,1)S(1)} %fusion.18) | data formatting | bytes 3538944 | tf_op jit(solution)/shard_map/ibae,ejp->ibajp/dot_general | solution.py:161
  18.3 1.4 %reshape.118.w_ref = bf16[4,256,256]{2,1,0:T(8,128)(2,1)S(1)} reshape(bf16[4,8,32,8,32]{4,3,2,1,0:T(8,128)(2,1)S(1)} %multiply_bitcast_fusion) | data formatting | bytes 1048576 | tf_op jit(solution)/shard_map/reshape | solution.py:166
  19.7 0.0 copy-start.4
  19.7 1.2 %copy.40 = bf16[24,45,256]{2,1,0:T(8,128)(2,1)S(1)} copy(bf16[24,45,256]{2,0,1:T(8,128)(2,1)} %param.11) | data formatting | bytes 1105920 | tf_op args[5]
  21.0 0.0 collective-permute-done.2
  21.0 2.1 %collective-permute-done.3 = bf16[26,8,264]{2,1,0:T(8,128)(2,1)} collective-permute-done((bf16[26,8,264]{2,1,0:T(8,128)(2,1)}, bf16[26,8,264]{2,1,0:T(8,128)(2,1)}, u32[]{:S(2)}, u32[]{:S(2)}) %collective-permute-start.3) | collective-permute-done | bytes 109856 | tf_op jit(solution)/shard_map/ppermute | solution.py:21
  23.1 1.2 %fusion.9 = bf16[26,64,264]{2,1,0:T(8,128)(2,1)S(1)} fusion(bf16[26,8,264]{2,1,0:T(8,128)(2,1)} %collective-permute-done.3, bf16[26,8,264]{2,1,0:T(8,128)(2,1)S(1)} %collective-permute-done.2, bf16[1,45,264]{2,1,0:T(8,128)(2,1)S(1)} %collective-permute-done.1, bf16[1,45,264]{2,1,0:T(8,128)(2,1)S(1)} %collective-permute-done, ...), kind=kLoop, calls=%fused_computation.15 | loop fusion | flops 8346624 | bytes 1716000 | tf_op jit(solution)/shard_map/concatenate | solution.py:22
  24.4 0.1 slice.54
  24.4 0.1 slice.53
  24.5 0.4 convolution_convert_fusion.m_ref
  24.9 18.4 %shard_map.85 = (bf16[24,45,256]{2,1,0:T(8,128)(2,1)S(1)}, f32[4,32,256]{2,1,0:T(8,128)S(1)}, bf16[24,192,256]{2,1,0:T(8,128)(2,1)S(1)}) custom-call(bf16[1664,256]{1,0:T(8,128)(2,1)S(1)} %bitcast.28, bf16[1664,256]{1,0:T(8,128)(2,1)S(1)} %convolution_convert_fusion.m_ref, bf16[24,4,3,48,64]{4,3,2,1,0:T(8,128)(2,1)} %copy.52.t_ref, ...), custom_call_target="tpu_custom_call" | custom-call | flops 2717908992 | bytes 3407872 | tf_op jit(solution)/shard_map/pallas_call | solution.py:171
  43.2 0.2 collective-permute-start.4
  43.5 1.2 %collective-permute-done.4.order_ref = f32[4,32,256]{2,1,0:T(8,128)S(1)} collective-permute-done((f32[4,32,256]{2,1,0:T(8,128)S(1)}, f32[4,32,256]{2,1,0:T(8,128)S(1)}, u32[]{:S(2)}, u32[]{:S(2)}) %collective-permute-start.4) | collective-permute-done | bytes 131104 | tf_op jit(solution)/shard_map/ppermute | solution.py:192
  44.7 2.8 %collective-permute-start.9 = (f32[4,32,256]{2,1,0:T(8,128)S(1)}, f32[4,32,256]{2,1,0:T(8,128)S(1)}, u32[]{:S(2)}, u32[]{:S(2)}) collective-permute-start(f32[4,32,256]{2,1,0:T(8,128)S(1)} %add.58), channel_id=1, source_target_pairs={{0,8},{4,12},{8,0},{12,4},{16,24},{20,28},{24,16},{28,20},{1,9},{5... | collective-permute-start | bytes 393224 | tf_op jit(solution)/shard_map/ppermute | solution.py:49
  47.5 7.4 %shard_map.86 = f32[1664,256]{1,0:T(8,128)S(1)} custom-call(bf16[24,4,3,48,64]{4,3,2,1,0:T(8,128)(2,1)} %copy.52.t_ref, bf16[24,192,256]{2,1,0:T(8,128)(2,1)S(1)} %get-tuple-element.7.pulled_ref, f32[4,32,256]{2,1,0:T(8,128)S(1)} %collective-permute-done.4.order_ref), custom_call_target="tpu_custom_call" | custom-call | flops 452984832 | bytes 2555904 | tf_op jit(solution)/shard_map/pallas_call | solution.py:200
  54.9 1.8 %collective-permute-start.5 = (f32[1,61,256]{2,1,0:T(8,128)S(1)}, f32[1,61,256]{2,1,0:T(8,128)S(1)}, u32[]{:S(2)}, u32[]{:S(2)}) collective-permute-start(f32[1,61,256]{2,1,0:T(8,128)S(1)} %get-tuple-element.18), channel_id=1, source_target_pairs={{0,4},{4,8},{8,12},{12,16},{16,20},{20,24},{24,28},{1,5},{5,9},{9,... | collective-permute-start | bytes 187400 | tf_op jit(solution)/shard_map/ppermute | solution.py:29
  56.7 1.3 %collective-permute-start.6 = (f32[1,61,256]{2,1,0:T(8,128)S(1)}, f32[1,61,256]{2,1,0:T(8,128)S(1)}, u32[]{:S(2)}, u32[]{:S(2)}) collective-permute-start(f32[1,61,256]{2,1,0:T(8,128)S(1)} %get-tuple-element.19), channel_id=1, source_target_pairs={{4,0},{8,4},{12,8},{16,12},{20,16},{24,20},{28,24},{5,1},{9,5},{13... | collective-permute-start | bytes 187400 | tf_op jit(solution)/shard_map/ppermute | solution.py:29
  58.0 0.0 collective-permute-done.9
  58.0 4.0 %collective-permute-start.10 = (f32[4,32,256]{2,1,0:T(8,128)S(1)}, f32[4,32,256]{2,1,0:T(8,128)S(1)}, u32[]{:S(2)}, u32[]{:S(2)}) collective-permute-start(f32[4,32,256]{2,1,0:T(8,128)S(1)} %add.59), channel_id=1, source_target_pairs={{0,16},{4,20},{8,24},{12,28},{16,0},{20,4},{24,8},{28,12},{1,17},{... | collective-permute-start | bytes 393224 | tf_op jit(solution)/shard_map/ppermute | solution.py:49
  62.0 0.0 collective-permute-done.5
  62.1 0.0 collective-permute-done.6
  62.1 0.1 fusion.7
  62.2 1.2 %collective-permute-start.8 = (f32[24,8,256]{2,1,0:T(8,128)S(1)}, f32[24,8,256]{2,1,0:T(8,128)S(1)}, u32[]{:S(2)}, u32[]{:S(2)}) collective-permute-start(f32[24,8,256]{2,1,0:T(8,128)S(1)} %slice.60), channel_id=1, source_target_pairs={{0,1},{1,2},{2,3},{3,0},{4,5},{5,6},{6,7},{7,4},{8,9},{9,10},{10,1... | collective-permute-start | bytes 589832 | tf_op jit(solution)/shard_map/ppermute | solution.py:34
  63.4 1.8 %collective-permute-done.10 = f32[4,32,256]{2,1,0:T(8,128)S(1)} collective-permute-done((f32[4,32,256]{2,1,0:T(8,128)S(1)}, f32[4,32,256]{2,1,0:T(8,128)S(1)}, u32[]{:S(2)}, u32[]{:S(2)}) %collective-permute-start.10) | collective-permute-done | bytes 131104 | tf_op jit(solution)/shard_map/ppermute | solution.py:49
  65.2 1.2 %collective-permute-start.11 = (f32[4,32,256]{2,1,0:T(8,128)S(1)}, f32[4,32,256]{2,1,0:T(8,128)S(1)}, u32[]{:S(2)}, u32[]{:S(2)}) collective-permute-start(f32[4,32,256]{2,1,0:T(8,128)S(1)} %add.60), channel_id=1, source_target_pairs={{0,1},{1,0},{2,3},{3,2},{4,5},{5,4},{6,7},{7,6},{8,9},{9,8},{10,11... | collective-permute-start | bytes 393224 | tf_op jit(solution)/shard_map/ppermute | solution.py:49
  66.4 1.6 %collective-permute-start.7 = (bf16[24,8,256]{2,1,0:T(8,128)(2,1)S(1)}, bf16[24,8,256]{2,1,0:T(8,128)(2,1)S(1)}, u32[]{:S(2)}, u32[]{:S(2)}) collective-permute-start(bf16[24,8,256]{2,1,0:T(8,128)(2,1)S(1)} %slice.72), channel_id=1, source_target_pairs={{0,3},{1,0},{2,1},{3,2},{4,7},{5,4},{6,5},{7,6},{8,11},{9,8},{10,9... | collective-permute-start | bytes 294920 | tf_op jit(solution)/shard_map/ppermute | solution.py:34
  68.0 1.0 %copy.43 = bf16[24,45,256]{2,0,1:T(8,128)(2,1)} copy(bf16[24,45,256]{2,1,0:T(8,128)(2,1)S(1)} %get-tuple-element.15) | data formatting | bytes 1105920
  69.0 5.3 %collective-permute-done.11 = f32[4,32,256]{2,1,0:T(8,128)S(1)} collective-permute-done((f32[4,32,256]{2,1,0:T(8,128)S(1)}, f32[4,32,256]{2,1,0:T(8,128)S(1)}, u32[]{:S(2)}, u32[]{:S(2)}) %collective-permute-start.11) | collective-permute-done | bytes 131104 | tf_op jit(solution)/shard_map/ppermute | solution.py:49
  74.3 1.0 %collective-permute-start.12 = (f32[4,32,256]{2,1,0:T(8,128)S(1)}, f32[4,32,256]{2,1,0:T(8,128)S(1)}, u32[]{:S(2)}, u32[]{:S(2)}) collective-permute-start(f32[4,32,256]{2,1,0:T(8,128)S(1)} %add.61), channel_id=1, source_target_pairs={{0,2},{1,3},{2,0},{3,1},{4,6},{5,7},{6,4},{7,5},{8,10},{9,11},{10,... | collective-permute-start | bytes 393224 | tf_op jit(solution)/shard_map/ppermute | solution.py:49
  75.3 0.6 collective-permute-done.7
  75.9 0.0 collective-permute-done.8
  75.9 0.2 fusion.15
  76.2 1.0 %copy.44 = bf16[24,45,256]{2,0,1:T(8,128)(2,1)} copy(bf16[24,45,256]{2,1,0:T(8,128)(2,1)S(1)} %fusion.15) | data formatting | bytes 1105920
  77.2 4.8 %collective-permute-done.12 = f32[4,32,256]{2,1,0:T(8,128)S(1)} collective-permute-done((f32[4,32,256]{2,1,0:T(8,128)S(1)}, f32[4,32,256]{2,1,0:T(8,128)S(1)}, u32[]{:S(2)}, u32[]{:S(2)}) %collective-permute-start.12) | collective-permute-done | bytes 131104 | tf_op jit(solution)/shard_map/ppermute | solution.py:49
  82.0 0.2 reshape.120
  82.1 0.9 %copy.55 = f32[4,32,8,32]{3,1,0,2:T(8,128)} copy(f32[4,32,8,32]{3,2,1,0:T(8,128)S(1)} %reshape.120) | data formatting | bytes 262144 | tf_op jit(solution)/shard_map/reshape | solution.py:198
  (23 shorter events, 0.3 us)
Async XLA Ops:
  0.6 5.9 %copy-start = (bf16[192,4,3,17]{0,1,3,2:T(4,128)(2,1)S(1)}, bf16[192,4,3,17]{0,1,3,2:T(4,128)(2,1)}, u32[]{:S(2)}) copy-start(bf16[192,4,3,17]{0,1,3,2:T(4,128)(2,1)} %param.8) | copy-start | bytes 235012
  0.6 1.9 %copy-start.5 = (bf16[24,45,256]{2,0,1:T(8,128)(2,1)S(1)}, bf16[24,45,256]{2,0,1:T(8,128)(2,1)}, u32[]{:S(2)}) copy-start(bf16[24,45,256]{2,0,1:T(8,128)(2,1)} %param.6) | copy-start | bytes 1658884
  1.9 8.5 %copy-start.3 = (bf16[24,45,8]{2,1,0:T(8,128)(2,1)}, bf16[24,45,8]{2,1,0:T(8,128)(2,1)S(1)}, u32[]{:S(2)}) copy-start(bf16[24,45,8]{2,1,0:T(8,128)(2,1)S(1)} %copy.35) | copy-start | bytes 51844
  2.6 5.6 %copy-start.1 = (bf16[24,45,256]{2,1,0:T(8,128)(2,1)}, bf16[24,45,256]{2,1,0:T(8,128)(2,1)S(1)}, u32[]{:S(2)}) copy-start(bf16[24,45,256]{2,1,0:T(8,128)(2,1)S(1)} %reshape.115) | copy-start | bytes 1658884
  2.6 4.2 %copy-start.7 = (s32[192]{0:T(256)S(1)}, s32[192]{0:T(256)}, u32[]{:S(2)}) copy-start(s32[192]{0:T(256)} %param.9) | copy-start | bytes 2308
  2.8 5.4 %collective-permute-start = (bf16[1,45,264]{2,1,0:T(8,128)(2,1)S(1)}, bf16[1,45,264]{2,1,0:T(8,128)(2,1)S(1)}, u32[]{:S(2)}, u32[]{:S(2)}) collective-permute-start(bf16[1,45,264]{2,1,0:T(8,128)(2,1)S(1)} %get-tuple-element.22), channel_id=1, source_target_pairs={{0,4},{4,8},{8,12},{12,16},{16,20},{20,24},{24,28},{1,5},{5,9},{9,... | collective-permute-start | bytes 71288 | tf_op jit(solution)/shard_map/ppermute | solution.py:18
  5.2 5.2 %collective-permute-start.1 = (bf16[1,45,264]{2,1,0:T(8,128)(2,1)S(1)}, bf16[1,45,264]{2,1,0:T(8,128)(2,1)S(1)}, u32[]{:S(2)}, u32[]{:S(2)}) collective-permute-start(bf16[1,45,264]{2,1,0:T(8,128)(2,1)S(1)} %get-tuple-element.23), channel_id=1, source_target_pairs={{4,0},{8,4},{12,8},{16,12},{20,16},{24,20},{28,24},{5,1},{9,5},{13... | collective-permute-start | bytes 71288 | tf_op jit(solution)/shard_map/ppermute | solution.py:21
  7.0 8.0 %copy-start.6 = (bf16[8,4,32,32]{3,2,1,0:T(8,128)(2,1)S(1)}, bf16[8,4,32,32]{3,2,1,0:T(8,128)(2,1)}, u32[]{:S(2)}) copy-start(bf16[8,4,32,32]{3,2,1,0:T(8,128)(2,1)} %param.10) | copy-start | bytes 196612
  11.2 9.8 %collective-permute-start.2 = (bf16[26,8,264]{2,1,0:T(8,128)(2,1)}, bf16[26,8,264]{2,1,0:T(8,128)(2,1)S(1)}, u32[]{:S(2)}, u32[]{:S(2)}) collective-permute-start(bf16[26,8,264]{2,1,0:T(8,128)(2,1)} %get-tuple-element.20), channel_id=1, source_target_pairs={{0,1},{1,2},{2,3},{3,0},{4,5},{5,6},{6,7},{7,4},{8,9},{9,10},{10,1... | collective-permute-start | bytes 329480 | tf_op jit(solution)/shard_map/ppermute | solution.py:18
  12.7 10.4 %collective-permute-start.3 = (bf16[26,8,264]{2,1,0:T(8,128)(2,1)}, bf16[26,8,264]{2,1,0:T(8,128)(2,1)}, u32[]{:S(2)}, u32[]{:S(2)}) collective-permute-start(bf16[26,8,264]{2,1,0:T(8,128)(2,1)} %get-tuple-element.21), channel_id=1, source_target_pairs={{1,0},{2,1},{3,2},{0,3},{5,4},{6,5},{7,6},{4,7},{9,8},{10,9},{11,1... | collective-permute-start | bytes 329480 | tf_op jit(solution)/shard_map/ppermute | solution.py:21
  19.7 3.4 %copy-start.4 = (bf16[24,45,8]{2,1,0:T(8,128)(2,1)S(1)}, bf16[24,45,8]{2,1,0:T(8,128)(2,1)}, u32[]{:S(2)}) copy-start(bf16[24,45,8]{2,1,0:T(8,128)(2,1)} %copy-done.3) | copy-start | bytes 51844
  43.2 1.4 %collective-permute-start.4 = (f32[4,32,256]{2,1,0:T(8,128)S(1)}, f32[4,32,256]{2,1,0:T(8,128)S(1)}, u32[]{:S(2)}, u32[]{:S(2)}) collective-permute-start(f32[4,32,256]{2,1,0:T(8,128)S(1)} %get-tuple-element.8), channel_id=1, source_target_pairs={{0,4},{4,0},{8,12},{12,8},{16,20},{20,16},{24,28},{28,24},{1,5},{5... | collective-permute-start | bytes 393224 | tf_op jit(solution)/shard_map/ppermute | solution.py:192
  44.7 13.3 %collective-permute-start.9 = (f32[4,32,256]{2,1,0:T(8,128)S(1)}, f32[4,32,256]{2,1,0:T(8,128)S(1)}, u32[]{:S(2)}, u32[]{:S(2)}) collective-permute-start(f32[4,32,256]{2,1,0:T(8,128)S(1)} %add.58), channel_id=1, source_target_pairs={{0,8},{4,12},{8,0},{12,4},{16,24},{20,28},{24,16},{28,20},{1,9},{5... | collective-permute-start | bytes 393224 | tf_op jit(solution)/shard_map/ppermute | solution.py:49
  54.9 7.1 %collective-permute-start.5 = (f32[1,61,256]{2,1,0:T(8,128)S(1)}, f32[1,61,256]{2,1,0:T(8,128)S(1)}, u32[]{:S(2)}, u32[]{:S(2)}) collective-permute-start(f32[1,61,256]{2,1,0:T(8,128)S(1)} %get-tuple-element.18), channel_id=1, source_target_pairs={{0,4},{4,8},{8,12},{12,16},{16,20},{20,24},{24,28},{1,5},{5,9},{9,... | collective-permute-start | bytes 187400 | tf_op jit(solution)/shard_map/ppermute | solution.py:29
  56.7 5.4 %collective-permute-start.6 = (f32[1,61,256]{2,1,0:T(8,128)S(1)}, f32[1,61,256]{2,1,0:T(8,128)S(1)}, u32[]{:S(2)}, u32[]{:S(2)}) collective-permute-start(f32[1,61,256]{2,1,0:T(8,128)S(1)} %get-tuple-element.19), channel_id=1, source_target_pairs={{4,0},{8,4},{12,8},{16,12},{20,16},{24,20},{28,24},{5,1},{9,5},{13... | collective-permute-start | bytes 187400 | tf_op jit(solution)/shard_map/ppermute | solution.py:29
  58.0 7.2 %collective-permute-start.10 = (f32[4,32,256]{2,1,0:T(8,128)S(1)}, f32[4,32,256]{2,1,0:T(8,128)S(1)}, u32[]{:S(2)}, u32[]{:S(2)}) collective-permute-start(f32[4,32,256]{2,1,0:T(8,128)S(1)} %add.59), channel_id=1, source_target_pairs={{0,16},{4,20},{8,24},{12,28},{16,0},{20,4},{24,8},{28,12},{1,17},{... | collective-permute-start | bytes 393224 | tf_op jit(solution)/shard_map/ppermute | solution.py:49
  62.2 13.8 %copy-start.2 = (bf16[24,45,256]{2,1,0:T(8,128)(2,1)S(1)}, bf16[24,45,256]{2,1,0:T(8,128)(2,1)}, u32[]{:S(2)}) copy-start(bf16[24,45,256]{2,1,0:T(8,128)(2,1)} %copy-done.1) | copy-start | bytes 1658884
  62.2 13.7 %collective-permute-start.8 = (f32[24,8,256]{2,1,0:T(8,128)S(1)}, f32[24,8,256]{2,1,0:T(8,128)S(1)}, u32[]{:S(2)}, u32[]{:S(2)}) collective-permute-start(f32[24,8,256]{2,1,0:T(8,128)S(1)} %slice.60), channel_id=1, source_target_pairs={{0,1},{1,2},{2,3},{3,0},{4,5},{5,6},{6,7},{7,4},{8,9},{9,10},{10,1... | collective-permute-start | bytes 589832 | tf_op jit(solution)/shard_map/ppermute | solution.py:34
  65.2 9.1 %collective-permute-start.11 = (f32[4,32,256]{2,1,0:T(8,128)S(1)}, f32[4,32,256]{2,1,0:T(8,128)S(1)}, u32[]{:S(2)}, u32[]{:S(2)}) collective-permute-start(f32[4,32,256]{2,1,0:T(8,128)S(1)} %add.60), channel_id=1, source_target_pairs={{0,1},{1,0},{2,3},{3,2},{4,5},{5,4},{6,7},{7,6},{8,9},{9,8},{10,11... | collective-permute-start | bytes 393224 | tf_op jit(solution)/shard_map/ppermute | solution.py:49
  66.4 9.5 %collective-permute-start.7 = (bf16[24,8,256]{2,1,0:T(8,128)(2,1)S(1)}, bf16[24,8,256]{2,1,0:T(8,128)(2,1)S(1)}, u32[]{:S(2)}, u32[]{:S(2)}) collective-permute-start(bf16[24,8,256]{2,1,0:T(8,128)(2,1)S(1)} %slice.72), channel_id=1, source_target_pairs={{0,3},{1,0},{2,1},{3,2},{4,7},{5,4},{6,5},{7,6},{8,11},{9,8},{10,9... | collective-permute-start | bytes 294920 | tf_op jit(solution)/shard_map/ppermute | solution.py:34
  74.3 7.7 %collective-permute-start.12 = (f32[4,32,256]{2,1,0:T(8,128)S(1)}, f32[4,32,256]{2,1,0:T(8,128)S(1)}, u32[]{:S(2)}, u32[]{:S(2)}) collective-permute-start(f32[4,32,256]{2,1,0:T(8,128)S(1)} %add.61), channel_id=1, source_target_pairs={{0,2},{1,3},{2,0},{3,1},{4,6},{5,7},{6,4},{7,5},{8,10},{9,11},{10,... | collective-permute-start | bytes 393224 | tf_op jit(solution)/shard_map/ppermute | solution.py:49

commit v8 on v7

--- a/solution.py
+++ b/solution.py
@@ -52,12 +52,11 @@
     return value
 
 
-def forward_kernel(x_ref, m_ref, t_ref, cot_ref, w_ref, inf_ref, wg_ref, pulled_ref, acc_ref):
+def forward_kernel(x_ref, m_ref, t_ref, cot_ref, w_ref, inf_ref, wg_ref, pulled_ref, scaled_ref):
     rows, basis_count, lat_taps, col_pad, lane_rows = t_ref.shape
     col_count = inf_ref.shape[1]
     chan_count = w_ref.shape[1]
     group_width = wg_ref.shape[1]
-    acc_ref[...] = jnp.zeros_like(acc_ref)
 
     def body(i, carry):
         numerator = None
@@ -76,9 +75,7 @@
         for b in range(basis_count):
             part = scaled[b * col_pad : (b + 1) * col_pad]
             out = out + jnp.dot(part, w_ref[b], preferred_element_type=jnp.float32)
-            acc_ref[b] += lax.dot_general(
-                part, upstream, (((0,), (0,)), ((), ())), preferred_element_type=jnp.float32
-            )
+            scaled_ref[b, pl.ds(pl.multiple_of(i * col_pad, col_pad), col_pad), :] = part
             back = lax.dot_general(
                 upstream, w_ref[b], (((1,), (1,)), ((), ())), preferred_element_type=jnp.float32
             )
@@ -90,10 +87,14 @@
 
     lax.fori_loop(0, rows, body, 0)
     lane = lax.broadcasted_iota(jnp.int32, (group_width, chan_count), 1) // group_width
+    upstream_all = cot_ref[...].reshape(rows * col_pad, chan_count)
     for b in range(basis_count):
+        grad = lax.dot_general(
+            scaled_ref[b], upstream_all, (((0,), (0,)), ((), ())), preferred_element_type=jnp.float32
+        )
         total = jnp.zeros((group_width, chan_count), jnp.float32)
         for g in range(chan_count // group_width):
-            block = acc_ref[b, g * group_width : (g + 1) * group_width, :]
+            block = grad[g * group_width : (g + 1) * group_width, :]
             total = total + jnp.where(lane == g, block, 0.0)
         wg_ref[b] = total
 
@@ -177,7 +178,7 @@
         ),
         in_specs=[vmem] * 5,
         out_specs=[vmem] * 3,
-        scratch_shapes=[pltpu.VMEM((basis_count, chan_count, chan_count), jnp.float32)],
+        scratch_shapes=[pltpu.VMEM((basis_count, row_count * col_pad, chan_count), jnp.bfloat16)],
         compiler_params=params,
         cost_estimate=pl.CostEstimate(
             flops=2 * row_count * basis_count * col_pad * chan_count * (6 * lane_rows + 3 * chan_count),

time: 83.4 us -> 81.8 us (0.981)
  Pallas kernels: 25.8 us -> 24.2 us
    pallas_call x1, Pallas kernels: 18.4 us -> 16.8 us  [local(): pl.pallas_call(forward_kernel, out_shape=(jax.ShapeDtypeStruct((row_count...]
where the time goes in v8:
time: 81.8 us; the launch traced here: 81.5 us
  Pallas kernels  24.2 us (30%)
  starting transfers between devices  22.6 us (28%)
  waiting for transfers between devices  18 us (22%)
  local copies, waits for them, and re-layouts  9.48 us (12%)
  other arithmetic  4.34 us (5%)
  matrix products  1.86 us (2%)
  between operations  1.01 us (1%)
    pallas_call x1, Pallas kernels, local(): pl.pallas_call(forward_kernel, out_shape=(jax.ShapeDtypeStruct((row_count...  16.8 us
    ppermute x4, waiting for transfers between devices, butterfly_sum(): partner = lax.ppermute(value, axis, [(i, i ^ step) for i in range(count)])  11.9 us
    ppermute x4, starting transfers between devices, butterfly_sum(): partner = lax.ppermute(value, axis, [(i, i ^ step) for i in range(count)])  9.06 us
    pallas_call x1, Pallas kernels, local(): pl.pallas_call(adjoint_kernel, out_shape=jax.ShapeDtypeStruct(((row_count...  7.42 us
    ppermute x2, waiting for transfers between devices, with_halo(): lax.ppermute(lax.slice_in_dim(block, 0, width, axis=dim), axis, backward)  4.3 us
    ppermute x2, starting transfers between devices, with_halo(): lax.ppermute(lax.slice_in_dim(block, block.shape[dim] - width, None, axis...  3.98 us
    ppermute x2, starting transfers between devices, with_halo(): lax.ppermute(lax.slice_in_dim(block, 0, width, axis=dim), axis, backward)  3.54 us
    unnamed x20, local copies, waits for them, and re-layouts  3.37 us
  transfers between devices with their start and end apart: 13, of which 7 were waited for; matrix products, arithmetic and copies ran while one was open for 12% of the time, Pallas kernels for 9%

profile of v8, /device:TPU:0, one launch (start us, length us, event | category | flops | bytes accessed | tf_op | source)
XLA Modules:
  0.0 81.5 jit_solution(5219358341740547535)
XLA Ops:
  0.6 0.0 copy-start
  0.6 0.0 copy-start.5
  0.7 1.0 %convert_element_type.46 = bf16[24,45,8]{1,2,0:T(8,128)(2,1)S(1)} convert(s32[24,45,8]{1,2,0:T(8,128)} %param.7) | non-fusion elementwise | flops 8640 | bytes 51840 | tf_op jit(solution)/shard_map/convert_element_type | solution.py:130
  1.6 0.2 copy.35
  1.9 0.1 reshape.114
  2.0 0.4 fusion.6
  2.4 0.2 reshape.115
  2.6 0.0 copy-done.5
  2.6 0.0 copy-start.1
  2.6 0.0 copy-start.7
  2.6 0.1 copy_multiply_fusion
  2.8 2.4 %collective-permute-start = (bf16[1,45,264]{2,1,0:T(8,128)(2,1)S(1)}, bf16[1,45,264]{2,1,0:T(8,128)(2,1)S(1)}, u32[]{:S(2)}, u32[]{:S(2)}) collective-permute-start(bf16[1,45,264]{2,1,0:T(8,128)(2,1)S(1)} %get-tuple-element.22), channel_id=1, source_target_pairs={{0,4},{4,8},{8,12},{12,16},{16,20},{20,24},{24,28},{1,5},{5,9},{9,... | collective-permute-start | bytes 71288 | tf_op jit(solution)/shard_map/ppermute | solution.py:18
  5.2 1.3 %collective-permute-start.1 = (bf16[1,45,264]{2,1,0:T(8,128)(2,1)S(1)}, bf16[1,45,264]{2,1,0:T(8,128)(2,1)S(1)}, u32[]{:S(2)}, u32[]{:S(2)}) collective-permute-start(bf16[1,45,264]{2,1,0:T(8,128)(2,1)S(1)} %get-tuple-element.23), channel_id=1, source_target_pairs={{4,0},{8,4},{12,8},{16,12},{20,16},{24,20},{28,24},{5,1},{9,5},{13... | collective-permute-start | bytes 71288 | tf_op jit(solution)/shard_map/ppermute | solution.py:21
  6.5 0.0 copy-done
  6.5 0.1 constant_dynamic-slice_fusion
  6.6 0.2 copy.48
  6.8 0.0 copy-done.7
  6.8 0.1 compare_convert_fusion
  6.9 0.1 copy.37
  7.0 0.0 copy-start.6
  7.0 1.1 %fusion.18 = bf16[24,4,3,48,64]{4,0,3,2,1:T(8,128)(2,1)S(1)} fusion(s32[48,64]{1,0:T(8,128)S(1)} %iota_subtract_fusion, pred[48]{0:T(512)(128)(4,1)S(1)} %iota_compare_fusion.6, bf16[24,4,3,17]{3,0,2,1:T(8,128)(2,1)S(1)} %copy.48, bf16[24,17]{1,0:T(8,128)(2,1)S(1)} %constant_dynamic-slice_fusion.1), kind=kOutput, calls=%fused_computation.27 | convolution fusion | flops 30205056 | bytes 1792416 | tf_op jit(solution)/shard_map/ibae,ejp->ibajp/dot_general | solution.py:162
  8.2 0.0 copy-done.1
  8.2 0.0 collective-permute-done
  8.2 2.2 %collective-permute-done.1 = bf16[1,45,264]{2,1,0:T(8,128)(2,1)S(1)} collective-permute-done((bf16[1,45,264]{2,1,0:T(8,128)(2,1)S(1)}, bf16[1,45,264]{2,1,0:T(8,128)(2,1)S(1)}, u32[]{:S(2)}, u32[]{:S(2)}) %collective-permute-start.1) | collective-permute-done | bytes 23792 | tf_op jit(solution)/shard_map/ppermute | solution.py:21
  10.4 0.8 pad_maximum_fusion.3
  11.2 1.6 %collective-permute-start.2 = (bf16[26,8,264]{2,1,0:T(8,128)(2,1)}, bf16[26,8,264]{2,1,0:T(8,128)(2,1)S(1)}, u32[]{:S(2)}, u32[]{:S(2)}) collective-permute-start(bf16[26,8,264]{2,1,0:T(8,128)(2,1)} %get-tuple-element.20), channel_id=1, source_target_pairs={{0,1},{1,2},{2,3},{3,0},{4,5},{5,6},{6,7},{7,4},{8,9},{9,10},{10,1... | collective-permute-start | bytes 329480 | tf_op jit(solution)/shard_map/ppermute | solution.py:18
  12.7 2.2 %collective-permute-start.3 = (bf16[26,8,264]{2,1,0:T(8,128)(2,1)}, bf16[26,8,264]{2,1,0:T(8,128)(2,1)}, u32[]{:S(2)}, u32[]{:S(2)}) collective-permute-start(bf16[26,8,264]{2,1,0:T(8,128)(2,1)} %get-tuple-element.21), channel_id=1, source_target_pairs={{1,0},{2,1},{3,2},{0,3},{5,4},{6,5},{7,6},{4,7},{9,8},{10,9},{11,1... | collective-permute-start | bytes 329480 | tf_op jit(solution)/shard_map/ppermute | solution.py:21
  15.0 0.7 multiply_bitcast_fusion
  15.7 2.6 %copy.52.t_ref = bf16[24,4,3,48,64]{4,3,2,1,0:T(8,128)(2,1)} copy(bf16[24,4,3,48,64]{4,0,3,2,1:T(8,128)(2,1)S(1)} %fusion.18) | data formatting | bytes 3538944 | tf_op jit(solution)/shard_map/ibae,ejp->ibajp/dot_general | solution.py:162
  18.3 1.4 %reshape.118.w_ref = bf16[4,256,256]{2,1,0:T(8,128)(2,1)S(1)} reshape(bf16[4,8,32,8,32]{4,3,2,1,0:T(8,128)(2,1)S(1)} %multiply_bitcast_fusion) | data formatting | bytes 1048576 | tf_op jit(solution)/shard_map/reshape | solution.py:167
  19.7 0.0 copy-start.4
  19.7 1.2 %copy.40 = bf16[24,45,256]{2,1,0:T(8,128)(2,1)S(1)} copy(bf16[24,45,256]{2,0,1:T(8,128)(2,1)} %param.11) | data formatting | bytes 1105920 | tf_op args[5]
  21.0 0.0 collective-permute-done.2
  21.0 2.1 %collective-permute-done.3 = bf16[26,8,264]{2,1,0:T(8,128)(2,1)} collective-permute-done((bf16[26,8,264]{2,1,0:T(8,128)(2,1)}, bf16[26,8,264]{2,1,0:T(8,128)(2,1)}, u32[]{:S(2)}, u32[]{:S(2)}) %collective-permute-start.3) | collective-permute-done | bytes 109856 | tf_op jit(solution)/shard_map/ppermute | solution.py:21
  23.1 1.2 %fusion.9 = bf16[26,64,264]{2,1,0:T(8,128)(2,1)S(1)} fusion(bf16[26,8,264]{2,1,0:T(8,128)(2,1)} %collective-permute-done.3, bf16[26,8,264]{2,1,0:T(8,128)(2,1)S(1)} %collective-permute-done.2, bf16[1,45,264]{2,1,0:T(8,128)(2,1)S(1)} %collective-permute-done.1, bf16[1,45,264]{2,1,0:T(8,128)(2,1)S(1)} %collective-permute-done, ...), kind=kLoop, calls=%fused_computation.15 | loop fusion | flops 8346624 | bytes 1716000 | tf_op jit(solution)/shard_map/concatenate | solution.py:22
  24.4 0.1 slice.54
  24.4 0.1 slice.53
  24.5 0.4 convolution_convert_fusion.m_ref
  24.9 16.8 %shard_map.85 = (bf16[24,45,256]{2,1,0:T(8,128)(2,1)S(1)}, f32[4,32,256]{2,1,0:T(8,128)S(1)}, bf16[24,192,256]{2,1,0:T(8,128)(2,1)S(1)}) custom-call(bf16[1664,256]{1,0:T(8,128)(2,1)S(1)} %bitcast.28, bf16[1664,256]{1,0:T(8,128)(2,1)S(1)} %convolution_convert_fusion.m_ref, bf16[24,4,3,48,64]{4,3,2,1,0:T(8,128)(2,1)} %copy.52.t_ref, ...), custom_call_target="tpu_custom_call" | custom-call | flops 2717908992 | bytes 3407872 | tf_op jit(solution)/shard_map/pallas_call | solution.py:172
  41.7 0.2 collective-permute-start.4
  41.9 1.2 %collective-permute-done.4.order_ref = f32[4,32,256]{2,1,0:T(8,128)S(1)} collective-permute-done((f32[4,32,256]{2,1,0:T(8,128)S(1)}, f32[4,32,256]{2,1,0:T(8,128)S(1)}, u32[]{:S(2)}, u32[]{:S(2)}) %collective-permute-start.4) | collective-permute-done | bytes 131104 | tf_op jit(solution)/shard_map/ppermute | solution.py:193
  43.1 2.8 %collective-permute-start.9 = (f32[4,32,256]{2,1,0:T(8,128)S(1)}, f32[4,32,256]{2,1,0:T(8,128)S(1)}, u32[]{:S(2)}, u32[]{:S(2)}) collective-permute-start(f32[4,32,256]{2,1,0:T(8,128)S(1)} %add.58), channel_id=1, source_target_pairs={{0,8},{4,12},{8,0},{12,4},{16,24},{20,28},{24,16},{28,20},{1,9},{5... | collective-permute-start | bytes 393224 | tf_op jit(solution)/shard_map/ppermute | solution.py:49
  45.9 7.4 %shard_map.86 = f32[1664,256]{1,0:T(8,128)S(1)} custom-call(bf16[24,4,3,48,64]{4,3,2,1,0:T(8,128)(2,1)} %copy.52.t_ref, bf16[24,192,256]{2,1,0:T(8,128)(2,1)S(1)} %get-tuple-element.7.pulled_ref, f32[4,32,256]{2,1,0:T(8,128)S(1)} %collective-permute-done.4.order_ref), custom_call_target="tpu_custom_call" | custom-call | flops 452984832 | bytes 2555904 | tf_op jit(solution)/shard_map/pallas_call | solution.py:201
  53.3 1.8 %collective-permute-start.5 = (f32[1,61,256]{2,1,0:T(8,128)S(1)}, f32[1,61,256]{2,1,0:T(8,128)S(1)}, u32[]{:S(2)}, u32[]{:S(2)}) collective-permute-start(f32[1,61,256]{2,1,0:T(8,128)S(1)} %get-tuple-element.18), channel_id=1, source_target_pairs={{0,4},{4,8},{8,12},{12,16},{16,20},{20,24},{24,28},{1,5},{5,9},{9,... | collective-permute-start | bytes 187400 | tf_op jit(solution)/shard_map/ppermute | solution.py:29
  55.1 1.3 %collective-permute-start.6 = (f32[1,61,256]{2,1,0:T(8,128)S(1)}, f32[1,61,256]{2,1,0:T(8,128)S(1)}, u32[]{:S(2)}, u32[]{:S(2)}) collective-permute-start(f32[1,61,256]{2,1,0:T(8,128)S(1)} %get-tuple-element.19), channel_id=1, source_target_pairs={{4,0},{8,4},{12,8},{16,12},{20,16},{24,20},{28,24},{5,1},{9,5},{13... | collective-permute-start | bytes 187400 | tf_op jit(solution)/shard_map/ppermute | solution.py:29
  56.4 0.0 collective-permute-done.9
  56.5 4.0 %collective-permute-start.10 = (f32[4,32,256]{2,1,0:T(8,128)S(1)}, f32[4,32,256]{2,1,0:T(8,128)S(1)}, u32[]{:S(2)}, u32[]{:S(2)}) collective-permute-start(f32[4,32,256]{2,1,0:T(8,128)S(1)} %add.59), channel_id=1, source_target_pairs={{0,16},{4,20},{8,24},{12,28},{16,0},{20,4},{24,8},{28,12},{1,17},{... | collective-permute-start | bytes 393224 | tf_op jit(solution)/shard_map/ppermute | solution.py:49
  60.5 0.0 collective-permute-done.5
  60.5 0.0 collective-permute-done.6
  60.5 0.1 fusion.7
  60.7 1.2 %collective-permute-start.8 = (f32[24,8,256]{2,1,0:T(8,128)S(1)}, f32[24,8,256]{2,1,0:T(8,128)S(1)}, u32[]{:S(2)}, u32[]{:S(2)}) collective-permute-start(f32[24,8,256]{2,1,0:T(8,128)S(1)} %slice.60), channel_id=1, source_target_pairs={{0,1},{1,2},{2,3},{3,0},{4,5},{5,6},{6,7},{7,4},{8,9},{9,10},{10,1... | collective-permute-start | bytes 589832 | tf_op jit(solution)/shard_map/ppermute | solution.py:34
  61.8 1.8 %collective-permute-done.10 = f32[4,32,256]{2,1,0:T(8,128)S(1)} collective-permute-done((f32[4,32,256]{2,1,0:T(8,128)S(1)}, f32[4,32,256]{2,1,0:T(8,128)S(1)}, u32[]{:S(2)}, u32[]{:S(2)}) %collective-permute-start.10) | collective-permute-done | bytes 131104 | tf_op jit(solution)/shard_map/ppermute | solution.py:49
  63.7 1.2 %collective-permute-start.11 = (f32[4,32,256]{2,1,0:T(8,128)S(1)}, f32[4,32,256]{2,1,0:T(8,128)S(1)}, u32[]{:S(2)}, u32[]{:S(2)}) collective-permute-start(f32[4,32,256]{2,1,0:T(8,128)S(1)} %add.60), channel_id=1, source_target_pairs={{0,1},{1,0},{2,3},{3,2},{4,5},{5,4},{6,7},{7,6},{8,9},{9,8},{10,11... | collective-permute-start | bytes 393224 | tf_op jit(solution)/shard_map/ppermute | solution.py:49
  64.9 1.6 %collective-permute-start.7 = (bf16[24,8,256]{2,1,0:T(8,128)(2,1)S(1)}, bf16[24,8,256]{2,1,0:T(8,128)(2,1)S(1)}, u32[]{:S(2)}, u32[]{:S(2)}) collective-permute-start(bf16[24,8,256]{2,1,0:T(8,128)(2,1)S(1)} %slice.72), channel_id=1, source_target_pairs={{0,3},{1,0},{2,1},{3,2},{4,7},{5,4},{6,5},{7,6},{8,11},{9,8},{10,9... | collective-permute-start | bytes 294920 | tf_op jit(solution)/shard_map/ppermute | solution.py:34
  66.4 1.0 %copy.43 = bf16[24,45,256]{2,0,1:T(8,128)(2,1)} copy(bf16[24,45,256]{2,1,0:T(8,128)(2,1)S(1)} %get-tuple-element.15) | data formatting | bytes 1105920
  67.4 5.3 %collective-permute-done.11 = f32[4,32,256]{2,1,0:T(8,128)S(1)} collective-permute-done((f32[4,32,256]{2,1,0:T(8,128)S(1)}, f32[4,32,256]{2,1,0:T(8,128)S(1)}, u32[]{:S(2)}, u32[]{:S(2)}) %collective-permute-start.11) | collective-permute-done | bytes 131104 | tf_op jit(solution)/shard_map/ppermute | solution.py:49
  72.7 1.1 %collective-permute-start.12 = (f32[4,32,256]{2,1,0:T(8,128)S(1)}, f32[4,32,256]{2,1,0:T(8,128)S(1)}, u32[]{:S(2)}, u32[]{:S(2)}) collective-permute-start(f32[4,32,256]{2,1,0:T(8,128)S(1)} %add.61), channel_id=1, source_target_pairs={{0,2},{1,3},{2,0},{3,1},{4,6},{5,7},{6,4},{7,5},{8,10},{9,11},{10,... | collective-permute-start | bytes 393224 | tf_op jit(solution)/shard_map/ppermute | solution.py:49
  73.8 0.6 collective-permute-done.7
  74.4 0.0 collective-permute-done.8
  74.4 0.2 fusion.15
  74.6 1.0 %copy.44 = bf16[24,45,256]{2,0,1:T(8,128)(2,1)} copy(bf16[24,45,256]{2,1,0:T(8,128)(2,1)S(1)} %fusion.15) | data formatting | bytes 1105920
  75.6 4.8 %collective-permute-done.12 = f32[4,32,256]{2,1,0:T(8,128)S(1)} collective-permute-done((f32[4,32,256]{2,1,0:T(8,128)S(1)}, f32[4,32,256]{2,1,0:T(8,128)S(1)}, u32[]{:S(2)}, u32[]{:S(2)}) %collective-permute-start.12) | collective-permute-done | bytes 131104 | tf_op jit(solution)/shard_map/ppermute | solution.py:49
  80.4 0.2 reshape.120
  80.6 0.9 %copy.55 = f32[4,32,8,32]{3,1,0,2:T(8,128)} copy(f32[4,32,8,32]{3,2,1,0:T(8,128)S(1)} %reshape.120) | data formatting | bytes 262144 | tf_op jit(solution)/shard_map/reshape | solution.py:199
  (23 shorter events, 0.3 us)
Async XLA Ops:
  0.6 5.9 %copy-start = (bf16[192,4,3,17]{0,1,3,2:T(4,128)(2,1)S(1)}, bf16[192,4,3,17]{0,1,3,2:T(4,128)(2,1)}, u32[]{:S(2)}) copy-start(bf16[192,4,3,17]{0,1,3,2:T(4,128)(2,1)} %param.8) | copy-start | bytes 235012
  0.6 1.9 %copy-start.5 = (bf16[24,45,256]{2,0,1:T(8,128)(2,1)S(1)}, bf16[24,45,256]{2,0,1:T(8,128)(2,1)}, u32[]{:S(2)}) copy-start(bf16[24,45,256]{2,0,1:T(8,128)(2,1)} %param.6) | copy-start | bytes 1658884
  1.9 8.5 %copy-start.3 = (bf16[24,45,8]{2,1,0:T(8,128)(2,1)}, bf16[24,45,8]{2,1,0:T(8,128)(2,1)S(1)}, u32[]{:S(2)}) copy-start(bf16[24,45,8]{2,1,0:T(8,128)(2,1)S(1)} %copy.35) | copy-start | bytes 51844
  2.6 5.6 %copy-start.1 = (bf16[24,45,256]{2,1,0:T(8,128)(2,1)}, bf16[24,45,256]{2,1,0:T(8,128)(2,1)S(1)}, u32[]{:S(2)}) copy-start(bf16[24,45,256]{2,1,0:T(8,128)(2,1)S(1)} %reshape.115) | copy-start | bytes 1658884
  2.6 4.2 %copy-start.7 = (s32[192]{0:T(256)S(1)}, s32[192]{0:T(256)}, u32[]{:S(2)}) copy-start(s32[192]{0:T(256)} %param.9) | copy-start | bytes 2308
  2.8 5.4 %collective-permute-start = (bf16[1,45,264]{2,1,0:T(8,128)(2,1)S(1)}, bf16[1,45,264]{2,1,0:T(8,128)(2,1)S(1)}, u32[]{:S(2)}, u32[]{:S(2)}) collective-permute-start(bf16[1,45,264]{2,1,0:T(8,128)(2,1)S(1)} %get-tuple-element.22), channel_id=1, source_target_pairs={{0,4},{4,8},{8,12},{12,16},{16,20},{20,24},{24,28},{1,5},{5,9},{9,... | collective-permute-start | bytes 71288 | tf_op jit(solution)/shard_map/ppermute | solution.py:18
  5.2 5.2 %collective-permute-start.1 = (bf16[1,45,264]{2,1,0:T(8,128)(2,1)S(1)}, bf16[1,45,264]{2,1,0:T(8,128)(2,1)S(1)}, u32[]{:S(2)}, u32[]{:S(2)}) collective-permute-start(bf16[1,45,264]{2,1,0:T(8,128)(2,1)S(1)} %get-tuple-element.23), channel_id=1, source_target_pairs={{4,0},{8,4},{12,8},{16,12},{20,16},{24,20},{28,24},{5,1},{9,5},{13... | collective-permute-start | bytes 71288 | tf_op jit(solution)/shard_map/ppermute | solution.py:21
  7.0 8.0 %copy-start.6 = (bf16[8,4,32,32]{3,2,1,0:T(8,128)(2,1)S(1)}, bf16[8,4,32,32]{3,2,1,0:T(8,128)(2,1)}, u32[]{:S(2)}) copy-start(bf16[8,4,32,32]{3,2,1,0:T(8,128)(2,1)} %param.10) | copy-start | bytes 196612
  11.2 9.8 %collective-permute-start.2 = (bf16[26,8,264]{2,1,0:T(8,128)(2,1)}, bf16[26,8,264]{2,1,0:T(8,128)(2,1)S(1)}, u32[]{:S(2)}, u32[]{:S(2)}) collective-permute-start(bf16[26,8,264]{2,1,0:T(8,128)(2,1)} %get-tuple-element.20), channel_id=1, source_target_pairs={{0,1},{1,2},{2,3},{3,0},{4,5},{5,6},{6,7},{7,4},{8,9},{9,10},{10,1... | collective-permute-start | bytes 329480 | tf_op jit(solution)/shard_map/ppermute | solution.py:18
  12.7 10.4 %collective-permute-start.3 = (bf16[26,8,264]{2,1,0:T(8,128)(2,1)}, bf16[26,8,264]{2,1,0:T(8,128)(2,1)}, u32[]{:S(2)}, u32[]{:S(2)}) collective-permute-start(bf16[26,8,264]{2,1,0:T(8,128)(2,1)} %get-tuple-element.21), channel_id=1, source_target_pairs={{1,0},{2,1},{3,2},{0,3},{5,4},{6,5},{7,6},{4,7},{9,8},{10,9},{11,1... | collective-permute-start | bytes 329480 | tf_op jit(solution)/shard_map/ppermute | solution.py:21
  19.7 3.4 %copy-start.4 = (bf16[24,45,8]{2,1,0:T(8,128)(2,1)S(1)}, bf16[24,45,8]{2,1,0:T(8,128)(2,1)}, u32[]{:S(2)}) copy-start(bf16[24,45,8]{2,1,0:T(8,128)(2,1)} %copy-done.3) | copy-start | bytes 51844
  41.7 1.4 %collective-permute-start.4 = (f32[4,32,256]{2,1,0:T(8,128)S(1)}, f32[4,32,256]{2,1,0:T(8,128)S(1)}, u32[]{:S(2)}, u32[]{:S(2)}) collective-permute-start(f32[4,32,256]{2,1,0:T(8,128)S(1)} %get-tuple-element.8), channel_id=1, source_target_pairs={{0,4},{4,0},{8,12},{12,8},{16,20},{20,16},{24,28},{28,24},{1,5},{5... | collective-permute-start | bytes 393224 | tf_op jit(solution)/shard_map/ppermute | solution.py:193
  43.1 13.3 %collective-permute-start.9 = (f32[4,32,256]{2,1,0:T(8,128)S(1)}, f32[4,32,256]{2,1,0:T(8,128)S(1)}, u32[]{:S(2)}, u32[]{:S(2)}) collective-permute-start(f32[4,32,256]{2,1,0:T(8,128)S(1)} %add.58), channel_id=1, source_target_pairs={{0,8},{4,12},{8,0},{12,4},{16,24},{20,28},{24,16},{28,20},{1,9},{5... | collective-permute-start | bytes 393224 | tf_op jit(solution)/shard_map/ppermute | solution.py:49
  53.3 7.2 %collective-permute-start.5 = (f32[1,61,256]{2,1,0:T(8,128)S(1)}, f32[1,61,256]{2,1,0:T(8,128)S(1)}, u32[]{:S(2)}, u32[]{:S(2)}) collective-permute-start(f32[1,61,256]{2,1,0:T(8,128)S(1)} %get-tuple-element.18), channel_id=1, source_target_pairs={{0,4},{4,8},{8,12},{12,16},{16,20},{20,24},{24,28},{1,5},{5,9},{9,... | collective-permute-start | bytes 187400 | tf_op jit(solution)/shard_map/ppermute | solution.py:29
  55.1 5.4 %collective-permute-start.6 = (f32[1,61,256]{2,1,0:T(8,128)S(1)}, f32[1,61,256]{2,1,0:T(8,128)S(1)}, u32[]{:S(2)}, u32[]{:S(2)}) collective-permute-start(f32[1,61,256]{2,1,0:T(8,128)S(1)} %get-tuple-element.19), channel_id=1, source_target_pairs={{4,0},{8,4},{12,8},{16,12},{20,16},{24,20},{28,24},{5,1},{9,5},{13... | collective-permute-start | bytes 187400 | tf_op jit(solution)/shard_map/ppermute | solution.py:29
  56.5 7.2 %collective-permute-start.10 = (f32[4,32,256]{2,1,0:T(8,128)S(1)}, f32[4,32,256]{2,1,0:T(8,128)S(1)}, u32[]{:S(2)}, u32[]{:S(2)}) collective-permute-start(f32[4,32,256]{2,1,0:T(8,128)S(1)} %add.59), channel_id=1, source_target_pairs={{0,16},{4,20},{8,24},{12,28},{16,0},{20,4},{24,8},{28,12},{1,17},{... | collective-permute-start | bytes 393224 | tf_op jit(solution)/shard_map/ppermute | solution.py:49
  60.6 13.8 %copy-start.2 = (bf16[24,45,256]{2,1,0:T(8,128)(2,1)S(1)}, bf16[24,45,256]{2,1,0:T(8,128)(2,1)}, u32[]{:S(2)}) copy-start(bf16[24,45,256]{2,1,0:T(8,128)(2,1)} %copy-done.1) | copy-start | bytes 1658884
  60.7 13.7 %collective-permute-start.8 = (f32[24,8,256]{2,1,0:T(8,128)S(1)}, f32[24,8,256]{2,1,0:T(8,128)S(1)}, u32[]{:S(2)}, u32[]{:S(2)}) collective-permute-start(f32[24,8,256]{2,1,0:T(8,128)S(1)} %slice.60), channel_id=1, source_target_pairs={{0,1},{1,2},{2,3},{3,0},{4,5},{5,6},{6,7},{7,4},{8,9},{9,10},{10,1... | collective-permute-start | bytes 589832 | tf_op jit(solution)/shard_map/ppermute | solution.py:34
  63.7 9.0 %collective-permute-start.11 = (f32[4,32,256]{2,1,0:T(8,128)S(1)}, f32[4,32,256]{2,1,0:T(8,128)S(1)}, u32[]{:S(2)}, u32[]{:S(2)}) collective-permute-start(f32[4,32,256]{2,1,0:T(8,128)S(1)} %add.60), channel_id=1, source_target_pairs={{0,1},{1,0},{2,3},{3,2},{4,5},{5,4},{6,7},{7,6},{8,9},{9,8},{10,11... | collective-permute-start | bytes 393224 | tf_op jit(solution)/shard_map/ppermute | solution.py:49
  64.9 9.5 %collective-permute-start.7 = (bf16[24,8,256]{2,1,0:T(8,128)(2,1)S(1)}, bf16[24,8,256]{2,1,0:T(8,128)(2,1)S(1)}, u32[]{:S(2)}, u32[]{:S(2)}) collective-permute-start(bf16[24,8,256]{2,1,0:T(8,128)(2,1)S(1)} %slice.72), channel_id=1, source_target_pairs={{0,3},{1,0},{2,1},{3,2},{4,7},{5,4},{6,5},{7,6},{8,11},{9,8},{10,9... | collective-permute-start | bytes 294920 | tf_op jit(solution)/shard_map/ppermute | solution.py:34
  72.7 7.7 %collective-permute-start.12 = (f32[4,32,256]{2,1,0:T(8,128)S(1)}, f32[4,32,256]{2,1,0:T(8,128)S(1)}, u32[]{:S(2)}, u32[]{:S(2)}) collective-permute-start(f32[4,32,256]{2,1,0:T(8,128)S(1)} %add.61), channel_id=1, source_target_pairs={{0,2},{1,3},{2,0},{3,1},{4,6},{5,7},{6,4},{7,5},{8,10},{9,11},{10,... | collective-permute-start | bytes 393224 | tf_op jit(solution)/shard_map/ppermute | solution.py:49

commit v9 on v8

--- a/solution.py
+++ b/solution.py
@@ -52,7 +52,7 @@
     return value
 
 
-def forward_kernel(x_ref, m_ref, t_ref, cot_ref, w_ref, inf_ref, wg_ref, pulled_ref, scaled_ref):
+def forward_kernel(x_ref, m_ref, t_ref, cot_ref, w_ref, inf_ref, wg_ref, pulled_ref, scaled_ref, safe_ref):
     rows, basis_count, lat_taps, col_pad, lane_rows = t_ref.shape
     col_count = inf_ref.shape[1]
     chan_count = w_ref.shape[1]
@@ -70,33 +70,34 @@
             denominator = den if denominator is None else denominator + den
         safe = jnp.maximum(denominator, 1.0)
         scaled = (numerator / safe).astype(jnp.bfloat16)
-        upstream = cot_ref[i]
-        out = jnp.zeros((col_pad, chan_count), jnp.float32)
+        rows_at = pl.ds(pl.multiple_of(i * col_pad, col_pad), col_pad)
         for b in range(basis_count):
-            part = scaled[b * col_pad : (b + 1) * col_pad]
-            out = out + jnp.dot(part, w_ref[b], preferred_element_type=jnp.float32)
-            scaled_ref[b, pl.ds(pl.multiple_of(i * col_pad, col_pad), col_pad), :] = part
-            back = lax.dot_general(
-                upstream, w_ref[b], (((1,), (1,)), ((), ())), preferred_element_type=jnp.float32
-            )
-            pulled_ref[i, b * col_pad : (b + 1) * col_pad, :] = (
-                back / safe[b * col_pad : (b + 1) * col_pad]
-            ).astype(jnp.bfloat16)
-        inf_ref[i] = out[:col_count].astype(inf_ref.dtype)
+            scaled_ref[b, rows_at, :] = scaled[b * col_pad : (b + 1) * col_pad]
+            safe_ref[b, rows_at, :] = safe[b * col_pad : (b + 1) * col_pad]
         return carry
 
     lax.fori_loop(0, rows, body, 0)
     lane = lax.broadcasted_iota(jnp.int32, (group_width, chan_count), 1) // group_width
     upstream_all = cot_ref[...].reshape(rows * col_pad, chan_count)
+    out = None
     for b in range(basis_count):
+        part = scaled_ref[b]
+        mixed = jnp.dot(part, w_ref[b], preferred_element_type=jnp.float32)
+        out = mixed if out is None else out + mixed
         grad = lax.dot_general(
-            scaled_ref[b], upstream_all, (((0,), (0,)), ((), ())), preferred_element_type=jnp.float32
+            part, upstream_all, (((0,), (0,)), ((), ())), preferred_element_type=jnp.float32
         )
         total = jnp.zeros((group_width, chan_count), jnp.float32)
         for g in range(chan_count // group_width):
             block = grad[g * group_width : (g + 1) * group_width, :]
             total = total + jnp.where(lane == g, block, 0.0)
         wg_ref[b] = total
+        back = lax.dot_general(
+            upstream_all, w_ref[b], (((1,), (1,)), ((), ())), preferred_element_type=jnp.float32
+        )
+        pulled_ref[b] = (back / safe_ref[b]).astype(jnp.bfloat16)
+    for i in range(rows):
+        inf_ref[i] = out[i * col_pad : i * col_pad + col_count].astype(inf_ref.dtype)
 
 
 def adjoint_kernel(t_ref, pulled_ref, order_ref, col_ref):
@@ -104,7 +105,8 @@
     col_ref[...] = jnp.zeros_like(col_ref)
 
     def body(i, carry):
-        pulled = pulled_ref[i]
+        rows_at = pl.ds(pl.multiple_of(i * col_pad, col_pad), col_pad)
+        pulled = jnp.concatenate([pulled_ref[b, rows_at, :] for b in range(basis_count)], axis=0)
         for a in range(lat_taps):
             band = t_ref[i, :, a].reshape(basis_count * col_pad, lane_rows)
             start = pl.multiple_of((i + a) * lane_rows, lane_rows)
@@ -174,11 +176,14 @@
         out_shape=(
             jax.ShapeDtypeStruct((row_count, col_count, chan_count), jnp.bfloat16),
             jax.ShapeDtypeStruct((basis_count, group_width, chan_count), jnp.float32),
-            jax.ShapeDtypeStruct((row_count, basis_count * col_pad, chan_count), jnp.bfloat16),
+            jax.ShapeDtypeStruct((basis_count, row_count * col_pad, chan_count), jnp.bfloat16),
         ),
         in_specs=[vmem] * 5,
         out_specs=[vmem] * 3,
-        scratch_shapes=[pltpu.VMEM((basis_count, row_count * col_pad, chan_count), jnp.bfloat16)],
+        scratch_shapes=[
+            pltpu.VMEM((basis_count, row_count * col_pad, chan_count), jnp.bfloat16),
+            pltpu.VMEM((basis_count, row_count * col_pad, chan_count), jnp.float32),
+        ],
         compiler_params=params,
         cost_estimate=pl.CostEstimate(
             flops=2 * row_count * basis_count * col_pad * chan_count * (6 * lane_rows + 3 * chan_count),

time: 81.8 us -> 76.5 us (0.935)
  Pallas kernels: 24.2 us -> 18.9 us
    pallas_call x1, Pallas kernels: 16.8 us -> 11.4 us  [local(): pl.pallas_call(forward_kernel, out_shape=(jax.ShapeDtypeStruct((row_count...]
  transfers between devices with their start and end apart: 13 -> 13, of which waited for: 7 -> 7; matrix products, arithmetic and copies ran while one was open for 12% -> 13% of each run, Pallas kernels for 9% -> 10%
where the time goes in v9:
time: 76.5 us; the launch traced here: 76.2 us
  starting transfers between devices  22.6 us (30%)
  Pallas kernels  18.9 us (25%)
  waiting for transfers between devices  18 us (24%)
  local copies, waits for them, and re-layouts  9.48 us (12%)
  other arithmetic  4.34 us (6%)
  matrix products  1.86 us (2%)
  between operations  1.01 us (1%)
    ppermute x4, waiting for transfers between devices, butterfly_sum(): partner = lax.ppermute(value, axis, [(i, i ^ step) for i in range(count)])  12 us
    pallas_call x1, Pallas kernels, local(): pl.pallas_call(forward_kernel, out_shape=(jax.ShapeDtypeStruct((row_count...  11.4 us
    ppermute x4, starting transfers between devices, butterfly_sum(): partner = lax.ppermute(value, axis, [(i, i ^ step) for i in range(count)])  9.06 us
    pallas_call x1, Pallas kernels, local(): pl.pallas_call(adjoint_kernel, out_shape=jax.ShapeDtypeStruct(((row_count...  7.45 us
    ppermute x2, waiting for transfers between devices, with_halo(): lax.ppermute(lax.slice_in_dim(block, 0, width, axis=dim), axis, backward)  4.3 us
    ppermute x2, starting transfers between devices, with_halo(): lax.ppermute(lax.slice_in_dim(block, block.shape[dim] - width, None, axis...  3.98 us
    ppermute x2, starting transfers between devices, with_halo(): lax.ppermute(lax.slice_in_dim(block, 0, width, axis=dim), axis, backward)  3.54 us
    unnamed x20, local copies, waits for them, and re-layouts  3.37 us
  transfers between devices with their start and end apart: 13, of which 7 were waited for; matrix products, arithmetic and copies ran while one was open for 13% of the time, Pallas kernels for 10%

profile of v9, /device:TPU:0, one launch (start us, length us, event | category | flops | bytes accessed | tf_op | source)
XLA Modules:
  0.0 76.2 jit_solution(13182885932144663025)
XLA Ops:
  0.6 0.0 copy-start
  0.7 1.0 %convert_element_type.46 = bf16[24,45,8]{1,2,0:T(8,128)(2,1)S(1)} convert(s32[24,45,8]{1,2,0:T(8,128)} %param.7) | non-fusion elementwise | flops 8640 | bytes 51840 | tf_op jit(solution)/shard_map/convert_element_type | solution.py:132
  1.6 0.2 copy.35
  1.9 0.1 reshape.114
  2.0 0.4 fusion.6
  2.4 0.2 reshape.115
  2.6 0.0 copy-done.5
  2.6 0.0 copy-start.1
  2.6 0.0 copy-start.7
  2.6 0.1 copy_multiply_fusion
  2.8 2.4 %collective-permute-start = (bf16[1,45,264]{2,1,0:T(8,128)(2,1)S(1)}, bf16[1,45,264]{2,1,0:T(8,128)(2,1)S(1)}, u32[]{:S(2)}, u32[]{:S(2)}) collective-permute-start(bf16[1,45,264]{2,1,0:T(8,128)(2,1)S(1)} %get-tuple-element.22), channel_id=1, source_target_pairs={{0,4},{4,8},{8,12},{12,16},{16,20},{20,24},{24,28},{1,5},{5,9},{9,... | collective-permute-start | bytes 71288 | tf_op jit(solution)/shard_map/ppermute | solution.py:18
  5.2 1.3 %collective-permute-start.1 = (bf16[1,45,264]{2,1,0:T(8,128)(2,1)S(1)}, bf16[1,45,264]{2,1,0:T(8,128)(2,1)S(1)}, u32[]{:S(2)}, u32[]{:S(2)}) collective-permute-start(bf16[1,45,264]{2,1,0:T(8,128)(2,1)S(1)} %get-tuple-element.23), channel_id=1, source_target_pairs={{4,0},{8,4},{12,8},{16,12},{20,16},{24,20},{28,24},{5,1},{9,5},{13... | collective-permute-start | bytes 71288 | tf_op jit(solution)/shard_map/ppermute | solution.py:21
  6.5 0.0 copy-done
  6.5 0.1 constant_dynamic-slice_fusion
  6.6 0.2 copy.48
  6.8 0.1 compare_convert_fusion
  6.9 0.1 copy.37
  7.0 0.0 copy-start.6
  7.0 1.1 %fusion.18 = bf16[24,4,3,48,64]{4,0,3,2,1:T(8,128)(2,1)S(1)} fusion(s32[48,64]{1,0:T(8,128)S(1)} %iota_subtract_fusion, pred[48]{0:T(512)(128)(4,1)S(1)} %iota_compare_fusion.6, bf16[24,4,3,17]{3,0,2,1:T(8,128)(2,1)S(1)} %copy.48, bf16[24,17]{1,0:T(8,128)(2,1)S(1)} %constant_dynamic-slice_fusion.1), kind=kOutput, calls=%fused_computation.27 | convolution fusion | flops 30205056 | bytes 1792416 | tf_op jit(solution)/shard_map/ibae,ejp->ibajp/dot_general | solution.py:164
  8.2 0.0 copy-done.1
  8.2 0.0 collective-permute-done
  8.2 2.2 %collective-permute-done.1 = bf16[1,45,264]{2,1,0:T(8,128)(2,1)S(1)} collective-permute-done((bf16[1,45,264]{2,1,0:T(8,128)(2,1)S(1)}, bf16[1,45,264]{2,1,0:T(8,128)(2,1)S(1)}, u32[]{:S(2)}, u32[]{:S(2)}) %collective-permute-start.1) | collective-permute-done | bytes 23792 | tf_op jit(solution)/shard_map/ppermute | solution.py:21
  10.4 0.8 %pad_maximum_fusion.3 = (bf16[26,8,264]{2,1,0:T(8,128)(2,1)}, bf16[26,8,264]{2,1,0:T(8,128)(2,1)}) fusion(bf16[1,45,264]{2,1,0:T(8,128)(2,1)S(1)} %collective-permute-done.1, bf16[1,45,264]{2,1,0:T(8,128)(2,1)S(1)} %collective-permute-done, bf16[24,45,8]{2,1,0:T(8,128)(2,1)S(1)} %copy.35, bf16[24,45,256]{2,1,0:T(8,128)(2,1)S(1)} %copy_multiply_fusion), kind=kLoop, calls=%fused_computation.35 | loop fusion | flops 878592 | bytes 837408 | tf_op jit(solution)/shard_map/slice | solution.py:19
  11.2 1.6 %collective-permute-start.2 = (bf16[26,8,264]{2,1,0:T(8,128)(2,1)}, bf16[26,8,264]{2,1,0:T(8,128)(2,1)S(1)}, u32[]{:S(2)}, u32[]{:S(2)}) collective-permute-start(bf16[26,8,264]{2,1,0:T(8,128)(2,1)} %get-tuple-element.20), channel_id=1, source_target_pairs={{0,1},{1,2},{2,3},{3,0},{4,5},{5,6},{6,7},{7,4},{8,9},{9,10},{10,1... | collective-permute-start | bytes 329480 | tf_op jit(solution)/shard_map/ppermute | solution.py:18
  12.7 2.2 %collective-permute-start.3 = (bf16[26,8,264]{2,1,0:T(8,128)(2,1)}, bf16[26,8,264]{2,1,0:T(8,128)(2,1)}, u32[]{:S(2)}, u32[]{:S(2)}) collective-permute-start(bf16[26,8,264]{2,1,0:T(8,128)(2,1)} %get-tuple-element.21), channel_id=1, source_target_pairs={{1,0},{2,1},{3,2},{0,3},{5,4},{6,5},{7,6},{4,7},{9,8},{10,9},{11,1... | collective-permute-start | bytes 329480 | tf_op jit(solution)/shard_map/ppermute | solution.py:21
  15.0 0.0 copy-done.6
  15.0 0.7 multiply_bitcast_fusion
  15.7 2.6 %copy.52.t_ref = bf16[24,4,3,48,64]{4,3,2,1,0:T(8,128)(2,1)} copy(bf16[24,4,3,48,64]{4,0,3,2,1:T(8,128)(2,1)S(1)} %fusion.18) | data formatting | bytes 3538944 | tf_op jit(solution)/shard_map/ibae,ejp->ibajp/dot_general | solution.py:164
  18.3 1.4 %reshape.118.w_ref = bf16[4,256,256]{2,1,0:T(8,128)(2,1)S(1)} reshape(bf16[4,8,32,8,32]{4,3,2,1,0:T(8,128)(2,1)S(1)} %multiply_bitcast_fusion) | data formatting | bytes 1048576 | tf_op jit(solution)/shard_map/reshape | solution.py:169
  19.7 0.0 copy-start.4
  19.7 1.2 %copy.40 = bf16[24,45,256]{2,1,0:T(8,128)(2,1)S(1)} copy(bf16[24,45,256]{2,0,1:T(8,128)(2,1)} %param.11) | data formatting | bytes 1105920 | tf_op args[5]
  21.0 0.0 collective-permute-done.2
  21.0 2.1 %collective-permute-done.3 = bf16[26,8,264]{2,1,0:T(8,128)(2,1)} collective-permute-done((bf16[26,8,264]{2,1,0:T(8,128)(2,1)}, bf16[26,8,264]{2,1,0:T(8,128)(2,1)}, u32[]{:S(2)}, u32[]{:S(2)}) %collective-permute-start.3) | collective-permute-done | bytes 109856 | tf_op jit(solution)/shard_map/ppermute | solution.py:21
  23.1 0.0 copy-done.4
  23.1 1.2 %fusion.9 = bf16[26,64,264]{2,1,0:T(8,128)(2,1)S(1)} fusion(bf16[26,8,264]{2,1,0:T(8,128)(2,1)} %collective-permute-done.3, bf16[26,8,264]{2,1,0:T(8,128)(2,1)S(1)} %collective-permute-done.2, bf16[1,45,264]{2,1,0:T(8,128)(2,1)S(1)} %collective-permute-done.1, bf16[1,45,264]{2,1,0:T(8,128)(2,1)S(1)} %collective-permute-done, ...), kind=kLoop, calls=%fused_computation.15 | loop fusion | flops 8346624 | bytes 1716000 | tf_op jit(solution)/shard_map/concatenate | solution.py:22
  24.4 0.1 slice.54
  24.4 0.1 slice.53
  24.5 0.4 convolution_convert_fusion.m_ref
  24.9 11.4 %shard_map.85 = (bf16[24,45,256]{2,1,0:T(8,128)(2,1)S(1)}, f32[4,32,256]{2,1,0:T(8,128)S(1)}, bf16[4,1152,256]{2,1,0:T(8,128)(2,1)S(1)}) custom-call(bf16[1664,256]{1,0:T(8,128)(2,1)S(1)} %bitcast.28, bf16[1664,256]{1,0:T(8,128)(2,1)S(1)} %convolution_convert_fusion.m_ref, bf16[24,4,3,48,64]{4,3,2,1,0:T(8,128)(2,1)} %copy.52.t_ref, ...), custom_call_target="tpu_custom_call" | custom-call | flops 2717908992 | bytes 3407872 | tf_op jit(solution)/shard_map/pallas_call | solution.py:174
  36.3 0.2 collective-permute-start.4
  36.5 1.2 %collective-permute-done.4.order_ref = f32[4,32,256]{2,1,0:T(8,128)S(1)} collective-permute-done((f32[4,32,256]{2,1,0:T(8,128)S(1)}, f32[4,32,256]{2,1,0:T(8,128)S(1)}, u32[]{:S(2)}, u32[]{:S(2)}) %collective-permute-start.4) | collective-permute-done | bytes 131104 | tf_op jit(solution)/shard_map/ppermute | solution.py:198
  37.7 2.9 %collective-permute-start.9 = (f32[4,32,256]{2,1,0:T(8,128)S(1)}, f32[4,32,256]{2,1,0:T(8,128)S(1)}, u32[]{:S(2)}, u32[]{:S(2)}) collective-permute-start(f32[4,32,256]{2,1,0:T(8,128)S(1)} %add.58), channel_id=1, source_target_pairs={{0,8},{4,12},{8,0},{12,4},{16,24},{20,28},{24,16},{28,20},{1,9},{5... | collective-permute-start | bytes 393224 | tf_op jit(solution)/shard_map/ppermute | solution.py:49
  40.6 7.5 %shard_map.86 = f32[1664,256]{1,0:T(8,128)S(1)} custom-call(bf16[24,4,3,48,64]{4,3,2,1,0:T(8,128)(2,1)} %copy.52.t_ref, bf16[4,1152,256]{2,1,0:T(8,128)(2,1)S(1)} %get-tuple-element.7.pulled_ref, f32[4,32,256]{2,1,0:T(8,128)S(1)} %collective-permute-done.4.order_ref), custom_call_target="tpu_custom_call" | custom-call | flops 452984832 | bytes 2555904 | tf_op jit(solution)/shard_map/pallas_call | solution.py:206
  48.1 1.8 %collective-permute-start.5 = (f32[1,61,256]{2,1,0:T(8,128)S(1)}, f32[1,61,256]{2,1,0:T(8,128)S(1)}, u32[]{:S(2)}, u32[]{:S(2)}) collective-permute-start(f32[1,61,256]{2,1,0:T(8,128)S(1)} %get-tuple-element.18), channel_id=1, source_target_pairs={{0,4},{4,8},{8,12},{12,16},{16,20},{20,24},{24,28},{1,5},{5,9},{9,... | collective-permute-start | bytes 187400 | tf_op jit(solution)/shard_map/ppermute | solution.py:29
  49.9 1.3 %collective-permute-start.6 = (f32[1,61,256]{2,1,0:T(8,128)S(1)}, f32[1,61,256]{2,1,0:T(8,128)S(1)}, u32[]{:S(2)}, u32[]{:S(2)}) collective-permute-start(f32[1,61,256]{2,1,0:T(8,128)S(1)} %get-tuple-element.19), channel_id=1, source_target_pairs={{4,0},{8,4},{12,8},{16,12},{20,16},{24,20},{28,24},{5,1},{9,5},{13... | collective-permute-start | bytes 187400 | tf_op jit(solution)/shard_map/ppermute | solution.py:29
  51.2 0.0 collective-permute-done.9
  51.2 3.9 %collective-permute-start.10 = (f32[4,32,256]{2,1,0:T(8,128)S(1)}, f32[4,32,256]{2,1,0:T(8,128)S(1)}, u32[]{:S(2)}, u32[]{:S(2)}) collective-permute-start(f32[4,32,256]{2,1,0:T(8,128)S(1)} %add.59), channel_id=1, source_target_pairs={{0,16},{4,20},{8,24},{12,28},{16,0},{20,4},{24,8},{28,12},{1,17},{... | collective-permute-start | bytes 393224 | tf_op jit(solution)/shard_map/ppermute | solution.py:49
  55.1 0.0 collective-permute-done.5
  55.1 0.0 collective-permute-done.6
  55.1 0.1 fusion.7
  55.3 1.3 %collective-permute-start.8 = (f32[24,8,256]{2,1,0:T(8,128)S(1)}, f32[24,8,256]{2,1,0:T(8,128)S(1)}, u32[]{:S(2)}, u32[]{:S(2)}) collective-permute-start(f32[24,8,256]{2,1,0:T(8,128)S(1)} %slice.60), channel_id=1, source_target_pairs={{0,1},{1,2},{2,3},{3,0},{4,5},{5,6},{6,7},{7,4},{8,9},{9,10},{10,1... | collective-permute-start | bytes 589832 | tf_op jit(solution)/shard_map/ppermute | solution.py:34
  56.6 1.7 %collective-permute-done.10 = f32[4,32,256]{2,1,0:T(8,128)S(1)} collective-permute-done((f32[4,32,256]{2,1,0:T(8,128)S(1)}, f32[4,32,256]{2,1,0:T(8,128)S(1)}, u32[]{:S(2)}, u32[]{:S(2)}) %collective-permute-start.10) | collective-permute-done | bytes 131104 | tf_op jit(solution)/shard_map/ppermute | solution.py:49
  58.3 1.3 %collective-permute-start.11 = (f32[4,32,256]{2,1,0:T(8,128)S(1)}, f32[4,32,256]{2,1,0:T(8,128)S(1)}, u32[]{:S(2)}, u32[]{:S(2)}) collective-permute-start(f32[4,32,256]{2,1,0:T(8,128)S(1)} %add.60), channel_id=1, source_target_pairs={{0,1},{1,0},{2,3},{3,2},{4,5},{5,4},{6,7},{7,6},{8,9},{9,8},{10,11... | collective-permute-start | bytes 393224 | tf_op jit(solution)/shard_map/ppermute | solution.py:49
  59.6 1.5 %collective-permute-start.7 = (bf16[24,8,256]{2,1,0:T(8,128)(2,1)S(1)}, bf16[24,8,256]{2,1,0:T(8,128)(2,1)S(1)}, u32[]{:S(2)}, u32[]{:S(2)}) collective-permute-start(bf16[24,8,256]{2,1,0:T(8,128)(2,1)S(1)} %slice.72), channel_id=1, source_target_pairs={{0,3},{1,0},{2,1},{3,2},{4,7},{5,4},{6,5},{7,6},{8,11},{9,8},{10,9... | collective-permute-start | bytes 294920 | tf_op jit(solution)/shard_map/ppermute | solution.py:34
  61.1 1.0 %copy.43 = bf16[24,45,256]{2,0,1:T(8,128)(2,1)} copy(bf16[24,45,256]{2,1,0:T(8,128)(2,1)S(1)} %get-tuple-element.15) | data formatting | bytes 1105920
  62.1 5.4 %collective-permute-done.11 = f32[4,32,256]{2,1,0:T(8,128)S(1)} collective-permute-done((f32[4,32,256]{2,1,0:T(8,128)S(1)}, f32[4,32,256]{2,1,0:T(8,128)S(1)}, u32[]{:S(2)}, u32[]{:S(2)}) %collective-permute-start.11) | collective-permute-done | bytes 131104 | tf_op jit(solution)/shard_map/ppermute | solution.py:49
  67.5 1.0 %collective-permute-start.12 = (f32[4,32,256]{2,1,0:T(8,128)S(1)}, f32[4,32,256]{2,1,0:T(8,128)S(1)}, u32[]{:S(2)}, u32[]{:S(2)}) collective-permute-start(f32[4,32,256]{2,1,0:T(8,128)S(1)} %add.61), channel_id=1, source_target_pairs={{0,2},{1,3},{2,0},{3,1},{4,6},{5,7},{6,4},{7,5},{8,10},{9,11},{10,... | collective-permute-start | bytes 393224 | tf_op jit(solution)/shard_map/ppermute | solution.py:49
  68.4 0.6 collective-permute-done.7
  69.0 0.0 collective-permute-done.8
  69.0 0.2 fusion.15
  69.3 1.0 %copy.44 = bf16[24,45,256]{2,0,1:T(8,128)(2,1)} copy(bf16[24,45,256]{2,1,0:T(8,128)(2,1)S(1)} %fusion.15) | data formatting | bytes 1105920
  70.2 4.9 %collective-permute-done.12 = f32[4,32,256]{2,1,0:T(8,128)S(1)} collective-permute-done((f32[4,32,256]{2,1,0:T(8,128)S(1)}, f32[4,32,256]{2,1,0:T(8,128)S(1)}, u32[]{:S(2)}, u32[]{:S(2)}) %collective-permute-start.12) | collective-permute-done | bytes 131104 | tf_op jit(solution)/shard_map/ppermute | solution.py:49
  75.1 0.2 reshape.120
  75.3 0.9 %copy.55 = f32[4,32,8,32]{3,1,0,2:T(8,128)} copy(f32[4,32,8,32]{3,2,1,0:T(8,128)S(1)} %reshape.120) | data formatting | bytes 262144 | tf_op jit(solution)/shard_map/reshape | solution.py:204
  (23 shorter events, 0.3 us)
Async XLA Ops:
  0.6 5.9 %copy-start = (bf16[192,4,3,17]{0,1,3,2:T(4,128)(2,1)S(1)}, bf16[192,4,3,17]{0,1,3,2:T(4,128)(2,1)}, u32[]{:S(2)}) copy-start(bf16[192,4,3,17]{0,1,3,2:T(4,128)(2,1)} %param.8) | copy-start | bytes 235012
  0.6 1.9 %copy-start.5 = (bf16[24,45,256]{2,0,1:T(8,128)(2,1)S(1)}, bf16[24,45,256]{2,0,1:T(8,128)(2,1)}, u32[]{:S(2)}) copy-start(bf16[24,45,256]{2,0,1:T(8,128)(2,1)} %param.6) | copy-start | bytes 1658884
  1.9 8.5 %copy-start.3 = (bf16[24,45,8]{2,1,0:T(8,128)(2,1)}, bf16[24,45,8]{2,1,0:T(8,128)(2,1)S(1)}, u32[]{:S(2)}) copy-start(bf16[24,45,8]{2,1,0:T(8,128)(2,1)S(1)} %copy.35) | copy-start | bytes 51844
  2.6 5.6 %copy-start.1 = (bf16[24,45,256]{2,1,0:T(8,128)(2,1)}, bf16[24,45,256]{2,1,0:T(8,128)(2,1)S(1)}, u32[]{:S(2)}) copy-start(bf16[24,45,256]{2,1,0:T(8,128)(2,1)S(1)} %reshape.115) | copy-start | bytes 1658884
  2.6 4.2 %copy-start.7 = (s32[192]{0:T(256)S(1)}, s32[192]{0:T(256)}, u32[]{:S(2)}) copy-start(s32[192]{0:T(256)} %param.9) | copy-start | bytes 2308
  2.8 5.4 %collective-permute-start = (bf16[1,45,264]{2,1,0:T(8,128)(2,1)S(1)}, bf16[1,45,264]{2,1,0:T(8,128)(2,1)S(1)}, u32[]{:S(2)}, u32[]{:S(2)}) collective-permute-start(bf16[1,45,264]{2,1,0:T(8,128)(2,1)S(1)} %get-tuple-element.22), channel_id=1, source_target_pairs={{0,4},{4,8},{8,12},{12,16},{16,20},{20,24},{24,28},{1,5},{5,9},{9,... | collective-permute-start | bytes 71288 | tf_op jit(solution)/shard_map/ppermute | solution.py:18
  5.2 5.2 %collective-permute-start.1 = (bf16[1,45,264]{2,1,0:T(8,128)(2,1)S(1)}, bf16[1,45,264]{2,1,0:T(8,128)(2,1)S(1)}, u32[]{:S(2)}, u32[]{:S(2)}) collective-permute-start(bf16[1,45,264]{2,1,0:T(8,128)(2,1)S(1)} %get-tuple-element.23), channel_id=1, source_target_pairs={{4,0},{8,4},{12,8},{16,12},{20,16},{24,20},{28,24},{5,1},{9,5},{13... | collective-permute-start | bytes 71288 | tf_op jit(solution)/shard_map/ppermute | solution.py:21
  7.0 8.0 %copy-start.6 = (bf16[8,4,32,32]{3,2,1,0:T(8,128)(2,1)S(1)}, bf16[8,4,32,32]{3,2,1,0:T(8,128)(2,1)}, u32[]{:S(2)}) copy-start(bf16[8,4,32,32]{3,2,1,0:T(8,128)(2,1)} %param.10) | copy-start | bytes 196612
  11.2 9.8 %collective-permute-start.2 = (bf16[26,8,264]{2,1,0:T(8,128)(2,1)}, bf16[26,8,264]{2,1,0:T(8,128)(2,1)S(1)}, u32[]{:S(2)}, u32[]{:S(2)}) collective-permute-start(bf16[26,8,264]{2,1,0:T(8,128)(2,1)} %get-tuple-element.20), channel_id=1, source_target_pairs={{0,1},{1,2},{2,3},{3,0},{4,5},{5,6},{6,7},{7,4},{8,9},{9,10},{10,1... | collective-permute-start | bytes 329480 | tf_op jit(solution)/shard_map/ppermute | solution.py:18
  12.7 10.4 %collective-permute-start.3 = (bf16[26,8,264]{2,1,0:T(8,128)(2,1)}, bf16[26,8,264]{2,1,0:T(8,128)(2,1)}, u32[]{:S(2)}, u32[]{:S(2)}) collective-permute-start(bf16[26,8,264]{2,1,0:T(8,128)(2,1)} %get-tuple-element.21), channel_id=1, source_target_pairs={{1,0},{2,1},{3,2},{0,3},{5,4},{6,5},{7,6},{4,7},{9,8},{10,9},{11,1... | collective-permute-start | bytes 329480 | tf_op jit(solution)/shard_map/ppermute | solution.py:21
  19.7 3.4 %copy-start.4 = (bf16[24,45,8]{2,1,0:T(8,128)(2,1)S(1)}, bf16[24,45,8]{2,1,0:T(8,128)(2,1)}, u32[]{:S(2)}) copy-start(bf16[24,45,8]{2,1,0:T(8,128)(2,1)} %copy-done.3) | copy-start | bytes 51844
  36.3 1.4 %collective-permute-start.4 = (f32[4,32,256]{2,1,0:T(8,128)S(1)}, f32[4,32,256]{2,1,0:T(8,128)S(1)}, u32[]{:S(2)}, u32[]{:S(2)}) collective-permute-start(f32[4,32,256]{2,1,0:T(8,128)S(1)} %get-tuple-element.8), channel_id=1, source_target_pairs={{0,4},{4,0},{8,12},{12,8},{16,20},{20,16},{24,28},{28,24},{1,5},{5... | collective-permute-start | bytes 393224 | tf_op jit(solution)/shard_map/ppermute | solution.py:198
  37.7 13.4 %collective-permute-start.9 = (f32[4,32,256]{2,1,0:T(8,128)S(1)}, f32[4,32,256]{2,1,0:T(8,128)S(1)}, u32[]{:S(2)}, u32[]{:S(2)}) collective-permute-start(f32[4,32,256]{2,1,0:T(8,128)S(1)} %add.58), channel_id=1, source_target_pairs={{0,8},{4,12},{8,0},{12,4},{16,24},{20,28},{24,16},{28,20},{1,9},{5... | collective-permute-start | bytes 393224 | tf_op jit(solution)/shard_map/ppermute | solution.py:49
  48.1 7.1 %collective-permute-start.5 = (f32[1,61,256]{2,1,0:T(8,128)S(1)}, f32[1,61,256]{2,1,0:T(8,128)S(1)}, u32[]{:S(2)}, u32[]{:S(2)}) collective-permute-start(f32[1,61,256]{2,1,0:T(8,128)S(1)} %get-tuple-element.18), channel_id=1, source_target_pairs={{0,4},{4,8},{8,12},{12,16},{16,20},{20,24},{24,28},{1,5},{5,9},{9,... | collective-permute-start | bytes 187400 | tf_op jit(solution)/shard_map/ppermute | solution.py:29
  49.9 5.3 %collective-permute-start.6 = (f32[1,61,256]{2,1,0:T(8,128)S(1)}, f32[1,61,256]{2,1,0:T(8,128)S(1)}, u32[]{:S(2)}, u32[]{:S(2)}) collective-permute-start(f32[1,61,256]{2,1,0:T(8,128)S(1)} %get-tuple-element.19), channel_id=1, source_target_pairs={{4,0},{8,4},{12,8},{16,12},{20,16},{24,20},{28,24},{5,1},{9,5},{13... | collective-permute-start | bytes 187400 | tf_op jit(solution)/shard_map/ppermute | solution.py:29
  51.2 7.1 %collective-permute-start.10 = (f32[4,32,256]{2,1,0:T(8,128)S(1)}, f32[4,32,256]{2,1,0:T(8,128)S(1)}, u32[]{:S(2)}, u32[]{:S(2)}) collective-permute-start(f32[4,32,256]{2,1,0:T(8,128)S(1)} %add.59), channel_id=1, source_target_pairs={{0,16},{4,20},{8,24},{12,28},{16,0},{20,4},{24,8},{28,12},{1,17},{... | collective-permute-start | bytes 393224 | tf_op jit(solution)/shard_map/ppermute | solution.py:49
  55.3 13.8 %copy-start.2 = (bf16[24,45,256]{2,1,0:T(8,128)(2,1)S(1)}, bf16[24,45,256]{2,1,0:T(8,128)(2,1)}, u32[]{:S(2)}) copy-start(bf16[24,45,256]{2,1,0:T(8,128)(2,1)} %copy-done.1) | copy-start | bytes 1658884
  55.3 13.7 %collective-permute-start.8 = (f32[24,8,256]{2,1,0:T(8,128)S(1)}, f32[24,8,256]{2,1,0:T(8,128)S(1)}, u32[]{:S(2)}, u32[]{:S(2)}) collective-permute-start(f32[24,8,256]{2,1,0:T(8,128)S(1)} %slice.60), channel_id=1, source_target_pairs={{0,1},{1,2},{2,3},{3,0},{4,5},{5,6},{6,7},{7,4},{8,9},{9,10},{10,1... | collective-permute-start | bytes 589832 | tf_op jit(solution)/shard_map/ppermute | solution.py:34
  58.3 9.1 %collective-permute-start.11 = (f32[4,32,256]{2,1,0:T(8,128)S(1)}, f32[4,32,256]{2,1,0:T(8,128)S(1)}, u32[]{:S(2)}, u32[]{:S(2)}) collective-permute-start(f32[4,32,256]{2,1,0:T(8,128)S(1)} %add.60), channel_id=1, source_target_pairs={{0,1},{1,0},{2,3},{3,2},{4,5},{5,4},{6,7},{7,6},{8,9},{9,8},{10,11... | collective-permute-start | bytes 393224 | tf_op jit(solution)/shard_map/ppermute | solution.py:49
  59.6 9.4 %collective-permute-start.7 = (bf16[24,8,256]{2,1,0:T(8,128)(2,1)S(1)}, bf16[24,8,256]{2,1,0:T(8,128)(2,1)S(1)}, u32[]{:S(2)}, u32[]{:S(2)}) collective-permute-start(bf16[24,8,256]{2,1,0:T(8,128)(2,1)S(1)} %slice.72), channel_id=1, source_target_pairs={{0,3},{1,0},{2,1},{3,2},{4,7},{5,4},{6,5},{7,6},{8,11},{9,8},{10,9... | collective-permute-start | bytes 294920 | tf_op jit(solution)/shard_map/ppermute | solution.py:34
  67.5 7.6 %collective-permute-start.12 = (f32[4,32,256]{2,1,0:T(8,128)S(1)}, f32[4,32,256]{2,1,0:T(8,128)S(1)}, u32[]{:S(2)}, u32[]{:S(2)}) collective-permute-start(f32[4,32,256]{2,1,0:T(8,128)S(1)} %add.61), channel_id=1, source_target_pairs={{0,2},{1,3},{2,0},{3,1},{4,6},{5,7},{6,4},{7,5},{8,10},{9,11},{10,... | collective-permute-start | bytes 393224 | tf_op jit(solution)/shard_map/ppermute | solution.py:49

commit v10 on v9

--- a/solution.py
+++ b/solution.py
@@ -34,9 +34,29 @@
     return lax.ppermute(x, axis, [(i, (i + by) % size) for i in range(size)])
 
 
+def ring_sum(value, axis):
+    count = lax.axis_size(axis)
+    me = lax.axis_index(axis)
+    received = [value] + [
+        lax.ppermute(value, axis, [(i, (i + shift) % count) for i in range(count)])
+        for shift in range(1, count)
+    ]
+    total = None
+    for owner in range(count):
+        piece = None
+        for shift in range(count):
+            chosen = jnp.where((me - shift) % count == owner, received[shift], 0.0)
+            piece = chosen if piece is None else piece + chosen
+        total = piece if total is None else total + piece
+    return total
+
+
 def butterfly_sum(value, axes, skip=0):
     for axis in axes:
         count = lax.axis_size(axis)
+        if count <= 4 and not skip:
+            value = ring_sum(value, axis)
+            continue
         if count & (count - 1):
             value = lax.psum(value, axis)
             continue

time: 76.5 us -> 77.6 us (1.014)
  the two profiles are of different devices: /device:TPU:0 before, /device:TPU:11 now
where the time goes in v10:
time: 77.6 us; the launch traced here: 77.2 us
  starting transfers between devices  20.1 us (26%)
  waiting for transfers between devices  20.1 us (26%)
  Pallas kernels  18.8 us (24%)
  local copies, waits for them, and re-layouts  10.1 us (13%)
  other arithmetic  5.36 us (7%)
  matrix products  1.85 us (2%)
  between operations  1.01 us (1%)
    pallas_call x1, Pallas kernels, local(): pl.pallas_call(forward_kernel, out_shape=(jax.ShapeDtypeStruct((row_count...  11.3 us
    ppermute x3, waiting for transfers between devices, ring_sum(): lax.ppermute(value, axis, [(i, (i + shift) % count) for i in range(count)])  8.98 us
    pallas_call x1, Pallas kernels, local(): pl.pallas_call(adjoint_kernel, out_shape=jax.ShapeDtypeStruct(((row_count...  7.46 us
    ppermute x2, starting transfers between devices, passed_along(): return lax.ppermute(block, axis, route)  5.93 us
    ppermute x2, starting transfers between devices, with_halo(): lax.ppermute(lax.slice_in_dim(block, block.shape[dim] - width, None, axis...  4.98 us
    ppermute x3, starting transfers between devices, ring_sum(): lax.ppermute(value, axis, [(i, (i + shift) % count) for i in range(count)])  4.84 us
    ppermute x2, waiting for transfers between devices, passed_along(): return lax.ppermute(block, axis, route)  4.44 us
    ppermute x2, waiting for transfers between devices, with_halo(): lax.ppermute(lax.slice_in_dim(block, 0, width, axis=dim), axis, backward)  4.2 us
  transfers between devices with their start and end apart: 14, of which 7 were waited for; matrix products, arithmetic and copies ran while one was open for 15% of the time, Pallas kernels for 0%

profile of v10, /device:TPU:11, one launch (start us, length us, event | category | flops | bytes accessed | tf_op | source)
XLA Modules:
  0.0 77.2 jit_solution(15753831684131851919)
XLA Ops:
  0.6 0.0 copy-start
  0.7 1.0 %convert_element_type.46 = bf16[24,45,8]{1,2,0:T(8,128)(2,1)S(1)} convert(s32[24,45,8]{1,2,0:T(8,128)} %param.7) | non-fusion elementwise | flops 8640 | bytes 51840 | tf_op jit(solution)/shard_map/convert_element_type | solution.py:152
  1.6 0.2 copy.35
  1.9 0.1 reshape.114
  2.0 0.4 fusion.6
  2.4 0.2 reshape.115
  2.6 0.0 copy-done.5
  2.6 0.0 copy-start.1
  2.6 0.0 copy-start.7
  2.6 0.1 copy_multiply_fusion
  2.7 3.7 %collective-permute-start = (bf16[1,45,264]{2,1,0:T(8,128)(2,1)S(1)}, bf16[1,45,264]{2,1,0:T(8,128)(2,1)S(1)}, u32[]{:S(2)}, u32[]{:S(2)}) collective-permute-start(bf16[1,45,264]{2,1,0:T(8,128)(2,1)S(1)} %get-tuple-element.22), channel_id=1, source_target_pairs={{0,4},{4,8},{8,12},{12,16},{16,20},{20,24},{24,28},{1,5},{5,9},{9,... | collective-permute-start | bytes 71288 | tf_op jit(solution)/shard_map/ppermute | solution.py:18
  6.4 1.9 %collective-permute-start.1 = (bf16[1,45,264]{2,1,0:T(8,128)(2,1)S(1)}, bf16[1,45,264]{2,1,0:T(8,128)(2,1)S(1)}, u32[]{:S(2)}, u32[]{:S(2)}) collective-permute-start(bf16[1,45,264]{2,1,0:T(8,128)(2,1)S(1)} %get-tuple-element.23), channel_id=1, source_target_pairs={{4,0},{8,4},{12,8},{16,12},{20,16},{24,20},{28,24},{5,1},{9,5},{13... | collective-permute-start | bytes 71288 | tf_op jit(solution)/shard_map/ppermute | solution.py:21
  8.4 0.1 constant_dynamic-slice_fusion
  8.5 0.2 copy.48
  8.7 0.1 compare_convert_fusion
  8.8 0.1 copy.37
  8.9 0.0 copy-start.6
  8.9 1.1 %fusion.18 = bf16[24,4,3,48,64]{4,0,3,2,1:T(8,128)(2,1)S(1)} fusion(s32[48,64]{1,0:T(8,128)S(1)} %iota_subtract_fusion, pred[48]{0:T(512)(128)(4,1)S(1)} %iota_compare_fusion.6, bf16[24,4,3,17]{3,0,2,1:T(8,128)(2,1)S(1)} %copy.48, bf16[24,17]{1,0:T(8,128)(2,1)S(1)} %constant_dynamic-slice_fusion.1), kind=kOutput, calls=%fused_computation.27 | convolution fusion | flops 30205056 | bytes 1792416 | tf_op jit(solution)/shard_map/ibae,ejp->ibajp/dot_general | solution.py:184
  10.1 0.0 collective-permute-done
  10.1 2.5 %collective-permute-done.1 = bf16[1,45,264]{2,1,0:T(8,128)(2,1)S(1)} collective-permute-done((bf16[1,45,264]{2,1,0:T(8,128)(2,1)S(1)}, bf16[1,45,264]{2,1,0:T(8,128)(2,1)S(1)}, u32[]{:S(2)}, u32[]{:S(2)}) %collective-permute-start.1) | collective-permute-done | bytes 23792 | tf_op jit(solution)/shard_map/ppermute | solution.py:21
  12.6 0.8 %pad_maximum_fusion.3 = (bf16[26,8,264]{2,1,0:T(8,128)(2,1)}, bf16[26,8,264]{2,1,0:T(8,128)(2,1)}) fusion(bf16[1,45,264]{2,1,0:T(8,128)(2,1)S(1)} %collective-permute-done.1, bf16[1,45,264]{2,1,0:T(8,128)(2,1)S(1)} %collective-permute-done, bf16[24,45,8]{2,1,0:T(8,128)(2,1)S(1)} %copy.35, bf16[24,45,256]{2,1,0:T(8,128)(2,1)S(1)} %copy_multiply_fusion), kind=kLoop, calls=%fused_computation.35 | loop fusion | flops 878592 | bytes 837408 | tf_op jit(solution)/shard_map/slice | solution.py:19
  13.4 1.3 %collective-permute-start.2 = (bf16[26,8,264]{2,1,0:T(8,128)(2,1)}, bf16[26,8,264]{2,1,0:T(8,128)(2,1)S(1)}, u32[]{:S(2)}, u32[]{:S(2)}) collective-permute-start(bf16[26,8,264]{2,1,0:T(8,128)(2,1)} %get-tuple-element.20), channel_id=1, source_target_pairs={{0,1},{1,2},{2,3},{3,0},{4,5},{5,6},{6,7},{7,4},{8,9},{9,10},{10,1... | collective-permute-start | bytes 329480 | tf_op jit(solution)/shard_map/ppermute | solution.py:18
  14.7 0.2 collective-permute-start.3
  14.9 0.7 multiply_bitcast_fusion
  15.6 2.6 %copy.52.t_ref = bf16[24,4,3,48,64]{4,3,2,1,0:T(8,128)(2,1)} copy(bf16[24,4,3,48,64]{4,0,3,2,1:T(8,128)(2,1)S(1)} %fusion.18) | data formatting | bytes 3538944 | tf_op jit(solution)/shard_map/ibae,ejp->ibajp/dot_general | solution.py:184
  18.2 1.4 %reshape.118.w_ref = bf16[4,256,256]{2,1,0:T(8,128)(2,1)S(1)} reshape(bf16[4,8,32,8,32]{4,3,2,1,0:T(8,128)(2,1)S(1)} %multiply_bitcast_fusion) | data formatting | bytes 1048576 | tf_op jit(solution)/shard_map/reshape | solution.py:189
  19.6 0.0 copy-start.4
  19.6 1.2 %copy.40 = bf16[24,45,256]{2,1,0:T(8,128)(2,1)S(1)} copy(bf16[24,45,256]{2,0,1:T(8,128)(2,1)} %param.11) | data formatting | bytes 1105920 | tf_op args[5]
  20.9 0.0 collective-permute-done.2
  20.9 1.7 %collective-permute-done.3 = bf16[26,8,264]{2,1,0:T(8,128)(2,1)} collective-permute-done((bf16[26,8,264]{2,1,0:T(8,128)(2,1)}, bf16[26,8,264]{2,1,0:T(8,128)(2,1)}, u32[]{:S(2)}, u32[]{:S(2)}) %collective-permute-start.3) | collective-permute-done | bytes 109856 | tf_op jit(solution)/shard_map/ppermute | solution.py:21
  22.6 1.2 %fusion.9 = bf16[26,64,264]{2,1,0:T(8,128)(2,1)S(1)} fusion(bf16[26,8,264]{2,1,0:T(8,128)(2,1)} %collective-permute-done.3, bf16[26,8,264]{2,1,0:T(8,128)(2,1)S(1)} %collective-permute-done.2, bf16[1,45,264]{2,1,0:T(8,128)(2,1)S(1)} %collective-permute-done.1, bf16[1,45,264]{2,1,0:T(8,128)(2,1)S(1)} %collective-permute-done, ...), kind=kLoop, calls=%fused_computation.15 | loop fusion | flops 8346624 | bytes 1716000 | tf_op jit(solution)/shard_map/concatenate | solution.py:22
  23.8 0.1 slice.54
  23.9 0.1 slice.53
  24.0 0.4 convolution_convert_fusion.m_ref
  24.3 11.3 %shard_map.85 = (bf16[24,45,256]{2,1,0:T(8,128)(2,1)S(1)}, f32[4,32,256]{2,1,0:T(8,128)S(1)}, bf16[4,1152,256]{2,1,0:T(8,128)(2,1)S(1)}) custom-call(bf16[1664,256]{1,0:T(8,128)(2,1)S(1)} %bitcast.28, bf16[1664,256]{1,0:T(8,128)(2,1)S(1)} %convolution_convert_fusion.m_ref, bf16[24,4,3,48,64]{4,3,2,1,0:T(8,128)(2,1)} %copy.52.t_ref, ...), custom_call_target="tpu_custom_call" | custom-call | flops 2717908992 | bytes 3407872 | tf_op jit(solution)/shard_map/pallas_call | solution.py:194
  35.6 0.6 collective-permute-start.4
  36.2 1.0 %collective-permute-done.4.order_ref = f32[4,32,256]{2,1,0:T(8,128)S(1)} collective-permute-done((f32[4,32,256]{2,1,0:T(8,128)S(1)}, f32[4,32,256]{2,1,0:T(8,128)S(1)}, u32[]{:S(2)}, u32[]{:S(2)}) %collective-permute-start.4) | collective-permute-done | bytes 131104 | tf_op jit(solution)/shard_map/ppermute | solution.py:218
  37.2 7.5 %shard_map.86 = f32[1664,256]{1,0:T(8,128)S(1)} custom-call(bf16[24,4,3,48,64]{4,3,2,1,0:T(8,128)(2,1)} %copy.52.t_ref, bf16[4,1152,256]{2,1,0:T(8,128)(2,1)S(1)} %get-tuple-element.7.pulled_ref, f32[4,32,256]{2,1,0:T(8,128)S(1)} %collective-permute-done.4.order_ref), custom_call_target="tpu_custom_call" | custom-call | flops 452984832 | bytes 2555904 | tf_op jit(solution)/shard_map/pallas_call | solution.py:226
  44.7 4.0 %collective-permute-start.5 = (f32[1,61,256]{2,1,0:T(8,128)S(1)}, f32[1,61,256]{2,1,0:T(8,128)S(1)}, u32[]{:S(2)}, u32[]{:S(2)}) collective-permute-start(f32[1,61,256]{2,1,0:T(8,128)S(1)} %get-tuple-element.18), channel_id=1, source_target_pairs={{0,4},{4,8},{8,12},{12,16},{16,20},{20,24},{24,28},{1,5},{5,9},{9,... | collective-permute-start | bytes 187400 | tf_op jit(solution)/shard_map/ppermute | solution.py:29
  48.7 1.9 %collective-permute-start.6 = (f32[1,61,256]{2,1,0:T(8,128)S(1)}, f32[1,61,256]{2,1,0:T(8,128)S(1)}, u32[]{:S(2)}, u32[]{:S(2)}) collective-permute-start(f32[1,61,256]{2,1,0:T(8,128)S(1)} %get-tuple-element.19), channel_id=1, source_target_pairs={{4,0},{8,4},{12,8},{16,12},{20,16},{24,20},{28,24},{5,1},{9,5},{13... | collective-permute-start | bytes 187400 | tf_op jit(solution)/shard_map/ppermute | solution.py:29
  50.6 0.1 collective-permute-start.9
  50.7 0.0 collective-permute-done.5
  50.7 4.4 %collective-permute-done.6 = f32[1,61,256]{2,1,0:T(8,128)S(1)} collective-permute-done((f32[1,61,256]{2,1,0:T(8,128)S(1)}, f32[1,61,256]{2,1,0:T(8,128)S(1)}, u32[]{:S(2)}, u32[]{:S(2)}) %collective-permute-start.6) | collective-permute-done | bytes 62496 | tf_op jit(solution)/shard_map/ppermute | solution.py:29
  55.2 0.1 fusion.7
  55.4 0.4 collective-permute-start.8
  55.8 0.0 collective-permute-done.9
  55.8 0.1 collective-permute-start.10
  55.9 0.7 slice.72
  56.5 1.1 %collective-permute-start.7 = (bf16[24,8,256]{2,1,0:T(8,128)(2,1)}, bf16[24,8,256]{2,1,0:T(8,128)(2,1)}, u32[]{:S(2)}, u32[]{:S(2)}) collective-permute-start(bf16[24,8,256]{2,1,0:T(8,128)(2,1)} %slice.72), channel_id=1, source_target_pairs={{0,3},{1,0},{2,1},{3,2},{4,7},{5,4},{6,5},{7,6},{8,11},{9,8},{10,9... | collective-permute-start | bytes 294920 | tf_op jit(solution)/shard_map/ppermute | solution.py:34
  57.6 1.0 %copy.43 = bf16[24,45,256]{2,0,1:T(8,128)(2,1)} copy(bf16[24,45,256]{2,1,0:T(8,128)(2,1)S(1)} %get-tuple-element.15) | data formatting | bytes 1105920
  58.6 1.4 %collective-permute-done.10 = f32[4,32,256]{2,1,0:T(8,128)S(1)} collective-permute-done((f32[4,32,256]{2,1,0:T(8,128)S(1)}, f32[4,32,256]{2,1,0:T(8,128)S(1)}, u32[]{:S(2)}, u32[]{:S(2)}) %collective-permute-start.10) | collective-permute-done | bytes 131104 | tf_op jit(solution)/shard_map/ppermute | solution.py:69
  60.1 2.6 %collective-permute-start.11 = (f32[4,32,256]{2,1,0:T(8,128)S(1)}, f32[4,32,256]{2,1,0:T(8,128)S(1)}, u32[]{:S(2)}, u32[]{:S(2)}) collective-permute-start(f32[4,32,256]{2,1,0:T(8,128)S(1)} %add.128), channel_id=1, source_target_pairs={{0,1},{1,2},{2,3},{3,0},{4,5},{5,6},{6,7},{7,4},{8,9},{9,10},{10,1... | collective-permute-start | bytes 393224 | tf_op jit(solution)/shard_map/ppermute | solution.py:41
  62.7 1.1 %collective-permute-start.12 = (f32[4,32,256]{2,1,0:T(8,128)S(1)}, f32[4,32,256]{2,1,0:T(8,128)S(1)}, u32[]{:S(2)}, u32[]{:S(2)}) collective-permute-start(f32[4,32,256]{2,1,0:T(8,128)S(1)} %add.128), channel_id=1, source_target_pairs={{0,2},{1,3},{2,0},{3,1},{4,6},{5,7},{6,4},{7,5},{8,10},{9,11},{10,... | collective-permute-start | bytes 393224 | tf_op jit(solution)/shard_map/ppermute | solution.py:41
  63.8 1.1 %collective-permute-start.13 = (f32[4,32,256]{2,1,0:T(8,128)S(1)}, f32[4,32,256]{2,1,0:T(8,128)S(1)}, u32[]{:S(2)}, u32[]{:S(2)}) collective-permute-start(f32[4,32,256]{2,1,0:T(8,128)S(1)} %add.128), channel_id=1, source_target_pairs={{0,3},{1,0},{2,1},{3,2},{4,7},{5,4},{6,5},{7,6},{8,11},{9,8},{10,9... | collective-permute-start | bytes 393224 | tf_op jit(solution)/shard_map/ppermute | solution.py:41
  64.9 0.0 collective-permute-done.7
  64.9 0.0 collective-permute-done.8
  64.9 1.1 %fusion.15 = bf16[24,45,256]{2,1,0:T(8,128)(2,1)S(1)} fusion(f32[24,61,256]{2,1,0:T(8,128)S(1)} %fusion.7, bf16[24,45,256]{2,1,0:T(8,128)(2,1)S(1)} %copy-done.2, f32[24,8,256]{2,1,0:T(8,128)S(1)} %collective-permute-done.8, bf16[24,8,256]{2,1,0:T(8,128)(2,1)} %collective-permute-done.7), kind=kLoop, calls=%fused_computation.22 | loop fusion | flops 1658880 | bytes 2506752 | tf_op jit(solution)/shard_map/convert_element_type | solution.py:256
  66.1 1.0 %copy.44 = bf16[24,45,256]{2,0,1:T(8,128)(2,1)} copy(bf16[24,45,256]{2,1,0:T(8,128)(2,1)S(1)} %fusion.15) | data formatting | bytes 1105920
  67.0 0.0 collective-permute-done.11
  67.0 7.4 %collective-permute-done.12 = f32[4,32,256]{2,1,0:T(8,128)S(1)} collective-permute-done((f32[4,32,256]{2,1,0:T(8,128)S(1)}, f32[4,32,256]{2,1,0:T(8,128)S(1)}, u32[]{:S(2)}, u32[]{:S(2)}) %collective-permute-start.12) | collective-permute-done | bytes 131104 | tf_op jit(solution)/shard_map/ppermute | solution.py:41
  74.4 1.6 %collective-permute-done.13 = f32[4,32,256]{2,1,0:T(8,128)S(1)} collective-permute-done((f32[4,32,256]{2,1,0:T(8,128)S(1)}, f32[4,32,256]{2,1,0:T(8,128)S(1)}, u32[]{:S(2)}, u32[]{:S(2)}) %collective-permute-start.13) | collective-permute-done | bytes 131104 | tf_op jit(solution)/shard_map/ppermute | solution.py:41
  76.0 0.1 add_multiply_fusion
  76.2 0.2 reshape.120
  76.3 0.9 %copy.55 = f32[4,32,8,32]{3,1,0,2:T(8,128)} copy(f32[4,32,8,32]{3,2,1,0:T(8,128)S(1)} %reshape.120) | data formatting | bytes 262144 | tf_op jit(solution)/shard_map/reshape | solution.py:224
  (24 shorter events, 0.2 us)
Async XLA Ops:
  0.6 7.8 %copy-start = (bf16[192,4,3,17]{0,1,3,2:T(4,128)(2,1)S(1)}, bf16[192,4,3,17]{0,1,3,2:T(4,128)(2,1)}, u32[]{:S(2)}) copy-start(bf16[192,4,3,17]{0,1,3,2:T(4,128)(2,1)} %param.8) | copy-start | bytes 235012
  0.6 1.9 %copy-start.5 = (bf16[24,45,256]{2,0,1:T(8,128)(2,1)S(1)}, bf16[24,45,256]{2,0,1:T(8,128)(2,1)}, u32[]{:S(2)}) copy-start(bf16[24,45,256]{2,0,1:T(8,128)(2,1)} %param.6) | copy-start | bytes 1658884
  1.9 10.7 %copy-start.3 = (bf16[24,45,8]{2,1,0:T(8,128)(2,1)}, bf16[24,45,8]{2,1,0:T(8,128)(2,1)S(1)}, u32[]{:S(2)}) copy-start(bf16[24,45,8]{2,1,0:T(8,128)(2,1)S(1)} %copy.35) | copy-start | bytes 51844
  2.6 7.5 %copy-start.1 = (bf16[24,45,256]{2,1,0:T(8,128)(2,1)}, bf16[24,45,256]{2,1,0:T(8,128)(2,1)S(1)}, u32[]{:S(2)}) copy-start(bf16[24,45,256]{2,1,0:T(8,128)(2,1)S(1)} %reshape.115) | copy-start | bytes 1658884
  2.6 6.1 %copy-start.7 = (s32[192]{0:T(256)S(1)}, s32[192]{0:T(256)}, u32[]{:S(2)}) copy-start(s32[192]{0:T(256)} %param.9) | copy-start | bytes 2308
  2.7 7.4 %collective-permute-start = (bf16[1,45,264]{2,1,0:T(8,128)(2,1)S(1)}, bf16[1,45,264]{2,1,0:T(8,128)(2,1)S(1)}, u32[]{:S(2)}, u32[]{:S(2)}) collective-permute-start(bf16[1,45,264]{2,1,0:T(8,128)(2,1)S(1)} %get-tuple-element.22), channel_id=1, source_target_pairs={{0,4},{4,8},{8,12},{12,16},{16,20},{20,24},{24,28},{1,5},{5,9},{9,... | collective-permute-start | bytes 71288 | tf_op jit(solution)/shard_map/ppermute | solution.py:18
  6.4 6.2 %collective-permute-start.1 = (bf16[1,45,264]{2,1,0:T(8,128)(2,1)S(1)}, bf16[1,45,264]{2,1,0:T(8,128)(2,1)S(1)}, u32[]{:S(2)}, u32[]{:S(2)}) collective-permute-start(bf16[1,45,264]{2,1,0:T(8,128)(2,1)S(1)} %get-tuple-element.23), channel_id=1, source_target_pairs={{4,0},{8,4},{12,8},{16,12},{20,16},{24,20},{28,24},{5,1},{9,5},{13... | collective-permute-start | bytes 71288 | tf_op jit(solution)/shard_map/ppermute | solution.py:21
  8.9 6.0 %copy-start.6 = (bf16[8,4,32,32]{3,2,1,0:T(8,128)(2,1)S(1)}, bf16[8,4,32,32]{3,2,1,0:T(8,128)(2,1)}, u32[]{:S(2)}) copy-start(bf16[8,4,32,32]{3,2,1,0:T(8,128)(2,1)} %param.10) | copy-start | bytes 196612
  13.4 7.5 %collective-permute-start.2 = (bf16[26,8,264]{2,1,0:T(8,128)(2,1)}, bf16[26,8,264]{2,1,0:T(8,128)(2,1)S(1)}, u32[]{:S(2)}, u32[]{:S(2)}) collective-permute-start(bf16[26,8,264]{2,1,0:T(8,128)(2,1)} %get-tuple-element.20), channel_id=1, source_target_pairs={{0,1},{1,2},{2,3},{3,0},{4,5},{5,6},{6,7},{7,4},{8,9},{9,10},{10,1... | collective-permute-start | bytes 329480 | tf_op jit(solution)/shard_map/ppermute | solution.py:18
  14.7 7.9 %collective-permute-start.3 = (bf16[26,8,264]{2,1,0:T(8,128)(2,1)}, bf16[26,8,264]{2,1,0:T(8,128)(2,1)}, u32[]{:S(2)}, u32[]{:S(2)}) collective-permute-start(bf16[26,8,264]{2,1,0:T(8,128)(2,1)} %get-tuple-element.21), channel_id=1, source_target_pairs={{1,0},{2,1},{3,2},{0,3},{5,4},{6,5},{7,6},{4,7},{9,8},{10,9},{11,1... | collective-permute-start | bytes 329480 | tf_op jit(solution)/shard_map/ppermute | solution.py:21
  19.6 3.0 %copy-start.4 = (bf16[24,45,8]{2,1,0:T(8,128)(2,1)S(1)}, bf16[24,45,8]{2,1,0:T(8,128)(2,1)}, u32[]{:S(2)}) copy-start(bf16[24,45,8]{2,1,0:T(8,128)(2,1)} %copy-done.3) | copy-start | bytes 51844
  35.6 1.5 %collective-permute-start.4 = (f32[4,32,256]{2,1,0:T(8,128)S(1)}, f32[4,32,256]{2,1,0:T(8,128)S(1)}, u32[]{:S(2)}, u32[]{:S(2)}) collective-permute-start(f32[4,32,256]{2,1,0:T(8,128)S(1)} %get-tuple-element.8), channel_id=1, source_target_pairs={{0,4},{4,0},{8,12},{12,8},{16,20},{20,16},{24,28},{28,24},{1,5},{5... | collective-permute-start | bytes 393224 | tf_op jit(solution)/shard_map/ppermute | solution.py:218
  44.7 6.1 %collective-permute-start.5 = (f32[1,61,256]{2,1,0:T(8,128)S(1)}, f32[1,61,256]{2,1,0:T(8,128)S(1)}, u32[]{:S(2)}, u32[]{:S(2)}) collective-permute-start(f32[1,61,256]{2,1,0:T(8,128)S(1)} %get-tuple-element.18), channel_id=1, source_target_pairs={{0,4},{4,8},{8,12},{12,16},{16,20},{20,24},{24,28},{1,5},{5,9},{9,... | collective-permute-start | bytes 187400 | tf_op jit(solution)/shard_map/ppermute | solution.py:29
  48.7 6.5 %collective-permute-start.6 = (f32[1,61,256]{2,1,0:T(8,128)S(1)}, f32[1,61,256]{2,1,0:T(8,128)S(1)}, u32[]{:S(2)}, u32[]{:S(2)}) collective-permute-start(f32[1,61,256]{2,1,0:T(8,128)S(1)} %get-tuple-element.19), channel_id=1, source_target_pairs={{4,0},{8,4},{12,8},{16,12},{20,16},{24,20},{28,24},{5,1},{9,5},{13... | collective-permute-start | bytes 187400 | tf_op jit(solution)/shard_map/ppermute | solution.py:29
  50.6 5.1 %collective-permute-start.9 = (f32[4,32,256]{2,1,0:T(8,128)S(1)}, f32[4,32,256]{2,1,0:T(8,128)S(1)}, u32[]{:S(2)}, u32[]{:S(2)}) collective-permute-start(f32[4,32,256]{2,1,0:T(8,128)S(1)} %add.126), channel_id=1, source_target_pairs={{0,8},{4,12},{8,0},{12,4},{16,24},{20,28},{24,16},{28,20},{1,9},{5... | collective-permute-start | bytes 393224 | tf_op jit(solution)/shard_map/ppermute | solution.py:69
  55.3 9.6 %copy-start.2 = (bf16[24,45,256]{2,1,0:T(8,128)(2,1)S(1)}, bf16[24,45,256]{2,1,0:T(8,128)(2,1)}, u32[]{:S(2)}) copy-start(bf16[24,45,256]{2,1,0:T(8,128)(2,1)} %copy-done.1) | copy-start | bytes 1658884
  55.4 9.6 %collective-permute-start.8 = (f32[24,8,256]{2,1,0:T(8,128)S(1)}, f32[24,8,256]{2,1,0:T(8,128)S(1)}, u32[]{:S(2)}, u32[]{:S(2)}) collective-permute-start(f32[24,8,256]{2,1,0:T(8,128)S(1)} %slice.60), channel_id=1, source_target_pairs={{0,1},{1,2},{2,3},{3,0},{4,5},{5,6},{6,7},{7,4},{8,9},{9,10},{10,1... | collective-permute-start | bytes 589832 | tf_op jit(solution)/shard_map/ppermute | solution.py:34
  55.8 4.3 %collective-permute-start.10 = (f32[4,32,256]{2,1,0:T(8,128)S(1)}, f32[4,32,256]{2,1,0:T(8,128)S(1)}, u32[]{:S(2)}, u32[]{:S(2)}) collective-permute-start(f32[4,32,256]{2,1,0:T(8,128)S(1)} %add.127), channel_id=1, source_target_pairs={{0,16},{4,20},{8,24},{12,28},{16,0},{20,4},{24,8},{28,12},{1,17},{... | collective-permute-start | bytes 393224 | tf_op jit(solution)/shard_map/ppermute | solution.py:69
  56.5 8.4 %collective-permute-start.7 = (bf16[24,8,256]{2,1,0:T(8,128)(2,1)}, bf16[24,8,256]{2,1,0:T(8,128)(2,1)}, u32[]{:S(2)}, u32[]{:S(2)}) collective-permute-start(bf16[24,8,256]{2,1,0:T(8,128)(2,1)} %slice.72), channel_id=1, source_target_pairs={{0,3},{1,0},{2,1},{3,2},{4,7},{5,4},{6,5},{7,6},{8,11},{9,8},{10,9... | collective-permute-start | bytes 294920 | tf_op jit(solution)/shard_map/ppermute | solution.py:34
  60.1 7.0 %collective-permute-start.11 = (f32[4,32,256]{2,1,0:T(8,128)S(1)}, f32[4,32,256]{2,1,0:T(8,128)S(1)}, u32[]{:S(2)}, u32[]{:S(2)}) collective-permute-start(f32[4,32,256]{2,1,0:T(8,128)S(1)} %add.128), channel_id=1, source_target_pairs={{0,1},{1,2},{2,3},{3,0},{4,5},{5,6},{6,7},{7,4},{8,9},{9,10},{10,1... | collective-permute-start | bytes 393224 | tf_op jit(solution)/shard_map/ppermute | solution.py:41
  62.7 11.7 %collective-permute-start.12 = (f32[4,32,256]{2,1,0:T(8,128)S(1)}, f32[4,32,256]{2,1,0:T(8,128)S(1)}, u32[]{:S(2)}, u32[]{:S(2)}) collective-permute-start(f32[4,32,256]{2,1,0:T(8,128)S(1)} %add.128), channel_id=1, source_target_pairs={{0,2},{1,3},{2,0},{3,1},{4,6},{5,7},{6,4},{7,5},{8,10},{9,11},{10,... | collective-permute-start | bytes 393224 | tf_op jit(solution)/shard_map/ppermute | solution.py:41
  63.8 12.2 %collective-permute-start.13 = (f32[4,32,256]{2,1,0:T(8,128)S(1)}, f32[4,32,256]{2,1,0:T(8,128)S(1)}, u32[]{:S(2)}, u32[]{:S(2)}) collective-permute-start(f32[4,32,256]{2,1,0:T(8,128)S(1)} %add.128), channel_id=1, source_target_pairs={{0,3},{1,0},{2,1},{3,2},{4,7},{5,4},{6,5},{7,6},{8,11},{9,8},{10,9... | collective-permute-start | bytes 393224 | tf_op jit(solution)/shard_map/ppermute | solution.py:41

commit v11 on v9

--- a/solution.py
+++ b/solution.py
@@ -34,22 +34,17 @@
     return lax.ppermute(x, axis, [(i, (i + by) % size) for i in range(size)])
 
 
-def butterfly_sum(value, axes, skip=0):
-    for axis in axes:
+def butterfly_sum(value, rounds):
+    for axis, step in rounds:
         count = lax.axis_size(axis)
-        if count & (count - 1):
-            value = lax.psum(value, axis)
-            continue
-        step = 1
-        while step < count:
-            if skip:
-                skip -= 1
-                step *= 2
-                continue
-            partner = lax.ppermute(value, axis, [(i, i ^ step) for i in range(count)])
-            value = value + partner
-            step *= 2
+        partner = lax.ppermute(value, axis, [(i, i ^ step) for i in range(count)])
+        value = value + partner
     return value
+
+
+def butterfly_rounds(axis):
+    count = lax.axis_size(axis)
+    return [(axis, 1 << k) for k in range(count.bit_length() - 1)]
 
 
 def forward_kernel(x_ref, m_ref, t_ref, cot_ref, w_ref, inf_ref, wg_ref, pulled_ref, scaled_ref, safe_ref):
@@ -194,12 +189,14 @@
 
     cell_count = row_count * lax.axis_size("lat") * col_count * lax.axis_size("lon")
     lat_count = lax.axis_size("lat")
-    if lat_count % 2 == 0:
+    lon_count = lax.axis_size("lon")
+    if lat_count & (lat_count - 1) or lon_count & (lon_count - 1):
+        first = grad_blocks
+        dense = lax.psum(grad_blocks, ("lat", "lon"))
+    else:
         first = lax.ppermute(grad_blocks, "lat", [(i, i ^ 1) for i in range(lat_count)])
-        dense = butterfly_sum(grad_blocks + first, ("lat", "lon"), skip=1)
-    else:
-        first = grad_blocks
-        dense = butterfly_sum(grad_blocks, ("lat", "lon"))
+        rounds = butterfly_rounds("lon") + butterfly_rounds("lat")[1:]
+        dense = butterfly_sum(grad_blocks + first, rounds)
     dense = dense * (1.0 / math.sqrt(cell_count))
     weight_grad = dense.reshape(basis_count, group_width, group_count, group_width).transpose(2, 0, 1, 3)
 

time: 76.5 us -> 78.6 us (1.027)
  starting transfers between devices: 22.6 us -> 28.4 us
  waiting for transfers between devices: 18 us -> 14.3 us
    ppermute x4, starting transfers between devices: 9.06 us -> 16.3 us  [butterfly_sum(): partner = lax.ppermute(value, axis, [(i, i ^ step) for i in range(count)])]
    ppermute x4, waiting for transfers between devices: 12 us -> 6.09 us  [butterfly_sum(): partner = lax.ppermute(value, axis, [(i, i ^ step) for i in range(count)])]
    ppermute x2, waiting for transfers between devices: 0.01 us -> 2.73 us  [passed_along(): return lax.ppermute(block, axis, route)]
    ppermute x2, starting transfers between devices: 2.75 us -> 1.23 us  [from_behind(): return lax.ppermute(x, axis, [(i, (i + by) % size) for i in range(size)])]
where the time goes in v11:
time: 78.6 us; the launch traced here: 78.3 us
  starting transfers between devices  28.4 us (36%)
  Pallas kernels  18.9 us (24%)
  waiting for transfers between devices  14.3 us (18%)
  local copies, waits for them, and re-layouts  9.48 us (12%)
  other arithmetic  4.34 us (6%)
  matrix products  1.86 us (2%)
  between operations  1.01 us (1%)
    ppermute x4, starting transfers between devices, butterfly_sum(): partner = lax.ppermute(value, axis, [(i, i ^ step) for i in range(count)])  16.3 us
    pallas_call x1, Pallas kernels, local(): pl.pallas_call(forward_kernel, out_shape=(jax.ShapeDtypeStruct((row_count...  11.4 us
    pallas_call x1, Pallas kernels, local(): pl.pallas_call(adjoint_kernel, out_shape=jax.ShapeDtypeStruct(((row_count...  7.46 us
    ppermute x4, waiting for transfers between devices, butterfly_sum(): partner = lax.ppermute(value, axis, [(i, i ^ step) for i in range(count)])  6.09 us
    ppermute x2, waiting for transfers between devices, with_halo(): lax.ppermute(lax.slice_in_dim(block, 0, width, axis=dim), axis, backward)  4.3 us
    ppermute x2, starting transfers between devices, with_halo(): lax.ppermute(lax.slice_in_dim(block, block.shape[dim] - width, None, axis...  3.98 us
    ppermute x2, starting transfers between devices, with_halo(): lax.ppermute(lax.slice_in_dim(block, 0, width, axis=dim), axis, backward)  3.54 us
    unnamed x20, local copies, waits for them, and re-layouts  3.37 us
  transfers between devices with their start and end apart: 13, of which 7 were waited for; matrix products, arithmetic and copies ran while one was open for 13% of the time, Pallas kernels for 10%

profile of v11, /device:TPU:0, one launch (start us, length us, event | category | flops | bytes accessed | tf_op | source)
XLA Modules:
  0.0 78.3 jit_solution(4107944997432188171)
XLA Ops:
  0.6 0.0 copy-start
  0.6 0.0 copy-start.5
  0.7 1.0 %convert_element_type.46 = bf16[24,45,8]{1,2,0:T(8,128)(2,1)S(1)} convert(s32[24,45,8]{1,2,0:T(8,128)} %param.7) | non-fusion elementwise | flops 8640 | bytes 51840 | tf_op jit(solution)/shard_map/convert_element_type | solution.py:127
  1.6 0.2 copy.35
  1.9 0.1 reshape.114
  2.0 0.4 fusion.6
  2.4 0.2 reshape.115
  2.6 0.0 copy-done.5
  2.6 0.0 copy-start.1
  2.6 0.0 copy-start.7
  2.6 0.1 copy_multiply_fusion
  2.8 2.4 %collective-permute-start = (bf16[1,45,264]{2,1,0:T(8,128)(2,1)S(1)}, bf16[1,45,264]{2,1,0:T(8,128)(2,1)S(1)}, u32[]{:S(2)}, u32[]{:S(2)}) collective-permute-start(bf16[1,45,264]{2,1,0:T(8,128)(2,1)S(1)} %get-tuple-element.22), channel_id=1, source_target_pairs={{0,4},{4,8},{8,12},{12,16},{16,20},{20,24},{24,28},{1,5},{5,9},{9,... | collective-permute-start | bytes 71288 | tf_op jit(solution)/shard_map/ppermute | solution.py:18
  5.2 1.3 %collective-permute-start.1 = (bf16[1,45,264]{2,1,0:T(8,128)(2,1)S(1)}, bf16[1,45,264]{2,1,0:T(8,128)(2,1)S(1)}, u32[]{:S(2)}, u32[]{:S(2)}) collective-permute-start(bf16[1,45,264]{2,1,0:T(8,128)(2,1)S(1)} %get-tuple-element.23), channel_id=1, source_target_pairs={{4,0},{8,4},{12,8},{16,12},{20,16},{24,20},{28,24},{5,1},{9,5},{13... | collective-permute-start | bytes 71288 | tf_op jit(solution)/shard_map/ppermute | solution.py:21
  6.5 0.0 copy-done
  6.5 0.1 constant_dynamic-slice_fusion
  6.6 0.2 copy.48
  6.8 0.0 copy-done.7
  6.8 0.1 compare_convert_fusion
  6.9 0.1 copy.37
  7.0 0.0 copy-start.6
  7.0 1.1 %fusion.18 = bf16[24,4,3,48,64]{4,0,3,2,1:T(8,128)(2,1)S(1)} fusion(s32[48,64]{1,0:T(8,128)S(1)} %iota_subtract_fusion, pred[48]{0:T(512)(128)(4,1)S(1)} %iota_compare_fusion.6, bf16[24,4,3,17]{3,0,2,1:T(8,128)(2,1)S(1)} %copy.48, bf16[24,17]{1,0:T(8,128)(2,1)S(1)} %constant_dynamic-slice_fusion.1), kind=kOutput, calls=%fused_computation.27 | convolution fusion | flops 30205056 | bytes 1792416 | tf_op jit(solution)/shard_map/ibae,ejp->ibajp/dot_general | solution.py:159
  8.2 0.0 collective-permute-done
  8.2 2.2 %collective-permute-done.1 = bf16[1,45,264]{2,1,0:T(8,128)(2,1)S(1)} collective-permute-done((bf16[1,45,264]{2,1,0:T(8,128)(2,1)S(1)}, bf16[1,45,264]{2,1,0:T(8,128)(2,1)S(1)}, u32[]{:S(2)}, u32[]{:S(2)}) %collective-permute-start.1) | collective-permute-done | bytes 23792 | tf_op jit(solution)/shard_map/ppermute | solution.py:21
  10.4 0.0 copy-done.3
  10.4 0.8 %pad_maximum_fusion.3 = (bf16[26,8,264]{2,1,0:T(8,128)(2,1)}, bf16[26,8,264]{2,1,0:T(8,128)(2,1)}) fusion(bf16[1,45,264]{2,1,0:T(8,128)(2,1)S(1)} %collective-permute-done.1, bf16[1,45,264]{2,1,0:T(8,128)(2,1)S(1)} %collective-permute-done, bf16[24,45,8]{2,1,0:T(8,128)(2,1)S(1)} %copy.35, bf16[24,45,256]{2,1,0:T(8,128)(2,1)S(1)} %copy_multiply_fusion), kind=kLoop, calls=%fused_computation.35 | loop fusion | flops 878592 | bytes 837408 | tf_op jit(solution)/shard_map/slice | solution.py:19
  11.2 1.6 %collective-permute-start.2 = (bf16[26,8,264]{2,1,0:T(8,128)(2,1)}, bf16[26,8,264]{2,1,0:T(8,128)(2,1)S(1)}, u32[]{:S(2)}, u32[]{:S(2)}) collective-permute-start(bf16[26,8,264]{2,1,0:T(8,128)(2,1)} %get-tuple-element.20), channel_id=1, source_target_pairs={{0,1},{1,2},{2,3},{3,0},{4,5},{5,6},{6,7},{7,4},{8,9},{9,10},{10,1... | collective-permute-start | bytes 329480 | tf_op jit(solution)/shard_map/ppermute | solution.py:18
  12.7 2.2 %collective-permute-start.3 = (bf16[26,8,264]{2,1,0:T(8,128)(2,1)}, bf16[26,8,264]{2,1,0:T(8,128)(2,1)}, u32[]{:S(2)}, u32[]{:S(2)}) collective-permute-start(bf16[26,8,264]{2,1,0:T(8,128)(2,1)} %get-tuple-element.21), channel_id=1, source_target_pairs={{1,0},{2,1},{3,2},{0,3},{5,4},{6,5},{7,6},{4,7},{9,8},{10,9},{11,1... | collective-permute-start | bytes 329480 | tf_op jit(solution)/shard_map/ppermute | solution.py:21
  15.0 0.7 multiply_bitcast_fusion
  15.7 2.6 %copy.52.t_ref = bf16[24,4,3,48,64]{4,3,2,1,0:T(8,128)(2,1)} copy(bf16[24,4,3,48,64]{4,0,3,2,1:T(8,128)(2,1)S(1)} %fusion.18) | data formatting | bytes 3538944 | tf_op jit(solution)/shard_map/ibae,ejp->ibajp/dot_general | solution.py:159
  18.3 1.4 %reshape.118.w_ref = bf16[4,256,256]{2,1,0:T(8,128)(2,1)S(1)} reshape(bf16[4,8,32,8,32]{4,3,2,1,0:T(8,128)(2,1)S(1)} %multiply_bitcast_fusion) | data formatting | bytes 1048576 | tf_op jit(solution)/shard_map/reshape | solution.py:164
  19.7 0.0 copy-start.4
  19.7 1.2 %copy.40 = bf16[24,45,256]{2,1,0:T(8,128)(2,1)S(1)} copy(bf16[24,45,256]{2,0,1:T(8,128)(2,1)} %param.11) | data formatting | bytes 1105920 | tf_op args[5]
  21.0 0.0 collective-permute-done.2
  21.0 2.1 %collective-permute-done.3 = bf16[26,8,264]{2,1,0:T(8,128)(2,1)} collective-permute-done((bf16[26,8,264]{2,1,0:T(8,128)(2,1)}, bf16[26,8,264]{2,1,0:T(8,128)(2,1)}, u32[]{:S(2)}, u32[]{:S(2)}) %collective-permute-start.3) | collective-permute-done | bytes 109856 | tf_op jit(solution)/shard_map/ppermute | solution.py:21
  23.1 1.2 %fusion.9 = bf16[26,64,264]{2,1,0:T(8,128)(2,1)S(1)} fusion(bf16[26,8,264]{2,1,0:T(8,128)(2,1)} %collective-permute-done.3, bf16[26,8,264]{2,1,0:T(8,128)(2,1)S(1)} %collective-permute-done.2, bf16[1,45,264]{2,1,0:T(8,128)(2,1)S(1)} %collective-permute-done.1, bf16[1,45,264]{2,1,0:T(8,128)(2,1)S(1)} %collective-permute-done, ...), kind=kLoop, calls=%fused_computation.15 | loop fusion | flops 8346624 | bytes 1716000 | tf_op jit(solution)/shard_map/concatenate | solution.py:22
  24.4 0.1 slice.54
  24.4 0.1 slice.53
  24.5 0.4 convolution_convert_fusion.m_ref
  24.9 11.4 %shard_map.85 = (bf16[24,45,256]{2,1,0:T(8,128)(2,1)S(1)}, f32[4,32,256]{2,1,0:T(8,128)S(1)}, bf16[4,1152,256]{2,1,0:T(8,128)(2,1)S(1)}) custom-call(bf16[1664,256]{1,0:T(8,128)(2,1)S(1)} %bitcast.28, bf16[1664,256]{1,0:T(8,128)(2,1)S(1)} %convolution_convert_fusion.m_ref, bf16[24,4,3,48,64]{4,3,2,1,0:T(8,128)(2,1)} %copy.52.t_ref, ...), custom_call_target="tpu_custom_call" | custom-call | flops 2717908992 | bytes 3407872 | tf_op jit(solution)/shard_map/pallas_call | solution.py:169
  36.3 0.2 collective-permute-start.4
  36.5 1.2 %collective-permute-done.4.order_ref = f32[4,32,256]{2,1,0:T(8,128)S(1)} collective-permute-done((f32[4,32,256]{2,1,0:T(8,128)S(1)}, f32[4,32,256]{2,1,0:T(8,128)S(1)}, u32[]{:S(2)}, u32[]{:S(2)}) %collective-permute-start.4) | collective-permute-done | bytes 131104 | tf_op jit(solution)/shard_map/ppermute | solution.py:197
  37.7 1.0 %collective-permute-start.9 = (f32[4,32,256]{2,1,0:T(8,128)S(1)}, f32[4,32,256]{2,1,0:T(8,128)S(1)}, u32[]{:S(2)}, u32[]{:S(2)}) collective-permute-start(f32[4,32,256]{2,1,0:T(8,128)S(1)} %add.58), channel_id=1, source_target_pairs={{0,1},{1,0},{2,3},{3,2},{4,5},{5,4},{6,7},{7,6},{8,9},{9,8},{10,11... | collective-permute-start | bytes 393224 | tf_op jit(solution)/shard_map/ppermute | solution.py:40
  38.7 7.5 %shard_map.86 = f32[1664,256]{1,0:T(8,128)S(1)} custom-call(bf16[24,4,3,48,64]{4,3,2,1,0:T(8,128)(2,1)} %copy.52.t_ref, bf16[4,1152,256]{2,1,0:T(8,128)(2,1)S(1)} %get-tuple-element.7.pulled_ref, f32[4,32,256]{2,1,0:T(8,128)S(1)} %collective-permute-done.4.order_ref), custom_call_target="tpu_custom_call" | custom-call | flops 452984832 | bytes 2555904 | tf_op jit(solution)/shard_map/pallas_call | solution.py:203
  46.2 1.8 %collective-permute-start.5 = (f32[1,61,256]{2,1,0:T(8,128)S(1)}, f32[1,61,256]{2,1,0:T(8,128)S(1)}, u32[]{:S(2)}, u32[]{:S(2)}) collective-permute-start(f32[1,61,256]{2,1,0:T(8,128)S(1)} %get-tuple-element.18), channel_id=1, source_target_pairs={{0,4},{4,8},{8,12},{12,16},{16,20},{20,24},{24,28},{1,5},{5,9},{9,... | collective-permute-start | bytes 187400 | tf_op jit(solution)/shard_map/ppermute | solution.py:29
  48.0 1.3 %collective-permute-start.6 = (f32[1,61,256]{2,1,0:T(8,128)S(1)}, f32[1,61,256]{2,1,0:T(8,128)S(1)}, u32[]{:S(2)}, u32[]{:S(2)}) collective-permute-start(f32[1,61,256]{2,1,0:T(8,128)S(1)} %get-tuple-element.19), channel_id=1, source_target_pairs={{4,0},{8,4},{12,8},{16,12},{20,16},{24,20},{28,24},{5,1},{9,5},{13... | collective-permute-start | bytes 187400 | tf_op jit(solution)/shard_map/ppermute | solution.py:29
  49.3 0.0 collective-permute-done.9
  49.3 1.6 %collective-permute-start.10 = (f32[4,32,256]{2,1,0:T(8,128)S(1)}, f32[4,32,256]{2,1,0:T(8,128)S(1)}, u32[]{:S(2)}, u32[]{:S(2)}) collective-permute-start(f32[4,32,256]{2,1,0:T(8,128)S(1)} %add.59), channel_id=1, source_target_pairs={{0,2},{1,3},{2,0},{3,1},{4,6},{5,7},{6,4},{7,5},{8,10},{9,11},{10,... | collective-permute-start | bytes 393224 | tf_op jit(solution)/shard_map/ppermute | solution.py:40
  50.9 0.0 collective-permute-done.5
  50.9 2.7 %collective-permute-done.6 = f32[1,61,256]{2,1,0:T(8,128)S(1)} collective-permute-done((f32[1,61,256]{2,1,0:T(8,128)S(1)}, f32[1,61,256]{2,1,0:T(8,128)S(1)}, u32[]{:S(2)}, u32[]{:S(2)}) %collective-permute-start.6) | collective-permute-done | bytes 62496 | tf_op jit(solution)/shard_map/ppermute | solution.py:29
  53.7 0.1 fusion.7
  53.8 1.2 %collective-permute-start.8 = (f32[24,8,256]{2,1,0:T(8,128)S(1)}, f32[24,8,256]{2,1,0:T(8,128)S(1)}, u32[]{:S(2)}, u32[]{:S(2)}) collective-permute-start(f32[24,8,256]{2,1,0:T(8,128)S(1)} %slice.60), channel_id=1, source_target_pairs={{0,1},{1,2},{2,3},{3,0},{4,5},{5,6},{6,7},{7,4},{8,9},{9,10},{10,1... | collective-permute-start | bytes 589832 | tf_op jit(solution)/shard_map/ppermute | solution.py:34
  55.0 1.8 %collective-permute-done.10 = f32[4,32,256]{2,1,0:T(8,128)S(1)} collective-permute-done((f32[4,32,256]{2,1,0:T(8,128)S(1)}, f32[4,32,256]{2,1,0:T(8,128)S(1)}, u32[]{:S(2)}, u32[]{:S(2)}) %collective-permute-start.10) | collective-permute-done | bytes 131104 | tf_op jit(solution)/shard_map/ppermute | solution.py:40
  56.8 11.8 %collective-permute-start.11 = (f32[4,32,256]{2,1,0:T(8,128)S(1)}, f32[4,32,256]{2,1,0:T(8,128)S(1)}, u32[]{:S(2)}, u32[]{:S(2)}) collective-permute-start(f32[4,32,256]{2,1,0:T(8,128)S(1)} %add.60), channel_id=1, source_target_pairs={{0,8},{4,12},{8,0},{12,4},{16,24},{20,28},{24,16},{28,20},{1,9},{5... | collective-permute-start | bytes 393224 | tf_op jit(solution)/shard_map/ppermute | solution.py:40
  68.7 0.1 collective-permute-start.7
  68.8 1.0 %copy.43 = bf16[24,45,256]{2,0,1:T(8,128)(2,1)} copy(bf16[24,45,256]{2,1,0:T(8,128)(2,1)S(1)} %get-tuple-element.15) | data formatting | bytes 1105920
  69.7 2.4 %collective-permute-done.11 = f32[4,32,256]{2,1,0:T(8,128)S(1)} collective-permute-done((f32[4,32,256]{2,1,0:T(8,128)S(1)}, f32[4,32,256]{2,1,0:T(8,128)S(1)}, u32[]{:S(2)}, u32[]{:S(2)}) %collective-permute-start.11) | collective-permute-done | bytes 131104 | tf_op jit(solution)/shard_map/ppermute | solution.py:40
  72.1 1.9 %collective-permute-start.12 = (f32[4,32,256]{2,1,0:T(8,128)S(1)}, f32[4,32,256]{2,1,0:T(8,128)S(1)}, u32[]{:S(2)}, u32[]{:S(2)}) collective-permute-start(f32[4,32,256]{2,1,0:T(8,128)S(1)} %add.61), channel_id=1, source_target_pairs={{0,16},{4,20},{8,24},{12,28},{16,0},{20,4},{24,8},{28,12},{1,17},{... | collective-permute-start | bytes 393224 | tf_op jit(solution)/shard_map/ppermute | solution.py:40
  74.0 0.0 collective-permute-done.7
  74.1 0.0 collective-permute-done.8
  74.1 0.2 fusion.15
  74.3 1.0 %copy.44 = bf16[24,45,256]{2,0,1:T(8,128)(2,1)} copy(bf16[24,45,256]{2,1,0:T(8,128)(2,1)S(1)} %fusion.15) | data formatting | bytes 1105920
  75.3 1.9 %collective-permute-done.12 = f32[4,32,256]{2,1,0:T(8,128)S(1)} collective-permute-done((f32[4,32,256]{2,1,0:T(8,128)S(1)}, f32[4,32,256]{2,1,0:T(8,128)S(1)}, u32[]{:S(2)}, u32[]{:S(2)}) %collective-permute-start.12) | collective-permute-done | bytes 131104 | tf_op jit(solution)/shard_map/ppermute | solution.py:40
  77.2 0.2 reshape.120
  77.4 0.9 %copy.55 = f32[4,32,8,32]{3,1,0,2:T(8,128)} copy(f32[4,32,8,32]{3,2,1,0:T(8,128)S(1)} %reshape.120) | data formatting | bytes 262144 | tf_op jit(solution)/shard_map/reshape | solution.py:201
  (23 shorter events, 0.3 us)
Async XLA Ops:
  0.6 5.9 %copy-start = (bf16[192,4,3,17]{0,1,3,2:T(4,128)(2,1)S(1)}, bf16[192,4,3,17]{0,1,3,2:T(4,128)(2,1)}, u32[]{:S(2)}) copy-start(bf16[192,4,3,17]{0,1,3,2:T(4,128)(2,1)} %param.8) | copy-start | bytes 235012
  0.6 1.9 %copy-start.5 = (bf16[24,45,256]{2,0,1:T(8,128)(2,1)S(1)}, bf16[24,45,256]{2,0,1:T(8,128)(2,1)}, u32[]{:S(2)}) copy-start(bf16[24,45,256]{2,0,1:T(8,128)(2,1)} %param.6) | copy-start | bytes 1658884
  1.9 8.5 %copy-start.3 = (bf16[24,45,8]{2,1,0:T(8,128)(2,1)}, bf16[24,45,8]{2,1,0:T(8,128)(2,1)S(1)}, u32[]{:S(2)}) copy-start(bf16[24,45,8]{2,1,0:T(8,128)(2,1)S(1)} %copy.35) | copy-start | bytes 51844
  2.6 5.6 %copy-start.1 = (bf16[24,45,256]{2,1,0:T(8,128)(2,1)}, bf16[24,45,256]{2,1,0:T(8,128)(2,1)S(1)}, u32[]{:S(2)}) copy-start(bf16[24,45,256]{2,1,0:T(8,128)(2,1)S(1)} %reshape.115) | copy-start | bytes 1658884
  2.6 4.2 %copy-start.7 = (s32[192]{0:T(256)S(1)}, s32[192]{0:T(256)}, u32[]{:S(2)}) copy-start(s32[192]{0:T(256)} %param.9) | copy-start | bytes 2308
  2.8 5.4 %collective-permute-start = (bf16[1,45,264]{2,1,0:T(8,128)(2,1)S(1)}, bf16[1,45,264]{2,1,0:T(8,128)(2,1)S(1)}, u32[]{:S(2)}, u32[]{:S(2)}) collective-permute-start(bf16[1,45,264]{2,1,0:T(8,128)(2,1)S(1)} %get-tuple-element.22), channel_id=1, source_target_pairs={{0,4},{4,8},{8,12},{12,16},{16,20},{20,24},{24,28},{1,5},{5,9},{9,... | collective-permute-start | bytes 71288 | tf_op jit(solution)/shard_map/ppermute | solution.py:18
  5.2 5.2 %collective-permute-start.1 = (bf16[1,45,264]{2,1,0:T(8,128)(2,1)S(1)}, bf16[1,45,264]{2,1,0:T(8,128)(2,1)S(1)}, u32[]{:S(2)}, u32[]{:S(2)}) collective-permute-start(bf16[1,45,264]{2,1,0:T(8,128)(2,1)S(1)} %get-tuple-element.23), channel_id=1, source_target_pairs={{4,0},{8,4},{12,8},{16,12},{20,16},{24,20},{28,24},{5,1},{9,5},{13... | collective-permute-start | bytes 71288 | tf_op jit(solution)/shard_map/ppermute | solution.py:21
  7.0 8.0 %copy-start.6 = (bf16[8,4,32,32]{3,2,1,0:T(8,128)(2,1)S(1)}, bf16[8,4,32,32]{3,2,1,0:T(8,128)(2,1)}, u32[]{:S(2)}) copy-start(bf16[8,4,32,32]{3,2,1,0:T(8,128)(2,1)} %param.10) | copy-start | bytes 196612
  11.2 9.8 %collective-permute-start.2 = (bf16[26,8,264]{2,1,0:T(8,128)(2,1)}, bf16[26,8,264]{2,1,0:T(8,128)(2,1)S(1)}, u32[]{:S(2)}, u32[]{:S(2)}) collective-permute-start(bf16[26,8,264]{2,1,0:T(8,128)(2,1)} %get-tuple-element.20), channel_id=1, source_target_pairs={{0,1},{1,2},{2,3},{3,0},{4,5},{5,6},{6,7},{7,4},{8,9},{9,10},{10,1... | collective-permute-start | bytes 329480 | tf_op jit(solution)/shard_map/ppermute | solution.py:18
  12.7 10.4 %collective-permute-start.3 = (bf16[26,8,264]{2,1,0:T(8,128)(2,1)}, bf16[26,8,264]{2,1,0:T(8,128)(2,1)}, u32[]{:S(2)}, u32[]{:S(2)}) collective-permute-start(bf16[26,8,264]{2,1,0:T(8,128)(2,1)} %get-tuple-element.21), channel_id=1, source_target_pairs={{1,0},{2,1},{3,2},{0,3},{5,4},{6,5},{7,6},{4,7},{9,8},{10,9},{11,1... | collective-permute-start | bytes 329480 | tf_op jit(solution)/shard_map/ppermute | solution.py:21
  19.7 3.4 %copy-start.4 = (bf16[24,45,8]{2,1,0:T(8,128)(2,1)S(1)}, bf16[24,45,8]{2,1,0:T(8,128)(2,1)}, u32[]{:S(2)}) copy-start(bf16[24,45,8]{2,1,0:T(8,128)(2,1)} %copy-done.3) | copy-start | bytes 51844
  36.3 1.4 %collective-permute-start.4 = (f32[4,32,256]{2,1,0:T(8,128)S(1)}, f32[4,32,256]{2,1,0:T(8,128)S(1)}, u32[]{:S(2)}, u32[]{:S(2)}) collective-permute-start(f32[4,32,256]{2,1,0:T(8,128)S(1)} %get-tuple-element.8), channel_id=1, source_target_pairs={{0,4},{4,0},{8,12},{12,8},{16,20},{20,16},{24,28},{28,24},{1,5},{5... | collective-permute-start | bytes 393224 | tf_op jit(solution)/shard_map/ppermute | solution.py:197
  37.7 11.6 %collective-permute-start.9 = (f32[4,32,256]{2,1,0:T(8,128)S(1)}, f32[4,32,256]{2,1,0:T(8,128)S(1)}, u32[]{:S(2)}, u32[]{:S(2)}) collective-permute-start(f32[4,32,256]{2,1,0:T(8,128)S(1)} %add.58), channel_id=1, source_target_pairs={{0,1},{1,0},{2,3},{3,2},{4,5},{5,4},{6,7},{7,6},{8,9},{9,8},{10,11... | collective-permute-start | bytes 393224 | tf_op jit(solution)/shard_map/ppermute | solution.py:40
  46.2 4.7 %collective-permute-start.5 = (f32[1,61,256]{2,1,0:T(8,128)S(1)}, f32[1,61,256]{2,1,0:T(8,128)S(1)}, u32[]{:S(2)}, u32[]{:S(2)}) collective-permute-start(f32[1,61,256]{2,1,0:T(8,128)S(1)} %get-tuple-element.18), channel_id=1, source_target_pairs={{0,4},{4,8},{8,12},{12,16},{16,20},{20,24},{24,28},{1,5},{5,9},{9,... | collective-permute-start | bytes 187400 | tf_op jit(solution)/shard_map/ppermute | solution.py:29
  48.0 5.7 %collective-permute-start.6 = (f32[1,61,256]{2,1,0:T(8,128)S(1)}, f32[1,61,256]{2,1,0:T(8,128)S(1)}, u32[]{:S(2)}, u32[]{:S(2)}) collective-permute-start(f32[1,61,256]{2,1,0:T(8,128)S(1)} %get-tuple-element.19), channel_id=1, source_target_pairs={{4,0},{8,4},{12,8},{16,12},{20,16},{24,20},{28,24},{5,1},{9,5},{13... | collective-permute-start | bytes 187400 | tf_op jit(solution)/shard_map/ppermute | solution.py:29
  49.3 7.5 %collective-permute-start.10 = (f32[4,32,256]{2,1,0:T(8,128)S(1)}, f32[4,32,256]{2,1,0:T(8,128)S(1)}, u32[]{:S(2)}, u32[]{:S(2)}) collective-permute-start(f32[4,32,256]{2,1,0:T(8,128)S(1)} %add.59), channel_id=1, source_target_pairs={{0,2},{1,3},{2,0},{3,1},{4,6},{5,7},{6,4},{7,5},{8,10},{9,11},{10,... | collective-permute-start | bytes 393224 | tf_op jit(solution)/shard_map/ppermute | solution.py:40
  53.8 20.3 %copy-start.2 = (bf16[24,45,256]{2,1,0:T(8,128)(2,1)S(1)}, bf16[24,45,256]{2,1,0:T(8,128)(2,1)}, u32[]{:S(2)}) copy-start(bf16[24,45,256]{2,1,0:T(8,128)(2,1)} %copy-done.1) | copy-start | bytes 1658884
  53.8 20.2 %collective-permute-start.8 = (f32[24,8,256]{2,1,0:T(8,128)S(1)}, f32[24,8,256]{2,1,0:T(8,128)S(1)}, u32[]{:S(2)}, u32[]{:S(2)}) collective-permute-start(f32[24,8,256]{2,1,0:T(8,128)S(1)} %slice.60), channel_id=1, source_target_pairs={{0,1},{1,2},{2,3},{3,0},{4,5},{5,6},{6,7},{7,4},{8,9},{9,10},{10,1... | collective-permute-start | bytes 589832 | tf_op jit(solution)/shard_map/ppermute | solution.py:34
  56.8 15.3 %collective-permute-start.11 = (f32[4,32,256]{2,1,0:T(8,128)S(1)}, f32[4,32,256]{2,1,0:T(8,128)S(1)}, u32[]{:S(2)}, u32[]{:S(2)}) collective-permute-start(f32[4,32,256]{2,1,0:T(8,128)S(1)} %add.60), channel_id=1, source_target_pairs={{0,8},{4,12},{8,0},{12,4},{16,24},{20,28},{24,16},{28,20},{1,9},{5... | collective-permute-start | bytes 393224 | tf_op jit(solution)/shard_map/ppermute | solution.py:40
  68.7 5.3 %collective-permute-start.7 = (bf16[24,8,256]{2,1,0:T(8,128)(2,1)S(1)}, bf16[24,8,256]{2,1,0:T(8,128)(2,1)S(1)}, u32[]{:S(2)}, u32[]{:S(2)}) collective-permute-start(bf16[24,8,256]{2,1,0:T(8,128)(2,1)S(1)} %slice.72), channel_id=1, source_target_pairs={{0,3},{1,0},{2,1},{3,2},{4,7},{5,4},{6,5},{7,6},{8,11},{9,8},{10,9... | collective-permute-start | bytes 294920 | tf_op jit(solution)/shard_map/ppermute | solution.py:34
  72.1 5.0 %collective-permute-start.12 = (f32[4,32,256]{2,1,0:T(8,128)S(1)}, f32[4,32,256]{2,1,0:T(8,128)S(1)}, u32[]{:S(2)}, u32[]{:S(2)}) collective-permute-start(f32[4,32,256]{2,1,0:T(8,128)S(1)} %add.61), channel_id=1, source_target_pairs={{0,16},{4,20},{8,24},{12,28},{16,0},{20,4},{24,8},{28,12},{1,17},{... | collective-permute-start | bytes 393224 | tf_op jit(solution)/shard_map/ppermute | solution.py:40

commit v12 on v9

--- a/solution.py
+++ b/solution.py
@@ -76,7 +76,7 @@
             safe_ref[b, rows_at, :] = safe[b * col_pad : (b + 1) * col_pad]
         return carry
 
-    lax.fori_loop(0, rows, body, 0)
+    lax.fori_loop(0, rows, body, 0, unroll=2)
     lane = lax.broadcasted_iota(jnp.int32, (group_width, chan_count), 1) // group_width
     upstream_all = cot_ref[...].reshape(rows * col_pad, chan_count)
     out = None
@@ -116,7 +116,7 @@
             col_ref[pl.ds(start, lane_rows), :] += term
         return carry
 
-    lax.fori_loop(0, rows, body, 0)
+    lax.fori_loop(0, rows, body, 0, unroll=2)
 
 
 def local(features, obs_mask, filter_taps, band_width, mixing, cotangent):

time: 76.5 us -> 72.4 us (0.946)
  Pallas kernels: 18.9 us -> 14.9 us
    pallas_call x1, Pallas kernels: 7.45 us -> 5.19 us  [local(): pl.pallas_call(adjoint_kernel, out_shape=jax.ShapeDtypeStruct(((row_count...]
    pallas_call x1, Pallas kernels: 11.4 us -> 9.68 us  [local(): pl.pallas_call(forward_kernel, out_shape=(jax.ShapeDtypeStruct((row_count...]
  transfers between devices with their start and end apart: 13 -> 13, of which waited for: 7 -> 7; matrix products, arithmetic and copies ran while one was open for 13% -> 14% of each run, Pallas kernels for 10% -> 7%
where the time goes in v12:
time: 72.4 us; the launch traced here: 72.1 us
  starting transfers between devices  22.6 us (31%)
  waiting for transfers between devices  18 us (25%)
  Pallas kernels  14.9 us (21%)
  local copies, waits for them, and re-layouts  9.48 us (13%)
  other arithmetic  4.34 us (6%)
  matrix products  1.86 us (3%)
  between operations  1.01 us (1%)
    ppermute x4, waiting for transfers between devices, butterfly_sum(): partner = lax.ppermute(value, axis, [(i, i ^ step) for i in range(count)])  11.9 us
    pallas_call x1, Pallas kernels, local(): pl.pallas_call(forward_kernel, out_shape=(jax.ShapeDtypeStruct((row_count...  9.68 us
    ppermute x4, starting transfers between devices, butterfly_sum(): partner = lax.ppermute(value, axis, [(i, i ^ step) for i in range(count)])  9.06 us
    pallas_call x1, Pallas kernels, local(): pl.pallas_call(adjoint_kernel, out_shape=jax.ShapeDtypeStruct(((row_count...  5.19 us
    ppermute x2, waiting for transfers between devices, with_halo(): lax.ppermute(lax.slice_in_dim(block, 0, width, axis=dim), axis, backward)  4.3 us
    ppermute x2, starting transfers between devices, with_halo(): lax.ppermute(lax.slice_in_dim(block, block.shape[dim] - width, None, axis...  3.98 us
    ppermute x2, starting transfers between devices, with_halo(): lax.ppermute(lax.slice_in_dim(block, 0, width, axis=dim), axis, backward)  3.54 us
    unnamed x20, local copies, waits for them, and re-layouts  3.37 us
  transfers between devices with their start and end apart: 13, of which 7 were waited for; matrix products, arithmetic and copies ran while one was open for 14% of the time, Pallas kernels for 7%

profile of v12, /device:TPU:0, one launch (start us, length us, event | category | flops | bytes accessed | tf_op | source)
XLA Modules:
  0.0 72.1 jit_solution(227070150006031837)
XLA Ops:
  0.6 0.0 copy-start
  0.6 0.0 copy-start.5
  0.7 1.0 %convert_element_type.46 = bf16[24,45,8]{1,2,0:T(8,128)(2,1)S(1)} convert(s32[24,45,8]{1,2,0:T(8,128)} %param.7) | non-fusion elementwise | flops 8640 | bytes 51840 | tf_op jit(solution)/shard_map/convert_element_type | solution.py:132
  1.6 0.2 copy.35
  1.9 0.1 reshape.114
  2.0 0.4 fusion.6
  2.4 0.2 reshape.115
  2.6 0.0 copy-done.5
  2.6 0.0 copy-start.1
  2.6 0.0 copy-start.7
  2.6 0.1 copy_multiply_fusion
  2.8 2.4 %collective-permute-start = (bf16[1,45,264]{2,1,0:T(8,128)(2,1)S(1)}, bf16[1,45,264]{2,1,0:T(8,128)(2,1)S(1)}, u32[]{:S(2)}, u32[]{:S(2)}) collective-permute-start(bf16[1,45,264]{2,1,0:T(8,128)(2,1)S(1)} %get-tuple-element.22), channel_id=1, source_target_pairs={{0,4},{4,8},{8,12},{12,16},{16,20},{20,24},{24,28},{1,5},{5,9},{9,... | collective-permute-start | bytes 71288 | tf_op jit(solution)/shard_map/ppermute | solution.py:18
  5.2 1.3 %collective-permute-start.1 = (bf16[1,45,264]{2,1,0:T(8,128)(2,1)S(1)}, bf16[1,45,264]{2,1,0:T(8,128)(2,1)S(1)}, u32[]{:S(2)}, u32[]{:S(2)}) collective-permute-start(bf16[1,45,264]{2,1,0:T(8,128)(2,1)S(1)} %get-tuple-element.23), channel_id=1, source_target_pairs={{4,0},{8,4},{12,8},{16,12},{20,16},{24,20},{28,24},{5,1},{9,5},{13... | collective-permute-start | bytes 71288 | tf_op jit(solution)/shard_map/ppermute | solution.py:21
  6.5 0.0 copy-done
  6.5 0.1 constant_dynamic-slice_fusion
  6.6 0.2 copy.48
  6.8 0.0 copy-done.7
  6.8 0.1 compare_convert_fusion
  6.9 0.1 copy.37
  7.0 0.0 copy-start.6
  7.0 1.1 %fusion.18 = bf16[24,4,3,48,64]{4,0,3,2,1:T(8,128)(2,1)S(1)} fusion(s32[48,64]{1,0:T(8,128)S(1)} %iota_subtract_fusion, pred[48]{0:T(512)(128)(4,1)S(1)} %iota_compare_fusion.6, bf16[24,4,3,17]{3,0,2,1:T(8,128)(2,1)S(1)} %copy.48, bf16[24,17]{1,0:T(8,128)(2,1)S(1)} %constant_dynamic-slice_fusion.1), kind=kOutput, calls=%fused_computation.27 | convolution fusion | flops 30205056 | bytes 1792416 | tf_op jit(solution)/shard_map/ibae,ejp->ibajp/dot_general | solution.py:164
  8.2 0.0 copy-done.1
  8.2 0.0 collective-permute-done
  8.2 2.2 %collective-permute-done.1 = bf16[1,45,264]{2,1,0:T(8,128)(2,1)S(1)} collective-permute-done((bf16[1,45,264]{2,1,0:T(8,128)(2,1)S(1)}, bf16[1,45,264]{2,1,0:T(8,128)(2,1)S(1)}, u32[]{:S(2)}, u32[]{:S(2)}) %collective-permute-start.1) | collective-permute-done | bytes 23792 | tf_op jit(solution)/shard_map/ppermute | solution.py:21
  10.4 0.8 %pad_maximum_fusion.3 = (bf16[26,8,264]{2,1,0:T(8,128)(2,1)}, bf16[26,8,264]{2,1,0:T(8,128)(2,1)}) fusion(bf16[1,45,264]{2,1,0:T(8,128)(2,1)S(1)} %collective-permute-done.1, bf16[1,45,264]{2,1,0:T(8,128)(2,1)S(1)} %collective-permute-done, bf16[24,45,8]{2,1,0:T(8,128)(2,1)S(1)} %copy.35, bf16[24,45,256]{2,1,0:T(8,128)(2,1)S(1)} %copy_multiply_fusion), kind=kLoop, calls=%fused_computation.35 | loop fusion | flops 878592 | bytes 837408 | tf_op jit(solution)/shard_map/slice | solution.py:19
  11.2 1.6 %collective-permute-start.2 = (bf16[26,8,264]{2,1,0:T(8,128)(2,1)}, bf16[26,8,264]{2,1,0:T(8,128)(2,1)S(1)}, u32[]{:S(2)}, u32[]{:S(2)}) collective-permute-start(bf16[26,8,264]{2,1,0:T(8,128)(2,1)} %get-tuple-element.20), channel_id=1, source_target_pairs={{0,1},{1,2},{2,3},{3,0},{4,5},{5,6},{6,7},{7,4},{8,9},{9,10},{10,1... | collective-permute-start | bytes 329480 | tf_op jit(solution)/shard_map/ppermute | solution.py:18
  12.7 2.2 %collective-permute-start.3 = (bf16[26,8,264]{2,1,0:T(8,128)(2,1)}, bf16[26,8,264]{2,1,0:T(8,128)(2,1)}, u32[]{:S(2)}, u32[]{:S(2)}) collective-permute-start(bf16[26,8,264]{2,1,0:T(8,128)(2,1)} %get-tuple-element.21), channel_id=1, source_target_pairs={{1,0},{2,1},{3,2},{0,3},{5,4},{6,5},{7,6},{4,7},{9,8},{10,9},{11,1... | collective-permute-start | bytes 329480 | tf_op jit(solution)/shard_map/ppermute | solution.py:21
  15.0 0.7 multiply_bitcast_fusion
  15.7 2.6 %copy.52.t_ref = bf16[24,4,3,48,64]{4,3,2,1,0:T(8,128)(2,1)} copy(bf16[24,4,3,48,64]{4,0,3,2,1:T(8,128)(2,1)S(1)} %fusion.18) | data formatting | bytes 3538944 | tf_op jit(solution)/shard_map/ibae,ejp->ibajp/dot_general | solution.py:164
  18.3 1.4 %reshape.118.w_ref = bf16[4,256,256]{2,1,0:T(8,128)(2,1)S(1)} reshape(bf16[4,8,32,8,32]{4,3,2,1,0:T(8,128)(2,1)S(1)} %multiply_bitcast_fusion) | data formatting | bytes 1048576 | tf_op jit(solution)/shard_map/reshape | solution.py:169
  19.7 0.0 copy-start.4
  19.7 1.2 %copy.40 = bf16[24,45,256]{2,1,0:T(8,128)(2,1)S(1)} copy(bf16[24,45,256]{2,0,1:T(8,128)(2,1)} %param.11) | data formatting | bytes 1105920 | tf_op args[5]
  21.0 0.0 collective-permute-done.2
  21.0 2.1 %collective-permute-done.3 = bf16[26,8,264]{2,1,0:T(8,128)(2,1)} collective-permute-done((bf16[26,8,264]{2,1,0:T(8,128)(2,1)}, bf16[26,8,264]{2,1,0:T(8,128)(2,1)}, u32[]{:S(2)}, u32[]{:S(2)}) %collective-permute-start.3) | collective-permute-done | bytes 109856 | tf_op jit(solution)/shard_map/ppermute | solution.py:21
  23.1 1.2 %fusion.9 = bf16[26,64,264]{2,1,0:T(8,128)(2,1)S(1)} fusion(bf16[26,8,264]{2,1,0:T(8,128)(2,1)} %collective-permute-done.3, bf16[26,8,264]{2,1,0:T(8,128)(2,1)S(1)} %collective-permute-done.2, bf16[1,45,264]{2,1,0:T(8,128)(2,1)S(1)} %collective-permute-done.1, bf16[1,45,264]{2,1,0:T(8,128)(2,1)S(1)} %collective-permute-done, ...), kind=kLoop, calls=%fused_computation.15 | loop fusion | flops 8346624 | bytes 1716000 | tf_op jit(solution)/shard_map/concatenate | solution.py:22
  24.4 0.1 slice.54
  24.4 0.1 slice.53
  24.5 0.4 convolution_convert_fusion.m_ref
  24.9 9.7 %shard_map.85 = (bf16[24,45,256]{2,1,0:T(8,128)(2,1)S(1)}, f32[4,32,256]{2,1,0:T(8,128)S(1)}, bf16[4,1152,256]{2,1,0:T(8,128)(2,1)S(1)}) custom-call(bf16[1664,256]{1,0:T(8,128)(2,1)S(1)} %bitcast.28, bf16[1664,256]{1,0:T(8,128)(2,1)S(1)} %convolution_convert_fusion.m_ref, bf16[24,4,3,48,64]{4,3,2,1,0:T(8,128)(2,1)} %copy.52.t_ref, ...), custom_call_target="tpu_custom_call" | custom-call | flops 2717908992 | bytes 3407872 | tf_op jit(solution)/shard_map/pallas_call | solution.py:174
  34.6 0.2 collective-permute-start.4
  34.8 1.2 %collective-permute-done.4.order_ref = f32[4,32,256]{2,1,0:T(8,128)S(1)} collective-permute-done((f32[4,32,256]{2,1,0:T(8,128)S(1)}, f32[4,32,256]{2,1,0:T(8,128)S(1)}, u32[]{:S(2)}, u32[]{:S(2)}) %collective-permute-start.4) | collective-permute-done | bytes 131104 | tf_op jit(solution)/shard_map/ppermute | solution.py:198
  36.0 2.8 %collective-permute-start.9 = (f32[4,32,256]{2,1,0:T(8,128)S(1)}, f32[4,32,256]{2,1,0:T(8,128)S(1)}, u32[]{:S(2)}, u32[]{:S(2)}) collective-permute-start(f32[4,32,256]{2,1,0:T(8,128)S(1)} %add.58), channel_id=1, source_target_pairs={{0,8},{4,12},{8,0},{12,4},{16,24},{20,28},{24,16},{28,20},{1,9},{5... | collective-permute-start | bytes 393224 | tf_op jit(solution)/shard_map/ppermute | solution.py:49
  38.8 5.2 %shard_map.86 = f32[1664,256]{1,0:T(8,128)S(1)} custom-call(bf16[24,4,3,48,64]{4,3,2,1,0:T(8,128)(2,1)} %copy.52.t_ref, bf16[4,1152,256]{2,1,0:T(8,128)(2,1)S(1)} %get-tuple-element.7.pulled_ref, f32[4,32,256]{2,1,0:T(8,128)S(1)} %collective-permute-done.4.order_ref), custom_call_target="tpu_custom_call" | custom-call | flops 452984832 | bytes 2555904 | tf_op jit(solution)/shard_map/pallas_call | solution.py:206
  44.0 1.8 %collective-permute-start.5 = (f32[1,61,256]{2,1,0:T(8,128)S(1)}, f32[1,61,256]{2,1,0:T(8,128)S(1)}, u32[]{:S(2)}, u32[]{:S(2)}) collective-permute-start(f32[1,61,256]{2,1,0:T(8,128)S(1)} %get-tuple-element.18), channel_id=1, source_target_pairs={{0,4},{4,8},{8,12},{12,16},{16,20},{20,24},{24,28},{1,5},{5,9},{9,... | collective-permute-start | bytes 187400 | tf_op jit(solution)/shard_map/ppermute | solution.py:29
  45.8 1.3 %collective-permute-start.6 = (f32[1,61,256]{2,1,0:T(8,128)S(1)}, f32[1,61,256]{2,1,0:T(8,128)S(1)}, u32[]{:S(2)}, u32[]{:S(2)}) collective-permute-start(f32[1,61,256]{2,1,0:T(8,128)S(1)} %get-tuple-element.19), channel_id=1, source_target_pairs={{4,0},{8,4},{12,8},{16,12},{20,16},{24,20},{28,24},{5,1},{9,5},{13... | collective-permute-start | bytes 187400 | tf_op jit(solution)/shard_map/ppermute | solution.py:29
  47.1 0.0 collective-permute-done.9
  47.1 4.0 %collective-permute-start.10 = (f32[4,32,256]{2,1,0:T(8,128)S(1)}, f32[4,32,256]{2,1,0:T(8,128)S(1)}, u32[]{:S(2)}, u32[]{:S(2)}) collective-permute-start(f32[4,32,256]{2,1,0:T(8,128)S(1)} %add.59), channel_id=1, source_target_pairs={{0,16},{4,20},{8,24},{12,28},{16,0},{20,4},{24,8},{28,12},{1,17},{... | collective-permute-start | bytes 393224 | tf_op jit(solution)/shard_map/ppermute | solution.py:49
  51.1 0.0 collective-permute-done.5
  51.2 0.0 collective-permute-done.6
  51.2 0.1 fusion.7
  51.3 1.2 %collective-permute-start.8 = (f32[24,8,256]{2,1,0:T(8,128)S(1)}, f32[24,8,256]{2,1,0:T(8,128)S(1)}, u32[]{:S(2)}, u32[]{:S(2)}) collective-permute-start(f32[24,8,256]{2,1,0:T(8,128)S(1)} %slice.60), channel_id=1, source_target_pairs={{0,1},{1,2},{2,3},{3,0},{4,5},{5,6},{6,7},{7,4},{8,9},{9,10},{10,1... | collective-permute-start | bytes 589832 | tf_op jit(solution)/shard_map/ppermute | solution.py:34
  52.5 1.8 %collective-permute-done.10 = f32[4,32,256]{2,1,0:T(8,128)S(1)} collective-permute-done((f32[4,32,256]{2,1,0:T(8,128)S(1)}, f32[4,32,256]{2,1,0:T(8,128)S(1)}, u32[]{:S(2)}, u32[]{:S(2)}) %collective-permute-start.10) | collective-permute-done | bytes 131104 | tf_op jit(solution)/shard_map/ppermute | solution.py:49
  54.3 1.2 %collective-permute-start.11 = (f32[4,32,256]{2,1,0:T(8,128)S(1)}, f32[4,32,256]{2,1,0:T(8,128)S(1)}, u32[]{:S(2)}, u32[]{:S(2)}) collective-permute-start(f32[4,32,256]{2,1,0:T(8,128)S(1)} %add.60), channel_id=1, source_target_pairs={{0,1},{1,0},{2,3},{3,2},{4,5},{5,4},{6,7},{7,6},{8,9},{9,8},{10,11... | collective-permute-start | bytes 393224 | tf_op jit(solution)/shard_map/ppermute | solution.py:49
  55.5 1.6 %collective-permute-start.7 = (bf16[24,8,256]{2,1,0:T(8,128)(2,1)S(1)}, bf16[24,8,256]{2,1,0:T(8,128)(2,1)S(1)}, u32[]{:S(2)}, u32[]{:S(2)}) collective-permute-start(bf16[24,8,256]{2,1,0:T(8,128)(2,1)S(1)} %slice.72), channel_id=1, source_target_pairs={{0,3},{1,0},{2,1},{3,2},{4,7},{5,4},{6,5},{7,6},{8,11},{9,8},{10,9... | collective-permute-start | bytes 294920 | tf_op jit(solution)/shard_map/ppermute | solution.py:34
  57.1 1.0 %copy.43 = bf16[24,45,256]{2,0,1:T(8,128)(2,1)} copy(bf16[24,45,256]{2,1,0:T(8,128)(2,1)S(1)} %get-tuple-element.15) | data formatting | bytes 1105920
  58.1 5.3 %collective-permute-done.11 = f32[4,32,256]{2,1,0:T(8,128)S(1)} collective-permute-done((f32[4,32,256]{2,1,0:T(8,128)S(1)}, f32[4,32,256]{2,1,0:T(8,128)S(1)}, u32[]{:S(2)}, u32[]{:S(2)}) %collective-permute-start.11) | collective-permute-done | bytes 131104 | tf_op jit(solution)/shard_map/ppermute | solution.py:49
  63.4 1.1 %collective-permute-start.12 = (f32[4,32,256]{2,1,0:T(8,128)S(1)}, f32[4,32,256]{2,1,0:T(8,128)S(1)}, u32[]{:S(2)}, u32[]{:S(2)}) collective-permute-start(f32[4,32,256]{2,1,0:T(8,128)S(1)} %add.61), channel_id=1, source_target_pairs={{0,2},{1,3},{2,0},{3,1},{4,6},{5,7},{6,4},{7,5},{8,10},{9,11},{10,... | collective-permute-start | bytes 393224 | tf_op jit(solution)/shard_map/ppermute | solution.py:49
  64.4 0.6 collective-permute-done.7
  65.0 0.0 collective-permute-done.8
  65.0 0.2 fusion.15
  65.3 1.0 %copy.44 = bf16[24,45,256]{2,0,1:T(8,128)(2,1)} copy(bf16[24,45,256]{2,1,0:T(8,128)(2,1)S(1)} %fusion.15) | data formatting | bytes 1105920
  66.3 4.8 %collective-permute-done.12 = f32[4,32,256]{2,1,0:T(8,128)S(1)} collective-permute-done((f32[4,32,256]{2,1,0:T(8,128)S(1)}, f32[4,32,256]{2,1,0:T(8,128)S(1)}, u32[]{:S(2)}, u32[]{:S(2)}) %collective-permute-start.12) | collective-permute-done | bytes 131104 | tf_op jit(solution)/shard_map/ppermute | solution.py:49
  71.0 0.2 reshape.120
  71.2 0.9 %copy.55 = f32[4,32,8,32]{3,1,0,2:T(8,128)} copy(f32[4,32,8,32]{3,2,1,0:T(8,128)S(1)} %reshape.120) | data formatting | bytes 262144 | tf_op jit(solution)/shard_map/reshape | solution.py:204
  (23 shorter events, 0.3 us)
Async XLA Ops:
  0.6 5.9 %copy-start = (bf16[192,4,3,17]{0,1,3,2:T(4,128)(2,1)S(1)}, bf16[192,4,3,17]{0,1,3,2:T(4,128)(2,1)}, u32[]{:S(2)}) copy-start(bf16[192,4,3,17]{0,1,3,2:T(4,128)(2,1)} %param.8) | copy-start | bytes 235012
  0.6 1.9 %copy-start.5 = (bf16[24,45,256]{2,0,1:T(8,128)(2,1)S(1)}, bf16[24,45,256]{2,0,1:T(8,128)(2,1)}, u32[]{:S(2)}) copy-start(bf16[24,45,256]{2,0,1:T(8,128)(2,1)} %param.6) | copy-start | bytes 1658884
  1.9 8.5 %copy-start.3 = (bf16[24,45,8]{2,1,0:T(8,128)(2,1)}, bf16[24,45,8]{2,1,0:T(8,128)(2,1)S(1)}, u32[]{:S(2)}) copy-start(bf16[24,45,8]{2,1,0:T(8,128)(2,1)S(1)} %copy.35) | copy-start | bytes 51844
  2.6 5.6 %copy-start.1 = (bf16[24,45,256]{2,1,0:T(8,128)(2,1)}, bf16[24,45,256]{2,1,0:T(8,128)(2,1)S(1)}, u32[]{:S(2)}) copy-start(bf16[24,45,256]{2,1,0:T(8,128)(2,1)S(1)} %reshape.115) | copy-start | bytes 1658884
  2.6 4.2 %copy-start.7 = (s32[192]{0:T(256)S(1)}, s32[192]{0:T(256)}, u32[]{:S(2)}) copy-start(s32[192]{0:T(256)} %param.9) | copy-start | bytes 2308
  2.8 5.4 %collective-permute-start = (bf16[1,45,264]{2,1,0:T(8,128)(2,1)S(1)}, bf16[1,45,264]{2,1,0:T(8,128)(2,1)S(1)}, u32[]{:S(2)}, u32[]{:S(2)}) collective-permute-start(bf16[1,45,264]{2,1,0:T(8,128)(2,1)S(1)} %get-tuple-element.22), channel_id=1, source_target_pairs={{0,4},{4,8},{8,12},{12,16},{16,20},{20,24},{24,28},{1,5},{5,9},{9,... | collective-permute-start | bytes 71288 | tf_op jit(solution)/shard_map/ppermute | solution.py:18
  5.2 5.2 %collective-permute-start.1 = (bf16[1,45,264]{2,1,0:T(8,128)(2,1)S(1)}, bf16[1,45,264]{2,1,0:T(8,128)(2,1)S(1)}, u32[]{:S(2)}, u32[]{:S(2)}) collective-permute-start(bf16[1,45,264]{2,1,0:T(8,128)(2,1)S(1)} %get-tuple-element.23), channel_id=1, source_target_pairs={{4,0},{8,4},{12,8},{16,12},{20,16},{24,20},{28,24},{5,1},{9,5},{13... | collective-permute-start | bytes 71288 | tf_op jit(solution)/shard_map/ppermute | solution.py:21
  7.0 8.0 %copy-start.6 = (bf16[8,4,32,32]{3,2,1,0:T(8,128)(2,1)S(1)}, bf16[8,4,32,32]{3,2,1,0:T(8,128)(2,1)}, u32[]{:S(2)}) copy-start(bf16[8,4,32,32]{3,2,1,0:T(8,128)(2,1)} %param.10) | copy-start | bytes 196612
  11.2 9.8 %collective-permute-start.2 = (bf16[26,8,264]{2,1,0:T(8,128)(2,1)}, bf16[26,8,264]{2,1,0:T(8,128)(2,1)S(1)}, u32[]{:S(2)}, u32[]{:S(2)}) collective-permute-start(bf16[26,8,264]{2,1,0:T(8,128)(2,1)} %get-tuple-element.20), channel_id=1, source_target_pairs={{0,1},{1,2},{2,3},{3,0},{4,5},{5,6},{6,7},{7,4},{8,9},{9,10},{10,1... | collective-permute-start | bytes 329480 | tf_op jit(solution)/shard_map/ppermute | solution.py:18
  12.7 10.4 %collective-permute-start.3 = (bf16[26,8,264]{2,1,0:T(8,128)(2,1)}, bf16[26,8,264]{2,1,0:T(8,128)(2,1)}, u32[]{:S(2)}, u32[]{:S(2)}) collective-permute-start(bf16[26,8,264]{2,1,0:T(8,128)(2,1)} %get-tuple-element.21), channel_id=1, source_target_pairs={{1,0},{2,1},{3,2},{0,3},{5,4},{6,5},{7,6},{4,7},{9,8},{10,9},{11,1... | collective-permute-start | bytes 329480 | tf_op jit(solution)/shard_map/ppermute | solution.py:21
  19.7 3.4 %copy-start.4 = (bf16[24,45,8]{2,1,0:T(8,128)(2,1)S(1)}, bf16[24,45,8]{2,1,0:T(8,128)(2,1)}, u32[]{:S(2)}) copy-start(bf16[24,45,8]{2,1,0:T(8,128)(2,1)} %copy-done.3) | copy-start | bytes 51844
  34.6 1.4 %collective-permute-start.4 = (f32[4,32,256]{2,1,0:T(8,128)S(1)}, f32[4,32,256]{2,1,0:T(8,128)S(1)}, u32[]{:S(2)}, u32[]{:S(2)}) collective-permute-start(f32[4,32,256]{2,1,0:T(8,128)S(1)} %get-tuple-element.8), channel_id=1, source_target_pairs={{0,4},{4,0},{8,12},{12,8},{16,20},{20,16},{24,28},{28,24},{1,5},{5... | collective-permute-start | bytes 393224 | tf_op jit(solution)/shard_map/ppermute | solution.py:198
  36.0 11.1 %collective-permute-start.9 = (f32[4,32,256]{2,1,0:T(8,128)S(1)}, f32[4,32,256]{2,1,0:T(8,128)S(1)}, u32[]{:S(2)}, u32[]{:S(2)}) collective-permute-start(f32[4,32,256]{2,1,0:T(8,128)S(1)} %add.58), channel_id=1, source_target_pairs={{0,8},{4,12},{8,0},{12,4},{16,24},{20,28},{24,16},{28,20},{1,9},{5... | collective-permute-start | bytes 393224 | tf_op jit(solution)/shard_map/ppermute | solution.py:49
  44.0 7.2 %collective-permute-start.5 = (f32[1,61,256]{2,1,0:T(8,128)S(1)}, f32[1,61,256]{2,1,0:T(8,128)S(1)}, u32[]{:S(2)}, u32[]{:S(2)}) collective-permute-start(f32[1,61,256]{2,1,0:T(8,128)S(1)} %get-tuple-element.18), channel_id=1, source_target_pairs={{0,4},{4,8},{8,12},{12,16},{16,20},{20,24},{24,28},{1,5},{5,9},{9,... | collective-permute-start | bytes 187400 | tf_op jit(solution)/shard_map/ppermute | solution.py:29
  45.8 5.4 %collective-permute-start.6 = (f32[1,61,256]{2,1,0:T(8,128)S(1)}, f32[1,61,256]{2,1,0:T(8,128)S(1)}, u32[]{:S(2)}, u32[]{:S(2)}) collective-permute-start(f32[1,61,256]{2,1,0:T(8,128)S(1)} %get-tuple-element.19), channel_id=1, source_target_pairs={{4,0},{8,4},{12,8},{16,12},{20,16},{24,20},{28,24},{5,1},{9,5},{13... | collective-permute-start | bytes 187400 | tf_op jit(solution)/shard_map/ppermute | solution.py:29
  47.1 7.2 %collective-permute-start.10 = (f32[4,32,256]{2,1,0:T(8,128)S(1)}, f32[4,32,256]{2,1,0:T(8,128)S(1)}, u32[]{:S(2)}, u32[]{:S(2)}) collective-permute-start(f32[4,32,256]{2,1,0:T(8,128)S(1)} %add.59), channel_id=1, source_target_pairs={{0,16},{4,20},{8,24},{12,28},{16,0},{20,4},{24,8},{28,12},{1,17},{... | collective-permute-start | bytes 393224 | tf_op jit(solution)/shard_map/ppermute | solution.py:49
  51.3 13.8 %copy-start.2 = (bf16[24,45,256]{2,1,0:T(8,128)(2,1)S(1)}, bf16[24,45,256]{2,1,0:T(8,128)(2,1)}, u32[]{:S(2)}) copy-start(bf16[24,45,256]{2,1,0:T(8,128)(2,1)} %copy-done.1) | copy-start | bytes 1658884
  51.3 13.7 %collective-permute-start.8 = (f32[24,8,256]{2,1,0:T(8,128)S(1)}, f32[24,8,256]{2,1,0:T(8,128)S(1)}, u32[]{:S(2)}, u32[]{:S(2)}) collective-permute-start(f32[24,8,256]{2,1,0:T(8,128)S(1)} %slice.60), channel_id=1, source_target_pairs={{0,1},{1,2},{2,3},{3,0},{4,5},{5,6},{6,7},{7,4},{8,9},{9,10},{10,1... | collective-permute-start | bytes 589832 | tf_op jit(solution)/shard_map/ppermute | solution.py:34
  54.3 9.0 %collective-permute-start.11 = (f32[4,32,256]{2,1,0:T(8,128)S(1)}, f32[4,32,256]{2,1,0:T(8,128)S(1)}, u32[]{:S(2)}, u32[]{:S(2)}) collective-permute-start(f32[4,32,256]{2,1,0:T(8,128)S(1)} %add.60), channel_id=1, source_target_pairs={{0,1},{1,0},{2,3},{3,2},{4,5},{5,4},{6,7},{7,6},{8,9},{9,8},{10,11... | collective-permute-start | bytes 393224 | tf_op jit(solution)/shard_map/ppermute | solution.py:49
  55.5 9.5 %collective-permute-start.7 = (bf16[24,8,256]{2,1,0:T(8,128)(2,1)S(1)}, bf16[24,8,256]{2,1,0:T(8,128)(2,1)S(1)}, u32[]{:S(2)}, u32[]{:S(2)}) collective-permute-start(bf16[24,8,256]{2,1,0:T(8,128)(2,1)S(1)} %slice.72), channel_id=1, source_target_pairs={{0,3},{1,0},{2,1},{3,2},{4,7},{5,4},{6,5},{7,6},{8,11},{9,8},{10,9... | collective-permute-start | bytes 294920 | tf_op jit(solution)/shard_map/ppermute | solution.py:34
  63.4 7.7 %collective-permute-start.12 = (f32[4,32,256]{2,1,0:T(8,128)S(1)}, f32[4,32,256]{2,1,0:T(8,128)S(1)}, u32[]{:S(2)}, u32[]{:S(2)}) collective-permute-start(f32[4,32,256]{2,1,0:T(8,128)S(1)} %add.61), channel_id=1, source_target_pairs={{0,2},{1,3},{2,0},{3,1},{4,6},{5,7},{6,4},{7,5},{8,10},{9,11},{10,... | collective-permute-start | bytes 393224 | tf_op jit(solution)/shard_map/ppermute | solution.py:49

commit v13 on v12

--- a/solution.py
+++ b/solution.py
@@ -76,7 +76,7 @@
             safe_ref[b, rows_at, :] = safe[b * col_pad : (b + 1) * col_pad]
         return carry
 
-    lax.fori_loop(0, rows, body, 0, unroll=2)
+    lax.fori_loop(0, rows, body, 0, unroll=4)
     lane = lax.broadcasted_iota(jnp.int32, (group_width, chan_count), 1) // group_width
     upstream_all = cot_ref[...].reshape(rows * col_pad, chan_count)
     out = None
@@ -116,7 +116,7 @@
             col_ref[pl.ds(start, lane_rows), :] += term
         return carry
 
-    lax.fori_loop(0, rows, body, 0, unroll=2)
+    lax.fori_loop(0, rows, body, 0, unroll=4)
 
 
 def local(features, obs_mask, filter_taps, band_width, mixing, cotangent):

time: 72.4 us -> 70.5 us (0.974)
  Pallas kernels: 14.9 us -> 12.9 us
    pallas_call x1, Pallas kernels: 5.19 us -> 4.13 us  [local(): pl.pallas_call(adjoint_kernel, out_shape=jax.ShapeDtypeStruct(((row_count...]
    pallas_call x1, Pallas kernels: 9.68 us -> 8.77 us  [local(): pl.pallas_call(forward_kernel, out_shape=(jax.ShapeDtypeStruct((row_count...]
  transfers between devices with their start and end apart: 13 -> 13, of which waited for: 7 -> 7; matrix products, arithmetic and copies ran while one was open for 14% -> 14% of each run, Pallas kernels for 7% -> 6%
where the time goes in v13:
time: 70.5 us; the launch traced here: 70.1 us
  starting transfers between devices  22.6 us (32%)
  waiting for transfers between devices  18 us (26%)
  Pallas kernels  12.9 us (18%)
  local copies, waits for them, and re-layouts  9.48 us (13%)
  other arithmetic  4.34 us (6%)
  matrix products  1.86 us (3%)
  between operations  1.01 us (1%)
    ppermute x4, waiting for transfers between devices, butterfly_sum(): partner = lax.ppermute(value, axis, [(i, i ^ step) for i in range(count)])  11.9 us
    ppermute x4, starting transfers between devices, butterfly_sum(): partner = lax.ppermute(value, axis, [(i, i ^ step) for i in range(count)])  9.06 us
    pallas_call x1, Pallas kernels, local(): pl.pallas_call(forward_kernel, out_shape=(jax.ShapeDtypeStruct((row_count...  8.77 us
    ppermute x2, waiting for transfers between devices, with_halo(): lax.ppermute(lax.slice_in_dim(block, 0, width, axis=dim), axis, backward)  4.3 us
    pallas_call x1, Pallas kernels, local(): pl.pallas_call(adjoint_kernel, out_shape=jax.ShapeDtypeStruct(((row_count...  4.13 us
    ppermute x2, starting transfers between devices, with_halo(): lax.ppermute(lax.slice_in_dim(block, block.shape[dim] - width, None, axis...  3.98 us
    ppermute x2, starting transfers between devices, with_halo(): lax.ppermute(lax.slice_in_dim(block, 0, width, axis=dim), axis, backward)  3.54 us
    unnamed x20, local copies, waits for them, and re-layouts  3.37 us
  transfers between devices with their start and end apart: 13, of which 7 were waited for; matrix products, arithmetic and copies ran while one was open for 14% of the time, Pallas kernels for 6%

profile of v13, /device:TPU:0, one launch (start us, length us, event | category | flops | bytes accessed | tf_op | source)
XLA Modules:
  0.0 70.1 jit_solution(4238496413858959491)
XLA Ops:
  0.6 0.0 copy-start
  0.6 0.0 copy-start.5
  0.7 1.0 %convert_element_type.46 = bf16[24,45,8]{1,2,0:T(8,128)(2,1)S(1)} convert(s32[24,45,8]{1,2,0:T(8,128)} %param.7) | non-fusion elementwise | flops 8640 | bytes 51840 | tf_op jit(solution)/shard_map/convert_element_type | solution.py:132
  1.6 0.2 copy.35
  1.9 0.1 reshape.114
  2.0 0.4 fusion.6
  2.4 0.2 reshape.115
  2.6 0.0 copy-done.5
  2.6 0.0 copy-start.1
  2.6 0.0 copy-start.7
  2.6 0.1 copy_multiply_fusion
  2.8 2.4 %collective-permute-start = (bf16[1,45,264]{2,1,0:T(8,128)(2,1)S(1)}, bf16[1,45,264]{2,1,0:T(8,128)(2,1)S(1)}, u32[]{:S(2)}, u32[]{:S(2)}) collective-permute-start(bf16[1,45,264]{2,1,0:T(8,128)(2,1)S(1)} %get-tuple-element.22), channel_id=1, source_target_pairs={{0,4},{4,8},{8,12},{12,16},{16,20},{20,24},{24,28},{1,5},{5,9},{9,... | collective-permute-start | bytes 71288 | tf_op jit(solution)/shard_map/ppermute | solution.py:18
  5.2 1.3 %collective-permute-start.1 = (bf16[1,45,264]{2,1,0:T(8,128)(2,1)S(1)}, bf16[1,45,264]{2,1,0:T(8,128)(2,1)S(1)}, u32[]{:S(2)}, u32[]{:S(2)}) collective-permute-start(bf16[1,45,264]{2,1,0:T(8,128)(2,1)S(1)} %get-tuple-element.23), channel_id=1, source_target_pairs={{4,0},{8,4},{12,8},{16,12},{20,16},{24,20},{28,24},{5,1},{9,5},{13... | collective-permute-start | bytes 71288 | tf_op jit(solution)/shard_map/ppermute | solution.py:21
  6.5 0.0 copy-done
  6.5 0.1 constant_dynamic-slice_fusion
  6.6 0.2 copy.48
  6.8 0.0 copy-done.7
  6.8 0.1 compare_convert_fusion
  6.9 0.1 copy.37
  7.0 0.0 copy-start.6
  7.0 1.1 %fusion.18 = bf16[24,4,3,48,64]{4,0,3,2,1:T(8,128)(2,1)S(1)} fusion(s32[48,64]{1,0:T(8,128)S(1)} %iota_subtract_fusion, pred[48]{0:T(512)(128)(4,1)S(1)} %iota_compare_fusion.6, bf16[24,4,3,17]{3,0,2,1:T(8,128)(2,1)S(1)} %copy.48, bf16[24,17]{1,0:T(8,128)(2,1)S(1)} %constant_dynamic-slice_fusion.1), kind=kOutput, calls=%fused_computation.27 | convolution fusion | flops 30205056 | bytes 1792416 | tf_op jit(solution)/shard_map/ibae,ejp->ibajp/dot_general | solution.py:164
  8.2 0.0 copy-done.1
  8.2 0.0 collective-permute-done
  8.2 2.2 %collective-permute-done.1 = bf16[1,45,264]{2,1,0:T(8,128)(2,1)S(1)} collective-permute-done((bf16[1,45,264]{2,1,0:T(8,128)(2,1)S(1)}, bf16[1,45,264]{2,1,0:T(8,128)(2,1)S(1)}, u32[]{:S(2)}, u32[]{:S(2)}) %collective-permute-start.1) | collective-permute-done | bytes 23792 | tf_op jit(solution)/shard_map/ppermute | solution.py:21
  10.4 0.8 %pad_maximum_fusion.3 = (bf16[26,8,264]{2,1,0:T(8,128)(2,1)}, bf16[26,8,264]{2,1,0:T(8,128)(2,1)}) fusion(bf16[1,45,264]{2,1,0:T(8,128)(2,1)S(1)} %collective-permute-done.1, bf16[1,45,264]{2,1,0:T(8,128)(2,1)S(1)} %collective-permute-done, bf16[24,45,8]{2,1,0:T(8,128)(2,1)S(1)} %copy.35, bf16[24,45,256]{2,1,0:T(8,128)(2,1)S(1)} %copy_multiply_fusion), kind=kLoop, calls=%fused_computation.35 | loop fusion | flops 878592 | bytes 837408 | tf_op jit(solution)/shard_map/slice | solution.py:19
  11.2 1.6 %collective-permute-start.2 = (bf16[26,8,264]{2,1,0:T(8,128)(2,1)}, bf16[26,8,264]{2,1,0:T(8,128)(2,1)S(1)}, u32[]{:S(2)}, u32[]{:S(2)}) collective-permute-start(bf16[26,8,264]{2,1,0:T(8,128)(2,1)} %get-tuple-element.20), channel_id=1, source_target_pairs={{0,1},{1,2},{2,3},{3,0},{4,5},{5,6},{6,7},{7,4},{8,9},{9,10},{10,1... | collective-permute-start | bytes 329480 | tf_op jit(solution)/shard_map/ppermute | solution.py:18
  12.7 2.2 %collective-permute-start.3 = (bf16[26,8,264]{2,1,0:T(8,128)(2,1)}, bf16[26,8,264]{2,1,0:T(8,128)(2,1)}, u32[]{:S(2)}, u32[]{:S(2)}) collective-permute-start(bf16[26,8,264]{2,1,0:T(8,128)(2,1)} %get-tuple-element.21), channel_id=1, source_target_pairs={{1,0},{2,1},{3,2},{0,3},{5,4},{6,5},{7,6},{4,7},{9,8},{10,9},{11,1... | collective-permute-start | bytes 329480 | tf_op jit(solution)/shard_map/ppermute | solution.py:21
  15.0 0.7 multiply_bitcast_fusion
  15.7 2.6 %copy.52.t_ref = bf16[24,4,3,48,64]{4,3,2,1,0:T(8,128)(2,1)} copy(bf16[24,4,3,48,64]{4,0,3,2,1:T(8,128)(2,1)S(1)} %fusion.18) | data formatting | bytes 3538944 | tf_op jit(solution)/shard_map/ibae,ejp->ibajp/dot_general | solution.py:164
  18.3 1.4 %reshape.118.w_ref = bf16[4,256,256]{2,1,0:T(8,128)(2,1)S(1)} reshape(bf16[4,8,32,8,32]{4,3,2,1,0:T(8,128)(2,1)S(1)} %multiply_bitcast_fusion) | data formatting | bytes 1048576 | tf_op jit(solution)/shard_map/reshape | solution.py:169
  19.7 0.0 copy-start.4
  19.7 1.2 %copy.40 = bf16[24,45,256]{2,1,0:T(8,128)(2,1)S(1)} copy(bf16[24,45,256]{2,0,1:T(8,128)(2,1)} %param.11) | data formatting | bytes 1105920 | tf_op args[5]
  21.0 0.0 collective-permute-done.2
  21.0 2.1 %collective-permute-done.3 = bf16[26,8,264]{2,1,0:T(8,128)(2,1)} collective-permute-done((bf16[26,8,264]{2,1,0:T(8,128)(2,1)}, bf16[26,8,264]{2,1,0:T(8,128)(2,1)}, u32[]{:S(2)}, u32[]{:S(2)}) %collective-permute-start.3) | collective-permute-done | bytes 109856 | tf_op jit(solution)/shard_map/ppermute | solution.py:21
  23.1 1.2 %fusion.9 = bf16[26,64,264]{2,1,0:T(8,128)(2,1)S(1)} fusion(bf16[26,8,264]{2,1,0:T(8,128)(2,1)} %collective-permute-done.3, bf16[26,8,264]{2,1,0:T(8,128)(2,1)S(1)} %collective-permute-done.2, bf16[1,45,264]{2,1,0:T(8,128)(2,1)S(1)} %collective-permute-done.1, bf16[1,45,264]{2,1,0:T(8,128)(2,1)S(1)} %collective-permute-done, ...), kind=kLoop, calls=%fused_computation.15 | loop fusion | flops 8346624 | bytes 1716000 | tf_op jit(solution)/shard_map/concatenate | solution.py:22
  24.4 0.1 slice.54
  24.4 0.1 slice.53
  24.5 0.4 convolution_convert_fusion.m_ref
  24.9 8.8 %shard_map.85 = (bf16[24,45,256]{2,1,0:T(8,128)(2,1)S(1)}, f32[4,32,256]{2,1,0:T(8,128)S(1)}, bf16[4,1152,256]{2,1,0:T(8,128)(2,1)S(1)}) custom-call(bf16[1664,256]{1,0:T(8,128)(2,1)S(1)} %bitcast.28, bf16[1664,256]{1,0:T(8,128)(2,1)S(1)} %convolution_convert_fusion.m_ref, bf16[24,4,3,48,64]{4,3,2,1,0:T(8,128)(2,1)} %copy.52.t_ref, ...), custom_call_target="tpu_custom_call" | custom-call | flops 2717908992 | bytes 3407872 | tf_op jit(solution)/shard_map/pallas_call | solution.py:174
  33.7 0.2 collective-permute-start.4
  33.9 1.2 %collective-permute-done.4.order_ref = f32[4,32,256]{2,1,0:T(8,128)S(1)} collective-permute-done((f32[4,32,256]{2,1,0:T(8,128)S(1)}, f32[4,32,256]{2,1,0:T(8,128)S(1)}, u32[]{:S(2)}, u32[]{:S(2)}) %collective-permute-start.4) | collective-permute-done | bytes 131104 | tf_op jit(solution)/shard_map/ppermute | solution.py:198
  35.1 2.8 %collective-permute-start.9 = (f32[4,32,256]{2,1,0:T(8,128)S(1)}, f32[4,32,256]{2,1,0:T(8,128)S(1)}, u32[]{:S(2)}, u32[]{:S(2)}) collective-permute-start(f32[4,32,256]{2,1,0:T(8,128)S(1)} %add.58), channel_id=1, source_target_pairs={{0,8},{4,12},{8,0},{12,4},{16,24},{20,28},{24,16},{28,20},{1,9},{5... | collective-permute-start | bytes 393224 | tf_op jit(solution)/shard_map/ppermute | solution.py:49
  37.9 4.1 %shard_map.86 = f32[1664,256]{1,0:T(8,128)S(1)} custom-call(bf16[24,4,3,48,64]{4,3,2,1,0:T(8,128)(2,1)} %copy.52.t_ref, bf16[4,1152,256]{2,1,0:T(8,128)(2,1)S(1)} %get-tuple-element.7.pulled_ref, f32[4,32,256]{2,1,0:T(8,128)S(1)} %collective-permute-done.4.order_ref), custom_call_target="tpu_custom_call" | custom-call | flops 452984832 | bytes 2555904 | tf_op jit(solution)/shard_map/pallas_call | solution.py:206
  42.0 1.8 %collective-permute-start.5 = (f32[1,61,256]{2,1,0:T(8,128)S(1)}, f32[1,61,256]{2,1,0:T(8,128)S(1)}, u32[]{:S(2)}, u32[]{:S(2)}) collective-permute-start(f32[1,61,256]{2,1,0:T(8,128)S(1)} %get-tuple-element.18), channel_id=1, source_target_pairs={{0,4},{4,8},{8,12},{12,16},{16,20},{20,24},{24,28},{1,5},{5,9},{9,... | collective-permute-start | bytes 187400 | tf_op jit(solution)/shard_map/ppermute | solution.py:29
  43.8 1.3 %collective-permute-start.6 = (f32[1,61,256]{2,1,0:T(8,128)S(1)}, f32[1,61,256]{2,1,0:T(8,128)S(1)}, u32[]{:S(2)}, u32[]{:S(2)}) collective-permute-start(f32[1,61,256]{2,1,0:T(8,128)S(1)} %get-tuple-element.19), channel_id=1, source_target_pairs={{4,0},{8,4},{12,8},{16,12},{20,16},{24,20},{28,24},{5,1},{9,5},{13... | collective-permute-start | bytes 187400 | tf_op jit(solution)/shard_map/ppermute | solution.py:29
  45.1 0.0 collective-permute-done.9
  45.2 4.0 %collective-permute-start.10 = (f32[4,32,256]{2,1,0:T(8,128)S(1)}, f32[4,32,256]{2,1,0:T(8,128)S(1)}, u32[]{:S(2)}, u32[]{:S(2)}) collective-permute-start(f32[4,32,256]{2,1,0:T(8,128)S(1)} %add.59), channel_id=1, source_target_pairs={{0,16},{4,20},{8,24},{12,28},{16,0},{20,4},{24,8},{28,12},{1,17},{... | collective-permute-start | bytes 393224 | tf_op jit(solution)/shard_map/ppermute | solution.py:49
  49.2 0.0 collective-permute-done.5
  49.2 0.0 collective-permute-done.6
  49.2 0.1 fusion.7
  49.3 1.2 %collective-permute-start.8 = (f32[24,8,256]{2,1,0:T(8,128)S(1)}, f32[24,8,256]{2,1,0:T(8,128)S(1)}, u32[]{:S(2)}, u32[]{:S(2)}) collective-permute-start(f32[24,8,256]{2,1,0:T(8,128)S(1)} %slice.60), channel_id=1, source_target_pairs={{0,1},{1,2},{2,3},{3,0},{4,5},{5,6},{6,7},{7,4},{8,9},{9,10},{10,1... | collective-permute-start | bytes 589832 | tf_op jit(solution)/shard_map/ppermute | solution.py:34
  50.5 1.8 %collective-permute-done.10 = f32[4,32,256]{2,1,0:T(8,128)S(1)} collective-permute-done((f32[4,32,256]{2,1,0:T(8,128)S(1)}, f32[4,32,256]{2,1,0:T(8,128)S(1)}, u32[]{:S(2)}, u32[]{:S(2)}) %collective-permute-start.10) | collective-permute-done | bytes 131104 | tf_op jit(solution)/shard_map/ppermute | solution.py:49
  52.4 1.2 %collective-permute-start.11 = (f32[4,32,256]{2,1,0:T(8,128)S(1)}, f32[4,32,256]{2,1,0:T(8,128)S(1)}, u32[]{:S(2)}, u32[]{:S(2)}) collective-permute-start(f32[4,32,256]{2,1,0:T(8,128)S(1)} %add.60), channel_id=1, source_target_pairs={{0,1},{1,0},{2,3},{3,2},{4,5},{5,4},{6,7},{7,6},{8,9},{9,8},{10,11... | collective-permute-start | bytes 393224 | tf_op jit(solution)/shard_map/ppermute | solution.py:49
  53.6 1.6 %collective-permute-start.7 = (bf16[24,8,256]{2,1,0:T(8,128)(2,1)S(1)}, bf16[24,8,256]{2,1,0:T(8,128)(2,1)S(1)}, u32[]{:S(2)}, u32[]{:S(2)}) collective-permute-start(bf16[24,8,256]{2,1,0:T(8,128)(2,1)S(1)} %slice.72), channel_id=1, source_target_pairs={{0,3},{1,0},{2,1},{3,2},{4,7},{5,4},{6,5},{7,6},{8,11},{9,8},{10,9... | collective-permute-start | bytes 294920 | tf_op jit(solution)/shard_map/ppermute | solution.py:34
  55.1 1.0 %copy.43 = bf16[24,45,256]{2,0,1:T(8,128)(2,1)} copy(bf16[24,45,256]{2,1,0:T(8,128)(2,1)S(1)} %get-tuple-element.15) | data formatting | bytes 1105920
  56.1 5.3 %collective-permute-done.11 = f32[4,32,256]{2,1,0:T(8,128)S(1)} collective-permute-done((f32[4,32,256]{2,1,0:T(8,128)S(1)}, f32[4,32,256]{2,1,0:T(8,128)S(1)}, u32[]{:S(2)}, u32[]{:S(2)}) %collective-permute-start.11) | collective-permute-done | bytes 131104 | tf_op jit(solution)/shard_map/ppermute | solution.py:49
  61.4 1.1 %collective-permute-start.12 = (f32[4,32,256]{2,1,0:T(8,128)S(1)}, f32[4,32,256]{2,1,0:T(8,128)S(1)}, u32[]{:S(2)}, u32[]{:S(2)}) collective-permute-start(f32[4,32,256]{2,1,0:T(8,128)S(1)} %add.61), channel_id=1, source_target_pairs={{0,2},{1,3},{2,0},{3,1},{4,6},{5,7},{6,4},{7,5},{8,10},{9,11},{10,... | collective-permute-start | bytes 393224 | tf_op jit(solution)/shard_map/ppermute | solution.py:49
  62.5 0.6 collective-permute-done.7
  63.1 0.0 collective-permute-done.8
  63.1 0.2 fusion.15
  63.3 1.0 %copy.44 = bf16[24,45,256]{2,0,1:T(8,128)(2,1)} copy(bf16[24,45,256]{2,1,0:T(8,128)(2,1)S(1)} %fusion.15) | data formatting | bytes 1105920
  64.3 4.8 %collective-permute-done.12 = f32[4,32,256]{2,1,0:T(8,128)S(1)} collective-permute-done((f32[4,32,256]{2,1,0:T(8,128)S(1)}, f32[4,32,256]{2,1,0:T(8,128)S(1)}, u32[]{:S(2)}, u32[]{:S(2)}) %collective-permute-start.12) | collective-permute-done | bytes 131104 | tf_op jit(solution)/shard_map/ppermute | solution.py:49
  69.1 0.2 reshape.120
  69.2 0.9 %copy.55 = f32[4,32,8,32]{3,1,0,2:T(8,128)} copy(f32[4,32,8,32]{3,2,1,0:T(8,128)S(1)} %reshape.120) | data formatting | bytes 262144 | tf_op jit(solution)/shard_map/reshape | solution.py:204
  (23 shorter events, 0.3 us)
Async XLA Ops:
  0.6 5.9 %copy-start = (bf16[192,4,3,17]{0,1,3,2:T(4,128)(2,1)S(1)}, bf16[192,4,3,17]{0,1,3,2:T(4,128)(2,1)}, u32[]{:S(2)}) copy-start(bf16[192,4,3,17]{0,1,3,2:T(4,128)(2,1)} %param.8) | copy-start | bytes 235012
  0.6 1.9 %copy-start.5 = (bf16[24,45,256]{2,0,1:T(8,128)(2,1)S(1)}, bf16[24,45,256]{2,0,1:T(8,128)(2,1)}, u32[]{:S(2)}) copy-start(bf16[24,45,256]{2,0,1:T(8,128)(2,1)} %param.6) | copy-start | bytes 1658884
  1.9 8.5 %copy-start.3 = (bf16[24,45,8]{2,1,0:T(8,128)(2,1)}, bf16[24,45,8]{2,1,0:T(8,128)(2,1)S(1)}, u32[]{:S(2)}) copy-start(bf16[24,45,8]{2,1,0:T(8,128)(2,1)S(1)} %copy.35) | copy-start | bytes 51844
  2.6 5.6 %copy-start.1 = (bf16[24,45,256]{2,1,0:T(8,128)(2,1)}, bf16[24,45,256]{2,1,0:T(8,128)(2,1)S(1)}, u32[]{:S(2)}) copy-start(bf16[24,45,256]{2,1,0:T(8,128)(2,1)S(1)} %reshape.115) | copy-start | bytes 1658884
  2.6 4.2 %copy-start.7 = (s32[192]{0:T(256)S(1)}, s32[192]{0:T(256)}, u32[]{:S(2)}) copy-start(s32[192]{0:T(256)} %param.9) | copy-start | bytes 2308
  2.8 5.4 %collective-permute-start = (bf16[1,45,264]{2,1,0:T(8,128)(2,1)S(1)}, bf16[1,45,264]{2,1,0:T(8,128)(2,1)S(1)}, u32[]{:S(2)}, u32[]{:S(2)}) collective-permute-start(bf16[1,45,264]{2,1,0:T(8,128)(2,1)S(1)} %get-tuple-element.22), channel_id=1, source_target_pairs={{0,4},{4,8},{8,12},{12,16},{16,20},{20,24},{24,28},{1,5},{5,9},{9,... | collective-permute-start | bytes 71288 | tf_op jit(solution)/shard_map/ppermute | solution.py:18
  5.2 5.2 %collective-permute-start.1 = (bf16[1,45,264]{2,1,0:T(8,128)(2,1)S(1)}, bf16[1,45,264]{2,1,0:T(8,128)(2,1)S(1)}, u32[]{:S(2)}, u32[]{:S(2)}) collective-permute-start(bf16[1,45,264]{2,1,0:T(8,128)(2,1)S(1)} %get-tuple-element.23), channel_id=1, source_target_pairs={{4,0},{8,4},{12,8},{16,12},{20,16},{24,20},{28,24},{5,1},{9,5},{13... | collective-permute-start | bytes 71288 | tf_op jit(solution)/shard_map/ppermute | solution.py:21
  7.0 8.0 %copy-start.6 = (bf16[8,4,32,32]{3,2,1,0:T(8,128)(2,1)S(1)}, bf16[8,4,32,32]{3,2,1,0:T(8,128)(2,1)}, u32[]{:S(2)}) copy-start(bf16[8,4,32,32]{3,2,1,0:T(8,128)(2,1)} %param.10) | copy-start | bytes 196612
  11.2 9.8 %collective-permute-start.2 = (bf16[26,8,264]{2,1,0:T(8,128)(2,1)}, bf16[26,8,264]{2,1,0:T(8,128)(2,1)S(1)}, u32[]{:S(2)}, u32[]{:S(2)}) collective-permute-start(bf16[26,8,264]{2,1,0:T(8,128)(2,1)} %get-tuple-element.20), channel_id=1, source_target_pairs={{0,1},{1,2},{2,3},{3,0},{4,5},{5,6},{6,7},{7,4},{8,9},{9,10},{10,1... | collective-permute-start | bytes 329480 | tf_op jit(solution)/shard_map/ppermute | solution.py:18
  12.7 10.4 %collective-permute-start.3 = (bf16[26,8,264]{2,1,0:T(8,128)(2,1)}, bf16[26,8,264]{2,1,0:T(8,128)(2,1)}, u32[]{:S(2)}, u32[]{:S(2)}) collective-permute-start(bf16[26,8,264]{2,1,0:T(8,128)(2,1)} %get-tuple-element.21), channel_id=1, source_target_pairs={{1,0},{2,1},{3,2},{0,3},{5,4},{6,5},{7,6},{4,7},{9,8},{10,9},{11,1... | collective-permute-start | bytes 329480 | tf_op jit(solution)/shard_map/ppermute | solution.py:21
  19.7 3.4 %copy-start.4 = (bf16[24,45,8]{2,1,0:T(8,128)(2,1)S(1)}, bf16[24,45,8]{2,1,0:T(8,128)(2,1)}, u32[]{:S(2)}) copy-start(bf16[24,45,8]{2,1,0:T(8,128)(2,1)} %copy-done.3) | copy-start | bytes 51844
  33.7 1.4 %collective-permute-start.4 = (f32[4,32,256]{2,1,0:T(8,128)S(1)}, f32[4,32,256]{2,1,0:T(8,128)S(1)}, u32[]{:S(2)}, u32[]{:S(2)}) collective-permute-start(f32[4,32,256]{2,1,0:T(8,128)S(1)} %get-tuple-element.8), channel_id=1, source_target_pairs={{0,4},{4,0},{8,12},{12,8},{16,20},{20,16},{24,28},{28,24},{1,5},{5... | collective-permute-start | bytes 393224 | tf_op jit(solution)/shard_map/ppermute | solution.py:198
  35.1 10.0 %collective-permute-start.9 = (f32[4,32,256]{2,1,0:T(8,128)S(1)}, f32[4,32,256]{2,1,0:T(8,128)S(1)}, u32[]{:S(2)}, u32[]{:S(2)}) collective-permute-start(f32[4,32,256]{2,1,0:T(8,128)S(1)} %add.58), channel_id=1, source_target_pairs={{0,8},{4,12},{8,0},{12,4},{16,24},{20,28},{24,16},{28,20},{1,9},{5... | collective-permute-start | bytes 393224 | tf_op jit(solution)/shard_map/ppermute | solution.py:49
  42.0 7.1 %collective-permute-start.5 = (f32[1,61,256]{2,1,0:T(8,128)S(1)}, f32[1,61,256]{2,1,0:T(8,128)S(1)}, u32[]{:S(2)}, u32[]{:S(2)}) collective-permute-start(f32[1,61,256]{2,1,0:T(8,128)S(1)} %get-tuple-element.18), channel_id=1, source_target_pairs={{0,4},{4,8},{8,12},{12,16},{16,20},{20,24},{24,28},{1,5},{5,9},{9,... | collective-permute-start | bytes 187400 | tf_op jit(solution)/shard_map/ppermute | solution.py:29
  43.8 5.4 %collective-permute-start.6 = (f32[1,61,256]{2,1,0:T(8,128)S(1)}, f32[1,61,256]{2,1,0:T(8,128)S(1)}, u32[]{:S(2)}, u32[]{:S(2)}) collective-permute-start(f32[1,61,256]{2,1,0:T(8,128)S(1)} %get-tuple-element.19), channel_id=1, source_target_pairs={{4,0},{8,4},{12,8},{16,12},{20,16},{24,20},{28,24},{5,1},{9,5},{13... | collective-permute-start | bytes 187400 | tf_op jit(solution)/shard_map/ppermute | solution.py:29
  45.2 7.2 %collective-permute-start.10 = (f32[4,32,256]{2,1,0:T(8,128)S(1)}, f32[4,32,256]{2,1,0:T(8,128)S(1)}, u32[]{:S(2)}, u32[]{:S(2)}) collective-permute-start(f32[4,32,256]{2,1,0:T(8,128)S(1)} %add.59), channel_id=1, source_target_pairs={{0,16},{4,20},{8,24},{12,28},{16,0},{20,4},{24,8},{28,12},{1,17},{... | collective-permute-start | bytes 393224 | tf_op jit(solution)/shard_map/ppermute | solution.py:49
  49.3 13.8 %copy-start.2 = (bf16[24,45,256]{2,1,0:T(8,128)(2,1)S(1)}, bf16[24,45,256]{2,1,0:T(8,128)(2,1)}, u32[]{:S(2)}) copy-start(bf16[24,45,256]{2,1,0:T(8,128)(2,1)} %copy-done.1) | copy-start | bytes 1658884
  49.3 13.7 %collective-permute-start.8 = (f32[24,8,256]{2,1,0:T(8,128)S(1)}, f32[24,8,256]{2,1,0:T(8,128)S(1)}, u32[]{:S(2)}, u32[]{:S(2)}) collective-permute-start(f32[24,8,256]{2,1,0:T(8,128)S(1)} %slice.60), channel_id=1, source_target_pairs={{0,1},{1,2},{2,3},{3,0},{4,5},{5,6},{6,7},{7,4},{8,9},{9,10},{10,1... | collective-permute-start | bytes 589832 | tf_op jit(solution)/shard_map/ppermute | solution.py:34
  52.4 9.0 %collective-permute-start.11 = (f32[4,32,256]{2,1,0:T(8,128)S(1)}, f32[4,32,256]{2,1,0:T(8,128)S(1)}, u32[]{:S(2)}, u32[]{:S(2)}) collective-permute-start(f32[4,32,256]{2,1,0:T(8,128)S(1)} %add.60), channel_id=1, source_target_pairs={{0,1},{1,0},{2,3},{3,2},{4,5},{5,4},{6,7},{7,6},{8,9},{9,8},{10,11... | collective-permute-start | bytes 393224 | tf_op jit(solution)/shard_map/ppermute | solution.py:49
  53.6 9.5 %collective-permute-start.7 = (bf16[24,8,256]{2,1,0:T(8,128)(2,1)S(1)}, bf16[24,8,256]{2,1,0:T(8,128)(2,1)S(1)}, u32[]{:S(2)}, u32[]{:S(2)}) collective-permute-start(bf16[24,8,256]{2,1,0:T(8,128)(2,1)S(1)} %slice.72), channel_id=1, source_target_pairs={{0,3},{1,0},{2,1},{3,2},{4,7},{5,4},{6,5},{7,6},{8,11},{9,8},{10,9... | collective-permute-start | bytes 294920 | tf_op jit(solution)/shard_map/ppermute | solution.py:34
  61.4 7.7 %collective-permute-start.12 = (f32[4,32,256]{2,1,0:T(8,128)S(1)}, f32[4,32,256]{2,1,0:T(8,128)S(1)}, u32[]{:S(2)}, u32[]{:S(2)}) collective-permute-start(f32[4,32,256]{2,1,0:T(8,128)S(1)} %add.61), channel_id=1, source_target_pairs={{0,2},{1,3},{2,0},{3,1},{4,6},{5,7},{6,4},{7,5},{8,10},{9,11},{10,... | collective-permute-start | bytes 393224 | tf_op jit(solution)/shard_map/ppermute | solution.py:49

commit v14 on v13

--- a/solution.py
+++ b/solution.py
@@ -76,7 +76,7 @@
             safe_ref[b, rows_at, :] = safe[b * col_pad : (b + 1) * col_pad]
         return carry
 
-    lax.fori_loop(0, rows, body, 0, unroll=4)
+    lax.fori_loop(0, rows, body, 0, unroll=8)
     lane = lax.broadcasted_iota(jnp.int32, (group_width, chan_count), 1) // group_width
     upstream_all = cot_ref[...].reshape(rows * col_pad, chan_count)
     out = None
@@ -116,7 +116,7 @@
             col_ref[pl.ds(start, lane_rows), :] += term
         return carry
 
-    lax.fori_loop(0, rows, body, 0, unroll=4)
+    lax.fori_loop(0, rows, body, 0, unroll=8)
 
 
 def local(features, obs_mask, filter_taps, band_width, mixing, cotangent):

time: 70.5 us -> 69.5 us (0.986)
  Pallas kernels: 12.9 us -> 12 us
  transfers between devices with their start and end apart: 13 -> 13, of which waited for: 7 -> 7; matrix products, arithmetic and copies ran while one was open for 14% -> 14% of each run, Pallas kernels for 6% -> 5%
where the time goes in v14:
time: 69.5 us; the launch traced here: 69.2 us
  starting transfers between devices  22.6 us (33%)
  waiting for transfers between devices  18 us (26%)
  Pallas kernels  12 us (17%)
  local copies, waits for them, and re-layouts  9.48 us (14%)
  other arithmetic  4.34 us (6%)
  matrix products  1.86 us (3%)
  between operations  1.01 us (1%)
    ppermute x4, waiting for transfers between devices, butterfly_sum(): partner = lax.ppermute(value, axis, [(i, i ^ step) for i in range(count)])  11.9 us
    ppermute x4, starting transfers between devices, butterfly_sum(): partner = lax.ppermute(value, axis, [(i, i ^ step) for i in range(count)])  9.05 us
    pallas_call x1, Pallas kernels, local(): pl.pallas_call(forward_kernel, out_shape=(jax.ShapeDtypeStruct((row_count...  8.34 us
    ppermute x2, waiting for transfers between devices, with_halo(): lax.ppermute(lax.slice_in_dim(block, 0, width, axis=dim), axis, backward)  4.3 us
    ppermute x2, starting transfers between devices, with_halo(): lax.ppermute(lax.slice_in_dim(block, block.shape[dim] - width, None, axis...  3.98 us
    pallas_call x1, Pallas kernels, local(): pl.pallas_call(adjoint_kernel, out_shape=jax.ShapeDtypeStruct(((row_count...  3.61 us
    ppermute x2, starting transfers between devices, with_halo(): lax.ppermute(lax.slice_in_dim(block, 0, width, axis=dim), axis, backward)  3.54 us
    unnamed x20, local copies, waits for them, and re-layouts  3.37 us
  transfers between devices with their start and end apart: 13, of which 7 were waited for; matrix products, arithmetic and copies ran while one was open for 14% of the time, Pallas kernels for 5%

profile of v14, /device:TPU:0, one launch (start us, length us, event | category | flops | bytes accessed | tf_op | source)
XLA Modules:
  0.0 69.2 jit_solution(865912925885908043)
XLA Ops:
  0.6 0.0 copy-start
  0.6 0.0 copy-start.5
  0.7 1.0 %convert_element_type.46 = bf16[24,45,8]{1,2,0:T(8,128)(2,1)S(1)} convert(s32[24,45,8]{1,2,0:T(8,128)} %param.7) | non-fusion elementwise | flops 8640 | bytes 51840 | tf_op jit(solution)/shard_map/convert_element_type | solution.py:132
  1.6 0.2 copy.35
  1.9 0.1 reshape.114
  2.0 0.4 fusion.6
  2.4 0.2 reshape.115
  2.6 0.0 copy-done.5
  2.6 0.0 copy-start.1
  2.6 0.0 copy-start.7
  2.6 0.1 copy_multiply_fusion
  2.8 2.4 %collective-permute-start = (bf16[1,45,264]{2,1,0:T(8,128)(2,1)S(1)}, bf16[1,45,264]{2,1,0:T(8,128)(2,1)S(1)}, u32[]{:S(2)}, u32[]{:S(2)}) collective-permute-start(bf16[1,45,264]{2,1,0:T(8,128)(2,1)S(1)} %get-tuple-element.22), channel_id=1, source_target_pairs={{0,4},{4,8},{8,12},{12,16},{16,20},{20,24},{24,28},{1,5},{5,9},{9,... | collective-permute-start | bytes 71288 | tf_op jit(solution)/shard_map/ppermute | solution.py:18
  5.2 1.3 %collective-permute-start.1 = (bf16[1,45,264]{2,1,0:T(8,128)(2,1)S(1)}, bf16[1,45,264]{2,1,0:T(8,128)(2,1)S(1)}, u32[]{:S(2)}, u32[]{:S(2)}) collective-permute-start(bf16[1,45,264]{2,1,0:T(8,128)(2,1)S(1)} %get-tuple-element.23), channel_id=1, source_target_pairs={{4,0},{8,4},{12,8},{16,12},{20,16},{24,20},{28,24},{5,1},{9,5},{13... | collective-permute-start | bytes 71288 | tf_op jit(solution)/shard_map/ppermute | solution.py:21
  6.5 0.0 copy-done
  6.5 0.1 constant_dynamic-slice_fusion
  6.6 0.2 copy.48
  6.8 0.0 copy-done.7
  6.8 0.1 compare_convert_fusion
  6.9 0.1 copy.37
  7.0 0.0 copy-start.6
  7.0 1.1 %fusion.18 = bf16[24,4,3,48,64]{4,0,3,2,1:T(8,128)(2,1)S(1)} fusion(s32[48,64]{1,0:T(8,128)S(1)} %iota_subtract_fusion, pred[48]{0:T(512)(128)(4,1)S(1)} %iota_compare_fusion.6, bf16[24,4,3,17]{3,0,2,1:T(8,128)(2,1)S(1)} %copy.48, bf16[24,17]{1,0:T(8,128)(2,1)S(1)} %constant_dynamic-slice_fusion.1), kind=kOutput, calls=%fused_computation.27 | convolution fusion | flops 30205056 | bytes 1792416 | tf_op jit(solution)/shard_map/ibae,ejp->ibajp/dot_general | solution.py:164
  8.2 0.0 copy-done.1
  8.2 0.0 collective-permute-done
  8.2 2.2 %collective-permute-done.1 = bf16[1,45,264]{2,1,0:T(8,128)(2,1)S(1)} collective-permute-done((bf16[1,45,264]{2,1,0:T(8,128)(2,1)S(1)}, bf16[1,45,264]{2,1,0:T(8,128)(2,1)S(1)}, u32[]{:S(2)}, u32[]{:S(2)}) %collective-permute-start.1) | collective-permute-done | bytes 23792 | tf_op jit(solution)/shard_map/ppermute | solution.py:21
  10.4 0.8 %pad_maximum_fusion.3 = (bf16[26,8,264]{2,1,0:T(8,128)(2,1)}, bf16[26,8,264]{2,1,0:T(8,128)(2,1)}) fusion(bf16[1,45,264]{2,1,0:T(8,128)(2,1)S(1)} %collective-permute-done.1, bf16[1,45,264]{2,1,0:T(8,128)(2,1)S(1)} %collective-permute-done, bf16[24,45,8]{2,1,0:T(8,128)(2,1)S(1)} %copy.35, bf16[24,45,256]{2,1,0:T(8,128)(2,1)S(1)} %copy_multiply_fusion), kind=kLoop, calls=%fused_computation.35 | loop fusion | flops 878592 | bytes 837408 | tf_op jit(solution)/shard_map/slice | solution.py:19
  11.2 1.6 %collective-permute-start.2 = (bf16[26,8,264]{2,1,0:T(8,128)(2,1)}, bf16[26,8,264]{2,1,0:T(8,128)(2,1)S(1)}, u32[]{:S(2)}, u32[]{:S(2)}) collective-permute-start(bf16[26,8,264]{2,1,0:T(8,128)(2,1)} %get-tuple-element.20), channel_id=1, source_target_pairs={{0,1},{1,2},{2,3},{3,0},{4,5},{5,6},{6,7},{7,4},{8,9},{9,10},{10,1... | collective-permute-start | bytes 329480 | tf_op jit(solution)/shard_map/ppermute | solution.py:18
  12.7 2.2 %collective-permute-start.3 = (bf16[26,8,264]{2,1,0:T(8,128)(2,1)}, bf16[26,8,264]{2,1,0:T(8,128)(2,1)}, u32[]{:S(2)}, u32[]{:S(2)}) collective-permute-start(bf16[26,8,264]{2,1,0:T(8,128)(2,1)} %get-tuple-element.21), channel_id=1, source_target_pairs={{1,0},{2,1},{3,2},{0,3},{5,4},{6,5},{7,6},{4,7},{9,8},{10,9},{11,1... | collective-permute-start | bytes 329480 | tf_op jit(solution)/shard_map/ppermute | solution.py:21
  15.0 0.7 multiply_bitcast_fusion
  15.7 2.6 %copy.52.t_ref = bf16[24,4,3,48,64]{4,3,2,1,0:T(8,128)(2,1)} copy(bf16[24,4,3,48,64]{4,0,3,2,1:T(8,128)(2,1)S(1)} %fusion.18) | data formatting | bytes 3538944 | tf_op jit(solution)/shard_map/ibae,ejp->ibajp/dot_general | solution.py:164
  18.3 1.4 %reshape.118.w_ref = bf16[4,256,256]{2,1,0:T(8,128)(2,1)S(1)} reshape(bf16[4,8,32,8,32]{4,3,2,1,0:T(8,128)(2,1)S(1)} %multiply_bitcast_fusion) | data formatting | bytes 1048576 | tf_op jit(solution)/shard_map/reshape | solution.py:169
  19.7 0.0 copy-start.4
  19.7 1.2 %copy.40 = bf16[24,45,256]{2,1,0:T(8,128)(2,1)S(1)} copy(bf16[24,45,256]{2,0,1:T(8,128)(2,1)} %param.11) | data formatting | bytes 1105920 | tf_op args[5]
  21.0 0.0 collective-permute-done.2
  21.0 2.1 %collective-permute-done.3 = bf16[26,8,264]{2,1,0:T(8,128)(2,1)} collective-permute-done((bf16[26,8,264]{2,1,0:T(8,128)(2,1)}, bf16[26,8,264]{2,1,0:T(8,128)(2,1)}, u32[]{:S(2)}, u32[]{:S(2)}) %collective-permute-start.3) | collective-permute-done | bytes 109856 | tf_op jit(solution)/shard_map/ppermute | solution.py:21
  23.1 1.2 %fusion.9 = bf16[26,64,264]{2,1,0:T(8,128)(2,1)S(1)} fusion(bf16[26,8,264]{2,1,0:T(8,128)(2,1)} %collective-permute-done.3, bf16[26,8,264]{2,1,0:T(8,128)(2,1)S(1)} %collective-permute-done.2, bf16[1,45,264]{2,1,0:T(8,128)(2,1)S(1)} %collective-permute-done.1, bf16[1,45,264]{2,1,0:T(8,128)(2,1)S(1)} %collective-permute-done, ...), kind=kLoop, calls=%fused_computation.15 | loop fusion | flops 8346624 | bytes 1716000 | tf_op jit(solution)/shard_map/concatenate | solution.py:22
  24.4 0.1 slice.54
  24.4 0.1 slice.53
  24.5 0.4 convolution_convert_fusion.m_ref
  24.9 8.3 %shard_map.85 = (bf16[24,45,256]{2,1,0:T(8,128)(2,1)S(1)}, f32[4,32,256]{2,1,0:T(8,128)S(1)}, bf16[4,1152,256]{2,1,0:T(8,128)(2,1)S(1)}) custom-call(bf16[1664,256]{1,0:T(8,128)(2,1)S(1)} %bitcast.28, bf16[1664,256]{1,0:T(8,128)(2,1)S(1)} %convolution_convert_fusion.m_ref, bf16[24,4,3,48,64]{4,3,2,1,0:T(8,128)(2,1)} %copy.52.t_ref, ...), custom_call_target="tpu_custom_call" | custom-call | flops 2717908992 | bytes 3407872 | tf_op jit(solution)/shard_map/pallas_call | solution.py:174
  33.2 0.2 collective-permute-start.4
  33.4 1.2 %collective-permute-done.4.order_ref = f32[4,32,256]{2,1,0:T(8,128)S(1)} collective-permute-done((f32[4,32,256]{2,1,0:T(8,128)S(1)}, f32[4,32,256]{2,1,0:T(8,128)S(1)}, u32[]{:S(2)}, u32[]{:S(2)}) %collective-permute-start.4) | collective-permute-done | bytes 131104 | tf_op jit(solution)/shard_map/ppermute | solution.py:198
  34.7 2.8 %collective-permute-start.9 = (f32[4,32,256]{2,1,0:T(8,128)S(1)}, f32[4,32,256]{2,1,0:T(8,128)S(1)}, u32[]{:S(2)}, u32[]{:S(2)}) collective-permute-start(f32[4,32,256]{2,1,0:T(8,128)S(1)} %add.58), channel_id=1, source_target_pairs={{0,8},{4,12},{8,0},{12,4},{16,24},{20,28},{24,16},{28,20},{1,9},{5... | collective-permute-start | bytes 393224 | tf_op jit(solution)/shard_map/ppermute | solution.py:49
  37.4 3.6 %shard_map.86 = f32[1664,256]{1,0:T(8,128)S(1)} custom-call(bf16[24,4,3,48,64]{4,3,2,1,0:T(8,128)(2,1)} %copy.52.t_ref, bf16[4,1152,256]{2,1,0:T(8,128)(2,1)S(1)} %get-tuple-element.7.pulled_ref, f32[4,32,256]{2,1,0:T(8,128)S(1)} %collective-permute-done.4.order_ref), custom_call_target="tpu_custom_call" | custom-call | flops 452984832 | bytes 2555904 | tf_op jit(solution)/shard_map/pallas_call | solution.py:206
  41.1 1.8 %collective-permute-start.5 = (f32[1,61,256]{2,1,0:T(8,128)S(1)}, f32[1,61,256]{2,1,0:T(8,128)S(1)}, u32[]{:S(2)}, u32[]{:S(2)}) collective-permute-start(f32[1,61,256]{2,1,0:T(8,128)S(1)} %get-tuple-element.18), channel_id=1, source_target_pairs={{0,4},{4,8},{8,12},{12,16},{16,20},{20,24},{24,28},{1,5},{5,9},{9,... | collective-permute-start | bytes 187400 | tf_op jit(solution)/shard_map/ppermute | solution.py:29
  42.9 1.3 %collective-permute-start.6 = (f32[1,61,256]{2,1,0:T(8,128)S(1)}, f32[1,61,256]{2,1,0:T(8,128)S(1)}, u32[]{:S(2)}, u32[]{:S(2)}) collective-permute-start(f32[1,61,256]{2,1,0:T(8,128)S(1)} %get-tuple-element.19), channel_id=1, source_target_pairs={{4,0},{8,4},{12,8},{16,12},{20,16},{24,20},{28,24},{5,1},{9,5},{13... | collective-permute-start | bytes 187400 | tf_op jit(solution)/shard_map/ppermute | solution.py:29
  44.2 0.0 collective-permute-done.9
  44.2 4.0 %collective-permute-start.10 = (f32[4,32,256]{2,1,0:T(8,128)S(1)}, f32[4,32,256]{2,1,0:T(8,128)S(1)}, u32[]{:S(2)}, u32[]{:S(2)}) collective-permute-start(f32[4,32,256]{2,1,0:T(8,128)S(1)} %add.59), channel_id=1, source_target_pairs={{0,16},{4,20},{8,24},{12,28},{16,0},{20,4},{24,8},{28,12},{1,17},{... | collective-permute-start | bytes 393224 | tf_op jit(solution)/shard_map/ppermute | solution.py:49
  48.2 0.0 collective-permute-done.5
  48.2 0.0 collective-permute-done.6
  48.2 0.1 fusion.7
  48.4 1.2 %collective-permute-start.8 = (f32[24,8,256]{2,1,0:T(8,128)S(1)}, f32[24,8,256]{2,1,0:T(8,128)S(1)}, u32[]{:S(2)}, u32[]{:S(2)}) collective-permute-start(f32[24,8,256]{2,1,0:T(8,128)S(1)} %slice.60), channel_id=1, source_target_pairs={{0,1},{1,2},{2,3},{3,0},{4,5},{5,6},{6,7},{7,4},{8,9},{9,10},{10,1... | collective-permute-start | bytes 589832 | tf_op jit(solution)/shard_map/ppermute | solution.py:34
  49.6 1.8 %collective-permute-done.10 = f32[4,32,256]{2,1,0:T(8,128)S(1)} collective-permute-done((f32[4,32,256]{2,1,0:T(8,128)S(1)}, f32[4,32,256]{2,1,0:T(8,128)S(1)}, u32[]{:S(2)}, u32[]{:S(2)}) %collective-permute-start.10) | collective-permute-done | bytes 131104 | tf_op jit(solution)/shard_map/ppermute | solution.py:49
  51.4 1.2 %collective-permute-start.11 = (f32[4,32,256]{2,1,0:T(8,128)S(1)}, f32[4,32,256]{2,1,0:T(8,128)S(1)}, u32[]{:S(2)}, u32[]{:S(2)}) collective-permute-start(f32[4,32,256]{2,1,0:T(8,128)S(1)} %add.60), channel_id=1, source_target_pairs={{0,1},{1,0},{2,3},{3,2},{4,5},{5,4},{6,7},{7,6},{8,9},{9,8},{10,11... | collective-permute-start | bytes 393224 | tf_op jit(solution)/shard_map/ppermute | solution.py:49
  52.6 1.6 %collective-permute-start.7 = (bf16[24,8,256]{2,1,0:T(8,128)(2,1)S(1)}, bf16[24,8,256]{2,1,0:T(8,128)(2,1)S(1)}, u32[]{:S(2)}, u32[]{:S(2)}) collective-permute-start(bf16[24,8,256]{2,1,0:T(8,128)(2,1)S(1)} %slice.72), channel_id=1, source_target_pairs={{0,3},{1,0},{2,1},{3,2},{4,7},{5,4},{6,5},{7,6},{8,11},{9,8},{10,9... | collective-permute-start | bytes 294920 | tf_op jit(solution)/shard_map/ppermute | solution.py:34
  54.2 1.0 %copy.43 = bf16[24,45,256]{2,0,1:T(8,128)(2,1)} copy(bf16[24,45,256]{2,1,0:T(8,128)(2,1)S(1)} %get-tuple-element.15) | data formatting | bytes 1105920
  55.2 5.3 %collective-permute-done.11 = f32[4,32,256]{2,1,0:T(8,128)S(1)} collective-permute-done((f32[4,32,256]{2,1,0:T(8,128)S(1)}, f32[4,32,256]{2,1,0:T(8,128)S(1)}, u32[]{:S(2)}, u32[]{:S(2)}) %collective-permute-start.11) | collective-permute-done | bytes 131104 | tf_op jit(solution)/shard_map/ppermute | solution.py:49
  60.5 1.1 %collective-permute-start.12 = (f32[4,32,256]{2,1,0:T(8,128)S(1)}, f32[4,32,256]{2,1,0:T(8,128)S(1)}, u32[]{:S(2)}, u32[]{:S(2)}) collective-permute-start(f32[4,32,256]{2,1,0:T(8,128)S(1)} %add.61), channel_id=1, source_target_pairs={{0,2},{1,3},{2,0},{3,1},{4,6},{5,7},{6,4},{7,5},{8,10},{9,11},{10,... | collective-permute-start | bytes 393224 | tf_op jit(solution)/shard_map/ppermute | solution.py:49
  61.5 0.6 collective-permute-done.7
  62.1 0.0 collective-permute-done.8
  62.1 0.2 fusion.15
  62.4 1.0 %copy.44 = bf16[24,45,256]{2,0,1:T(8,128)(2,1)} copy(bf16[24,45,256]{2,1,0:T(8,128)(2,1)S(1)} %fusion.15) | data formatting | bytes 1105920
  63.3 4.8 %collective-permute-done.12 = f32[4,32,256]{2,1,0:T(8,128)S(1)} collective-permute-done((f32[4,32,256]{2,1,0:T(8,128)S(1)}, f32[4,32,256]{2,1,0:T(8,128)S(1)}, u32[]{:S(2)}, u32[]{:S(2)}) %collective-permute-start.12) | collective-permute-done | bytes 131104 | tf_op jit(solution)/shard_map/ppermute | solution.py:49
  68.1 0.2 reshape.120
  68.3 0.9 %copy.55 = f32[4,32,8,32]{3,1,0,2:T(8,128)} copy(f32[4,32,8,32]{3,2,1,0:T(8,128)S(1)} %reshape.120) | data formatting | bytes 262144 | tf_op jit(solution)/shard_map/reshape | solution.py:204
  (23 shorter events, 0.3 us)
Async XLA Ops:
  0.6 5.9 %copy-start = (bf16[192,4,3,17]{0,1,3,2:T(4,128)(2,1)S(1)}, bf16[192,4,3,17]{0,1,3,2:T(4,128)(2,1)}, u32[]{:S(2)}) copy-start(bf16[192,4,3,17]{0,1,3,2:T(4,128)(2,1)} %param.8) | copy-start | bytes 235012
  0.6 1.9 %copy-start.5 = (bf16[24,45,256]{2,0,1:T(8,128)(2,1)S(1)}, bf16[24,45,256]{2,0,1:T(8,128)(2,1)}, u32[]{:S(2)}) copy-start(bf16[24,45,256]{2,0,1:T(8,128)(2,1)} %param.6) | copy-start | bytes 1658884
  1.9 8.5 %copy-start.3 = (bf16[24,45,8]{2,1,0:T(8,128)(2,1)}, bf16[24,45,8]{2,1,0:T(8,128)(2,1)S(1)}, u32[]{:S(2)}) copy-start(bf16[24,45,8]{2,1,0:T(8,128)(2,1)S(1)} %copy.35) | copy-start | bytes 51844
  2.6 5.6 %copy-start.1 = (bf16[24,45,256]{2,1,0:T(8,128)(2,1)}, bf16[24,45,256]{2,1,0:T(8,128)(2,1)S(1)}, u32[]{:S(2)}) copy-start(bf16[24,45,256]{2,1,0:T(8,128)(2,1)S(1)} %reshape.115) | copy-start | bytes 1658884
  2.6 4.2 %copy-start.7 = (s32[192]{0:T(256)S(1)}, s32[192]{0:T(256)}, u32[]{:S(2)}) copy-start(s32[192]{0:T(256)} %param.9) | copy-start | bytes 2308
  2.8 5.4 %collective-permute-start = (bf16[1,45,264]{2,1,0:T(8,128)(2,1)S(1)}, bf16[1,45,264]{2,1,0:T(8,128)(2,1)S(1)}, u32[]{:S(2)}, u32[]{:S(2)}) collective-permute-start(bf16[1,45,264]{2,1,0:T(8,128)(2,1)S(1)} %get-tuple-element.22), channel_id=1, source_target_pairs={{0,4},{4,8},{8,12},{12,16},{16,20},{20,24},{24,28},{1,5},{5,9},{9,... | collective-permute-start | bytes 71288 | tf_op jit(solution)/shard_map/ppermute | solution.py:18
  5.2 5.2 %collective-permute-start.1 = (bf16[1,45,264]{2,1,0:T(8,128)(2,1)S(1)}, bf16[1,45,264]{2,1,0:T(8,128)(2,1)S(1)}, u32[]{:S(2)}, u32[]{:S(2)}) collective-permute-start(bf16[1,45,264]{2,1,0:T(8,128)(2,1)S(1)} %get-tuple-element.23), channel_id=1, source_target_pairs={{4,0},{8,4},{12,8},{16,12},{20,16},{24,20},{28,24},{5,1},{9,5},{13... | collective-permute-start | bytes 71288 | tf_op jit(solution)/shard_map/ppermute | solution.py:21
  7.0 8.0 %copy-start.6 = (bf16[8,4,32,32]{3,2,1,0:T(8,128)(2,1)S(1)}, bf16[8,4,32,32]{3,2,1,0:T(8,128)(2,1)}, u32[]{:S(2)}) copy-start(bf16[8,4,32,32]{3,2,1,0:T(8,128)(2,1)} %param.10) | copy-start | bytes 196612
  11.2 9.8 %collective-permute-start.2 = (bf16[26,8,264]{2,1,0:T(8,128)(2,1)}, bf16[26,8,264]{2,1,0:T(8,128)(2,1)S(1)}, u32[]{:S(2)}, u32[]{:S(2)}) collective-permute-start(bf16[26,8,264]{2,1,0:T(8,128)(2,1)} %get-tuple-element.20), channel_id=1, source_target_pairs={{0,1},{1,2},{2,3},{3,0},{4,5},{5,6},{6,7},{7,4},{8,9},{9,10},{10,1... | collective-permute-start | bytes 329480 | tf_op jit(solution)/shard_map/ppermute | solution.py:18
  12.7 10.4 %collective-permute-start.3 = (bf16[26,8,264]{2,1,0:T(8,128)(2,1)}, bf16[26,8,264]{2,1,0:T(8,128)(2,1)}, u32[]{:S(2)}, u32[]{:S(2)}) collective-permute-start(bf16[26,8,264]{2,1,0:T(8,128)(2,1)} %get-tuple-element.21), channel_id=1, source_target_pairs={{1,0},{2,1},{3,2},{0,3},{5,4},{6,5},{7,6},{4,7},{9,8},{10,9},{11,1... | collective-permute-start | bytes 329480 | tf_op jit(solution)/shard_map/ppermute | solution.py:21
  19.7 3.4 %copy-start.4 = (bf16[24,45,8]{2,1,0:T(8,128)(2,1)S(1)}, bf16[24,45,8]{2,1,0:T(8,128)(2,1)}, u32[]{:S(2)}) copy-start(bf16[24,45,8]{2,1,0:T(8,128)(2,1)} %copy-done.3) | copy-start | bytes 51844
  33.2 1.4 %collective-permute-start.4 = (f32[4,32,256]{2,1,0:T(8,128)S(1)}, f32[4,32,256]{2,1,0:T(8,128)S(1)}, u32[]{:S(2)}, u32[]{:S(2)}) collective-permute-start(f32[4,32,256]{2,1,0:T(8,128)S(1)} %get-tuple-element.8), channel_id=1, source_target_pairs={{0,4},{4,0},{8,12},{12,8},{16,20},{20,16},{24,28},{28,24},{1,5},{5... | collective-permute-start | bytes 393224 | tf_op jit(solution)/shard_map/ppermute | solution.py:198
  34.7 9.5 %collective-permute-start.9 = (f32[4,32,256]{2,1,0:T(8,128)S(1)}, f32[4,32,256]{2,1,0:T(8,128)S(1)}, u32[]{:S(2)}, u32[]{:S(2)}) collective-permute-start(f32[4,32,256]{2,1,0:T(8,128)S(1)} %add.58), channel_id=1, source_target_pairs={{0,8},{4,12},{8,0},{12,4},{16,24},{20,28},{24,16},{28,20},{1,9},{5... | collective-permute-start | bytes 393224 | tf_op jit(solution)/shard_map/ppermute | solution.py:49
  41.1 7.2 %collective-permute-start.5 = (f32[1,61,256]{2,1,0:T(8,128)S(1)}, f32[1,61,256]{2,1,0:T(8,128)S(1)}, u32[]{:S(2)}, u32[]{:S(2)}) collective-permute-start(f32[1,61,256]{2,1,0:T(8,128)S(1)} %get-tuple-element.18), channel_id=1, source_target_pairs={{0,4},{4,8},{8,12},{12,16},{16,20},{20,24},{24,28},{1,5},{5,9},{9,... | collective-permute-start | bytes 187400 | tf_op jit(solution)/shard_map/ppermute | solution.py:29
  42.9 5.4 %collective-permute-start.6 = (f32[1,61,256]{2,1,0:T(8,128)S(1)}, f32[1,61,256]{2,1,0:T(8,128)S(1)}, u32[]{:S(2)}, u32[]{:S(2)}) collective-permute-start(f32[1,61,256]{2,1,0:T(8,128)S(1)} %get-tuple-element.19), channel_id=1, source_target_pairs={{4,0},{8,4},{12,8},{16,12},{20,16},{24,20},{28,24},{5,1},{9,5},{13... | collective-permute-start | bytes 187400 | tf_op jit(solution)/shard_map/ppermute | solution.py:29
  44.2 7.2 %collective-permute-start.10 = (f32[4,32,256]{2,1,0:T(8,128)S(1)}, f32[4,32,256]{2,1,0:T(8,128)S(1)}, u32[]{:S(2)}, u32[]{:S(2)}) collective-permute-start(f32[4,32,256]{2,1,0:T(8,128)S(1)} %add.59), channel_id=1, source_target_pairs={{0,16},{4,20},{8,24},{12,28},{16,0},{20,4},{24,8},{28,12},{1,17},{... | collective-permute-start | bytes 393224 | tf_op jit(solution)/shard_map/ppermute | solution.py:49
  48.4 13.8 %copy-start.2 = (bf16[24,45,256]{2,1,0:T(8,128)(2,1)S(1)}, bf16[24,45,256]{2,1,0:T(8,128)(2,1)}, u32[]{:S(2)}) copy-start(bf16[24,45,256]{2,1,0:T(8,128)(2,1)} %copy-done.1) | copy-start | bytes 1658884
  48.4 13.7 %collective-permute-start.8 = (f32[24,8,256]{2,1,0:T(8,128)S(1)}, f32[24,8,256]{2,1,0:T(8,128)S(1)}, u32[]{:S(2)}, u32[]{:S(2)}) collective-permute-start(f32[24,8,256]{2,1,0:T(8,128)S(1)} %slice.60), channel_id=1, source_target_pairs={{0,1},{1,2},{2,3},{3,0},{4,5},{5,6},{6,7},{7,4},{8,9},{9,10},{10,1... | collective-permute-start | bytes 589832 | tf_op jit(solution)/shard_map/ppermute | solution.py:34
  51.4 9.0 %collective-permute-start.11 = (f32[4,32,256]{2,1,0:T(8,128)S(1)}, f32[4,32,256]{2,1,0:T(8,128)S(1)}, u32[]{:S(2)}, u32[]{:S(2)}) collective-permute-start(f32[4,32,256]{2,1,0:T(8,128)S(1)} %add.60), channel_id=1, source_target_pairs={{0,1},{1,0},{2,3},{3,2},{4,5},{5,4},{6,7},{7,6},{8,9},{9,8},{10,11... | collective-permute-start | bytes 393224 | tf_op jit(solution)/shard_map/ppermute | solution.py:49
  52.6 9.5 %collective-permute-start.7 = (bf16[24,8,256]{2,1,0:T(8,128)(2,1)S(1)}, bf16[24,8,256]{2,1,0:T(8,128)(2,1)S(1)}, u32[]{:S(2)}, u32[]{:S(2)}) collective-permute-start(bf16[24,8,256]{2,1,0:T(8,128)(2,1)S(1)} %slice.72), channel_id=1, source_target_pairs={{0,3},{1,0},{2,1},{3,2},{4,7},{5,4},{6,5},{7,6},{8,11},{9,8},{10,9... | collective-permute-start | bytes 294920 | tf_op jit(solution)/shard_map/ppermute | solution.py:34
  60.5 7.7 %collective-permute-start.12 = (f32[4,32,256]{2,1,0:T(8,128)S(1)}, f32[4,32,256]{2,1,0:T(8,128)S(1)}, u32[]{:S(2)}, u32[]{:S(2)}) collective-permute-start(f32[4,32,256]{2,1,0:T(8,128)S(1)} %add.61), channel_id=1, source_target_pairs={{0,2},{1,3},{2,0},{3,1},{4,6},{5,7},{6,4},{7,5},{8,10},{9,11},{10,... | collective-permute-start | bytes 393224 | tf_op jit(solution)/shard_map/ppermute | solution.py:49

commit v15 on v14

--- a/solution.py
+++ b/solution.py
@@ -76,7 +76,7 @@
             safe_ref[b, rows_at, :] = safe[b * col_pad : (b + 1) * col_pad]
         return carry
 
-    lax.fori_loop(0, rows, body, 0, unroll=8)
+    lax.fori_loop(0, rows, body, 0, unroll=True)
     lane = lax.broadcasted_iota(jnp.int32, (group_width, chan_count), 1) // group_width
     upstream_all = cot_ref[...].reshape(rows * col_pad, chan_count)
     out = None
@@ -116,7 +116,7 @@
             col_ref[pl.ds(start, lane_rows), :] += term
         return carry
 
-    lax.fori_loop(0, rows, body, 0, unroll=8)
+    lax.fori_loop(0, rows, body, 0, unroll=True)
 
 
 def local(features, obs_mask, filter_taps, band_width, mixing, cotangent):

time: 69.5 us -> 68.9 us (level)
  transfers between devices with their start and end apart: 13 -> 13, of which waited for: 7 -> 7; matrix products, arithmetic and copies ran while one was open for 14% -> 15% of each run, Pallas kernels for 5% -> 5%
where the time goes in v15:
time: 68.9 us; the launch traced here: 68.6 us
  starting transfers between devices  22.6 us (33%)
  waiting for transfers between devices  18 us (26%)
  Pallas kernels  11.4 us (17%)
  local copies, waits for them, and re-layouts  9.48 us (14%)
  other arithmetic  4.34 us (6%)
  matrix products  1.86 us (3%)
  between operations  1.01 us (1%)
    ppermute x4, waiting for transfers between devices, butterfly_sum(): partner = lax.ppermute(value, axis, [(i, i ^ step) for i in range(count)])  11.8 us
    ppermute x4, starting transfers between devices, butterfly_sum(): partner = lax.ppermute(value, axis, [(i, i ^ step) for i in range(count)])  9.06 us
    pallas_call x1, Pallas kernels, local(): pl.pallas_call(forward_kernel, out_shape=(jax.ShapeDtypeStruct((row_count...  7.89 us
    ppermute x2, waiting for transfers between devices, with_halo(): lax.ppermute(lax.slice_in_dim(block, 0, width, axis=dim), axis, backward)  4.3 us
    ppermute x2, starting transfers between devices, with_halo(): lax.ppermute(lax.slice_in_dim(block, block.shape[dim] - width, None, axis...  3.98 us
    ppermute x2, starting transfers between devices, with_halo(): lax.ppermute(lax.slice_in_dim(block, 0, width, axis=dim), axis, backward)  3.54 us
    pallas_call x1, Pallas kernels, local(): pl.pallas_call(adjoint_kernel, out_shape=jax.ShapeDtypeStruct(((row_count...  3.48 us
    unnamed x20, local copies, waits for them, and re-layouts  3.37 us
  transfers between devices with their start and end apart: 13, of which 7 were waited for; matrix products, arithmetic and copies ran while one was open for 15% of the time, Pallas kernels for 5%

profile of v15, /device:TPU:0, one launch (start us, length us, event | category | flops | bytes accessed | tf_op | source)
XLA Modules:
  0.0 68.6 jit_solution(11394029813733577672)
XLA Ops:
  0.6 0.0 copy-start
  0.6 0.0 copy-start.5
  0.7 1.0 %convert_element_type.46 = bf16[24,45,8]{1,2,0:T(8,128)(2,1)S(1)} convert(s32[24,45,8]{1,2,0:T(8,128)} %param.7) | non-fusion elementwise | flops 8640 | bytes 51840 | tf_op jit(solution)/shard_map/convert_element_type | solution.py:132
  1.6 0.2 copy.35
  1.9 0.1 reshape.114
  2.0 0.4 fusion.6
  2.4 0.2 reshape.115
  2.6 0.0 copy-done.5
  2.6 0.0 copy-start.1
  2.6 0.0 copy-start.7
  2.6 0.1 copy_multiply_fusion
  2.8 2.4 %collective-permute-start = (bf16[1,45,264]{2,1,0:T(8,128)(2,1)S(1)}, bf16[1,45,264]{2,1,0:T(8,128)(2,1)S(1)}, u32[]{:S(2)}, u32[]{:S(2)}) collective-permute-start(bf16[1,45,264]{2,1,0:T(8,128)(2,1)S(1)} %get-tuple-element.22), channel_id=1, source_target_pairs={{0,4},{4,8},{8,12},{12,16},{16,20},{20,24},{24,28},{1,5},{5,9},{9,... | collective-permute-start | bytes 71288 | tf_op jit(solution)/shard_map/ppermute | solution.py:18
  5.2 1.3 %collective-permute-start.1 = (bf16[1,45,264]{2,1,0:T(8,128)(2,1)S(1)}, bf16[1,45,264]{2,1,0:T(8,128)(2,1)S(1)}, u32[]{:S(2)}, u32[]{:S(2)}) collective-permute-start(bf16[1,45,264]{2,1,0:T(8,128)(2,1)S(1)} %get-tuple-element.23), channel_id=1, source_target_pairs={{4,0},{8,4},{12,8},{16,12},{20,16},{24,20},{28,24},{5,1},{9,5},{13... | collective-permute-start | bytes 71288 | tf_op jit(solution)/shard_map/ppermute | solution.py:21
  6.5 0.0 copy-done
  6.5 0.1 constant_dynamic-slice_fusion
  6.6 0.2 copy.48
  6.8 0.0 copy-done.7
  6.8 0.1 compare_convert_fusion
  6.9 0.1 copy.37
  7.0 0.0 copy-start.6
  7.0 1.1 %fusion.18 = bf16[24,4,3,48,64]{4,0,3,2,1:T(8,128)(2,1)S(1)} fusion(s32[48,64]{1,0:T(8,128)S(1)} %iota_subtract_fusion, pred[48]{0:T(512)(128)(4,1)S(1)} %iota_compare_fusion.6, bf16[24,4,3,17]{3,0,2,1:T(8,128)(2,1)S(1)} %copy.48, bf16[24,17]{1,0:T(8,128)(2,1)S(1)} %constant_dynamic-slice_fusion.1), kind=kOutput, calls=%fused_computation.27 | convolution fusion | flops 30205056 | bytes 1792416 | tf_op jit(solution)/shard_map/ibae,ejp->ibajp/dot_general | solution.py:164
  8.2 0.0 copy-done.1
  8.2 0.0 collective-permute-done
  8.2 2.2 %collective-permute-done.1 = bf16[1,45,264]{2,1,0:T(8,128)(2,1)S(1)} collective-permute-done((bf16[1,45,264]{2,1,0:T(8,128)(2,1)S(1)}, bf16[1,45,264]{2,1,0:T(8,128)(2,1)S(1)}, u32[]{:S(2)}, u32[]{:S(2)}) %collective-permute-start.1) | collective-permute-done | bytes 23792 | tf_op jit(solution)/shard_map/ppermute | solution.py:21
  10.4 0.8 %pad_maximum_fusion.3 = (bf16[26,8,264]{2,1,0:T(8,128)(2,1)}, bf16[26,8,264]{2,1,0:T(8,128)(2,1)}) fusion(bf16[1,45,264]{2,1,0:T(8,128)(2,1)S(1)} %collective-permute-done.1, bf16[1,45,264]{2,1,0:T(8,128)(2,1)S(1)} %collective-permute-done, bf16[24,45,8]{2,1,0:T(8,128)(2,1)S(1)} %copy.35, bf16[24,45,256]{2,1,0:T(8,128)(2,1)S(1)} %copy_multiply_fusion), kind=kLoop, calls=%fused_computation.35 | loop fusion | flops 878592 | bytes 837408 | tf_op jit(solution)/shard_map/slice | solution.py:19
  11.2 1.6 %collective-permute-start.2 = (bf16[26,8,264]{2,1,0:T(8,128)(2,1)}, bf16[26,8,264]{2,1,0:T(8,128)(2,1)S(1)}, u32[]{:S(2)}, u32[]{:S(2)}) collective-permute-start(bf16[26,8,264]{2,1,0:T(8,128)(2,1)} %get-tuple-element.20), channel_id=1, source_target_pairs={{0,1},{1,2},{2,3},{3,0},{4,5},{5,6},{6,7},{7,4},{8,9},{9,10},{10,1... | collective-permute-start | bytes 329480 | tf_op jit(solution)/shard_map/ppermute | solution.py:18
  12.7 2.2 %collective-permute-start.3 = (bf16[26,8,264]{2,1,0:T(8,128)(2,1)}, bf16[26,8,264]{2,1,0:T(8,128)(2,1)}, u32[]{:S(2)}, u32[]{:S(2)}) collective-permute-start(bf16[26,8,264]{2,1,0:T(8,128)(2,1)} %get-tuple-element.21), channel_id=1, source_target_pairs={{1,0},{2,1},{3,2},{0,3},{5,4},{6,5},{7,6},{4,7},{9,8},{10,9},{11,1... | collective-permute-start | bytes 329480 | tf_op jit(solution)/shard_map/ppermute | solution.py:21
  15.0 0.7 multiply_bitcast_fusion
  15.7 2.6 %copy.52.t_ref = bf16[24,4,3,48,64]{4,3,2,1,0:T(8,128)(2,1)} copy(bf16[24,4,3,48,64]{4,0,3,2,1:T(8,128)(2,1)S(1)} %fusion.18) | data formatting | bytes 3538944 | tf_op jit(solution)/shard_map/ibae,ejp->ibajp/dot_general | solution.py:164
  18.3 1.4 %reshape.118.w_ref = bf16[4,256,256]{2,1,0:T(8,128)(2,1)S(1)} reshape(bf16[4,8,32,8,32]{4,3,2,1,0:T(8,128)(2,1)S(1)} %multiply_bitcast_fusion) | data formatting | bytes 1048576 | tf_op jit(solution)/shard_map/reshape | solution.py:169
  19.7 0.0 copy-start.4
  19.7 1.2 %copy.40 = bf16[24,45,256]{2,1,0:T(8,128)(2,1)S(1)} copy(bf16[24,45,256]{2,0,1:T(8,128)(2,1)} %param.11) | data formatting | bytes 1105920 | tf_op args[5]
  21.0 0.0 collective-permute-done.2
  21.0 2.1 %collective-permute-done.3 = bf16[26,8,264]{2,1,0:T(8,128)(2,1)} collective-permute-done((bf16[26,8,264]{2,1,0:T(8,128)(2,1)}, bf16[26,8,264]{2,1,0:T(8,128)(2,1)}, u32[]{:S(2)}, u32[]{:S(2)}) %collective-permute-start.3) | collective-permute-done | bytes 109856 | tf_op jit(solution)/shard_map/ppermute | solution.py:21
  23.1 1.2 %fusion.9 = bf16[26,64,264]{2,1,0:T(8,128)(2,1)S(1)} fusion(bf16[26,8,264]{2,1,0:T(8,128)(2,1)} %collective-permute-done.3, bf16[26,8,264]{2,1,0:T(8,128)(2,1)S(1)} %collective-permute-done.2, bf16[1,45,264]{2,1,0:T(8,128)(2,1)S(1)} %collective-permute-done.1, bf16[1,45,264]{2,1,0:T(8,128)(2,1)S(1)} %collective-permute-done, ...), kind=kLoop, calls=%fused_computation.15 | loop fusion | flops 8346624 | bytes 1716000 | tf_op jit(solution)/shard_map/concatenate | solution.py:22
  24.4 0.1 slice.54
  24.4 0.1 slice.53
  24.5 0.4 convolution_convert_fusion.m_ref
  24.9 7.9 %shard_map.85 = (bf16[24,45,256]{2,1,0:T(8,128)(2,1)S(1)}, f32[4,32,256]{2,1,0:T(8,128)S(1)}, bf16[4,1152,256]{2,1,0:T(8,128)(2,1)S(1)}) custom-call(bf16[1664,256]{1,0:T(8,128)(2,1)S(1)} %bitcast.28, bf16[1664,256]{1,0:T(8,128)(2,1)S(1)} %convolution_convert_fusion.m_ref, bf16[24,4,3,48,64]{4,3,2,1,0:T(8,128)(2,1)} %copy.52.t_ref, ...), custom_call_target="tpu_custom_call" | custom-call | flops 2717908992 | bytes 3407872 | tf_op jit(solution)/shard_map/pallas_call | solution.py:174
  32.8 0.2 collective-permute-start.4
  33.0 1.2 %collective-permute-done.4.order_ref = f32[4,32,256]{2,1,0:T(8,128)S(1)} collective-permute-done((f32[4,32,256]{2,1,0:T(8,128)S(1)}, f32[4,32,256]{2,1,0:T(8,128)S(1)}, u32[]{:S(2)}, u32[]{:S(2)}) %collective-permute-start.4) | collective-permute-done | bytes 131104 | tf_op jit(solution)/shard_map/ppermute | solution.py:198
  34.2 2.8 %collective-permute-start.9 = (f32[4,32,256]{2,1,0:T(8,128)S(1)}, f32[4,32,256]{2,1,0:T(8,128)S(1)}, u32[]{:S(2)}, u32[]{:S(2)}) collective-permute-start(f32[4,32,256]{2,1,0:T(8,128)S(1)} %add.58), channel_id=1, source_target_pairs={{0,8},{4,12},{8,0},{12,4},{16,24},{20,28},{24,16},{28,20},{1,9},{5... | collective-permute-start | bytes 393224 | tf_op jit(solution)/shard_map/ppermute | solution.py:49
  37.0 3.5 %shard_map.86 = f32[1664,256]{1,0:T(8,128)S(1)} custom-call(bf16[24,4,3,48,64]{4,3,2,1,0:T(8,128)(2,1)} %copy.52.t_ref, bf16[4,1152,256]{2,1,0:T(8,128)(2,1)S(1)} %get-tuple-element.7.pulled_ref, f32[4,32,256]{2,1,0:T(8,128)S(1)} %collective-permute-done.4.order_ref), custom_call_target="tpu_custom_call" | custom-call | flops 452984832 | bytes 2555904 | tf_op jit(solution)/shard_map/pallas_call | solution.py:206
  40.5 1.8 %collective-permute-start.5 = (f32[1,61,256]{2,1,0:T(8,128)S(1)}, f32[1,61,256]{2,1,0:T(8,128)S(1)}, u32[]{:S(2)}, u32[]{:S(2)}) collective-permute-start(f32[1,61,256]{2,1,0:T(8,128)S(1)} %get-tuple-element.18), channel_id=1, source_target_pairs={{0,4},{4,8},{8,12},{12,16},{16,20},{20,24},{24,28},{1,5},{5,9},{9,... | collective-permute-start | bytes 187400 | tf_op jit(solution)/shard_map/ppermute | solution.py:29
  42.3 1.3 %collective-permute-start.6 = (f32[1,61,256]{2,1,0:T(8,128)S(1)}, f32[1,61,256]{2,1,0:T(8,128)S(1)}, u32[]{:S(2)}, u32[]{:S(2)}) collective-permute-start(f32[1,61,256]{2,1,0:T(8,128)S(1)} %get-tuple-element.19), channel_id=1, source_target_pairs={{4,0},{8,4},{12,8},{16,12},{20,16},{24,20},{28,24},{5,1},{9,5},{13... | collective-permute-start | bytes 187400 | tf_op jit(solution)/shard_map/ppermute | solution.py:29
  43.6 0.0 collective-permute-done.9
  43.6 4.0 %collective-permute-start.10 = (f32[4,32,256]{2,1,0:T(8,128)S(1)}, f32[4,32,256]{2,1,0:T(8,128)S(1)}, u32[]{:S(2)}, u32[]{:S(2)}) collective-permute-start(f32[4,32,256]{2,1,0:T(8,128)S(1)} %add.59), channel_id=1, source_target_pairs={{0,16},{4,20},{8,24},{12,28},{16,0},{20,4},{24,8},{28,12},{1,17},{... | collective-permute-start | bytes 393224 | tf_op jit(solution)/shard_map/ppermute | solution.py:49
  47.6 0.0 collective-permute-done.5
  47.6 0.0 collective-permute-done.6
  47.6 0.1 fusion.7
  47.8 1.2 %collective-permute-start.8 = (f32[24,8,256]{2,1,0:T(8,128)S(1)}, f32[24,8,256]{2,1,0:T(8,128)S(1)}, u32[]{:S(2)}, u32[]{:S(2)}) collective-permute-start(f32[24,8,256]{2,1,0:T(8,128)S(1)} %slice.60), channel_id=1, source_target_pairs={{0,1},{1,2},{2,3},{3,0},{4,5},{5,6},{6,7},{7,4},{8,9},{9,10},{10,1... | collective-permute-start | bytes 589832 | tf_op jit(solution)/shard_map/ppermute | solution.py:34
  49.0 1.8 %collective-permute-done.10 = f32[4,32,256]{2,1,0:T(8,128)S(1)} collective-permute-done((f32[4,32,256]{2,1,0:T(8,128)S(1)}, f32[4,32,256]{2,1,0:T(8,128)S(1)}, u32[]{:S(2)}, u32[]{:S(2)}) %collective-permute-start.10) | collective-permute-done | bytes 131104 | tf_op jit(solution)/shard_map/ppermute | solution.py:49
  50.8 1.2 %collective-permute-start.11 = (f32[4,32,256]{2,1,0:T(8,128)S(1)}, f32[4,32,256]{2,1,0:T(8,128)S(1)}, u32[]{:S(2)}, u32[]{:S(2)}) collective-permute-start(f32[4,32,256]{2,1,0:T(8,128)S(1)} %add.60), channel_id=1, source_target_pairs={{0,1},{1,0},{2,3},{3,2},{4,5},{5,4},{6,7},{7,6},{8,9},{9,8},{10,11... | collective-permute-start | bytes 393224 | tf_op jit(solution)/shard_map/ppermute | solution.py:49
  52.0 1.6 %collective-permute-start.7 = (bf16[24,8,256]{2,1,0:T(8,128)(2,1)S(1)}, bf16[24,8,256]{2,1,0:T(8,128)(2,1)S(1)}, u32[]{:S(2)}, u32[]{:S(2)}) collective-permute-start(bf16[24,8,256]{2,1,0:T(8,128)(2,1)S(1)} %slice.72), channel_id=1, source_target_pairs={{0,3},{1,0},{2,1},{3,2},{4,7},{5,4},{6,5},{7,6},{8,11},{9,8},{10,9... | collective-permute-start | bytes 294920 | tf_op jit(solution)/shard_map/ppermute | solution.py:34
  53.6 1.0 %copy.43 = bf16[24,45,256]{2,0,1:T(8,128)(2,1)} copy(bf16[24,45,256]{2,1,0:T(8,128)(2,1)S(1)} %get-tuple-element.15) | data formatting | bytes 1105920
  54.6 5.3 %collective-permute-done.11 = f32[4,32,256]{2,1,0:T(8,128)S(1)} collective-permute-done((f32[4,32,256]{2,1,0:T(8,128)S(1)}, f32[4,32,256]{2,1,0:T(8,128)S(1)}, u32[]{:S(2)}, u32[]{:S(2)}) %collective-permute-start.11) | collective-permute-done | bytes 131104 | tf_op jit(solution)/shard_map/ppermute | solution.py:49
  59.9 1.1 %collective-permute-start.12 = (f32[4,32,256]{2,1,0:T(8,128)S(1)}, f32[4,32,256]{2,1,0:T(8,128)S(1)}, u32[]{:S(2)}, u32[]{:S(2)}) collective-permute-start(f32[4,32,256]{2,1,0:T(8,128)S(1)} %add.61), channel_id=1, source_target_pairs={{0,2},{1,3},{2,0},{3,1},{4,6},{5,7},{6,4},{7,5},{8,10},{9,11},{10,... | collective-permute-start | bytes 393224 | tf_op jit(solution)/shard_map/ppermute | solution.py:49
  60.9 0.6 collective-permute-done.7
  61.5 0.0 collective-permute-done.8
  61.5 0.2 fusion.15
  61.8 1.0 %copy.44 = bf16[24,45,256]{2,0,1:T(8,128)(2,1)} copy(bf16[24,45,256]{2,1,0:T(8,128)(2,1)S(1)} %fusion.15) | data formatting | bytes 1105920
  62.8 4.8 %collective-permute-done.12 = f32[4,32,256]{2,1,0:T(8,128)S(1)} collective-permute-done((f32[4,32,256]{2,1,0:T(8,128)S(1)}, f32[4,32,256]{2,1,0:T(8,128)S(1)}, u32[]{:S(2)}, u32[]{:S(2)}) %collective-permute-start.12) | collective-permute-done | bytes 131104 | tf_op jit(solution)/shard_map/ppermute | solution.py:49
  67.5 0.2 reshape.120
  67.7 0.9 %copy.55 = f32[4,32,8,32]{3,1,0,2:T(8,128)} copy(f32[4,32,8,32]{3,2,1,0:T(8,128)S(1)} %reshape.120) | data formatting | bytes 262144 | tf_op jit(solution)/shard_map/reshape | solution.py:204
  (23 shorter events, 0.3 us)
Async XLA Ops:
  0.6 5.9 %copy-start = (bf16[192,4,3,17]{0,1,3,2:T(4,128)(2,1)S(1)}, bf16[192,4,3,17]{0,1,3,2:T(4,128)(2,1)}, u32[]{:S(2)}) copy-start(bf16[192,4,3,17]{0,1,3,2:T(4,128)(2,1)} %param.8) | copy-start | bytes 235012
  0.6 1.9 %copy-start.5 = (bf16[24,45,256]{2,0,1:T(8,128)(2,1)S(1)}, bf16[24,45,256]{2,0,1:T(8,128)(2,1)}, u32[]{:S(2)}) copy-start(bf16[24,45,256]{2,0,1:T(8,128)(2,1)} %param.6) | copy-start | bytes 1658884
  1.9 8.5 %copy-start.3 = (bf16[24,45,8]{2,1,0:T(8,128)(2,1)}, bf16[24,45,8]{2,1,0:T(8,128)(2,1)S(1)}, u32[]{:S(2)}) copy-start(bf16[24,45,8]{2,1,0:T(8,128)(2,1)S(1)} %copy.35) | copy-start | bytes 51844
  2.6 5.6 %copy-start.1 = (bf16[24,45,256]{2,1,0:T(8,128)(2,1)}, bf16[24,45,256]{2,1,0:T(8,128)(2,1)S(1)}, u32[]{:S(2)}) copy-start(bf16[24,45,256]{2,1,0:T(8,128)(2,1)S(1)} %reshape.115) | copy-start | bytes 1658884
  2.6 4.2 %copy-start.7 = (s32[192]{0:T(256)S(1)}, s32[192]{0:T(256)}, u32[]{:S(2)}) copy-start(s32[192]{0:T(256)} %param.9) | copy-start | bytes 2308
  2.8 5.4 %collective-permute-start = (bf16[1,45,264]{2,1,0:T(8,128)(2,1)S(1)}, bf16[1,45,264]{2,1,0:T(8,128)(2,1)S(1)}, u32[]{:S(2)}, u32[]{:S(2)}) collective-permute-start(bf16[1,45,264]{2,1,0:T(8,128)(2,1)S(1)} %get-tuple-element.22), channel_id=1, source_target_pairs={{0,4},{4,8},{8,12},{12,16},{16,20},{20,24},{24,28},{1,5},{5,9},{9,... | collective-permute-start | bytes 71288 | tf_op jit(solution)/shard_map/ppermute | solution.py:18
  5.2 5.2 %collective-permute-start.1 = (bf16[1,45,264]{2,1,0:T(8,128)(2,1)S(1)}, bf16[1,45,264]{2,1,0:T(8,128)(2,1)S(1)}, u32[]{:S(2)}, u32[]{:S(2)}) collective-permute-start(bf16[1,45,264]{2,1,0:T(8,128)(2,1)S(1)} %get-tuple-element.23), channel_id=1, source_target_pairs={{4,0},{8,4},{12,8},{16,12},{20,16},{24,20},{28,24},{5,1},{9,5},{13... | collective-permute-start | bytes 71288 | tf_op jit(solution)/shard_map/ppermute | solution.py:21
  7.0 8.0 %copy-start.6 = (bf16[8,4,32,32]{3,2,1,0:T(8,128)(2,1)S(1)}, bf16[8,4,32,32]{3,2,1,0:T(8,128)(2,1)}, u32[]{:S(2)}) copy-start(bf16[8,4,32,32]{3,2,1,0:T(8,128)(2,1)} %param.10) | copy-start | bytes 196612
  11.2 9.8 %collective-permute-start.2 = (bf16[26,8,264]{2,1,0:T(8,128)(2,1)}, bf16[26,8,264]{2,1,0:T(8,128)(2,1)S(1)}, u32[]{:S(2)}, u32[]{:S(2)}) collective-permute-start(bf16[26,8,264]{2,1,0:T(8,128)(2,1)} %get-tuple-element.20), channel_id=1, source_target_pairs={{0,1},{1,2},{2,3},{3,0},{4,5},{5,6},{6,7},{7,4},{8,9},{9,10},{10,1... | collective-permute-start | bytes 329480 | tf_op jit(solution)/shard_map/ppermute | solution.py:18
  12.7 10.4 %collective-permute-start.3 = (bf16[26,8,264]{2,1,0:T(8,128)(2,1)}, bf16[26,8,264]{2,1,0:T(8,128)(2,1)}, u32[]{:S(2)}, u32[]{:S(2)}) collective-permute-start(bf16[26,8,264]{2,1,0:T(8,128)(2,1)} %get-tuple-element.21), channel_id=1, source_target_pairs={{1,0},{2,1},{3,2},{0,3},{5,4},{6,5},{7,6},{4,7},{9,8},{10,9},{11,1... | collective-permute-start | bytes 329480 | tf_op jit(solution)/shard_map/ppermute | solution.py:21
  19.7 3.4 %copy-start.4 = (bf16[24,45,8]{2,1,0:T(8,128)(2,1)S(1)}, bf16[24,45,8]{2,1,0:T(8,128)(2,1)}, u32[]{:S(2)}) copy-start(bf16[24,45,8]{2,1,0:T(8,128)(2,1)} %copy-done.3) | copy-start | bytes 51844
  32.8 1.4 %collective-permute-start.4 = (f32[4,32,256]{2,1,0:T(8,128)S(1)}, f32[4,32,256]{2,1,0:T(8,128)S(1)}, u32[]{:S(2)}, u32[]{:S(2)}) collective-permute-start(f32[4,32,256]{2,1,0:T(8,128)S(1)} %get-tuple-element.8), channel_id=1, source_target_pairs={{0,4},{4,0},{8,12},{12,8},{16,20},{20,16},{24,28},{28,24},{1,5},{5... | collective-permute-start | bytes 393224 | tf_op jit(solution)/shard_map/ppermute | solution.py:198
  34.2 9.3 %collective-permute-start.9 = (f32[4,32,256]{2,1,0:T(8,128)S(1)}, f32[4,32,256]{2,1,0:T(8,128)S(1)}, u32[]{:S(2)}, u32[]{:S(2)}) collective-permute-start(f32[4,32,256]{2,1,0:T(8,128)S(1)} %add.58), channel_id=1, source_target_pairs={{0,8},{4,12},{8,0},{12,4},{16,24},{20,28},{24,16},{28,20},{1,9},{5... | collective-permute-start | bytes 393224 | tf_op jit(solution)/shard_map/ppermute | solution.py:49
  40.5 7.2 %collective-permute-start.5 = (f32[1,61,256]{2,1,0:T(8,128)S(1)}, f32[1,61,256]{2,1,0:T(8,128)S(1)}, u32[]{:S(2)}, u32[]{:S(2)}) collective-permute-start(f32[1,61,256]{2,1,0:T(8,128)S(1)} %get-tuple-element.18), channel_id=1, source_target_pairs={{0,4},{4,8},{8,12},{12,16},{16,20},{20,24},{24,28},{1,5},{5,9},{9,... | collective-permute-start | bytes 187400 | tf_op jit(solution)/shard_map/ppermute | solution.py:29
  42.3 5.4 %collective-permute-start.6 = (f32[1,61,256]{2,1,0:T(8,128)S(1)}, f32[1,61,256]{2,1,0:T(8,128)S(1)}, u32[]{:S(2)}, u32[]{:S(2)}) collective-permute-start(f32[1,61,256]{2,1,0:T(8,128)S(1)} %get-tuple-element.19), channel_id=1, source_target_pairs={{4,0},{8,4},{12,8},{16,12},{20,16},{24,20},{28,24},{5,1},{9,5},{13... | collective-permute-start | bytes 187400 | tf_op jit(solution)/shard_map/ppermute | solution.py:29
  43.6 7.2 %collective-permute-start.10 = (f32[4,32,256]{2,1,0:T(8,128)S(1)}, f32[4,32,256]{2,1,0:T(8,128)S(1)}, u32[]{:S(2)}, u32[]{:S(2)}) collective-permute-start(f32[4,32,256]{2,1,0:T(8,128)S(1)} %add.59), channel_id=1, source_target_pairs={{0,16},{4,20},{8,24},{12,28},{16,0},{20,4},{24,8},{28,12},{1,17},{... | collective-permute-start | bytes 393224 | tf_op jit(solution)/shard_map/ppermute | solution.py:49
  47.8 13.8 %copy-start.2 = (bf16[24,45,256]{2,1,0:T(8,128)(2,1)S(1)}, bf16[24,45,256]{2,1,0:T(8,128)(2,1)}, u32[]{:S(2)}) copy-start(bf16[24,45,256]{2,1,0:T(8,128)(2,1)} %copy-done.1) | copy-start | bytes 1658884
  47.8 13.7 %collective-permute-start.8 = (f32[24,8,256]{2,1,0:T(8,128)S(1)}, f32[24,8,256]{2,1,0:T(8,128)S(1)}, u32[]{:S(2)}, u32[]{:S(2)}) collective-permute-start(f32[24,8,256]{2,1,0:T(8,128)S(1)} %slice.60), channel_id=1, source_target_pairs={{0,1},{1,2},{2,3},{3,0},{4,5},{5,6},{6,7},{7,4},{8,9},{9,10},{10,1... | collective-permute-start | bytes 589832 | tf_op jit(solution)/shard_map/ppermute | solution.py:34
  50.8 9.0 %collective-permute-start.11 = (f32[4,32,256]{2,1,0:T(8,128)S(1)}, f32[4,32,256]{2,1,0:T(8,128)S(1)}, u32[]{:S(2)}, u32[]{:S(2)}) collective-permute-start(f32[4,32,256]{2,1,0:T(8,128)S(1)} %add.60), channel_id=1, source_target_pairs={{0,1},{1,0},{2,3},{3,2},{4,5},{5,4},{6,7},{7,6},{8,9},{9,8},{10,11... | collective-permute-start | bytes 393224 | tf_op jit(solution)/shard_map/ppermute | solution.py:49
  52.0 9.5 %collective-permute-start.7 = (bf16[24,8,256]{2,1,0:T(8,128)(2,1)S(1)}, bf16[24,8,256]{2,1,0:T(8,128)(2,1)S(1)}, u32[]{:S(2)}, u32[]{:S(2)}) collective-permute-start(bf16[24,8,256]{2,1,0:T(8,128)(2,1)S(1)} %slice.72), channel_id=1, source_target_pairs={{0,3},{1,0},{2,1},{3,2},{4,7},{5,4},{6,5},{7,6},{8,11},{9,8},{10,9... | collective-permute-start | bytes 294920 | tf_op jit(solution)/shard_map/ppermute | solution.py:34
  59.9 7.7 %collective-permute-start.12 = (f32[4,32,256]{2,1,0:T(8,128)S(1)}, f32[4,32,256]{2,1,0:T(8,128)S(1)}, u32[]{:S(2)}, u32[]{:S(2)}) collective-permute-start(f32[4,32,256]{2,1,0:T(8,128)S(1)} %add.61), channel_id=1, source_target_pairs={{0,2},{1,3},{2,0},{3,1},{4,6},{5,7},{6,4},{7,5},{8,10},{9,11},{10,... | collective-permute-start | bytes 393224 | tf_op jit(solution)/shard_map/ppermute | solution.py:49

commit v16 on v15

--- a/solution.py
+++ b/solution.py
@@ -50,6 +50,34 @@
             value = value + partner
             step *= 2
     return value
+
+
+def pair_round(value, lat_step, lon_step):
+    lat_count = lax.axis_size("lat")
+    lon_count = lax.axis_size("lon")
+    across_lat = lax.ppermute(value, "lat", [(i, i ^ lat_step) for i in range(lat_count)])
+    across_lon = lax.ppermute(value, "lon", [(i, i ^ lon_step) for i in range(lon_count)])
+    diagonal = lax.ppermute(
+        value,
+        ("lat", "lon"),
+        [
+            (a * lon_count + b, (a ^ lat_step) * lon_count + (b ^ lon_step))
+            for a in range(lat_count)
+            for b in range(lon_count)
+        ],
+    )
+    held = {(0, 0): value, (1, 0): across_lat, (0, 1): across_lon, (1, 1): diagonal}
+    my_lat = (lax.axis_index("lat") // lat_step) % 2
+    my_lon = (lax.axis_index("lon") // lon_step) % 2
+    total = None
+    for x in (0, 1):
+        for y in (0, 1):
+            piece = None
+            for (dx, dy), part in held.items():
+                chosen = jnp.where(((my_lat ^ x) == dx) & ((my_lon ^ y) == dy), part, 0.0)
+                piece = chosen if piece is None else piece + chosen
+            total = piece if total is None else total + piece
+    return total
 
 
 def forward_kernel(x_ref, m_ref, t_ref, cot_ref, w_ref, inf_ref, wg_ref, pulled_ref, scaled_ref, safe_ref):
@@ -194,9 +222,18 @@
 
     cell_count = row_count * lax.axis_size("lat") * col_count * lax.axis_size("lon")
     lat_count = lax.axis_size("lat")
-    if lat_count % 2 == 0:
+    lon_count = lax.axis_size("lon")
+    if lat_count > 1 and not lat_count & (lat_count - 1) and not lon_count & (lon_count - 1):
         first = lax.ppermute(grad_blocks, "lat", [(i, i ^ 1) for i in range(lat_count)])
-        dense = butterfly_sum(grad_blocks + first, ("lat", "lon"), skip=1)
+        dense = grad_blocks + first
+        lat_steps = [1 << k for k in range(1, lat_count.bit_length() - 1)]
+        lon_steps = [1 << k for k in range(lon_count.bit_length() - 1)]
+        while lat_steps and lon_steps:
+            dense = pair_round(dense, lat_steps.pop(0), lon_steps.pop(0))
+        for step in lat_steps:
+            dense = dense + lax.ppermute(dense, "lat", [(i, i ^ step) for i in range(lat_count)])
+        for step in lon_steps:
+            dense = dense + lax.ppermute(dense, "lon", [(i, i ^ step) for i in range(lon_count)])
     else:
         first = grad_blocks
         dense = butterfly_sum(grad_blocks, ("lat", "lon"))

time: 68.9 us -> 73.3 us (1.064)
  starting transfers between devices: 22.6 us -> 25.9 us
  waiting for transfers between devices: 18 us -> 18.8 us
    ppermute x4 -> x6, starting transfers between devices: 9.06 us -> 10.9 us  [the longest x2 7.94 us: pair_round(): lax.ppermute(value, ('lat', 'lon'), [(a * lon_count + b, (a ^ lat_step) *...]
    ppermute x4 -> x6, waiting for transfers between devices: 11.8 us -> 13.3 us  [the longest x2 6.7 us: pair_round(): lax.ppermute(value, 'lon', [(i, i ^ lon_step) for i in range(lon_count)])]
    ppermute x2, starting transfers between devices: 2.75 us -> 3.88 us  [from_behind(): return lax.ppermute(x, axis, [(i, (i + by) % size) for i in range(size)])]
  transfers between devices with their start and end apart: 13 -> 15, of which waited for: 7 -> 7; matrix products, arithmetic and copies ran while one was open for 15% -> 14% of each run, Pallas kernels for 5% -> 0%
where the time goes in v16:
time: 73.3 us; the launch traced here: 72.9 us
  starting transfers between devices  25.9 us (35%)
  waiting for transfers between devices  18.8 us (26%)
  Pallas kernels  11.2 us (15%)
  local copies, waits for them, and re-layouts  9.47 us (13%)
  other arithmetic  4.56 us (6%)
  matrix products  1.85 us (3%)
  between operations  1.16 us (2%)
    ppermute x2, starting transfers between devices, pair_round(): lax.ppermute(value, ('lat', 'lon'), [(a * lon_count + b, (a ^ lat_step) *...  7.94 us
    pallas_call x1, Pallas kernels, local(): pl.pallas_call(forward_kernel, out_shape=(jax.ShapeDtypeStruct((row_count...  7.74 us
    ppermute x2, waiting for transfers between devices, pair_round(): lax.ppermute(value, 'lon', [(i, i ^ lon_step) for i in range(lon_count)])  6.7 us
    ppermute x2, waiting for transfers between devices, pair_round(): lax.ppermute(value, ('lat', 'lon'), [(a * lon_count + b, (a ^ lat_step) *...  5.77 us
    ppermute x2, waiting for transfers between devices, with_halo(): lax.ppermute(lax.slice_in_dim(block, 0, width, axis=dim), axis, backward)  4.3 us
    ppermute x2, starting transfers between devices, with_halo(): lax.ppermute(lax.slice_in_dim(block, block.shape[dim] - width, None, axis...  3.98 us
    ppermute x2, starting transfers between devices, from_behind(): return lax.ppermute(x, axis, [(i, (i + by) % size) for i in range(size)])  3.88 us
    ppermute x2, starting transfers between devices, with_halo(): lax.ppermute(lax.slice_in_dim(block, 0, width, axis=dim), axis, backward)  3.54 us
  transfers between devices with their start and end apart: 15, of which 7 were waited for; matrix products, arithmetic and copies ran while one was open for 14% of the time, Pallas kernels for 0%

profile of v16, /device:TPU:0, one launch (start us, length us, event | category | flops | bytes accessed | tf_op | source)
XLA Modules:
  0.0 72.9 jit_solution(6800521628853507940)
XLA Ops:
  0.6 0.0 copy-start
  0.7 1.0 %convert_element_type.46 = bf16[24,45,8]{1,2,0:T(8,128)(2,1)S(1)} convert(s32[24,45,8]{1,2,0:T(8,128)} %param.7) | non-fusion elementwise | flops 8640 | bytes 51840 | tf_op jit(solution)/shard_map/convert_element_type | solution.py:160
  1.6 0.2 copy.35
  1.9 0.1 reshape.114
  2.0 0.4 fusion.6
  2.4 0.2 reshape.115
  2.6 0.0 copy-start.7
  2.6 0.1 copy_multiply_fusion
  2.7 2.4 %collective-permute-start = (bf16[1,45,264]{2,1,0:T(8,128)(2,1)S(1)}, bf16[1,45,264]{2,1,0:T(8,128)(2,1)S(1)}, u32[]{:S(2)}, u32[]{:S(2)}) collective-permute-start(bf16[1,45,264]{2,1,0:T(8,128)(2,1)S(1)} %get-tuple-element.22), channel_id=1, source_target_pairs={{0,4},{4,8},{8,12},{12,16},{16,20},{20,24},{24,28},{1,5},{5,9},{9,... | collective-permute-start | bytes 71288 | tf_op jit(solution)/shard_map/ppermute | solution.py:18
  5.2 1.3 %collective-permute-start.1 = (bf16[1,45,264]{2,1,0:T(8,128)(2,1)S(1)}, bf16[1,45,264]{2,1,0:T(8,128)(2,1)S(1)}, u32[]{:S(2)}, u32[]{:S(2)}) collective-permute-start(bf16[1,45,264]{2,1,0:T(8,128)(2,1)S(1)} %get-tuple-element.23), channel_id=1, source_target_pairs={{4,0},{8,4},{12,8},{16,12},{20,16},{24,20},{28,24},{5,1},{9,5},{13... | collective-permute-start | bytes 71288 | tf_op jit(solution)/shard_map/ppermute | solution.py:21
  6.5 0.1 constant_dynamic-slice_fusion
  6.6 0.2 copy.48
  6.8 0.1 compare_convert_fusion
  6.9 0.1 copy.37
  7.0 0.0 copy-start.6
  7.0 1.1 %fusion.18 = bf16[24,4,3,48,64]{4,0,3,2,1:T(8,128)(2,1)S(1)} fusion(s32[48,64]{1,0:T(8,128)S(1)} %iota_subtract_fusion, pred[48]{0:T(512)(128)(4,1)S(1)} %iota_compare_fusion.6, bf16[24,4,3,17]{3,0,2,1:T(8,128)(2,1)S(1)} %copy.48, bf16[24,17]{1,0:T(8,128)(2,1)S(1)} %constant_dynamic-slice_fusion.1), kind=kOutput, calls=%fused_computation.27 | convolution fusion | flops 30205056 | bytes 1792416 | tf_op jit(solution)/shard_map/ibae,ejp->ibajp/dot_general | solution.py:192
  8.2 0.0 collective-permute-done
  8.2 2.2 %collective-permute-done.1 = bf16[1,45,264]{2,1,0:T(8,128)(2,1)S(1)} collective-permute-done((bf16[1,45,264]{2,1,0:T(8,128)(2,1)S(1)}, bf16[1,45,264]{2,1,0:T(8,128)(2,1)S(1)}, u32[]{:S(2)}, u32[]{:S(2)}) %collective-permute-start.1) | collective-permute-done | bytes 23792 | tf_op jit(solution)/shard_map/ppermute | solution.py:21
  10.4 0.8 %pad_maximum_fusion.3 = (bf16[26,8,264]{2,1,0:T(8,128)(2,1)}, bf16[26,8,264]{2,1,0:T(8,128)(2,1)}) fusion(bf16[1,45,264]{2,1,0:T(8,128)(2,1)S(1)} %collective-permute-done.1, bf16[1,45,264]{2,1,0:T(8,128)(2,1)S(1)} %collective-permute-done, bf16[24,45,8]{2,1,0:T(8,128)(2,1)S(1)} %copy.35, bf16[24,45,256]{2,1,0:T(8,128)(2,1)S(1)} %copy_multiply_fusion), kind=kLoop, calls=%fused_computation.35 | loop fusion | flops 878592 | bytes 837408 | tf_op jit(solution)/shard_map/slice | solution.py:19
  11.2 1.6 %collective-permute-start.2 = (bf16[26,8,264]{2,1,0:T(8,128)(2,1)}, bf16[26,8,264]{2,1,0:T(8,128)(2,1)S(1)}, u32[]{:S(2)}, u32[]{:S(2)}) collective-permute-start(bf16[26,8,264]{2,1,0:T(8,128)(2,1)} %get-tuple-element.20), channel_id=1, source_target_pairs={{0,1},{1,2},{2,3},{3,0},{4,5},{5,6},{6,7},{7,4},{8,9},{9,10},{10,1... | collective-permute-start | bytes 329480 | tf_op jit(solution)/shard_map/ppermute | solution.py:18
  12.7 2.2 %collective-permute-start.3 = (bf16[26,8,264]{2,1,0:T(8,128)(2,1)}, bf16[26,8,264]{2,1,0:T(8,128)(2,1)}, u32[]{:S(2)}, u32[]{:S(2)}) collective-permute-start(bf16[26,8,264]{2,1,0:T(8,128)(2,1)} %get-tuple-element.21), channel_id=1, source_target_pairs={{1,0},{2,1},{3,2},{0,3},{5,4},{6,5},{7,6},{4,7},{9,8},{10,9},{11,1... | collective-permute-start | bytes 329480 | tf_op jit(solution)/shard_map/ppermute | solution.py:21
  15.0 0.7 multiply_bitcast_fusion
  15.7 2.6 %copy.52.t_ref = bf16[24,4,3,48,64]{4,3,2,1,0:T(8,128)(2,1)} copy(bf16[24,4,3,48,64]{4,0,3,2,1:T(8,128)(2,1)S(1)} %fusion.18) | data formatting | bytes 3538944 | tf_op jit(solution)/shard_map/ibae,ejp->ibajp/dot_general | solution.py:192
  18.3 1.4 %reshape.118.w_ref = bf16[4,256,256]{2,1,0:T(8,128)(2,1)S(1)} reshape(bf16[4,8,32,8,32]{4,3,2,1,0:T(8,128)(2,1)S(1)} %multiply_bitcast_fusion) | data formatting | bytes 1048576 | tf_op jit(solution)/shard_map/reshape | solution.py:197
  19.7 0.0 copy-start.4
  19.7 1.2 %copy.40 = bf16[24,45,256]{2,1,0:T(8,128)(2,1)S(1)} copy(bf16[24,45,256]{2,0,1:T(8,128)(2,1)} %param.11) | data formatting | bytes 1105920 | tf_op args[5]
  21.0 0.0 collective-permute-done.2
  21.0 2.1 %collective-permute-done.3 = bf16[26,8,264]{2,1,0:T(8,128)(2,1)} collective-permute-done((bf16[26,8,264]{2,1,0:T(8,128)(2,1)}, bf16[26,8,264]{2,1,0:T(8,128)(2,1)}, u32[]{:S(2)}, u32[]{:S(2)}) %collective-permute-start.3) | collective-permute-done | bytes 109856 | tf_op jit(solution)/shard_map/ppermute | solution.py:21
  23.1 1.2 %fusion.9 = bf16[26,64,264]{2,1,0:T(8,128)(2,1)S(1)} fusion(bf16[26,8,264]{2,1,0:T(8,128)(2,1)} %collective-permute-done.3, bf16[26,8,264]{2,1,0:T(8,128)(2,1)S(1)} %collective-permute-done.2, bf16[1,45,264]{2,1,0:T(8,128)(2,1)S(1)} %collective-permute-done.1, bf16[1,45,264]{2,1,0:T(8,128)(2,1)S(1)} %collective-permute-done, ...), kind=kLoop, calls=%fused_computation.15 | loop fusion | flops 8346624 | bytes 1716000 | tf_op jit(solution)/shard_map/concatenate | solution.py:22
  24.4 0.1 slice.54
  24.4 0.1 slice.53
  24.5 0.4 convolution_convert_fusion.m_ref
  24.9 7.7 %shard_map.85 = (bf16[24,45,256]{2,1,0:T(8,128)(2,1)S(1)}, f32[4,32,256]{2,1,0:T(8,128)S(1)}, bf16[4,1152,256]{2,1,0:T(8,128)(2,1)S(1)}) custom-call(bf16[1664,256]{1,0:T(8,128)(2,1)S(1)} %bitcast.28, bf16[1664,256]{1,0:T(8,128)(2,1)S(1)} %convolution_convert_fusion.m_ref, bf16[24,4,3,48,64]{4,3,2,1,0:T(8,128)(2,1)} %copy.52.t_ref, ...), custom_call_target="tpu_custom_call" | custom-call | flops 2717908992 | bytes 3407872 | tf_op jit(solution)/shard_map/pallas_call | solution.py:202
  32.6 0.2 collective-permute-start.4
  32.8 1.2 %collective-permute-done.4.order_ref = f32[4,32,256]{2,1,0:T(8,128)S(1)} collective-permute-done((f32[4,32,256]{2,1,0:T(8,128)S(1)}, f32[4,32,256]{2,1,0:T(8,128)S(1)}, u32[]{:S(2)}, u32[]{:S(2)}) %collective-permute-start.4) | collective-permute-done | bytes 131104 | tf_op jit(solution)/shard_map/ppermute | solution.py:227
  34.0 3.4 %shard_map.86 = f32[1664,256]{1,0:T(8,128)S(1)} custom-call(bf16[24,4,3,48,64]{4,3,2,1,0:T(8,128)(2,1)} %copy.52.t_ref, bf16[4,1152,256]{2,1,0:T(8,128)(2,1)S(1)} %get-tuple-element.7.pulled_ref, f32[4,32,256]{2,1,0:T(8,128)S(1)} %collective-permute-done.4.order_ref), custom_call_target="tpu_custom_call" | custom-call | flops 452984832 | bytes 2555904 | tf_op jit(solution)/shard_map/pallas_call | solution.py:243
  37.5 2.1 %collective-permute-start.5 = (f32[1,61,256]{2,1,0:T(8,128)S(1)}, f32[1,61,256]{2,1,0:T(8,128)S(1)}, u32[]{:S(2)}, u32[]{:S(2)}) collective-permute-start(f32[1,61,256]{2,1,0:T(8,128)S(1)} %get-tuple-element.18), channel_id=1, source_target_pairs={{0,4},{4,8},{8,12},{12,16},{16,20},{20,24},{24,28},{1,5},{5,9},{9,... | collective-permute-start | bytes 187400 | tf_op jit(solution)/shard_map/ppermute | solution.py:29
  39.6 1.3 %collective-permute-start.6 = (f32[1,61,256]{2,1,0:T(8,128)S(1)}, f32[1,61,256]{2,1,0:T(8,128)S(1)}, u32[]{:S(2)}, u32[]{:S(2)}) collective-permute-start(f32[1,61,256]{2,1,0:T(8,128)S(1)} %get-tuple-element.19), channel_id=1, source_target_pairs={{4,0},{8,4},{12,8},{16,12},{20,16},{24,20},{28,24},{5,1},{9,5},{13... | collective-permute-start | bytes 187400 | tf_op jit(solution)/shard_map/ppermute | solution.py:29
  41.0 1.0 %copy.43 = bf16[24,45,256]{2,0,1:T(8,128)(2,1)} copy(bf16[24,45,256]{2,1,0:T(8,128)(2,1)S(1)} %get-tuple-element.15) | data formatting | bytes 1105920
  42.0 0.9 %collective-permute-start.10 = (f32[4,32,256]{2,1,0:T(8,128)S(1)}, f32[4,32,256]{2,1,0:T(8,128)S(1)}, u32[]{:S(2)}, u32[]{:S(2)}) collective-permute-start(f32[4,32,256]{2,1,0:T(8,128)S(1)} %add.157), channel_id=1, source_target_pairs={{0,1},{1,0},{2,3},{3,2},{4,5},{5,4},{6,7},{7,6},{8,9},{9,8},{10,11... | collective-permute-start | bytes 393224 | tf_op jit(solution)/shard_map/ppermute | solution.py:59
  43.0 5.5 %collective-permute-start.11 = (f32[4,32,256]{2,1,0:T(8,128)S(1)}, f32[4,32,256]{2,1,0:T(8,128)S(1)}, u32[]{:S(2)}, u32[]{:S(2)}) collective-permute-start(f32[4,32,256]{2,1,0:T(8,128)S(1)} %add.157), channel_id=1, source_target_pairs={{0,9},{1,8},{2,11},{3,10},{4,13},{5,12},{6,15},{7,14},{8,1},{9,0},... | collective-permute-start | bytes 393224 | tf_op jit(solution)/shard_map/ppermute | solution.py:60
  48.5 0.0 collective-permute-start.9
  48.5 0.0 collective-permute-done.5
  48.5 0.0 collective-permute-done.6
  48.5 0.1 fusion.7
  48.7 1.1 %collective-permute-start.8 = (f32[24,8,256]{2,1,0:T(8,128)S(1)}, f32[24,8,256]{2,1,0:T(8,128)S(1)}, u32[]{:S(2)}, u32[]{:S(2)}) collective-permute-start(f32[24,8,256]{2,1,0:T(8,128)S(1)} %slice.60), channel_id=1, source_target_pairs={{0,1},{1,2},{2,3},{3,0},{4,5},{5,6},{6,7},{7,4},{8,9},{9,10},{10,1... | collective-permute-start | bytes 589832 | tf_op jit(solution)/shard_map/ppermute | solution.py:34
  49.7 2.8 %collective-permute-start.7 = (bf16[24,8,256]{2,1,0:T(8,128)(2,1)S(1)}, bf16[24,8,256]{2,1,0:T(8,128)(2,1)S(1)}, u32[]{:S(2)}, u32[]{:S(2)}) collective-permute-start(bf16[24,8,256]{2,1,0:T(8,128)(2,1)S(1)} %slice.72), channel_id=1, source_target_pairs={{0,3},{1,0},{2,1},{3,2},{4,7},{5,4},{6,5},{7,6},{8,11},{9,8},{10,9... | collective-permute-start | bytes 294920 | tf_op jit(solution)/shard_map/ppermute | solution.py:34
  52.6 0.0 collective-permute-done.10
  52.6 3.1 %collective-permute-done.11 = f32[4,32,256]{2,1,0:T(8,128)S(1)} collective-permute-done((f32[4,32,256]{2,1,0:T(8,128)S(1)}, f32[4,32,256]{2,1,0:T(8,128)S(1)}, u32[]{:S(2)}, u32[]{:S(2)}) %collective-permute-start.11) | collective-permute-done | bytes 131104 | tf_op jit(solution)/shard_map/ppermute | solution.py:60
  55.7 0.8 %collective-permute-done.9 = f32[4,32,256]{2,1,0:T(8,128)S(1)} collective-permute-done((f32[4,32,256]{2,1,0:T(8,128)S(1)}, f32[4,32,256]{2,1,0:T(8,128)S(1)}, u32[]{:S(2)}, u32[]{:S(2)}) %collective-permute-start.9) | collective-permute-done | bytes 131104 | tf_op jit(solution)/shard_map/ppermute | solution.py:58
  56.5 0.1 add_add_fusion
  56.7 1.6 %collective-permute-start.12 = (f32[4,32,256]{2,1,0:T(8,128)S(1)}, f32[4,32,256]{2,1,0:T(8,128)S(1)}, u32[]{:S(2)}, u32[]{:S(2)}) collective-permute-start(f32[4,32,256]{2,1,0:T(8,128)S(1)} %add_add_fusion), channel_id=1, source_target_pairs={{0,16},{4,20},{8,24},{12,28},{16,0},{20,4},{24,8},{28,12},{1,17},{... | collective-permute-start | bytes 393224 | tf_op jit(solution)/shard_map/ppermute | solution.py:58
  58.3 0.5 collective-permute-start.13
  58.7 2.4 %collective-permute-start.14 = (f32[4,32,256]{2,1,0:T(8,128)S(1)}, f32[4,32,256]{2,1,0:T(8,128)S(1)}, u32[]{:S(2)}, u32[]{:S(2)}) collective-permute-start(f32[4,32,256]{2,1,0:T(8,128)S(1)} %add_add_fusion), channel_id=1, source_target_pairs={{0,18},{1,19},{2,16},{3,17},{4,22},{5,23},{6,20},{7,21},{8,26},{9,... | collective-permute-start | bytes 393224 | tf_op jit(solution)/shard_map/ppermute | solution.py:60
  61.1 0.0 collective-permute-done.7
  61.1 0.0 collective-permute-done.8
  61.1 0.3 fusion.15
  61.4 1.0 %copy.44 = bf16[24,45,256]{2,0,1:T(8,128)(2,1)} copy(bf16[24,45,256]{2,1,0:T(8,128)(2,1)S(1)} %fusion.15) | data formatting | bytes 1105920
  62.4 0.0 collective-permute-done.12
  62.4 6.7 %collective-permute-done.13 = f32[4,32,256]{2,1,0:T(8,128)S(1)} collective-permute-done((f32[4,32,256]{2,1,0:T(8,128)S(1)}, f32[4,32,256]{2,1,0:T(8,128)S(1)}, u32[]{:S(2)}, u32[]{:S(2)}) %collective-permute-start.13) | collective-permute-done | bytes 131104 | tf_op jit(solution)/shard_map/ppermute | solution.py:59
  69.1 2.6 %collective-permute-done.14 = f32[4,32,256]{2,1,0:T(8,128)S(1)} collective-permute-done((f32[4,32,256]{2,1,0:T(8,128)S(1)}, f32[4,32,256]{2,1,0:T(8,128)S(1)}, u32[]{:S(2)}, u32[]{:S(2)}) %collective-permute-start.14) | collective-permute-done | bytes 131104 | tf_op jit(solution)/shard_map/ppermute | solution.py:60
  71.7 0.1 add_multiply_fusion
  71.9 0.2 reshape.120
  72.0 0.9 %copy.55 = f32[4,32,8,32]{3,1,0,2:T(8,128)} copy(f32[4,32,8,32]{3,2,1,0:T(8,128)S(1)} %reshape.120) | data formatting | bytes 262144 | tf_op jit(solution)/shard_map/reshape | solution.py:241
  (25 shorter events, 0.2 us)
Async XLA Ops:
  0.6 5.9 %copy-start = (bf16[192,4,3,17]{0,1,3,2:T(4,128)(2,1)S(1)}, bf16[192,4,3,17]{0,1,3,2:T(4,128)(2,1)}, u32[]{:S(2)}) copy-start(bf16[192,4,3,17]{0,1,3,2:T(4,128)(2,1)} %param.8) | copy-start | bytes 235012
  0.6 1.9 %copy-start.5 = (bf16[24,45,256]{2,0,1:T(8,128)(2,1)S(1)}, bf16[24,45,256]{2,0,1:T(8,128)(2,1)}, u32[]{:S(2)}) copy-start(bf16[24,45,256]{2,0,1:T(8,128)(2,1)} %param.6) | copy-start | bytes 1658884
  1.9 8.5 %copy-start.3 = (bf16[24,45,8]{2,1,0:T(8,128)(2,1)}, bf16[24,45,8]{2,1,0:T(8,128)(2,1)S(1)}, u32[]{:S(2)}) copy-start(bf16[24,45,8]{2,1,0:T(8,128)(2,1)S(1)} %copy.35) | copy-start | bytes 51844
  2.6 5.6 %copy-start.1 = (bf16[24,45,256]{2,1,0:T(8,128)(2,1)}, bf16[24,45,256]{2,1,0:T(8,128)(2,1)S(1)}, u32[]{:S(2)}) copy-start(bf16[24,45,256]{2,1,0:T(8,128)(2,1)S(1)} %reshape.115) | copy-start | bytes 1658884
  2.6 4.2 %copy-start.7 = (s32[192]{0:T(256)S(1)}, s32[192]{0:T(256)}, u32[]{:S(2)}) copy-start(s32[192]{0:T(256)} %param.9) | copy-start | bytes 2308
  2.7 5.5 %collective-permute-start = (bf16[1,45,264]{2,1,0:T(8,128)(2,1)S(1)}, bf16[1,45,264]{2,1,0:T(8,128)(2,1)S(1)}, u32[]{:S(2)}, u32[]{:S(2)}) collective-permute-start(bf16[1,45,264]{2,1,0:T(8,128)(2,1)S(1)} %get-tuple-element.22), channel_id=1, source_target_pairs={{0,4},{4,8},{8,12},{12,16},{16,20},{20,24},{24,28},{1,5},{5,9},{9,... | collective-permute-start | bytes 71288 | tf_op jit(solution)/shard_map/ppermute | solution.py:18
  5.2 5.2 %collective-permute-start.1 = (bf16[1,45,264]{2,1,0:T(8,128)(2,1)S(1)}, bf16[1,45,264]{2,1,0:T(8,128)(2,1)S(1)}, u32[]{:S(2)}, u32[]{:S(2)}) collective-permute-start(bf16[1,45,264]{2,1,0:T(8,128)(2,1)S(1)} %get-tuple-element.23), channel_id=1, source_target_pairs={{4,0},{8,4},{12,8},{16,12},{20,16},{24,20},{28,24},{5,1},{9,5},{13... | collective-permute-start | bytes 71288 | tf_op jit(solution)/shard_map/ppermute | solution.py:21
  7.0 8.0 %copy-start.6 = (bf16[8,4,32,32]{3,2,1,0:T(8,128)(2,1)S(1)}, bf16[8,4,32,32]{3,2,1,0:T(8,128)(2,1)}, u32[]{:S(2)}) copy-start(bf16[8,4,32,32]{3,2,1,0:T(8,128)(2,1)} %param.10) | copy-start | bytes 196612
  11.2 9.8 %collective-permute-start.2 = (bf16[26,8,264]{2,1,0:T(8,128)(2,1)}, bf16[26,8,264]{2,1,0:T(8,128)(2,1)S(1)}, u32[]{:S(2)}, u32[]{:S(2)}) collective-permute-start(bf16[26,8,264]{2,1,0:T(8,128)(2,1)} %get-tuple-element.20), channel_id=1, source_target_pairs={{0,1},{1,2},{2,3},{3,0},{4,5},{5,6},{6,7},{7,4},{8,9},{9,10},{10,1... | collective-permute-start | bytes 329480 | tf_op jit(solution)/shard_map/ppermute | solution.py:18
  12.7 10.4 %collective-permute-start.3 = (bf16[26,8,264]{2,1,0:T(8,128)(2,1)}, bf16[26,8,264]{2,1,0:T(8,128)(2,1)}, u32[]{:S(2)}, u32[]{:S(2)}) collective-permute-start(bf16[26,8,264]{2,1,0:T(8,128)(2,1)} %get-tuple-element.21), channel_id=1, source_target_pairs={{1,0},{2,1},{3,2},{0,3},{5,4},{6,5},{7,6},{4,7},{9,8},{10,9},{11,1... | collective-permute-start | bytes 329480 | tf_op jit(solution)/shard_map/ppermute | solution.py:21
  19.7 3.4 %copy-start.4 = (bf16[24,45,8]{2,1,0:T(8,128)(2,1)S(1)}, bf16[24,45,8]{2,1,0:T(8,128)(2,1)}, u32[]{:S(2)}) copy-start(bf16[24,45,8]{2,1,0:T(8,128)(2,1)} %copy-done.3) | copy-start | bytes 51844
  32.6 1.4 %collective-permute-start.4 = (f32[4,32,256]{2,1,0:T(8,128)S(1)}, f32[4,32,256]{2,1,0:T(8,128)S(1)}, u32[]{:S(2)}, u32[]{:S(2)}) collective-permute-start(f32[4,32,256]{2,1,0:T(8,128)S(1)} %get-tuple-element.8), channel_id=1, source_target_pairs={{0,4},{4,0},{8,12},{12,8},{16,20},{20,16},{24,28},{28,24},{1,5},{5... | collective-permute-start | bytes 393224 | tf_op jit(solution)/shard_map/ppermute | solution.py:227
  37.5 11.0 %collective-permute-start.5 = (f32[1,61,256]{2,1,0:T(8,128)S(1)}, f32[1,61,256]{2,1,0:T(8,128)S(1)}, u32[]{:S(2)}, u32[]{:S(2)}) collective-permute-start(f32[1,61,256]{2,1,0:T(8,128)S(1)} %get-tuple-element.18), channel_id=1, source_target_pairs={{0,4},{4,8},{8,12},{12,16},{16,20},{20,24},{24,28},{1,5},{5,9},{9,... | collective-permute-start | bytes 187400 | tf_op jit(solution)/shard_map/ppermute | solution.py:29
  39.6 8.9 %collective-permute-start.6 = (f32[1,61,256]{2,1,0:T(8,128)S(1)}, f32[1,61,256]{2,1,0:T(8,128)S(1)}, u32[]{:S(2)}, u32[]{:S(2)}) collective-permute-start(f32[1,61,256]{2,1,0:T(8,128)S(1)} %get-tuple-element.19), channel_id=1, source_target_pairs={{4,0},{8,4},{12,8},{16,12},{20,16},{24,20},{28,24},{5,1},{9,5},{13... | collective-permute-start | bytes 187400 | tf_op jit(solution)/shard_map/ppermute | solution.py:29
  42.0 19.1 %copy-start.2 = (bf16[24,45,256]{2,1,0:T(8,128)(2,1)S(1)}, bf16[24,45,256]{2,1,0:T(8,128)(2,1)}, u32[]{:S(2)}) copy-start(bf16[24,45,256]{2,1,0:T(8,128)(2,1)} %copy-done.1) | copy-start | bytes 1658884
  42.0 10.5 %collective-permute-start.10 = (f32[4,32,256]{2,1,0:T(8,128)S(1)}, f32[4,32,256]{2,1,0:T(8,128)S(1)}, u32[]{:S(2)}, u32[]{:S(2)}) collective-permute-start(f32[4,32,256]{2,1,0:T(8,128)S(1)} %add.157), channel_id=1, source_target_pairs={{0,1},{1,0},{2,3},{3,2},{4,5},{5,4},{6,7},{7,6},{8,9},{9,8},{10,11... | collective-permute-start | bytes 393224 | tf_op jit(solution)/shard_map/ppermute | solution.py:59
  43.0 12.7 %collective-permute-start.11 = (f32[4,32,256]{2,1,0:T(8,128)S(1)}, f32[4,32,256]{2,1,0:T(8,128)S(1)}, u32[]{:S(2)}, u32[]{:S(2)}) collective-permute-start(f32[4,32,256]{2,1,0:T(8,128)S(1)} %add.157), channel_id=1, source_target_pairs={{0,9},{1,8},{2,11},{3,10},{4,13},{5,12},{6,15},{7,14},{8,1},{9,0},... | collective-permute-start | bytes 393224 | tf_op jit(solution)/shard_map/ppermute | solution.py:60
  48.5 8.1 %collective-permute-start.9 = (f32[4,32,256]{2,1,0:T(8,128)S(1)}, f32[4,32,256]{2,1,0:T(8,128)S(1)}, u32[]{:S(2)}, u32[]{:S(2)}) collective-permute-start(f32[4,32,256]{2,1,0:T(8,128)S(1)} %add.157), channel_id=1, source_target_pairs={{0,8},{4,12},{8,0},{12,4},{16,24},{20,28},{24,16},{28,20},{1,9},{5... | collective-permute-start | bytes 393224 | tf_op jit(solution)/shard_map/ppermute | solution.py:58
  48.7 12.5 %collective-permute-start.8 = (f32[24,8,256]{2,1,0:T(8,128)S(1)}, f32[24,8,256]{2,1,0:T(8,128)S(1)}, u32[]{:S(2)}, u32[]{:S(2)}) collective-permute-start(f32[24,8,256]{2,1,0:T(8,128)S(1)} %slice.60), channel_id=1, source_target_pairs={{0,1},{1,2},{2,3},{3,0},{4,5},{5,6},{6,7},{7,4},{8,9},{9,10},{10,1... | collective-permute-start | bytes 589832 | tf_op jit(solution)/shard_map/ppermute | solution.py:34
  49.7 11.4 %collective-permute-start.7 = (bf16[24,8,256]{2,1,0:T(8,128)(2,1)S(1)}, bf16[24,8,256]{2,1,0:T(8,128)(2,1)S(1)}, u32[]{:S(2)}, u32[]{:S(2)}) collective-permute-start(bf16[24,8,256]{2,1,0:T(8,128)(2,1)S(1)} %slice.72), channel_id=1, source_target_pairs={{0,3},{1,0},{2,1},{3,2},{4,7},{5,4},{6,5},{7,6},{8,11},{9,8},{10,9... | collective-permute-start | bytes 294920 | tf_op jit(solution)/shard_map/ppermute | solution.py:34
  56.7 5.7 %collective-permute-start.12 = (f32[4,32,256]{2,1,0:T(8,128)S(1)}, f32[4,32,256]{2,1,0:T(8,128)S(1)}, u32[]{:S(2)}, u32[]{:S(2)}) collective-permute-start(f32[4,32,256]{2,1,0:T(8,128)S(1)} %add_add_fusion), channel_id=1, source_target_pairs={{0,16},{4,20},{8,24},{12,28},{16,0},{20,4},{24,8},{28,12},{1,17},{... | collective-permute-start | bytes 393224 | tf_op jit(solution)/shard_map/ppermute | solution.py:58
  58.3 10.8 %collective-permute-start.13 = (f32[4,32,256]{2,1,0:T(8,128)S(1)}, f32[4,32,256]{2,1,0:T(8,128)S(1)}, u32[]{:S(2)}, u32[]{:S(2)}) collective-permute-start(f32[4,32,256]{2,1,0:T(8,128)S(1)} %add_add_fusion), channel_id=1, source_target_pairs={{0,2},{1,3},{2,0},{3,1},{4,6},{5,7},{6,4},{7,5},{8,10},{9,11},{10,... | collective-permute-start | bytes 393224 | tf_op jit(solution)/shard_map/ppermute | solution.py:59
  58.7 13.0 %collective-permute-start.14 = (f32[4,32,256]{2,1,0:T(8,128)S(1)}, f32[4,32,256]{2,1,0:T(8,128)S(1)}, u32[]{:S(2)}, u32[]{:S(2)}) collective-permute-start(f32[4,32,256]{2,1,0:T(8,128)S(1)} %add_add_fusion), channel_id=1, source_target_pairs={{0,18},{1,19},{2,16},{3,17},{4,22},{5,23},{6,20},{7,21},{8,26},{9,... | collective-permute-start | bytes 393224 | tf_op jit(solution)/shard_map/ppermute | solution.py:60

commit v17 on v15

--- a/solution.py
+++ b/solution.py
@@ -52,7 +52,7 @@
     return value
 
 
-def forward_kernel(x_ref, m_ref, t_ref, cot_ref, w_ref, inf_ref, wg_ref, pulled_ref, scaled_ref, safe_ref):
+def forward_kernel(x_ref, m_ref, t_ref, cot_ref, w_ref, inf_ref, wg_ref, scaled_ref):
     rows, basis_count, lat_taps, col_pad, lane_rows = t_ref.shape
     col_count = inf_ref.shape[1]
     chan_count = w_ref.shape[1]
@@ -73,7 +73,6 @@
         rows_at = pl.ds(pl.multiple_of(i * col_pad, col_pad), col_pad)
         for b in range(basis_count):
             scaled_ref[b, rows_at, :] = scaled[b * col_pad : (b + 1) * col_pad]
-            safe_ref[b, rows_at, :] = safe[b * col_pad : (b + 1) * col_pad]
         return carry
 
     lax.fori_loop(0, rows, body, 0, unroll=True)
@@ -82,8 +81,6 @@
     out = None
     for b in range(basis_count):
         part = scaled_ref[b]
-        mixed = jnp.dot(part, w_ref[b], preferred_element_type=jnp.float32)
-        out = mixed if out is None else out + mixed
         grad = lax.dot_general(
             part, upstream_all, (((0,), (0,)), ((), ())), preferred_element_type=jnp.float32
         )
@@ -92,17 +89,37 @@
             block = grad[g * group_width : (g + 1) * group_width, :]
             total = total + jnp.where(lane == g, block, 0.0)
         wg_ref[b] = total
+        mixed = jnp.dot(part, w_ref[b], preferred_element_type=jnp.float32)
+        out = mixed if out is None else out + mixed
+    for i in range(rows):
+        inf_ref[i] = out[i * col_pad : i * col_pad + col_count].astype(inf_ref.dtype)
+
+
+def adjoint_kernel(m_ref, t_ref, cot_ref, w_ref, order_ref, col_ref, safe_ref, pulled_ref):
+    rows, basis_count, lat_taps, col_pad, lane_rows = t_ref.shape
+    chan_count = w_ref.shape[1]
+    col_ref[...] = jnp.zeros_like(col_ref)
+
+    def guard(i, carry):
+        denominator = None
+        for a in range(lat_taps):
+            band = t_ref[i, :, a].reshape(basis_count * col_pad, lane_rows)
+            start = pl.multiple_of((i + a) * lane_rows, lane_rows)
+            den = jnp.dot(band, m_ref[pl.ds(start, lane_rows), :], preferred_element_type=jnp.float32)
+            denominator = den if denominator is None else denominator + den
+        safe = jnp.maximum(denominator, 1.0)
+        rows_at = pl.ds(pl.multiple_of(i * col_pad, col_pad), col_pad)
+        for b in range(basis_count):
+            safe_ref[b, rows_at, :] = safe[b * col_pad : (b + 1) * col_pad]
+        return carry
+
+    lax.fori_loop(0, rows, guard, 0, unroll=True)
+    upstream_all = cot_ref[...].reshape(rows * col_pad, chan_count)
+    for b in range(basis_count):
         back = lax.dot_general(
             upstream_all, w_ref[b], (((1,), (1,)), ((), ())), preferred_element_type=jnp.float32
         )
         pulled_ref[b] = (back / safe_ref[b]).astype(jnp.bfloat16)
-    for i in range(rows):
-        inf_ref[i] = out[i * col_pad : i * col_pad + col_count].astype(inf_ref.dtype)
-
-
-def adjoint_kernel(t_ref, pulled_ref, order_ref, col_ref):
-    rows, basis_count, lat_taps, col_pad, lane_rows = t_ref.shape
-    col_ref[...] = jnp.zeros_like(col_ref)
 
     def body(i, carry):
         rows_at = pl.ds(pl.multiple_of(i * col_pad, col_pad), col_pad)
@@ -171,18 +188,16 @@
 
     vmem = pl.BlockSpec(memory_space=pltpu.VMEM)
     params = pltpu.CompilerParams(vmem_limit_bytes=48 * 1024 * 1024)
-    infilled, grad_blocks, pulled = pl.pallas_call(
+    infilled, grad_blocks = pl.pallas_call(
         forward_kernel,
         out_shape=(
             jax.ShapeDtypeStruct((row_count, col_count, chan_count), jnp.bfloat16),
             jax.ShapeDtypeStruct((basis_count, group_width, chan_count), jnp.float32),
-            jax.ShapeDtypeStruct((basis_count, row_count * col_pad, chan_count), jnp.bfloat16),
         ),
         in_specs=[vmem] * 5,
-        out_specs=[vmem] * 3,
+        out_specs=[vmem] * 2,
         scratch_shapes=[
             pltpu.VMEM((basis_count, row_count * col_pad, chan_count), jnp.bfloat16),
-            pltpu.VMEM((basis_count, row_count * col_pad, chan_count), jnp.float32),
         ],
         compiler_params=params,
         cost_estimate=pl.CostEstimate(
@@ -206,15 +221,19 @@
     collected = pl.pallas_call(
         adjoint_kernel,
         out_shape=jax.ShapeDtypeStruct(((row_count + 2) * lane_rows, chan_count), jnp.float32),
-        in_specs=[vmem, vmem, pl.BlockSpec(memory_space=pl.ANY)],
+        in_specs=[vmem] * 4 + [pl.BlockSpec(memory_space=pl.ANY)],
         out_specs=vmem,
+        scratch_shapes=[
+            pltpu.VMEM((basis_count, row_count * col_pad, chan_count), jnp.float32),
+            pltpu.VMEM((basis_count, row_count * col_pad, chan_count), jnp.bfloat16),
+        ],
         compiler_params=params,
         cost_estimate=pl.CostEstimate(
             flops=6 * row_count * basis_count * col_pad * lane_rows * chan_count,
             transcendentals=0,
             bytes_accessed=6 * (row_count + 2) * lane_rows * chan_count,
         ),
-    )(band, pulled, first)
+    )(full_mask, band, upstream, mix_blocks, first)
 
     collected = collected.reshape(row_count + 2, lane_rows, chan_count)[:, :padded_cols]
     from_below = passed_along(collected[0:1], "lat", -1)

time: 68.9 us -> 70.8 us (1.028)
  Pallas kernels: 11.4 us -> 13.2 us
    pallas_call x1, Pallas kernels: 3.48 us -> 5.97 us  [local(): pl.pallas_call(adjoint_kernel, out_shape=jax.ShapeDtypeStruct(((row_count...]
  transfers between devices with their start and end apart: 13 -> 13, of which waited for: 7 -> 7; matrix products, arithmetic and copies ran while one was open for 15% -> 14% of each run, Pallas kernels for 5% -> 8%
where the time goes in v17:
time: 70.8 us; the launch traced here: 70.4 us
  starting transfers between devices  22.6 us (32%)
  waiting for transfers between devices  18 us (25%)
  Pallas kernels  13.2 us (19%)
  local copies, waits for them, and re-layouts  9.48 us (13%)
  other arithmetic  4.34 us (6%)
  matrix products  1.86 us (3%)
  between operations  1.01 us (1%)
    ppermute x4, waiting for transfers between devices, butterfly_sum(): partner = lax.ppermute(value, axis, [(i, i ^ step) for i in range(count)])  11.9 us
    ppermute x4, starting transfers between devices, butterfly_sum(): partner = lax.ppermute(value, axis, [(i, i ^ step) for i in range(count)])  9.05 us
    pallas_call x1, Pallas kernels, local(): pl.pallas_call(forward_kernel, out_shape=(jax.ShapeDtypeStruct((row_count...  7.19 us
    pallas_call x1, Pallas kernels, local(): pl.pallas_call(adjoint_kernel, out_shape=jax.ShapeDtypeStruct(((row_count...  5.97 us
    ppermute x2, waiting for transfers between devices, with_halo(): lax.ppermute(lax.slice_in_dim(block, 0, width, axis=dim), axis, backward)  4.3 us
    ppermute x2, starting transfers between devices, with_halo(): lax.ppermute(lax.slice_in_dim(block, block.shape[dim] - width, None, axis...  3.98 us
    ppermute x2, starting transfers between devices, with_halo(): lax.ppermute(lax.slice_in_dim(block, 0, width, axis=dim), axis, backward)  3.54 us
    unnamed x20, local copies, waits for them, and re-layouts  3.37 us
  transfers between devices with their start and end apart: 13, of which 7 were waited for; matrix products, arithmetic and copies ran while one was open for 14% of the time, Pallas kernels for 8%

profile of v17, /device:TPU:0, one launch (start us, length us, event | category | flops | bytes accessed | tf_op | source)
XLA Modules:
  0.0 70.4 jit_solution(7422966302209169625)
XLA Ops:
  0.6 0.0 copy-start
  0.6 0.0 copy-start.5
  0.7 1.0 %convert_element_type.46 = bf16[24,45,8]{1,2,0:T(8,128)(2,1)S(1)} convert(s32[24,45,8]{1,2,0:T(8,128)} %param.7) | non-fusion elementwise | flops 8640 | bytes 51840 | tf_op jit(solution)/shard_map/convert_element_type | solution.py:149
  1.6 0.2 copy.35
  1.9 0.1 reshape.114
  2.0 0.4 fusion.6
  2.4 0.2 reshape.115
  2.6 0.0 copy-done.5
  2.6 0.0 copy-start.7
  2.6 0.1 copy_multiply_fusion
  2.8 2.4 %collective-permute-start = (bf16[1,45,264]{2,1,0:T(8,128)(2,1)S(1)}, bf16[1,45,264]{2,1,0:T(8,128)(2,1)S(1)}, u32[]{:S(2)}, u32[]{:S(2)}) collective-permute-start(bf16[1,45,264]{2,1,0:T(8,128)(2,1)S(1)} %get-tuple-element.20), channel_id=1, source_target_pairs={{0,4},{4,8},{8,12},{12,16},{16,20},{20,24},{24,28},{1,5},{5,9},{9,... | collective-permute-start | bytes 71288 | tf_op jit(solution)/shard_map/ppermute | solution.py:18
  5.2 1.3 %collective-permute-start.1 = (bf16[1,45,264]{2,1,0:T(8,128)(2,1)S(1)}, bf16[1,45,264]{2,1,0:T(8,128)(2,1)S(1)}, u32[]{:S(2)}, u32[]{:S(2)}) collective-permute-start(bf16[1,45,264]{2,1,0:T(8,128)(2,1)S(1)} %get-tuple-element.21), channel_id=1, source_target_pairs={{4,0},{8,4},{12,8},{16,12},{20,16},{24,20},{28,24},{5,1},{9,5},{13... | collective-permute-start | bytes 71288 | tf_op jit(solution)/shard_map/ppermute | solution.py:21
  6.5 0.0 copy-done
  6.5 0.1 constant_dynamic-slice_fusion
  6.6 0.2 copy.48
  6.8 0.1 compare_convert_fusion
  6.9 0.1 copy.37
  7.0 0.0 copy-start.6
  7.0 1.1 %fusion.18 = bf16[24,4,3,48,64]{4,0,3,2,1:T(8,128)(2,1)S(1)} fusion(s32[48,64]{1,0:T(8,128)S(1)} %iota_subtract_fusion, pred[48]{0:T(512)(128)(4,1)S(1)} %iota_compare_fusion.6, bf16[24,4,3,17]{3,0,2,1:T(8,128)(2,1)S(1)} %copy.48, bf16[24,17]{1,0:T(8,128)(2,1)S(1)} %constant_dynamic-slice_fusion.1), kind=kOutput, calls=%fused_computation.27 | convolution fusion | flops 30205056 | bytes 1792416 | tf_op jit(solution)/shard_map/ibae,ejp->ibajp/dot_general | solution.py:181
  8.2 0.0 copy-done.1
  8.2 0.0 collective-permute-done
  8.2 2.2 %collective-permute-done.1 = bf16[1,45,264]{2,1,0:T(8,128)(2,1)S(1)} collective-permute-done((bf16[1,45,264]{2,1,0:T(8,128)(2,1)S(1)}, bf16[1,45,264]{2,1,0:T(8,128)(2,1)S(1)}, u32[]{:S(2)}, u32[]{:S(2)}) %collective-permute-start.1) | collective-permute-done | bytes 23792 | tf_op jit(solution)/shard_map/ppermute | solution.py:21
  10.4 0.8 %pad_maximum_fusion.3 = (bf16[26,8,264]{2,1,0:T(8,128)(2,1)}, bf16[26,8,264]{2,1,0:T(8,128)(2,1)}) fusion(bf16[1,45,264]{2,1,0:T(8,128)(2,1)S(1)} %collective-permute-done.1, bf16[1,45,264]{2,1,0:T(8,128)(2,1)S(1)} %collective-permute-done, bf16[24,45,8]{2,1,0:T(8,128)(2,1)S(1)} %copy.35, bf16[24,45,256]{2,1,0:T(8,128)(2,1)S(1)} %copy_multiply_fusion), kind=kLoop, calls=%fused_computation.35 | loop fusion | flops 878592 | bytes 837408 | tf_op jit(solution)/shard_map/slice | solution.py:19
  11.2 1.6 %collective-permute-start.2 = (bf16[26,8,264]{2,1,0:T(8,128)(2,1)}, bf16[26,8,264]{2,1,0:T(8,128)(2,1)S(1)}, u32[]{:S(2)}, u32[]{:S(2)}) collective-permute-start(bf16[26,8,264]{2,1,0:T(8,128)(2,1)} %get-tuple-element.18), channel_id=1, source_target_pairs={{0,1},{1,2},{2,3},{3,0},{4,5},{5,6},{6,7},{7,4},{8,9},{9,10},{10,1... | collective-permute-start | bytes 329480 | tf_op jit(solution)/shard_map/ppermute | solution.py:18
  12.7 2.2 %collective-permute-start.3 = (bf16[26,8,264]{2,1,0:T(8,128)(2,1)}, bf16[26,8,264]{2,1,0:T(8,128)(2,1)}, u32[]{:S(2)}, u32[]{:S(2)}) collective-permute-start(bf16[26,8,264]{2,1,0:T(8,128)(2,1)} %get-tuple-element.19), channel_id=1, source_target_pairs={{1,0},{2,1},{3,2},{0,3},{5,4},{6,5},{7,6},{4,7},{9,8},{10,9},{11,1... | collective-permute-start | bytes 329480 | tf_op jit(solution)/shard_map/ppermute | solution.py:21
  15.0 0.7 multiply_bitcast_fusion
  15.7 2.6 %copy.52.t_ref = bf16[24,4,3,48,64]{4,3,2,1,0:T(8,128)(2,1)} copy(bf16[24,4,3,48,64]{4,0,3,2,1:T(8,128)(2,1)S(1)} %fusion.18) | data formatting | bytes 3538944 | tf_op jit(solution)/shard_map/ibae,ejp->ibajp/dot_general | solution.py:181
  18.3 1.4 %reshape.118.w_ref = bf16[4,256,256]{2,1,0:T(8,128)(2,1)S(1)} reshape(bf16[4,8,32,8,32]{4,3,2,1,0:T(8,128)(2,1)S(1)} %multiply_bitcast_fusion) | data formatting | bytes 1048576 | tf_op jit(solution)/shard_map/reshape | solution.py:186
  19.7 0.0 copy-start.4
  19.7 1.2 %copy.40 = bf16[24,45,256]{2,1,0:T(8,128)(2,1)S(1)} copy(bf16[24,45,256]{2,0,1:T(8,128)(2,1)} %param.11) | data formatting | bytes 1105920 | tf_op args[5]
  21.0 0.0 collective-permute-done.2
  21.0 2.1 %collective-permute-done.3 = bf16[26,8,264]{2,1,0:T(8,128)(2,1)} collective-permute-done((bf16[26,8,264]{2,1,0:T(8,128)(2,1)}, bf16[26,8,264]{2,1,0:T(8,128)(2,1)}, u32[]{:S(2)}, u32[]{:S(2)}) %collective-permute-start.3) | collective-permute-done | bytes 109856 | tf_op jit(solution)/shard_map/ppermute | solution.py:21
  23.1 0.0 copy-done.4
  23.1 1.2 %fusion.9 = bf16[26,64,264]{2,1,0:T(8,128)(2,1)S(1)} fusion(bf16[26,8,264]{2,1,0:T(8,128)(2,1)} %collective-permute-done.3, bf16[26,8,264]{2,1,0:T(8,128)(2,1)S(1)} %collective-permute-done.2, bf16[1,45,264]{2,1,0:T(8,128)(2,1)S(1)} %collective-permute-done.1, bf16[1,45,264]{2,1,0:T(8,128)(2,1)S(1)} %collective-permute-done, ...), kind=kLoop, calls=%fused_computation.15 | loop fusion | flops 8346624 | bytes 1716000 | tf_op jit(solution)/shard_map/concatenate | solution.py:22
  24.4 0.1 slice.54
  24.4 0.1 slice.53
  24.5 0.4 convolution_convert_fusion.m_ref
  24.9 7.2 %shard_map.85 = (bf16[24,45,256]{2,1,0:T(8,128)(2,1)S(1)}, f32[4,32,256]{2,1,0:T(8,128)S(1)}) custom-call(bf16[1664,256]{1,0:T(8,128)(2,1)S(1)} %bitcast.28, bf16[1664,256]{1,0:T(8,128)(2,1)S(1)} %convolution_convert_fusion.m_ref, bf16[24,4,3,48,64]{4,3,2,1,0:T(8,128)(2,1)} %copy.52.t_ref, bf16[24,48,256]{2,1,0:T(8,128)(2,1)S(1)} %pad.28.cot_ref, ...), custom_call_target="tpu_custom_call" | custom-call | flops 2717908992 | bytes 3407872 | tf_op jit(solution)/shard_map/pallas_call | solution.py:191
  32.1 0.2 collective-permute-start.4
  32.3 1.2 %collective-permute-done.4.order_ref = f32[4,32,256]{2,1,0:T(8,128)S(1)} collective-permute-done((f32[4,32,256]{2,1,0:T(8,128)S(1)}, f32[4,32,256]{2,1,0:T(8,128)S(1)}, u32[]{:S(2)}, u32[]{:S(2)}) %collective-permute-start.4) | collective-permute-done | bytes 131104 | tf_op jit(solution)/shard_map/ppermute | solution.py:213
  33.5 2.8 %collective-permute-start.9 = (f32[4,32,256]{2,1,0:T(8,128)S(1)}, f32[4,32,256]{2,1,0:T(8,128)S(1)}, u32[]{:S(2)}, u32[]{:S(2)}) collective-permute-start(f32[4,32,256]{2,1,0:T(8,128)S(1)} %add.58), channel_id=1, source_target_pairs={{0,8},{4,12},{8,0},{12,4},{16,24},{20,28},{24,16},{28,20},{1,9},{5... | collective-permute-start | bytes 393224 | tf_op jit(solution)/shard_map/ppermute | solution.py:49
  36.3 6.0 %shard_map.86 = f32[1664,256]{1,0:T(8,128)S(1)} custom-call(bf16[1664,256]{1,0:T(8,128)(2,1)S(1)} %convolution_convert_fusion.m_ref, bf16[24,4,3,48,64]{4,3,2,1,0:T(8,128)(2,1)} %copy.52.t_ref, bf16[24,48,256]{2,1,0:T(8,128)(2,1)S(1)} %pad.28.cot_ref, bf16[4,256,256]{2,1,0:T(8,128)(2,1)S(1)} %reshape.118.w_ref, ...), custom_call_target="tpu_custom_call" | custom-call | flops 452984832 | bytes 2555904 | tf_op jit(solution)/shard_map/pallas_call | solution.py:221
  42.3 1.8 %collective-permute-start.5 = (f32[1,61,256]{2,1,0:T(8,128)S(1)}, f32[1,61,256]{2,1,0:T(8,128)S(1)}, u32[]{:S(2)}, u32[]{:S(2)}) collective-permute-start(f32[1,61,256]{2,1,0:T(8,128)S(1)} %get-tuple-element.16), channel_id=1, source_target_pairs={{0,4},{4,8},{8,12},{12,16},{16,20},{20,24},{24,28},{1,5},{5,9},{9,... | collective-permute-start | bytes 187400 | tf_op jit(solution)/shard_map/ppermute | solution.py:29
  44.1 1.3 %collective-permute-start.6 = (f32[1,61,256]{2,1,0:T(8,128)S(1)}, f32[1,61,256]{2,1,0:T(8,128)S(1)}, u32[]{:S(2)}, u32[]{:S(2)}) collective-permute-start(f32[1,61,256]{2,1,0:T(8,128)S(1)} %get-tuple-element.17), channel_id=1, source_target_pairs={{4,0},{8,4},{12,8},{16,12},{20,16},{24,20},{28,24},{5,1},{9,5},{13... | collective-permute-start | bytes 187400 | tf_op jit(solution)/shard_map/ppermute | solution.py:29
  45.4 0.0 collective-permute-done.9
  45.4 4.0 %collective-permute-start.10 = (f32[4,32,256]{2,1,0:T(8,128)S(1)}, f32[4,32,256]{2,1,0:T(8,128)S(1)}, u32[]{:S(2)}, u32[]{:S(2)}) collective-permute-start(f32[4,32,256]{2,1,0:T(8,128)S(1)} %add.59), channel_id=1, source_target_pairs={{0,16},{4,20},{8,24},{12,28},{16,0},{20,4},{24,8},{28,12},{1,17},{... | collective-permute-start | bytes 393224 | tf_op jit(solution)/shard_map/ppermute | solution.py:49
  49.4 0.0 collective-permute-done.5
  49.4 0.0 collective-permute-done.6
  49.5 0.1 fusion.7
  49.6 1.2 %collective-permute-start.8 = (f32[24,8,256]{2,1,0:T(8,128)S(1)}, f32[24,8,256]{2,1,0:T(8,128)S(1)}, u32[]{:S(2)}, u32[]{:S(2)}) collective-permute-start(f32[24,8,256]{2,1,0:T(8,128)S(1)} %slice.60), channel_id=1, source_target_pairs={{0,1},{1,2},{2,3},{3,0},{4,5},{5,6},{6,7},{7,4},{8,9},{9,10},{10,1... | collective-permute-start | bytes 589832 | tf_op jit(solution)/shard_map/ppermute | solution.py:34
  50.8 1.8 %collective-permute-done.10 = f32[4,32,256]{2,1,0:T(8,128)S(1)} collective-permute-done((f32[4,32,256]{2,1,0:T(8,128)S(1)}, f32[4,32,256]{2,1,0:T(8,128)S(1)}, u32[]{:S(2)}, u32[]{:S(2)}) %collective-permute-start.10) | collective-permute-done | bytes 131104 | tf_op jit(solution)/shard_map/ppermute | solution.py:49
  52.6 1.2 %collective-permute-start.11 = (f32[4,32,256]{2,1,0:T(8,128)S(1)}, f32[4,32,256]{2,1,0:T(8,128)S(1)}, u32[]{:S(2)}, u32[]{:S(2)}) collective-permute-start(f32[4,32,256]{2,1,0:T(8,128)S(1)} %add.60), channel_id=1, source_target_pairs={{0,1},{1,0},{2,3},{3,2},{4,5},{5,4},{6,7},{7,6},{8,9},{9,8},{10,11... | collective-permute-start | bytes 393224 | tf_op jit(solution)/shard_map/ppermute | solution.py:49
  53.8 1.6 %collective-permute-start.7 = (bf16[24,8,256]{2,1,0:T(8,128)(2,1)S(1)}, bf16[24,8,256]{2,1,0:T(8,128)(2,1)S(1)}, u32[]{:S(2)}, u32[]{:S(2)}) collective-permute-start(bf16[24,8,256]{2,1,0:T(8,128)(2,1)S(1)} %slice.72), channel_id=1, source_target_pairs={{0,3},{1,0},{2,1},{3,2},{4,7},{5,4},{6,5},{7,6},{8,11},{9,8},{10,9... | collective-permute-start | bytes 294920 | tf_op jit(solution)/shard_map/ppermute | solution.py:34
  55.4 1.0 %copy.43 = bf16[24,45,256]{2,0,1:T(8,128)(2,1)} copy(bf16[24,45,256]{2,1,0:T(8,128)(2,1)S(1)} %get-tuple-element.13) | data formatting | bytes 1105920
  56.4 5.3 %collective-permute-done.11 = f32[4,32,256]{2,1,0:T(8,128)S(1)} collective-permute-done((f32[4,32,256]{2,1,0:T(8,128)S(1)}, f32[4,32,256]{2,1,0:T(8,128)S(1)}, u32[]{:S(2)}, u32[]{:S(2)}) %collective-permute-start.11) | collective-permute-done | bytes 131104 | tf_op jit(solution)/shard_map/ppermute | solution.py:49
  61.7 1.1 %collective-permute-start.12 = (f32[4,32,256]{2,1,0:T(8,128)S(1)}, f32[4,32,256]{2,1,0:T(8,128)S(1)}, u32[]{:S(2)}, u32[]{:S(2)}) collective-permute-start(f32[4,32,256]{2,1,0:T(8,128)S(1)} %add.61), channel_id=1, source_target_pairs={{0,2},{1,3},{2,0},{3,1},{4,6},{5,7},{6,4},{7,5},{8,10},{9,11},{10,... | collective-permute-start | bytes 393224 | tf_op jit(solution)/shard_map/ppermute | solution.py:49
  62.8 0.6 collective-permute-done.7
  63.4 0.0 collective-permute-done.8
  63.4 0.0 copy-done.2
  63.4 0.2 fusion.15
  63.6 1.0 %copy.44 = bf16[24,45,256]{2,0,1:T(8,128)(2,1)} copy(bf16[24,45,256]{2,1,0:T(8,128)(2,1)S(1)} %fusion.15) | data formatting | bytes 1105920
  64.6 4.8 %collective-permute-done.12 = f32[4,32,256]{2,1,0:T(8,128)S(1)} collective-permute-done((f32[4,32,256]{2,1,0:T(8,128)S(1)}, f32[4,32,256]{2,1,0:T(8,128)S(1)}, u32[]{:S(2)}, u32[]{:S(2)}) %collective-permute-start.12) | collective-permute-done | bytes 131104 | tf_op jit(solution)/shard_map/ppermute | solution.py:49
  69.4 0.2 reshape.120
  69.5 0.9 %copy.55 = f32[4,32,8,32]{3,1,0,2:T(8,128)} copy(f32[4,32,8,32]{3,2,1,0:T(8,128)S(1)} %reshape.120) | data formatting | bytes 262144 | tf_op jit(solution)/shard_map/reshape | solution.py:219
  (23 shorter events, 0.3 us)
Async XLA Ops:
  0.6 5.9 %copy-start = (bf16[192,4,3,17]{0,1,3,2:T(4,128)(2,1)S(1)}, bf16[192,4,3,17]{0,1,3,2:T(4,128)(2,1)}, u32[]{:S(2)}) copy-start(bf16[192,4,3,17]{0,1,3,2:T(4,128)(2,1)} %param.8) | copy-start | bytes 235012
  0.6 1.9 %copy-start.5 = (bf16[24,45,256]{2,0,1:T(8,128)(2,1)S(1)}, bf16[24,45,256]{2,0,1:T(8,128)(2,1)}, u32[]{:S(2)}) copy-start(bf16[24,45,256]{2,0,1:T(8,128)(2,1)} %param.6) | copy-start | bytes 1658884
  1.9 8.5 %copy-start.3 = (bf16[24,45,8]{2,1,0:T(8,128)(2,1)}, bf16[24,45,8]{2,1,0:T(8,128)(2,1)S(1)}, u32[]{:S(2)}) copy-start(bf16[24,45,8]{2,1,0:T(8,128)(2,1)S(1)} %copy.35) | copy-start | bytes 51844
  2.6 5.6 %copy-start.1 = (bf16[24,45,256]{2,1,0:T(8,128)(2,1)}, bf16[24,45,256]{2,1,0:T(8,128)(2,1)S(1)}, u32[]{:S(2)}) copy-start(bf16[24,45,256]{2,1,0:T(8,128)(2,1)S(1)} %reshape.115) | copy-start | bytes 1658884
  2.6 4.2 %copy-start.7 = (s32[192]{0:T(256)S(1)}, s32[192]{0:T(256)}, u32[]{:S(2)}) copy-start(s32[192]{0:T(256)} %param.9) | copy-start | bytes 2308
  2.8 5.4 %collective-permute-start = (bf16[1,45,264]{2,1,0:T(8,128)(2,1)S(1)}, bf16[1,45,264]{2,1,0:T(8,128)(2,1)S(1)}, u32[]{:S(2)}, u32[]{:S(2)}) collective-permute-start(bf16[1,45,264]{2,1,0:T(8,128)(2,1)S(1)} %get-tuple-element.20), channel_id=1, source_target_pairs={{0,4},{4,8},{8,12},{12,16},{16,20},{20,24},{24,28},{1,5},{5,9},{9,... | collective-permute-start | bytes 71288 | tf_op jit(solution)/shard_map/ppermute | solution.py:18
  5.2 5.2 %collective-permute-start.1 = (bf16[1,45,264]{2,1,0:T(8,128)(2,1)S(1)}, bf16[1,45,264]{2,1,0:T(8,128)(2,1)S(1)}, u32[]{:S(2)}, u32[]{:S(2)}) collective-permute-start(bf16[1,45,264]{2,1,0:T(8,128)(2,1)S(1)} %get-tuple-element.21), channel_id=1, source_target_pairs={{4,0},{8,4},{12,8},{16,12},{20,16},{24,20},{28,24},{5,1},{9,5},{13... | collective-permute-start | bytes 71288 | tf_op jit(solution)/shard_map/ppermute | solution.py:21
  7.0 8.0 %copy-start.6 = (bf16[8,4,32,32]{3,2,1,0:T(8,128)(2,1)S(1)}, bf16[8,4,32,32]{3,2,1,0:T(8,128)(2,1)}, u32[]{:S(2)}) copy-start(bf16[8,4,32,32]{3,2,1,0:T(8,128)(2,1)} %param.10) | copy-start | bytes 196612
  11.2 9.8 %collective-permute-start.2 = (bf16[26,8,264]{2,1,0:T(8,128)(2,1)}, bf16[26,8,264]{2,1,0:T(8,128)(2,1)S(1)}, u32[]{:S(2)}, u32[]{:S(2)}) collective-permute-start(bf16[26,8,264]{2,1,0:T(8,128)(2,1)} %get-tuple-element.18), channel_id=1, source_target_pairs={{0,1},{1,2},{2,3},{3,0},{4,5},{5,6},{6,7},{7,4},{8,9},{9,10},{10,1... | collective-permute-start | bytes 329480 | tf_op jit(solution)/shard_map/ppermute | solution.py:18
  12.7 10.4 %collective-permute-start.3 = (bf16[26,8,264]{2,1,0:T(8,128)(2,1)}, bf16[26,8,264]{2,1,0:T(8,128)(2,1)}, u32[]{:S(2)}, u32[]{:S(2)}) collective-permute-start(bf16[26,8,264]{2,1,0:T(8,128)(2,1)} %get-tuple-element.19), channel_id=1, source_target_pairs={{1,0},{2,1},{3,2},{0,3},{5,4},{6,5},{7,6},{4,7},{9,8},{10,9},{11,1... | collective-permute-start | bytes 329480 | tf_op jit(solution)/shard_map/ppermute | solution.py:21
  19.7 3.4 %copy-start.4 = (bf16[24,45,8]{2,1,0:T(8,128)(2,1)S(1)}, bf16[24,45,8]{2,1,0:T(8,128)(2,1)}, u32[]{:S(2)}) copy-start(bf16[24,45,8]{2,1,0:T(8,128)(2,1)} %copy-done.3) | copy-start | bytes 51844
  32.1 1.4 %collective-permute-start.4 = (f32[4,32,256]{2,1,0:T(8,128)S(1)}, f32[4,32,256]{2,1,0:T(8,128)S(1)}, u32[]{:S(2)}, u32[]{:S(2)}) collective-permute-start(f32[4,32,256]{2,1,0:T(8,128)S(1)} %get-tuple-element.6), channel_id=1, source_target_pairs={{0,4},{4,0},{8,12},{12,8},{16,20},{20,16},{24,28},{28,24},{1,5},{5... | collective-permute-start | bytes 393224 | tf_op jit(solution)/shard_map/ppermute | solution.py:213
  33.5 11.9 %collective-permute-start.9 = (f32[4,32,256]{2,1,0:T(8,128)S(1)}, f32[4,32,256]{2,1,0:T(8,128)S(1)}, u32[]{:S(2)}, u32[]{:S(2)}) collective-permute-start(f32[4,32,256]{2,1,0:T(8,128)S(1)} %add.58), channel_id=1, source_target_pairs={{0,8},{4,12},{8,0},{12,4},{16,24},{20,28},{24,16},{28,20},{1,9},{5... | collective-permute-start | bytes 393224 | tf_op jit(solution)/shard_map/ppermute | solution.py:49
  42.3 7.2 %collective-permute-start.5 = (f32[1,61,256]{2,1,0:T(8,128)S(1)}, f32[1,61,256]{2,1,0:T(8,128)S(1)}, u32[]{:S(2)}, u32[]{:S(2)}) collective-permute-start(f32[1,61,256]{2,1,0:T(8,128)S(1)} %get-tuple-element.16), channel_id=1, source_target_pairs={{0,4},{4,8},{8,12},{12,16},{16,20},{20,24},{24,28},{1,5},{5,9},{9,... | collective-permute-start | bytes 187400 | tf_op jit(solution)/shard_map/ppermute | solution.py:29
  44.1 5.4 %collective-permute-start.6 = (f32[1,61,256]{2,1,0:T(8,128)S(1)}, f32[1,61,256]{2,1,0:T(8,128)S(1)}, u32[]{:S(2)}, u32[]{:S(2)}) collective-permute-start(f32[1,61,256]{2,1,0:T(8,128)S(1)} %get-tuple-element.17), channel_id=1, source_target_pairs={{4,0},{8,4},{12,8},{16,12},{20,16},{24,20},{28,24},{5,1},{9,5},{13... | collective-permute-start | bytes 187400 | tf_op jit(solution)/shard_map/ppermute | solution.py:29
  45.4 7.2 %collective-permute-start.10 = (f32[4,32,256]{2,1,0:T(8,128)S(1)}, f32[4,32,256]{2,1,0:T(8,128)S(1)}, u32[]{:S(2)}, u32[]{:S(2)}) collective-permute-start(f32[4,32,256]{2,1,0:T(8,128)S(1)} %add.59), channel_id=1, source_target_pairs={{0,16},{4,20},{8,24},{12,28},{16,0},{20,4},{24,8},{28,12},{1,17},{... | collective-permute-start | bytes 393224 | tf_op jit(solution)/shard_map/ppermute | solution.py:49
  49.6 13.8 %copy-start.2 = (bf16[24,45,256]{2,1,0:T(8,128)(2,1)S(1)}, bf16[24,45,256]{2,1,0:T(8,128)(2,1)}, u32[]{:S(2)}) copy-start(bf16[24,45,256]{2,1,0:T(8,128)(2,1)} %copy-done.1) | copy-start | bytes 1658884
  49.6 13.7 %collective-permute-start.8 = (f32[24,8,256]{2,1,0:T(8,128)S(1)}, f32[24,8,256]{2,1,0:T(8,128)S(1)}, u32[]{:S(2)}, u32[]{:S(2)}) collective-permute-start(f32[24,8,256]{2,1,0:T(8,128)S(1)} %slice.60), channel_id=1, source_target_pairs={{0,1},{1,2},{2,3},{3,0},{4,5},{5,6},{6,7},{7,4},{8,9},{9,10},{10,1... | collective-permute-start | bytes 589832 | tf_op jit(solution)/shard_map/ppermute | solution.py:34
  52.6 9.1 %collective-permute-start.11 = (f32[4,32,256]{2,1,0:T(8,128)S(1)}, f32[4,32,256]{2,1,0:T(8,128)S(1)}, u32[]{:S(2)}, u32[]{:S(2)}) collective-permute-start(f32[4,32,256]{2,1,0:T(8,128)S(1)} %add.60), channel_id=1, source_target_pairs={{0,1},{1,0},{2,3},{3,2},{4,5},{5,4},{6,7},{7,6},{8,9},{9,8},{10,11... | collective-permute-start | bytes 393224 | tf_op jit(solution)/shard_map/ppermute | solution.py:49
  53.8 9.5 %collective-permute-start.7 = (bf16[24,8,256]{2,1,0:T(8,128)(2,1)S(1)}, bf16[24,8,256]{2,1,0:T(8,128)(2,1)S(1)}, u32[]{:S(2)}, u32[]{:S(2)}) collective-permute-start(bf16[24,8,256]{2,1,0:T(8,128)(2,1)S(1)} %slice.72), channel_id=1, source_target_pairs={{0,3},{1,0},{2,1},{3,2},{4,7},{5,4},{6,5},{7,6},{8,11},{9,8},{10,9... | collective-permute-start | bytes 294920 | tf_op jit(solution)/shard_map/ppermute | solution.py:34
  61.7 7.6 %collective-permute-start.12 = (f32[4,32,256]{2,1,0:T(8,128)S(1)}, f32[4,32,256]{2,1,0:T(8,128)S(1)}, u32[]{:S(2)}, u32[]{:S(2)}) collective-permute-start(f32[4,32,256]{2,1,0:T(8,128)S(1)} %add.61), channel_id=1, source_target_pairs={{0,2},{1,3},{2,0},{3,1},{4,6},{5,7},{6,4},{7,5},{8,10},{9,11},{10,... | collective-permute-start | bytes 393224 | tf_op jit(solution)/shard_map/ppermute | solution.py:49

commit v18 on v15

--- a/solution.py
+++ b/solution.py
@@ -73,7 +73,7 @@
         rows_at = pl.ds(pl.multiple_of(i * col_pad, col_pad), col_pad)
         for b in range(basis_count):
             scaled_ref[b, rows_at, :] = scaled[b * col_pad : (b + 1) * col_pad]
-            safe_ref[b, rows_at, :] = safe[b * col_pad : (b + 1) * col_pad]
+            safe_ref[b, rows_at, :] = 1.0 / safe[b * col_pad : (b + 1) * col_pad]
         return carry
 
     lax.fori_loop(0, rows, body, 0, unroll=True)
@@ -95,7 +95,7 @@
         back = lax.dot_general(
             upstream_all, w_ref[b], (((1,), (1,)), ((), ())), preferred_element_type=jnp.float32
         )
-        pulled_ref[b] = (back / safe_ref[b]).astype(jnp.bfloat16)
+        pulled_ref[b] = (back * safe_ref[b]).astype(jnp.bfloat16)
     for i in range(rows):
         inf_ref[i] = out[i * col_pad : i * col_pad + col_count].astype(inf_ref.dtype)
 

time: 68.9 us -> 68.9 us (level)
  no operation moved by 1% of the time
where the time goes in v18:
time: 68.9 us; the launch traced here: 68.6 us
  starting transfers between devices  22.6 us (33%)
  waiting for transfers between devices  18 us (26%)
  Pallas kernels  11.4 us (17%)
  local copies, waits for them, and re-layouts  9.48 us (14%)
  other arithmetic  4.34 us (6%)
  matrix products  1.86 us (3%)
  between operations  1.01 us (1%)
    ppermute x4, waiting for transfers between devices, butterfly_sum(): partner = lax.ppermute(value, axis, [(i, i ^ step) for i in range(count)])  11.8 us
    ppermute x4, starting transfers between devices, butterfly_sum(): partner = lax.ppermute(value, axis, [(i, i ^ step) for i in range(count)])  9.06 us
    pallas_call x1, Pallas kernels, local(): pl.pallas_call(forward_kernel, out_shape=(jax.ShapeDtypeStruct((row_count...  7.89 us
    ppermute x2, waiting for transfers between devices, with_halo(): lax.ppermute(lax.slice_in_dim(block, 0, width, axis=dim), axis, backward)  4.3 us
    ppermute x2, starting transfers between devices, with_halo(): lax.ppermute(lax.slice_in_dim(block, block.shape[dim] - width, None, axis...  3.98 us
    ppermute x2, starting transfers between devices, with_halo(): lax.ppermute(lax.slice_in_dim(block, 0, width, axis=dim), axis, backward)  3.54 us
    pallas_call x1, Pallas kernels, local(): pl.pallas_call(adjoint_kernel, out_shape=jax.ShapeDtypeStruct(((row_count...  3.48 us
    unnamed x20, local copies, waits for them, and re-layouts  3.37 us
  transfers between devices with their start and end apart: 13, of which 7 were waited for; matrix products, arithmetic and copies ran while one was open for 15% of the time, Pallas kernels for 5%

profile of v18, /device:TPU:0, one launch (start us, length us, event | category | flops | bytes accessed | tf_op | source)
XLA Modules:
  0.0 68.6 jit_solution(11394029813733577672)
XLA Ops:
  0.6 0.0 copy-start
  0.6 0.0 copy-start.5
  0.7 1.0 %convert_element_type.46 = bf16[24,45,8]{1,2,0:T(8,128)(2,1)S(1)} convert(s32[24,45,8]{1,2,0:T(8,128)} %param.7) | non-fusion elementwise | flops 8640 | bytes 51840 | tf_op jit(solution)/shard_map/convert_element_type | solution.py:132
  1.6 0.2 copy.35
  1.9 0.1 reshape.114
  2.0 0.4 fusion.6
  2.4 0.2 reshape.115
  2.6 0.0 copy-done.5
  2.6 0.0 copy-start.1
  2.6 0.0 copy-start.7
  2.6 0.1 copy_multiply_fusion
  2.8 2.4 %collective-permute-start = (bf16[1,45,264]{2,1,0:T(8,128)(2,1)S(1)}, bf16[1,45,264]{2,1,0:T(8,128)(2,1)S(1)}, u32[]{:S(2)}, u32[]{:S(2)}) collective-permute-start(bf16[1,45,264]{2,1,0:T(8,128)(2,1)S(1)} %get-tuple-element.22), channel_id=1, source_target_pairs={{0,4},{4,8},{8,12},{12,16},{16,20},{20,24},{24,28},{1,5},{5,9},{9,... | collective-permute-start | bytes 71288 | tf_op jit(solution)/shard_map/ppermute | solution.py:18
  5.2 1.3 %collective-permute-start.1 = (bf16[1,45,264]{2,1,0:T(8,128)(2,1)S(1)}, bf16[1,45,264]{2,1,0:T(8,128)(2,1)S(1)}, u32[]{:S(2)}, u32[]{:S(2)}) collective-permute-start(bf16[1,45,264]{2,1,0:T(8,128)(2,1)S(1)} %get-tuple-element.23), channel_id=1, source_target_pairs={{4,0},{8,4},{12,8},{16,12},{20,16},{24,20},{28,24},{5,1},{9,5},{13... | collective-permute-start | bytes 71288 | tf_op jit(solution)/shard_map/ppermute | solution.py:21
  6.5 0.0 copy-done
  6.5 0.1 constant_dynamic-slice_fusion
  6.6 0.2 copy.48
  6.8 0.0 copy-done.7
  6.8 0.1 compare_convert_fusion
  6.9 0.1 copy.37
  7.0 0.0 copy-start.6
  7.0 1.1 %fusion.18 = bf16[24,4,3,48,64]{4,0,3,2,1:T(8,128)(2,1)S(1)} fusion(s32[48,64]{1,0:T(8,128)S(1)} %iota_subtract_fusion, pred[48]{0:T(512)(128)(4,1)S(1)} %iota_compare_fusion.6, bf16[24,4,3,17]{3,0,2,1:T(8,128)(2,1)S(1)} %copy.48, bf16[24,17]{1,0:T(8,128)(2,1)S(1)} %constant_dynamic-slice_fusion.1), kind=kOutput, calls=%fused_computation.27 | convolution fusion | flops 30205056 | bytes 1792416 | tf_op jit(solution)/shard_map/ibae,ejp->ibajp/dot_general | solution.py:164
  8.2 0.0 copy-done.1
  8.2 0.0 collective-permute-done
  8.2 2.2 %collective-permute-done.1 = bf16[1,45,264]{2,1,0:T(8,128)(2,1)S(1)} collective-permute-done((bf16[1,45,264]{2,1,0:T(8,128)(2,1)S(1)}, bf16[1,45,264]{2,1,0:T(8,128)(2,1)S(1)}, u32[]{:S(2)}, u32[]{:S(2)}) %collective-permute-start.1) | collective-permute-done | bytes 23792 | tf_op jit(solution)/shard_map/ppermute | solution.py:21
  10.4 0.8 %pad_maximum_fusion.3 = (bf16[26,8,264]{2,1,0:T(8,128)(2,1)}, bf16[26,8,264]{2,1,0:T(8,128)(2,1)}) fusion(bf16[1,45,264]{2,1,0:T(8,128)(2,1)S(1)} %collective-permute-done.1, bf16[1,45,264]{2,1,0:T(8,128)(2,1)S(1)} %collective-permute-done, bf16[24,45,8]{2,1,0:T(8,128)(2,1)S(1)} %copy.35, bf16[24,45,256]{2,1,0:T(8,128)(2,1)S(1)} %copy_multiply_fusion), kind=kLoop, calls=%fused_computation.35 | loop fusion | flops 878592 | bytes 837408 | tf_op jit(solution)/shard_map/slice | solution.py:19
  11.2 1.6 %collective-permute-start.2 = (bf16[26,8,264]{2,1,0:T(8,128)(2,1)}, bf16[26,8,264]{2,1,0:T(8,128)(2,1)S(1)}, u32[]{:S(2)}, u32[]{:S(2)}) collective-permute-start(bf16[26,8,264]{2,1,0:T(8,128)(2,1)} %get-tuple-element.20), channel_id=1, source_target_pairs={{0,1},{1,2},{2,3},{3,0},{4,5},{5,6},{6,7},{7,4},{8,9},{9,10},{10,1... | collective-permute-start | bytes 329480 | tf_op jit(solution)/shard_map/ppermute | solution.py:18
  12.7 2.2 %collective-permute-start.3 = (bf16[26,8,264]{2,1,0:T(8,128)(2,1)}, bf16[26,8,264]{2,1,0:T(8,128)(2,1)}, u32[]{:S(2)}, u32[]{:S(2)}) collective-permute-start(bf16[26,8,264]{2,1,0:T(8,128)(2,1)} %get-tuple-element.21), channel_id=1, source_target_pairs={{1,0},{2,1},{3,2},{0,3},{5,4},{6,5},{7,6},{4,7},{9,8},{10,9},{11,1... | collective-permute-start | bytes 329480 | tf_op jit(solution)/shard_map/ppermute | solution.py:21
  15.0 0.7 multiply_bitcast_fusion
  15.7 2.6 %copy.52.t_ref = bf16[24,4,3,48,64]{4,3,2,1,0:T(8,128)(2,1)} copy(bf16[24,4,3,48,64]{4,0,3,2,1:T(8,128)(2,1)S(1)} %fusion.18) | data formatting | bytes 3538944 | tf_op jit(solution)/shard_map/ibae,ejp->ibajp/dot_general | solution.py:164
  18.3 1.4 %reshape.118.w_ref = bf16[4,256,256]{2,1,0:T(8,128)(2,1)S(1)} reshape(bf16[4,8,32,8,32]{4,3,2,1,0:T(8,128)(2,1)S(1)} %multiply_bitcast_fusion) | data formatting | bytes 1048576 | tf_op jit(solution)/shard_map/reshape | solution.py:169
  19.7 0.0 copy-start.4
  19.7 1.2 %copy.40 = bf16[24,45,256]{2,1,0:T(8,128)(2,1)S(1)} copy(bf16[24,45,256]{2,0,1:T(8,128)(2,1)} %param.11) | data formatting | bytes 1105920 | tf_op args[5]
  21.0 0.0 collective-permute-done.2
  21.0 2.1 %collective-permute-done.3 = bf16[26,8,264]{2,1,0:T(8,128)(2,1)} collective-permute-done((bf16[26,8,264]{2,1,0:T(8,128)(2,1)}, bf16[26,8,264]{2,1,0:T(8,128)(2,1)}, u32[]{:S(2)}, u32[]{:S(2)}) %collective-permute-start.3) | collective-permute-done | bytes 109856 | tf_op jit(solution)/shard_map/ppermute | solution.py:21
  23.1 1.2 %fusion.9 = bf16[26,64,264]{2,1,0:T(8,128)(2,1)S(1)} fusion(bf16[26,8,264]{2,1,0:T(8,128)(2,1)} %collective-permute-done.3, bf16[26,8,264]{2,1,0:T(8,128)(2,1)S(1)} %collective-permute-done.2, bf16[1,45,264]{2,1,0:T(8,128)(2,1)S(1)} %collective-permute-done.1, bf16[1,45,264]{2,1,0:T(8,128)(2,1)S(1)} %collective-permute-done, ...), kind=kLoop, calls=%fused_computation.15 | loop fusion | flops 8346624 | bytes 1716000 | tf_op jit(solution)/shard_map/concatenate | solution.py:22
  24.4 0.1 slice.54
  24.4 0.1 slice.53
  24.5 0.4 convolution_convert_fusion.m_ref
  24.9 7.9 %shard_map.85 = (bf16[24,45,256]{2,1,0:T(8,128)(2,1)S(1)}, f32[4,32,256]{2,1,0:T(8,128)S(1)}, bf16[4,1152,256]{2,1,0:T(8,128)(2,1)S(1)}) custom-call(bf16[1664,256]{1,0:T(8,128)(2,1)S(1)} %bitcast.28, bf16[1664,256]{1,0:T(8,128)(2,1)S(1)} %convolution_convert_fusion.m_ref, bf16[24,4,3,48,64]{4,3,2,1,0:T(8,128)(2,1)} %copy.52.t_ref, ...), custom_call_target="tpu_custom_call" | custom-call | flops 2717908992 | bytes 3407872 | tf_op jit(solution)/shard_map/pallas_call | solution.py:174
  32.8 0.2 collective-permute-start.4
  33.0 1.2 %collective-permute-done.4.order_ref = f32[4,32,256]{2,1,0:T(8,128)S(1)} collective-permute-done((f32[4,32,256]{2,1,0:T(8,128)S(1)}, f32[4,32,256]{2,1,0:T(8,128)S(1)}, u32[]{:S(2)}, u32[]{:S(2)}) %collective-permute-start.4) | collective-permute-done | bytes 131104 | tf_op jit(solution)/shard_map/ppermute | solution.py:198
  34.2 2.8 %collective-permute-start.9 = (f32[4,32,256]{2,1,0:T(8,128)S(1)}, f32[4,32,256]{2,1,0:T(8,128)S(1)}, u32[]{:S(2)}, u32[]{:S(2)}) collective-permute-start(f32[4,32,256]{2,1,0:T(8,128)S(1)} %add.58), channel_id=1, source_target_pairs={{0,8},{4,12},{8,0},{12,4},{16,24},{20,28},{24,16},{28,20},{1,9},{5... | collective-permute-start | bytes 393224 | tf_op jit(solution)/shard_map/ppermute | solution.py:49
  37.0 3.5 %shard_map.86 = f32[1664,256]{1,0:T(8,128)S(1)} custom-call(bf16[24,4,3,48,64]{4,3,2,1,0:T(8,128)(2,1)} %copy.52.t_ref, bf16[4,1152,256]{2,1,0:T(8,128)(2,1)S(1)} %get-tuple-element.7.pulled_ref, f32[4,32,256]{2,1,0:T(8,128)S(1)} %collective-permute-done.4.order_ref), custom_call_target="tpu_custom_call" | custom-call | flops 452984832 | bytes 2555904 | tf_op jit(solution)/shard_map/pallas_call | solution.py:206
  40.5 1.8 %collective-permute-start.5 = (f32[1,61,256]{2,1,0:T(8,128)S(1)}, f32[1,61,256]{2,1,0:T(8,128)S(1)}, u32[]{:S(2)}, u32[]{:S(2)}) collective-permute-start(f32[1,61,256]{2,1,0:T(8,128)S(1)} %get-tuple-element.18), channel_id=1, source_target_pairs={{0,4},{4,8},{8,12},{12,16},{16,20},{20,24},{24,28},{1,5},{5,9},{9,... | collective-permute-start | bytes 187400 | tf_op jit(solution)/shard_map/ppermute | solution.py:29
  42.3 1.3 %collective-permute-start.6 = (f32[1,61,256]{2,1,0:T(8,128)S(1)}, f32[1,61,256]{2,1,0:T(8,128)S(1)}, u32[]{:S(2)}, u32[]{:S(2)}) collective-permute-start(f32[1,61,256]{2,1,0:T(8,128)S(1)} %get-tuple-element.19), channel_id=1, source_target_pairs={{4,0},{8,4},{12,8},{16,12},{20,16},{24,20},{28,24},{5,1},{9,5},{13... | collective-permute-start | bytes 187400 | tf_op jit(solution)/shard_map/ppermute | solution.py:29
  43.6 0.0 collective-permute-done.9
  43.6 4.0 %collective-permute-start.10 = (f32[4,32,256]{2,1,0:T(8,128)S(1)}, f32[4,32,256]{2,1,0:T(8,128)S(1)}, u32[]{:S(2)}, u32[]{:S(2)}) collective-permute-start(f32[4,32,256]{2,1,0:T(8,128)S(1)} %add.59), channel_id=1, source_target_pairs={{0,16},{4,20},{8,24},{12,28},{16,0},{20,4},{24,8},{28,12},{1,17},{... | collective-permute-start | bytes 393224 | tf_op jit(solution)/shard_map/ppermute | solution.py:49
  47.6 0.0 collective-permute-done.5
  47.6 0.0 collective-permute-done.6
  47.6 0.1 fusion.7
  47.8 1.2 %collective-permute-start.8 = (f32[24,8,256]{2,1,0:T(8,128)S(1)}, f32[24,8,256]{2,1,0:T(8,128)S(1)}, u32[]{:S(2)}, u32[]{:S(2)}) collective-permute-start(f32[24,8,256]{2,1,0:T(8,128)S(1)} %slice.60), channel_id=1, source_target_pairs={{0,1},{1,2},{2,3},{3,0},{4,5},{5,6},{6,7},{7,4},{8,9},{9,10},{10,1... | collective-permute-start | bytes 589832 | tf_op jit(solution)/shard_map/ppermute | solution.py:34
  49.0 1.8 %collective-permute-done.10 = f32[4,32,256]{2,1,0:T(8,128)S(1)} collective-permute-done((f32[4,32,256]{2,1,0:T(8,128)S(1)}, f32[4,32,256]{2,1,0:T(8,128)S(1)}, u32[]{:S(2)}, u32[]{:S(2)}) %collective-permute-start.10) | collective-permute-done | bytes 131104 | tf_op jit(solution)/shard_map/ppermute | solution.py:49
  50.8 1.2 %collective-permute-start.11 = (f32[4,32,256]{2,1,0:T(8,128)S(1)}, f32[4,32,256]{2,1,0:T(8,128)S(1)}, u32[]{:S(2)}, u32[]{:S(2)}) collective-permute-start(f32[4,32,256]{2,1,0:T(8,128)S(1)} %add.60), channel_id=1, source_target_pairs={{0,1},{1,0},{2,3},{3,2},{4,5},{5,4},{6,7},{7,6},{8,9},{9,8},{10,11... | collective-permute-start | bytes 393224 | tf_op jit(solution)/shard_map/ppermute | solution.py:49
  52.0 1.6 %collective-permute-start.7 = (bf16[24,8,256]{2,1,0:T(8,128)(2,1)S(1)}, bf16[24,8,256]{2,1,0:T(8,128)(2,1)S(1)}, u32[]{:S(2)}, u32[]{:S(2)}) collective-permute-start(bf16[24,8,256]{2,1,0:T(8,128)(2,1)S(1)} %slice.72), channel_id=1, source_target_pairs={{0,3},{1,0},{2,1},{3,2},{4,7},{5,4},{6,5},{7,6},{8,11},{9,8},{10,9... | collective-permute-start | bytes 294920 | tf_op jit(solution)/shard_map/ppermute | solution.py:34
  53.6 1.0 %copy.43 = bf16[24,45,256]{2,0,1:T(8,128)(2,1)} copy(bf16[24,45,256]{2,1,0:T(8,128)(2,1)S(1)} %get-tuple-element.15) | data formatting | bytes 1105920
  54.6 5.3 %collective-permute-done.11 = f32[4,32,256]{2,1,0:T(8,128)S(1)} collective-permute-done((f32[4,32,256]{2,1,0:T(8,128)S(1)}, f32[4,32,256]{2,1,0:T(8,128)S(1)}, u32[]{:S(2)}, u32[]{:S(2)}) %collective-permute-start.11) | collective-permute-done | bytes 131104 | tf_op jit(solution)/shard_map/ppermute | solution.py:49
  59.9 1.1 %collective-permute-start.12 = (f32[4,32,256]{2,1,0:T(8,128)S(1)}, f32[4,32,256]{2,1,0:T(8,128)S(1)}, u32[]{:S(2)}, u32[]{:S(2)}) collective-permute-start(f32[4,32,256]{2,1,0:T(8,128)S(1)} %add.61), channel_id=1, source_target_pairs={{0,2},{1,3},{2,0},{3,1},{4,6},{5,7},{6,4},{7,5},{8,10},{9,11},{10,... | collective-permute-start | bytes 393224 | tf_op jit(solution)/shard_map/ppermute | solution.py:49
  60.9 0.6 collective-permute-done.7
  61.5 0.0 collective-permute-done.8
  61.5 0.2 fusion.15
  61.8 1.0 %copy.44 = bf16[24,45,256]{2,0,1:T(8,128)(2,1)} copy(bf16[24,45,256]{2,1,0:T(8,128)(2,1)S(1)} %fusion.15) | data formatting | bytes 1105920
  62.8 4.8 %collective-permute-done.12 = f32[4,32,256]{2,1,0:T(8,128)S(1)} collective-permute-done((f32[4,32,256]{2,1,0:T(8,128)S(1)}, f32[4,32,256]{2,1,0:T(8,128)S(1)}, u32[]{:S(2)}, u32[]{:S(2)}) %collective-permute-start.12) | collective-permute-done | bytes 131104 | tf_op jit(solution)/shard_map/ppermute | solution.py:49
  67.5 0.2 reshape.120
  67.7 0.9 %copy.55 = f32[4,32,8,32]{3,1,0,2:T(8,128)} copy(f32[4,32,8,32]{3,2,1,0:T(8,128)S(1)} %reshape.120) | data formatting | bytes 262144 | tf_op jit(solution)/shard_map/reshape | solution.py:204
  (23 shorter events, 0.3 us)
Async XLA Ops:
  0.6 5.9 %copy-start = (bf16[192,4,3,17]{0,1,3,2:T(4,128)(2,1)S(1)}, bf16[192,4,3,17]{0,1,3,2:T(4,128)(2,1)}, u32[]{:S(2)}) copy-start(bf16[192,4,3,17]{0,1,3,2:T(4,128)(2,1)} %param.8) | copy-start | bytes 235012
  0.6 1.9 %copy-start.5 = (bf16[24,45,256]{2,0,1:T(8,128)(2,1)S(1)}, bf16[24,45,256]{2,0,1:T(8,128)(2,1)}, u32[]{:S(2)}) copy-start(bf16[24,45,256]{2,0,1:T(8,128)(2,1)} %param.6) | copy-start | bytes 1658884
  1.9 8.5 %copy-start.3 = (bf16[24,45,8]{2,1,0:T(8,128)(2,1)}, bf16[24,45,8]{2,1,0:T(8,128)(2,1)S(1)}, u32[]{:S(2)}) copy-start(bf16[24,45,8]{2,1,0:T(8,128)(2,1)S(1)} %copy.35) | copy-start | bytes 51844
  2.6 5.6 %copy-start.1 = (bf16[24,45,256]{2,1,0:T(8,128)(2,1)}, bf16[24,45,256]{2,1,0:T(8,128)(2,1)S(1)}, u32[]{:S(2)}) copy-start(bf16[24,45,256]{2,1,0:T(8,128)(2,1)S(1)} %reshape.115) | copy-start | bytes 1658884
  2.6 4.2 %copy-start.7 = (s32[192]{0:T(256)S(1)}, s32[192]{0:T(256)}, u32[]{:S(2)}) copy-start(s32[192]{0:T(256)} %param.9) | copy-start | bytes 2308
  2.8 5.4 %collective-permute-start = (bf16[1,45,264]{2,1,0:T(8,128)(2,1)S(1)}, bf16[1,45,264]{2,1,0:T(8,128)(2,1)S(1)}, u32[]{:S(2)}, u32[]{:S(2)}) collective-permute-start(bf16[1,45,264]{2,1,0:T(8,128)(2,1)S(1)} %get-tuple-element.22), channel_id=1, source_target_pairs={{0,4},{4,8},{8,12},{12,16},{16,20},{20,24},{24,28},{1,5},{5,9},{9,... | collective-permute-start | bytes 71288 | tf_op jit(solution)/shard_map/ppermute | solution.py:18
  5.2 5.2 %collective-permute-start.1 = (bf16[1,45,264]{2,1,0:T(8,128)(2,1)S(1)}, bf16[1,45,264]{2,1,0:T(8,128)(2,1)S(1)}, u32[]{:S(2)}, u32[]{:S(2)}) collective-permute-start(bf16[1,45,264]{2,1,0:T(8,128)(2,1)S(1)} %get-tuple-element.23), channel_id=1, source_target_pairs={{4,0},{8,4},{12,8},{16,12},{20,16},{24,20},{28,24},{5,1},{9,5},{13... | collective-permute-start | bytes 71288 | tf_op jit(solution)/shard_map/ppermute | solution.py:21
  7.0 8.0 %copy-start.6 = (bf16[8,4,32,32]{3,2,1,0:T(8,128)(2,1)S(1)}, bf16[8,4,32,32]{3,2,1,0:T(8,128)(2,1)}, u32[]{:S(2)}) copy-start(bf16[8,4,32,32]{3,2,1,0:T(8,128)(2,1)} %param.10) | copy-start | bytes 196612
  11.2 9.8 %collective-permute-start.2 = (bf16[26,8,264]{2,1,0:T(8,128)(2,1)}, bf16[26,8,264]{2,1,0:T(8,128)(2,1)S(1)}, u32[]{:S(2)}, u32[]{:S(2)}) collective-permute-start(bf16[26,8,264]{2,1,0:T(8,128)(2,1)} %get-tuple-element.20), channel_id=1, source_target_pairs={{0,1},{1,2},{2,3},{3,0},{4,5},{5,6},{6,7},{7,4},{8,9},{9,10},{10,1... | collective-permute-start | bytes 329480 | tf_op jit(solution)/shard_map/ppermute | solution.py:18
  12.7 10.4 %collective-permute-start.3 = (bf16[26,8,264]{2,1,0:T(8,128)(2,1)}, bf16[26,8,264]{2,1,0:T(8,128)(2,1)}, u32[]{:S(2)}, u32[]{:S(2)}) collective-permute-start(bf16[26,8,264]{2,1,0:T(8,128)(2,1)} %get-tuple-element.21), channel_id=1, source_target_pairs={{1,0},{2,1},{3,2},{0,3},{5,4},{6,5},{7,6},{4,7},{9,8},{10,9},{11,1... | collective-permute-start | bytes 329480 | tf_op jit(solution)/shard_map/ppermute | solution.py:21
  19.7 3.4 %copy-start.4 = (bf16[24,45,8]{2,1,0:T(8,128)(2,1)S(1)}, bf16[24,45,8]{2,1,0:T(8,128)(2,1)}, u32[]{:S(2)}) copy-start(bf16[24,45,8]{2,1,0:T(8,128)(2,1)} %copy-done.3) | copy-start | bytes 51844
  32.8 1.4 %collective-permute-start.4 = (f32[4,32,256]{2,1,0:T(8,128)S(1)}, f32[4,32,256]{2,1,0:T(8,128)S(1)}, u32[]{:S(2)}, u32[]{:S(2)}) collective-permute-start(f32[4,32,256]{2,1,0:T(8,128)S(1)} %get-tuple-element.8), channel_id=1, source_target_pairs={{0,4},{4,0},{8,12},{12,8},{16,20},{20,16},{24,28},{28,24},{1,5},{5... | collective-permute-start | bytes 393224 | tf_op jit(solution)/shard_map/ppermute | solution.py:198
  34.2 9.3 %collective-permute-start.9 = (f32[4,32,256]{2,1,0:T(8,128)S(1)}, f32[4,32,256]{2,1,0:T(8,128)S(1)}, u32[]{:S(2)}, u32[]{:S(2)}) collective-permute-start(f32[4,32,256]{2,1,0:T(8,128)S(1)} %add.58), channel_id=1, source_target_pairs={{0,8},{4,12},{8,0},{12,4},{16,24},{20,28},{24,16},{28,20},{1,9},{5... | collective-permute-start | bytes 393224 | tf_op jit(solution)/shard_map/ppermute | solution.py:49
  40.5 7.2 %collective-permute-start.5 = (f32[1,61,256]{2,1,0:T(8,128)S(1)}, f32[1,61,256]{2,1,0:T(8,128)S(1)}, u32[]{:S(2)}, u32[]{:S(2)}) collective-permute-start(f32[1,61,256]{2,1,0:T(8,128)S(1)} %get-tuple-element.18), channel_id=1, source_target_pairs={{0,4},{4,8},{8,12},{12,16},{16,20},{20,24},{24,28},{1,5},{5,9},{9,... | collective-permute-start | bytes 187400 | tf_op jit(solution)/shard_map/ppermute | solution.py:29
  42.3 5.4 %collective-permute-start.6 = (f32[1,61,256]{2,1,0:T(8,128)S(1)}, f32[1,61,256]{2,1,0:T(8,128)S(1)}, u32[]{:S(2)}, u32[]{:S(2)}) collective-permute-start(f32[1,61,256]{2,1,0:T(8,128)S(1)} %get-tuple-element.19), channel_id=1, source_target_pairs={{4,0},{8,4},{12,8},{16,12},{20,16},{24,20},{28,24},{5,1},{9,5},{13... | collective-permute-start | bytes 187400 | tf_op jit(solution)/shard_map/ppermute | solution.py:29
  43.6 7.2 %collective-permute-start.10 = (f32[4,32,256]{2,1,0:T(8,128)S(1)}, f32[4,32,256]{2,1,0:T(8,128)S(1)}, u32[]{:S(2)}, u32[]{:S(2)}) collective-permute-start(f32[4,32,256]{2,1,0:T(8,128)S(1)} %add.59), channel_id=1, source_target_pairs={{0,16},{4,20},{8,24},{12,28},{16,0},{20,4},{24,8},{28,12},{1,17},{... | collective-permute-start | bytes 393224 | tf_op jit(solution)/shard_map/ppermute | solution.py:49
  47.8 13.8 %copy-start.2 = (bf16[24,45,256]{2,1,0:T(8,128)(2,1)S(1)}, bf16[24,45,256]{2,1,0:T(8,128)(2,1)}, u32[]{:S(2)}) copy-start(bf16[24,45,256]{2,1,0:T(8,128)(2,1)} %copy-done.1) | copy-start | bytes 1658884
  47.8 13.7 %collective-permute-start.8 = (f32[24,8,256]{2,1,0:T(8,128)S(1)}, f32[24,8,256]{2,1,0:T(8,128)S(1)}, u32[]{:S(2)}, u32[]{:S(2)}) collective-permute-start(f32[24,8,256]{2,1,0:T(8,128)S(1)} %slice.60), channel_id=1, source_target_pairs={{0,1},{1,2},{2,3},{3,0},{4,5},{5,6},{6,7},{7,4},{8,9},{9,10},{10,1... | collective-permute-start | bytes 589832 | tf_op jit(solution)/shard_map/ppermute | solution.py:34
  50.8 9.0 %collective-permute-start.11 = (f32[4,32,256]{2,1,0:T(8,128)S(1)}, f32[4,32,256]{2,1,0:T(8,128)S(1)}, u32[]{:S(2)}, u32[]{:S(2)}) collective-permute-start(f32[4,32,256]{2,1,0:T(8,128)S(1)} %add.60), channel_id=1, source_target_pairs={{0,1},{1,0},{2,3},{3,2},{4,5},{5,4},{6,7},{7,6},{8,9},{9,8},{10,11... | collective-permute-start | bytes 393224 | tf_op jit(solution)/shard_map/ppermute | solution.py:49
  52.0 9.5 %collective-permute-start.7 = (bf16[24,8,256]{2,1,0:T(8,128)(2,1)S(1)}, bf16[24,8,256]{2,1,0:T(8,128)(2,1)S(1)}, u32[]{:S(2)}, u32[]{:S(2)}) collective-permute-start(bf16[24,8,256]{2,1,0:T(8,128)(2,1)S(1)} %slice.72), channel_id=1, source_target_pairs={{0,3},{1,0},{2,1},{3,2},{4,7},{5,4},{6,5},{7,6},{8,11},{9,8},{10,9... | collective-permute-start | bytes 294920 | tf_op jit(solution)/shard_map/ppermute | solution.py:34
  59.9 7.7 %collective-permute-start.12 = (f32[4,32,256]{2,1,0:T(8,128)S(1)}, f32[4,32,256]{2,1,0:T(8,128)S(1)}, u32[]{:S(2)}, u32[]{:S(2)}) collective-permute-start(f32[4,32,256]{2,1,0:T(8,128)S(1)} %add.61), channel_id=1, source_target_pairs={{0,2},{1,3},{2,0},{3,1},{4,6},{5,7},{6,4},{7,5},{8,10},{9,11},{10,... | collective-permute-start | bytes 393224 | tf_op jit(solution)/shard_map/ppermute | solution.py:49

commit v19 on v15

--- a/solution.py
+++ b/solution.py
@@ -40,15 +40,13 @@
         if count & (count - 1):
             value = lax.psum(value, axis)
             continue
-        step = 1
-        while step < count:
-            if skip:
-                skip -= 1
-                step *= 2
-                continue
+        steps = [1 << k for k in range(count.bit_length() - 1)]
+        steps = steps[skip:]
+        skip = 0
+        steps = steps[::-1] if axis == "lat" else steps
+        for step in steps:
             partner = lax.ppermute(value, axis, [(i, i ^ step) for i in range(count)])
             value = value + partner
-            step *= 2
     return value
 
 

time: 68.9 us -> 68.8 us (level)
  starting transfers between devices: 22.6 us -> 20.4 us
  waiting for transfers between devices: 18 us -> 19.9 us
    ppermute x4, starting transfers between devices: 9.06 us -> 6.89 us  [butterfly_sum(): partner = lax.ppermute(value, axis, [(i, i ^ step) for i in range(count)])]
    ppermute x2, waiting for transfers between devices: 0.59 us -> 1.92 us  [from_behind(): return lax.ppermute(x, axis, [(i, (i + by) % size) for i in range(size)])]
where the time goes in v19:
time: 68.8 us; the launch traced here: 68.4 us
  starting transfers between devices  20.4 us (30%)
  waiting for transfers between devices  19.9 us (29%)
  Pallas kernels  11.4 us (17%)
  local copies, waits for them, and re-layouts  9.48 us (14%)
  other arithmetic  4.34 us (6%)
  matrix products  1.86 us (3%)
  between operations  1.01 us (1%)
    ppermute x4, waiting for transfers between devices, butterfly_sum(): partner = lax.ppermute(value, axis, [(i, i ^ step) for i in range(count)])  12.5 us
    pallas_call x1, Pallas kernels, local(): pl.pallas_call(forward_kernel, out_shape=(jax.ShapeDtypeStruct((row_count...  7.89 us
    ppermute x4, starting transfers between devices, butterfly_sum(): partner = lax.ppermute(value, axis, [(i, i ^ step) for i in range(count)])  6.89 us
    ppermute x2, waiting for transfers between devices, with_halo(): lax.ppermute(lax.slice_in_dim(block, 0, width, axis=dim), axis, backward)  4.3 us
    ppermute x2, starting transfers between devices, with_halo(): lax.ppermute(lax.slice_in_dim(block, block.shape[dim] - width, None, axis...  3.98 us
    ppermute x2, starting transfers between devices, with_halo(): lax.ppermute(lax.slice_in_dim(block, 0, width, axis=dim), axis, backward)  3.54 us
    pallas_call x1, Pallas kernels, local(): pl.pallas_call(adjoint_kernel, out_shape=jax.ShapeDtypeStruct(((row_count...  3.47 us
    unnamed x20, local copies, waits for them, and re-layouts  3.37 us
  transfers between devices with their start and end apart: 13, of which 7 were waited for; matrix products, arithmetic and copies ran while one was open for 15% of the time, Pallas kernels for 5%

profile of v19, /device:TPU:0, one launch (start us, length us, event | category | flops | bytes accessed | tf_op | source)
XLA Modules:
  0.0 68.4 jit_solution(1047827290912945271)
XLA Ops:
  0.6 0.0 copy-start
  0.6 0.0 copy-start.5
  0.7 1.0 %convert_element_type.46 = bf16[24,45,8]{1,2,0:T(8,128)(2,1)S(1)} convert(s32[24,45,8]{1,2,0:T(8,128)} %param.7) | non-fusion elementwise | flops 8640 | bytes 51840 | tf_op jit(solution)/shard_map/convert_element_type | solution.py:130
  1.6 0.2 copy.35
  1.9 0.1 reshape.114
  2.0 0.4 fusion.6
  2.4 0.2 reshape.115
  2.6 0.0 copy-done.5
  2.6 0.0 copy-start.1
  2.6 0.0 copy-start.7
  2.6 0.1 copy_multiply_fusion
  2.8 2.4 %collective-permute-start = (bf16[1,45,264]{2,1,0:T(8,128)(2,1)S(1)}, bf16[1,45,264]{2,1,0:T(8,128)(2,1)S(1)}, u32[]{:S(2)}, u32[]{:S(2)}) collective-permute-start(bf16[1,45,264]{2,1,0:T(8,128)(2,1)S(1)} %get-tuple-element.22), channel_id=1, source_target_pairs={{0,4},{4,8},{8,12},{12,16},{16,20},{20,24},{24,28},{1,5},{5,9},{9,... | collective-permute-start | bytes 71288 | tf_op jit(solution)/shard_map/ppermute | solution.py:18
  5.2 1.3 %collective-permute-start.1 = (bf16[1,45,264]{2,1,0:T(8,128)(2,1)S(1)}, bf16[1,45,264]{2,1,0:T(8,128)(2,1)S(1)}, u32[]{:S(2)}, u32[]{:S(2)}) collective-permute-start(bf16[1,45,264]{2,1,0:T(8,128)(2,1)S(1)} %get-tuple-element.23), channel_id=1, source_target_pairs={{4,0},{8,4},{12,8},{16,12},{20,16},{24,20},{28,24},{5,1},{9,5},{13... | collective-permute-start | bytes 71288 | tf_op jit(solution)/shard_map/ppermute | solution.py:21
  6.5 0.0 copy-done
  6.5 0.1 constant_dynamic-slice_fusion
  6.6 0.2 copy.48
  6.8 0.0 copy-done.7
  6.8 0.1 compare_convert_fusion
  6.9 0.1 copy.37
  7.0 0.0 copy-start.6
  7.0 1.1 %fusion.18 = bf16[24,4,3,48,64]{4,0,3,2,1:T(8,128)(2,1)S(1)} fusion(s32[48,64]{1,0:T(8,128)S(1)} %iota_subtract_fusion, pred[48]{0:T(512)(128)(4,1)S(1)} %iota_compare_fusion.6, bf16[24,4,3,17]{3,0,2,1:T(8,128)(2,1)S(1)} %copy.48, bf16[24,17]{1,0:T(8,128)(2,1)S(1)} %constant_dynamic-slice_fusion.1), kind=kOutput, calls=%fused_computation.27 | convolution fusion | flops 30205056 | bytes 1792416 | tf_op jit(solution)/shard_map/ibae,ejp->ibajp/dot_general | solution.py:162
  8.2 0.0 collective-permute-done
  8.2 2.2 %collective-permute-done.1 = bf16[1,45,264]{2,1,0:T(8,128)(2,1)S(1)} collective-permute-done((bf16[1,45,264]{2,1,0:T(8,128)(2,1)S(1)}, bf16[1,45,264]{2,1,0:T(8,128)(2,1)S(1)}, u32[]{:S(2)}, u32[]{:S(2)}) %collective-permute-start.1) | collective-permute-done | bytes 23792 | tf_op jit(solution)/shard_map/ppermute | solution.py:21
  10.4 0.8 %pad_maximum_fusion.3 = (bf16[26,8,264]{2,1,0:T(8,128)(2,1)}, bf16[26,8,264]{2,1,0:T(8,128)(2,1)}) fusion(bf16[1,45,264]{2,1,0:T(8,128)(2,1)S(1)} %collective-permute-done.1, bf16[1,45,264]{2,1,0:T(8,128)(2,1)S(1)} %collective-permute-done, bf16[24,45,8]{2,1,0:T(8,128)(2,1)S(1)} %copy.35, bf16[24,45,256]{2,1,0:T(8,128)(2,1)S(1)} %copy_multiply_fusion), kind=kLoop, calls=%fused_computation.35 | loop fusion | flops 878592 | bytes 837408 | tf_op jit(solution)/shard_map/slice | solution.py:19
  11.2 1.6 %collective-permute-start.2 = (bf16[26,8,264]{2,1,0:T(8,128)(2,1)}, bf16[26,8,264]{2,1,0:T(8,128)(2,1)S(1)}, u32[]{:S(2)}, u32[]{:S(2)}) collective-permute-start(bf16[26,8,264]{2,1,0:T(8,128)(2,1)} %get-tuple-element.20), channel_id=1, source_target_pairs={{0,1},{1,2},{2,3},{3,0},{4,5},{5,6},{6,7},{7,4},{8,9},{9,10},{10,1... | collective-permute-start | bytes 329480 | tf_op jit(solution)/shard_map/ppermute | solution.py:18
  12.7 2.2 %collective-permute-start.3 = (bf16[26,8,264]{2,1,0:T(8,128)(2,1)}, bf16[26,8,264]{2,1,0:T(8,128)(2,1)}, u32[]{:S(2)}, u32[]{:S(2)}) collective-permute-start(bf16[26,8,264]{2,1,0:T(8,128)(2,1)} %get-tuple-element.21), channel_id=1, source_target_pairs={{1,0},{2,1},{3,2},{0,3},{5,4},{6,5},{7,6},{4,7},{9,8},{10,9},{11,1... | collective-permute-start | bytes 329480 | tf_op jit(solution)/shard_map/ppermute | solution.py:21
  15.0 0.7 multiply_bitcast_fusion
  15.7 2.6 %copy.52.t_ref = bf16[24,4,3,48,64]{4,3,2,1,0:T(8,128)(2,1)} copy(bf16[24,4,3,48,64]{4,0,3,2,1:T(8,128)(2,1)S(1)} %fusion.18) | data formatting | bytes 3538944 | tf_op jit(solution)/shard_map/ibae,ejp->ibajp/dot_general | solution.py:162
  18.3 1.4 %reshape.118.w_ref = bf16[4,256,256]{2,1,0:T(8,128)(2,1)S(1)} reshape(bf16[4,8,32,8,32]{4,3,2,1,0:T(8,128)(2,1)S(1)} %multiply_bitcast_fusion) | data formatting | bytes 1048576 | tf_op jit(solution)/shard_map/reshape | solution.py:167
  19.7 0.0 copy-start.4
  19.7 1.2 %copy.40 = bf16[24,45,256]{2,1,0:T(8,128)(2,1)S(1)} copy(bf16[24,45,256]{2,0,1:T(8,128)(2,1)} %param.11) | data formatting | bytes 1105920 | tf_op args[5]
  21.0 0.0 collective-permute-done.2
  21.0 2.1 %collective-permute-done.3 = bf16[26,8,264]{2,1,0:T(8,128)(2,1)} collective-permute-done((bf16[26,8,264]{2,1,0:T(8,128)(2,1)}, bf16[26,8,264]{2,1,0:T(8,128)(2,1)}, u32[]{:S(2)}, u32[]{:S(2)}) %collective-permute-start.3) | collective-permute-done | bytes 109856 | tf_op jit(solution)/shard_map/ppermute | solution.py:21
  23.1 1.2 %fusion.9 = bf16[26,64,264]{2,1,0:T(8,128)(2,1)S(1)} fusion(bf16[26,8,264]{2,1,0:T(8,128)(2,1)} %collective-permute-done.3, bf16[26,8,264]{2,1,0:T(8,128)(2,1)S(1)} %collective-permute-done.2, bf16[1,45,264]{2,1,0:T(8,128)(2,1)S(1)} %collective-permute-done.1, bf16[1,45,264]{2,1,0:T(8,128)(2,1)S(1)} %collective-permute-done, ...), kind=kLoop, calls=%fused_computation.15 | loop fusion | flops 8346624 | bytes 1716000 | tf_op jit(solution)/shard_map/concatenate | solution.py:22
  24.4 0.1 slice.54
  24.4 0.1 slice.53
  24.5 0.4 convolution_convert_fusion.m_ref
  24.9 7.9 %shard_map.85 = (bf16[24,45,256]{2,1,0:T(8,128)(2,1)S(1)}, f32[4,32,256]{2,1,0:T(8,128)S(1)}, bf16[4,1152,256]{2,1,0:T(8,128)(2,1)S(1)}) custom-call(bf16[1664,256]{1,0:T(8,128)(2,1)S(1)} %bitcast.28, bf16[1664,256]{1,0:T(8,128)(2,1)S(1)} %convolution_convert_fusion.m_ref, bf16[24,4,3,48,64]{4,3,2,1,0:T(8,128)(2,1)} %copy.52.t_ref, ...), custom_call_target="tpu_custom_call" | custom-call | flops 2717908992 | bytes 3407872 | tf_op jit(solution)/shard_map/pallas_call | solution.py:172
  32.8 0.2 collective-permute-start.4
  33.0 1.2 %collective-permute-done.4.order_ref = f32[4,32,256]{2,1,0:T(8,128)S(1)} collective-permute-done((f32[4,32,256]{2,1,0:T(8,128)S(1)}, f32[4,32,256]{2,1,0:T(8,128)S(1)}, u32[]{:S(2)}, u32[]{:S(2)}) %collective-permute-start.4) | collective-permute-done | bytes 131104 | tf_op jit(solution)/shard_map/ppermute | solution.py:196
  34.2 3.3 %collective-permute-start.9 = (f32[4,32,256]{2,1,0:T(8,128)S(1)}, f32[4,32,256]{2,1,0:T(8,128)S(1)}, u32[]{:S(2)}, u32[]{:S(2)}) collective-permute-start(f32[4,32,256]{2,1,0:T(8,128)S(1)} %add.58), channel_id=1, source_target_pairs={{0,16},{4,20},{8,24},{12,28},{16,0},{20,4},{24,8},{28,12},{1,17},{... | collective-permute-start | bytes 393224 | tf_op jit(solution)/shard_map/ppermute | solution.py:48
  37.5 3.5 %shard_map.86 = f32[1664,256]{1,0:T(8,128)S(1)} custom-call(bf16[24,4,3,48,64]{4,3,2,1,0:T(8,128)(2,1)} %copy.52.t_ref, bf16[4,1152,256]{2,1,0:T(8,128)(2,1)S(1)} %get-tuple-element.7.pulled_ref, f32[4,32,256]{2,1,0:T(8,128)S(1)} %collective-permute-done.4.order_ref), custom_call_target="tpu_custom_call" | custom-call | flops 452984832 | bytes 2555904 | tf_op jit(solution)/shard_map/pallas_call | solution.py:204
  41.0 1.8 %collective-permute-start.5 = (f32[1,61,256]{2,1,0:T(8,128)S(1)}, f32[1,61,256]{2,1,0:T(8,128)S(1)}, u32[]{:S(2)}, u32[]{:S(2)}) collective-permute-start(f32[1,61,256]{2,1,0:T(8,128)S(1)} %get-tuple-element.18), channel_id=1, source_target_pairs={{0,4},{4,8},{8,12},{12,16},{16,20},{20,24},{24,28},{1,5},{5,9},{9,... | collective-permute-start | bytes 187400 | tf_op jit(solution)/shard_map/ppermute | solution.py:29
  42.8 1.3 %collective-permute-start.6 = (f32[1,61,256]{2,1,0:T(8,128)S(1)}, f32[1,61,256]{2,1,0:T(8,128)S(1)}, u32[]{:S(2)}, u32[]{:S(2)}) collective-permute-start(f32[1,61,256]{2,1,0:T(8,128)S(1)} %get-tuple-element.19), channel_id=1, source_target_pairs={{4,0},{8,4},{12,8},{16,12},{20,16},{24,20},{28,24},{5,1},{9,5},{13... | collective-permute-start | bytes 187400 | tf_op jit(solution)/shard_map/ppermute | solution.py:29
  44.1 0.0 collective-permute-done.9
  44.2 2.3 %collective-permute-start.10 = (f32[4,32,256]{2,1,0:T(8,128)S(1)}, f32[4,32,256]{2,1,0:T(8,128)S(1)}, u32[]{:S(2)}, u32[]{:S(2)}) collective-permute-start(f32[4,32,256]{2,1,0:T(8,128)S(1)} %add.59), channel_id=1, source_target_pairs={{0,8},{4,12},{8,0},{12,4},{16,24},{20,28},{24,16},{28,20},{1,9},{5... | collective-permute-start | bytes 393224 | tf_op jit(solution)/shard_map/ppermute | solution.py:48
  46.5 0.0 collective-permute-done.5
  46.5 0.0 collective-permute-done.6
  46.5 0.1 fusion.7
  46.6 0.0 copy-start.2
  46.7 1.2 %collective-permute-start.8 = (f32[24,8,256]{2,1,0:T(8,128)S(1)}, f32[24,8,256]{2,1,0:T(8,128)S(1)}, u32[]{:S(2)}, u32[]{:S(2)}) collective-permute-start(f32[24,8,256]{2,1,0:T(8,128)S(1)} %slice.60), channel_id=1, source_target_pairs={{0,1},{1,2},{2,3},{3,0},{4,5},{5,6},{6,7},{7,4},{8,9},{9,10},{10,1... | collective-permute-start | bytes 589832 | tf_op jit(solution)/shard_map/ppermute | solution.py:34
  47.8 3.6 %collective-permute-done.10 = f32[4,32,256]{2,1,0:T(8,128)S(1)} collective-permute-done((f32[4,32,256]{2,1,0:T(8,128)S(1)}, f32[4,32,256]{2,1,0:T(8,128)S(1)}, u32[]{:S(2)}, u32[]{:S(2)}) %collective-permute-start.10) | collective-permute-done | bytes 131104 | tf_op jit(solution)/shard_map/ppermute | solution.py:48
  51.4 1.2 %collective-permute-start.11 = (f32[4,32,256]{2,1,0:T(8,128)S(1)}, f32[4,32,256]{2,1,0:T(8,128)S(1)}, u32[]{:S(2)}, u32[]{:S(2)}) collective-permute-start(f32[4,32,256]{2,1,0:T(8,128)S(1)} %add.60), channel_id=1, source_target_pairs={{0,1},{1,0},{2,3},{3,2},{4,5},{5,4},{6,7},{7,6},{8,9},{9,8},{10,11... | collective-permute-start | bytes 393224 | tf_op jit(solution)/shard_map/ppermute | solution.py:48
  52.6 1.6 %collective-permute-start.7 = (bf16[24,8,256]{2,1,0:T(8,128)(2,1)S(1)}, bf16[24,8,256]{2,1,0:T(8,128)(2,1)S(1)}, u32[]{:S(2)}, u32[]{:S(2)}) collective-permute-start(bf16[24,8,256]{2,1,0:T(8,128)(2,1)S(1)} %slice.72), channel_id=1, source_target_pairs={{0,3},{1,0},{2,1},{3,2},{4,7},{5,4},{6,5},{7,6},{8,11},{9,8},{10,9... | collective-permute-start | bytes 294920 | tf_op jit(solution)/shard_map/ppermute | solution.py:34
  54.2 1.0 %copy.43 = bf16[24,45,256]{2,0,1:T(8,128)(2,1)} copy(bf16[24,45,256]{2,1,0:T(8,128)(2,1)S(1)} %get-tuple-element.15) | data formatting | bytes 1105920
  55.2 4.0 %collective-permute-done.11 = f32[4,32,256]{2,1,0:T(8,128)S(1)} collective-permute-done((f32[4,32,256]{2,1,0:T(8,128)S(1)}, f32[4,32,256]{2,1,0:T(8,128)S(1)}, u32[]{:S(2)}, u32[]{:S(2)}) %collective-permute-start.11) | collective-permute-done | bytes 131104 | tf_op jit(solution)/shard_map/ppermute | solution.py:48
  59.2 0.1 collective-permute-start.12
  59.3 1.9 %collective-permute-done.7 = bf16[24,8,256]{2,1,0:T(8,128)(2,1)S(1)} collective-permute-done((bf16[24,8,256]{2,1,0:T(8,128)(2,1)S(1)}, bf16[24,8,256]{2,1,0:T(8,128)(2,1)S(1)}, u32[]{:S(2)}, u32[]{:S(2)}) %collective-permute-start.7) | collective-permute-done | bytes 98336 | tf_op jit(solution)/shard_map/ppermute | solution.py:34
  61.2 0.0 collective-permute-done.8
  61.2 0.2 fusion.15
  61.5 1.0 %copy.44 = bf16[24,45,256]{2,0,1:T(8,128)(2,1)} copy(bf16[24,45,256]{2,1,0:T(8,128)(2,1)S(1)} %fusion.15) | data formatting | bytes 1105920
  62.4 4.9 %collective-permute-done.12 = f32[4,32,256]{2,1,0:T(8,128)S(1)} collective-permute-done((f32[4,32,256]{2,1,0:T(8,128)S(1)}, f32[4,32,256]{2,1,0:T(8,128)S(1)}, u32[]{:S(2)}, u32[]{:S(2)}) %collective-permute-start.12) | collective-permute-done | bytes 131104 | tf_op jit(solution)/shard_map/ppermute | solution.py:48
  67.3 0.2 reshape.120
  67.5 0.9 %copy.55 = f32[4,32,8,32]{3,1,0,2:T(8,128)} copy(f32[4,32,8,32]{3,2,1,0:T(8,128)S(1)} %reshape.120) | data formatting | bytes 262144 | tf_op jit(solution)/shard_map/reshape | solution.py:202
  (23 shorter events, 0.3 us)
Async XLA Ops:
  0.6 5.9 %copy-start = (bf16[192,4,3,17]{0,1,3,2:T(4,128)(2,1)S(1)}, bf16[192,4,3,17]{0,1,3,2:T(4,128)(2,1)}, u32[]{:S(2)}) copy-start(bf16[192,4,3,17]{0,1,3,2:T(4,128)(2,1)} %param.8) | copy-start | bytes 235012
  0.6 1.9 %copy-start.5 = (bf16[24,45,256]{2,0,1:T(8,128)(2,1)S(1)}, bf16[24,45,256]{2,0,1:T(8,128)(2,1)}, u32[]{:S(2)}) copy-start(bf16[24,45,256]{2,0,1:T(8,128)(2,1)} %param.6) | copy-start | bytes 1658884
  1.9 8.5 %copy-start.3 = (bf16[24,45,8]{2,1,0:T(8,128)(2,1)}, bf16[24,45,8]{2,1,0:T(8,128)(2,1)S(1)}, u32[]{:S(2)}) copy-start(bf16[24,45,8]{2,1,0:T(8,128)(2,1)S(1)} %copy.35) | copy-start | bytes 51844
  2.6 5.6 %copy-start.1 = (bf16[24,45,256]{2,1,0:T(8,128)(2,1)}, bf16[24,45,256]{2,1,0:T(8,128)(2,1)S(1)}, u32[]{:S(2)}) copy-start(bf16[24,45,256]{2,1,0:T(8,128)(2,1)S(1)} %reshape.115) | copy-start | bytes 1658884
  2.6 4.2 %copy-start.7 = (s32[192]{0:T(256)S(1)}, s32[192]{0:T(256)}, u32[]{:S(2)}) copy-start(s32[192]{0:T(256)} %param.9) | copy-start | bytes 2308
  2.8 5.4 %collective-permute-start = (bf16[1,45,264]{2,1,0:T(8,128)(2,1)S(1)}, bf16[1,45,264]{2,1,0:T(8,128)(2,1)S(1)}, u32[]{:S(2)}, u32[]{:S(2)}) collective-permute-start(bf16[1,45,264]{2,1,0:T(8,128)(2,1)S(1)} %get-tuple-element.22), channel_id=1, source_target_pairs={{0,4},{4,8},{8,12},{12,16},{16,20},{20,24},{24,28},{1,5},{5,9},{9,... | collective-permute-start | bytes 71288 | tf_op jit(solution)/shard_map/ppermute | solution.py:18
  5.2 5.2 %collective-permute-start.1 = (bf16[1,45,264]{2,1,0:T(8,128)(2,1)S(1)}, bf16[1,45,264]{2,1,0:T(8,128)(2,1)S(1)}, u32[]{:S(2)}, u32[]{:S(2)}) collective-permute-start(bf16[1,45,264]{2,1,0:T(8,128)(2,1)S(1)} %get-tuple-element.23), channel_id=1, source_target_pairs={{4,0},{8,4},{12,8},{16,12},{20,16},{24,20},{28,24},{5,1},{9,5},{13... | collective-permute-start | bytes 71288 | tf_op jit(solution)/shard_map/ppermute | solution.py:21
  7.0 8.0 %copy-start.6 = (bf16[8,4,32,32]{3,2,1,0:T(8,128)(2,1)S(1)}, bf16[8,4,32,32]{3,2,1,0:T(8,128)(2,1)}, u32[]{:S(2)}) copy-start(bf16[8,4,32,32]{3,2,1,0:T(8,128)(2,1)} %param.10) | copy-start | bytes 196612
  11.2 9.8 %collective-permute-start.2 = (bf16[26,8,264]{2,1,0:T(8,128)(2,1)}, bf16[26,8,264]{2,1,0:T(8,128)(2,1)S(1)}, u32[]{:S(2)}, u32[]{:S(2)}) collective-permute-start(bf16[26,8,264]{2,1,0:T(8,128)(2,1)} %get-tuple-element.20), channel_id=1, source_target_pairs={{0,1},{1,2},{2,3},{3,0},{4,5},{5,6},{6,7},{7,4},{8,9},{9,10},{10,1... | collective-permute-start | bytes 329480 | tf_op jit(solution)/shard_map/ppermute | solution.py:18
  12.7 10.4 %collective-permute-start.3 = (bf16[26,8,264]{2,1,0:T(8,128)(2,1)}, bf16[26,8,264]{2,1,0:T(8,128)(2,1)}, u32[]{:S(2)}, u32[]{:S(2)}) collective-permute-start(bf16[26,8,264]{2,1,0:T(8,128)(2,1)} %get-tuple-element.21), channel_id=1, source_target_pairs={{1,0},{2,1},{3,2},{0,3},{5,4},{6,5},{7,6},{4,7},{9,8},{10,9},{11,1... | collective-permute-start | bytes 329480 | tf_op jit(solution)/shard_map/ppermute | solution.py:21
  19.7 3.4 %copy-start.4 = (bf16[24,45,8]{2,1,0:T(8,128)(2,1)S(1)}, bf16[24,45,8]{2,1,0:T(8,128)(2,1)}, u32[]{:S(2)}) copy-start(bf16[24,45,8]{2,1,0:T(8,128)(2,1)} %copy-done.3) | copy-start | bytes 51844
  32.8 1.4 %collective-permute-start.4 = (f32[4,32,256]{2,1,0:T(8,128)S(1)}, f32[4,32,256]{2,1,0:T(8,128)S(1)}, u32[]{:S(2)}, u32[]{:S(2)}) collective-permute-start(f32[4,32,256]{2,1,0:T(8,128)S(1)} %get-tuple-element.8), channel_id=1, source_target_pairs={{0,4},{4,0},{8,12},{12,8},{16,20},{20,16},{24,28},{28,24},{1,5},{5... | collective-permute-start | bytes 393224 | tf_op jit(solution)/shard_map/ppermute | solution.py:196
  34.2 9.9 %collective-permute-start.9 = (f32[4,32,256]{2,1,0:T(8,128)S(1)}, f32[4,32,256]{2,1,0:T(8,128)S(1)}, u32[]{:S(2)}, u32[]{:S(2)}) collective-permute-start(f32[4,32,256]{2,1,0:T(8,128)S(1)} %add.58), channel_id=1, source_target_pairs={{0,16},{4,20},{8,24},{12,28},{16,0},{20,4},{24,8},{28,12},{1,17},{... | collective-permute-start | bytes 393224 | tf_op jit(solution)/shard_map/ppermute | solution.py:48
  41.0 5.5 %collective-permute-start.5 = (f32[1,61,256]{2,1,0:T(8,128)S(1)}, f32[1,61,256]{2,1,0:T(8,128)S(1)}, u32[]{:S(2)}, u32[]{:S(2)}) collective-permute-start(f32[1,61,256]{2,1,0:T(8,128)S(1)} %get-tuple-element.18), channel_id=1, source_target_pairs={{0,4},{4,8},{8,12},{12,16},{16,20},{20,24},{24,28},{1,5},{5,9},{9,... | collective-permute-start | bytes 187400 | tf_op jit(solution)/shard_map/ppermute | solution.py:29
  42.8 3.7 %collective-permute-start.6 = (f32[1,61,256]{2,1,0:T(8,128)S(1)}, f32[1,61,256]{2,1,0:T(8,128)S(1)}, u32[]{:S(2)}, u32[]{:S(2)}) collective-permute-start(f32[1,61,256]{2,1,0:T(8,128)S(1)} %get-tuple-element.19), channel_id=1, source_target_pairs={{4,0},{8,4},{12,8},{16,12},{20,16},{24,20},{28,24},{5,1},{9,5},{13... | collective-permute-start | bytes 187400 | tf_op jit(solution)/shard_map/ppermute | solution.py:29
  44.2 7.2 %collective-permute-start.10 = (f32[4,32,256]{2,1,0:T(8,128)S(1)}, f32[4,32,256]{2,1,0:T(8,128)S(1)}, u32[]{:S(2)}, u32[]{:S(2)}) collective-permute-start(f32[4,32,256]{2,1,0:T(8,128)S(1)} %add.59), channel_id=1, source_target_pairs={{0,8},{4,12},{8,0},{12,4},{16,24},{20,28},{24,16},{28,20},{1,9},{5... | collective-permute-start | bytes 393224 | tf_op jit(solution)/shard_map/ppermute | solution.py:48
  46.6 14.6 %copy-start.2 = (bf16[24,45,256]{2,1,0:T(8,128)(2,1)S(1)}, bf16[24,45,256]{2,1,0:T(8,128)(2,1)}, u32[]{:S(2)}) copy-start(bf16[24,45,256]{2,1,0:T(8,128)(2,1)} %copy-done.1) | copy-start | bytes 1658884
  46.7 14.5 %collective-permute-start.8 = (f32[24,8,256]{2,1,0:T(8,128)S(1)}, f32[24,8,256]{2,1,0:T(8,128)S(1)}, u32[]{:S(2)}, u32[]{:S(2)}) collective-permute-start(f32[24,8,256]{2,1,0:T(8,128)S(1)} %slice.60), channel_id=1, source_target_pairs={{0,1},{1,2},{2,3},{3,0},{4,5},{5,6},{6,7},{7,4},{8,9},{9,10},{10,1... | collective-permute-start | bytes 589832 | tf_op jit(solution)/shard_map/ppermute | solution.py:34
  51.4 7.8 %collective-permute-start.11 = (f32[4,32,256]{2,1,0:T(8,128)S(1)}, f32[4,32,256]{2,1,0:T(8,128)S(1)}, u32[]{:S(2)}, u32[]{:S(2)}) collective-permute-start(f32[4,32,256]{2,1,0:T(8,128)S(1)} %add.60), channel_id=1, source_target_pairs={{0,1},{1,0},{2,3},{3,2},{4,5},{5,4},{6,7},{7,6},{8,9},{9,8},{10,11... | collective-permute-start | bytes 393224 | tf_op jit(solution)/shard_map/ppermute | solution.py:48
  52.6 8.6 %collective-permute-start.7 = (bf16[24,8,256]{2,1,0:T(8,128)(2,1)S(1)}, bf16[24,8,256]{2,1,0:T(8,128)(2,1)S(1)}, u32[]{:S(2)}, u32[]{:S(2)}) collective-permute-start(bf16[24,8,256]{2,1,0:T(8,128)(2,1)S(1)} %slice.72), channel_id=1, source_target_pairs={{0,3},{1,0},{2,1},{3,2},{4,7},{5,4},{6,5},{7,6},{8,11},{9,8},{10,9... | collective-permute-start | bytes 294920 | tf_op jit(solution)/shard_map/ppermute | solution.py:34
  59.2 8.1 %collective-permute-start.12 = (f32[4,32,256]{2,1,0:T(8,128)S(1)}, f32[4,32,256]{2,1,0:T(8,128)S(1)}, u32[]{:S(2)}, u32[]{:S(2)}) collective-permute-start(f32[4,32,256]{2,1,0:T(8,128)S(1)} %add.61), channel_id=1, source_target_pairs={{0,2},{1,3},{2,0},{3,1},{4,6},{5,7},{6,4},{7,5},{8,10},{9,11},{10,... | collective-permute-start | bytes 393224 | tf_op jit(solution)/shard_map/ppermute | solution.py:48
